TPU v7x, 128 devices: a whole 4x4x4 slice. The times are simulated.
128 devices in a mesh: seq: 32 (over x, y_hi, z), mp: 4 (over y_lo, core).
Axes of the slice: x: 4, y: 4 (y_hi: 2, y_lo: 2; y = y_hi * 2 + y_lo), z: 4, core: 2. Of those that a mesh axis runs over, the one named last changes fastest.
Arguments:
- hidden_in: bfloat16 [8192, 1536], P('seq', 'mp'), may hold values from -6 to 6
- wq: bfloat16 [1536, 1536], P('seq', 'mp'), may hold values from -1 to 1
- wkv: bfloat16 [1536, 512], P('seq'), may hold values from -0.15625 to 0.15625
- wo: bfloat16 [1536, 1536], P('mp', 'seq'), may hold values from -0.15625 to 0.15625
- lengths: int32 [3], replicated, may hold values from 1 to 6144, 8192 in all
- routes: int32 [8192, 4], P('seq'), may hold values from 0 to 31, all different within a row; in each aligned block of 256 rows (0 to 255, 256 to 511, ...) at most 64 rows name the same one
- gate_logits: float32 [8192, 4], P('seq'), may hold values from -6 to 6
- expert_gate: bfloat16 [32, 768, 1536], P('seq', 'mp'), may hold values from -0.15625 to 0.15625
- expert_up: bfloat16 [32, 768, 1536], P('seq', 'mp'), may hold values from -0.15625 to 0.15625
- expert_down: bfloat16 [32, 768, 1536], P('seq', 'mp'), may hold values from -0.21875 to 0.21875
Outputs:
- layer_out: bfloat16 [8192, 1536], P('seq', 'mp')
Inputs may be any that keep to these rules, and one draw needn't show every extreme that they name: `lengths`: sum to 8192; the longest is exactly 6144. `routes`: a token's 4 experts differ; among the rows of one device no expert is named more than 64 times, a bound that some block reaches.
All inputs are finite; a program needn't handle non-finite values.
Results may differ from a plain program's by a relative error of at most 0.018.
Values may be sent and summed in bfloat16 or wider, within the bound.
No kernel may reach another device: no remote copies, remote signals or barrier semaphores. Data moves between devices by JAX's collectives and lax.ppermute only.
A program may use at most 128 MiB of HBM per device.

v0:
```python
import math

import jax
import jax.numpy as jnp
from jax import lax
from jax.sharding import PartitionSpec as P

D = 1536
HQ = 12
KVH = 2
HD = 128
WINDOW = 4096


ROPE_BASE = 1500000.0
EPSILON = 1e-06


def prompt_ids(index, lengths):
    first_end = lengths[0]
    second_end = lengths[0] + lengths[1]
    prompt = (index >= first_end).astype(jnp.int32) + (index >= second_end).astype(jnp.int32)
    begin = jnp.where(index >= second_end, second_end, jnp.where(index >= first_end, first_end, 0))
    return (prompt, index - begin)


def rotary(values, position):
    half_dim = values.shape[-1] // 2
    freqs = jnp.exp(
        jnp.arange(half_dim, dtype=jnp.float32) * (-2.0 * math.log(ROPE_BASE) / values.shape[-1])
    )
    angles = position.astype(jnp.float32)[:, None] * freqs[None, :]
    cosine = jnp.cos(angles)[:, None, :]
    sine = jnp.sin(angles)[:, None, :]
    front = values[..., :half_dim]
    latter = values[..., half_dim:]
    return jnp.concatenate(
        [front * cosine - latter * sine, latter * cosine + front * sine], axis=-1
    )


def attend(carry, piece, queries, query_index, lengths):
    peak, total, accum = carry
    key_rows = piece[:, 0, :]
    value_rows = piece[:, 1, :].astype(jnp.float32)
    scores = jnp.einsum(
        "hqd,kd->hqk", queries, key_rows, preferred_element_type=jnp.float32
    ) * HD ** (-0.5)
    key_index = jnp.arange(piece.shape[0], dtype=jnp.int32)
    query_prompt, _ = prompt_ids(query_index, lengths)
    key_prompt, _ = prompt_ids(key_index, lengths)
    spacing = query_index[:, None] - key_index[None, :]
    allowed = (
        (query_prompt[:, None] == key_prompt[None, :])
        & (spacing >= 0)
        & (spacing < WINDOW)
        & (key_index[None, :] >= 0)
    )[None]
    masked = jnp.where(allowed, scores, -1e30)
    new_peak = jnp.maximum(peak, jnp.max(masked, axis=-1))
    weights = jnp.where(allowed, jnp.exp(masked - new_peak[..., None]), 0.0)
    total = jnp.sum(weights, axis=-1)
    accum = jnp.einsum("hqk,kd->hqd", weights, value_rows)
    return (new_peak, total, accum)


def local(
    hidden_in, wq, wkv, wo, lengths, routes, gate_logits, expert_gate, expert_up, expert_down
):
    tok_rows = hidden_in.shape[0]
    seq_index = lax.axis_index("seq")
    mp_index = lax.axis_index("mp")
    seq_count = lax.axis_size("seq")
    whole = lax.all_gather(hidden_in, "mp", axis=1, tiled=True)
    whole_f = whole.astype(jnp.float32)
    normed = (
        whole_f * lax.rsqrt(jnp.sum(whole_f * whole_f, axis=-1, keepdims=True) / D + EPSILON)
    ).astype(jnp.bfloat16)
    heads_here = wq.shape[1] // HD
    query_lin = jnp.dot(
        normed, lax.all_gather(wq, "seq", axis=0, tiled=True), preferred_element_type=jnp.float32
    )
    kv_lin = jnp.dot(
        normed, lax.all_gather(wkv, "seq", axis=0, tiled=True), preferred_element_type=jnp.float32
    )
    own_index = seq_index * tok_rows + jnp.arange(tok_rows, dtype=jnp.int32)
    _, own_pos = prompt_ids(own_index, lengths)
    queries = (
        rotary(query_lin.reshape(tok_rows, heads_here, HD), own_pos)
        .astype(jnp.bfloat16)
        .transpose(1, 0, 2)
    )
    kv_group = mp_index * heads_here // (HQ // KVH)
    key_all = kv_lin[:, : KVH * HD].reshape(tok_rows, KVH, HD)
    value_all = kv_lin[:, KVH * HD :].reshape(tok_rows, KVH, HD)
    key_own = rotary(lax.dynamic_slice_in_dim(key_all, kv_group, 1, 1), own_pos)[:, 0, :]
    value_own = lax.dynamic_slice_in_dim(value_all, kv_group, 1, 1)[:, 0, :]
    kv_own = jnp.stack([key_own.astype(jnp.bfloat16), value_own.astype(jnp.bfloat16)], axis=1)
    start_attn = (
        jnp.full((heads_here, tok_rows), -1e30, jnp.float32),
        jnp.zeros((heads_here, tok_rows), jnp.float32),
        jnp.zeros((heads_here, tok_rows, HD), jnp.float32),
    )
    carry = attend(
        start_attn, lax.all_gather(kv_own, "seq", axis=0, tiled=True), queries, own_index, lengths
    )
    _, total, accum = carry
    attended = (
        (accum / total[..., None])
        .transpose(1, 0, 2)
        .reshape(tok_rows, heads_here * HD)
        .astype(jnp.bfloat16)
    )
    partial_out = jnp.dot(
        attended, lax.all_gather(wo, "seq", axis=1, tiled=True), preferred_element_type=jnp.float32
    )
    attn_mine = lax.psum_scatter(
        partial_out.astype(jnp.bfloat16), "mp", scatter_dimension=1, tiled=True
    ).astype(jnp.float32)
    residual = (hidden_in.astype(jnp.float32) + attn_mine).astype(jnp.bfloat16)
    residual_f = residual.astype(jnp.float32)
    square_sum = lax.psum(jnp.sum(residual_f * residual_f, axis=-1), "mp")
    moe_local = (residual_f * lax.rsqrt(square_sum / D + EPSILON)[:, None]).astype(jnp.bfloat16)
    local_experts = expert_gate.shape[0]
    experts = seq_count * local_experts
    top_count = routes.shape[1]
    capacity = 2 * tok_rows * top_count // experts
    flat_ids = routes.reshape(-1)
    one_hot = (flat_ids[:, None] == jnp.arange(experts, dtype=jnp.int32)[None, :]).astype(jnp.int32)
    earlier_count = jnp.sum((jnp.cumsum(one_hot, axis=0) - one_hot) * one_hot, axis=1)
    slot_index = flat_ids * capacity + earlier_count
    source_row = jnp.arange(tok_rows * top_count, dtype=jnp.int32) // top_count
    full_rows = lax.all_gather(moe_local, "mp", axis=1, tiled=True)
    buffer = (
        jnp.zeros((experts * capacity, full_rows.shape[1]), jnp.bfloat16)
        .at[slot_index]
        .set(full_rows[source_row])
    )
    arrived = lax.all_to_all(
        buffer.reshape(experts, capacity, full_rows.shape[1]),
        "seq",
        split_axis=0,
        concat_axis=0,
        tiled=True,
    )
    arrived = arrived.reshape(seq_count, local_experts, capacity, D)
    gate_act = jnp.einsum(
        "secd,efd->secf", arrived, expert_gate, preferred_element_type=jnp.float32
    )
    up_act = jnp.einsum("secd,efd->secf", arrived, expert_up, preferred_element_type=jnp.float32)
    active = (jnp.maximum(gate_act, 0.0) * up_act).astype(jnp.bfloat16)
    partial_expert = jnp.einsum(
        "secf,efd->secd", active, expert_down, preferred_element_type=jnp.float32
    )
    summed = lax.psum_scatter(
        partial_expert.astype(jnp.bfloat16), "mp", scatter_dimension=3, tiled=True
    )
    feature_part = summed.shape[3]
    returned = lax.all_to_all(
        summed.reshape(seq_count * local_experts, capacity, feature_part),
        "seq",
        split_axis=0,
        concat_axis=0,
        tiled=True,
    )
    picked_back = returned.reshape(experts * capacity, feature_part)[slot_index]
    gate_weights = jax.nn.softmax(gate_logits, axis=-1)
    weighted = picked_back.astype(jnp.float32) * gate_weights.reshape(-1)[:, None]
    moe_total = jnp.sum(weighted.reshape(tok_rows, top_count, feature_part), axis=1)
    return (residual_f + moe_total).astype(jnp.bfloat16)


def solution(mesh):
    return jax.shard_map(
        local,
        mesh=mesh,
        in_specs=(
            P("seq", "mp"),
            P("seq", "mp"),
            P("seq", None),
            P("mp", "seq"),
            P(),
            P("seq", None),
            P("seq", None),
            P("seq", "mp", None),
            P("seq", "mp", None),
            P("seq", "mp", None),
        ),
        out_specs=P("seq", "mp"),
        check_vma=False,
    )
```

profile of v0, /device:TPU:1, one launch (start us, length us, event | category | flops | bytes accessed | tf_op | source)
XLA Modules:
  0.0 609.8 jit_solution(7796226806283322392)
XLA Ops:
  11.4 10.2 %all_gather.18 = bf16[256,1536]{1,0:T(8,128)(2,1)S(1)} all-gather(bf16[256,384]{1,0:T(8,128)(2,1)} %param.10), channel_id=1, replica_groups=mesh['seq'=32,'mp'=4] {'mp'}, dimensions={1}, use_global_device_ids=true | all-gather | bytes 983040 | tf_op jit(solution)/shard_map/all_gather | solution.py:74
  21.9 58.6 %all-gather.7.cloned.1.call-done = bf16[1536,512]{1,0:T(8,128)(2,1)} async-done(((bf16[48,512]{1,0:T(8,128)(2,1)}), bf16[1536,512]{1,0:T(8,128)(2,1)}) %all-gather.7.cloned.1.call-update) | async-done | bytes 1572880 | tf_op jit(solution)/shard_map/all_gather | solution.py:84
  89.8 57.8 %all-gather.5.cloned.1.call-done = bf16[1536,384]{1,0:T(8,128)(2,1)} async-done(((bf16[48,384]{1,0:T(8,128)(2,1)}), bf16[1536,384]{1,0:T(8,128)(2,1)}) %all-gather.5.cloned.1.call-update) | async-done | bytes 1179664 | tf_op jit(solution)/shard_map/all_gather | solution.py:81
  153.3 75.6 %all-gather.9.cloned.1.call-done = bf16[8192,2,128]{0,2,1:T(8,128)(2,1)} async-done(((bf16[256,2,128]{0,2,1:T(8,128)(2,1)}), bf16[8192,2,128]{0,2,1:T(8,128)(2,1)}) %all-gather.9.cloned.1.call-update) | async-done | bytes 4194320 | tf_op jit(solution)/shard_map/all_gather | solution.py:105
  228.9 12.2 %fusion = (f32[3,256]{1,0:T(4,128)S(1)}, f32[3,256,8192]{2,1,0:T(8,128)}) fusion(pred[256,8192]{1,0:T(8,128)(4,1)S(1)} %fusion.11, bf16[8192,2,128]{0,2,1:T(8,128)(2,1)} %all-gather.9.cloned.1.call-done, bf16[256,3,64]{2,0,1:T(8,128)(2,1)} %get-tuple-element.6, bf16[256,3,64]{2,0,1:T(8,128)(2,1)} %get-tuple-element.5), kind=kOutput, calls=%fused_computation.5 | convolution fusion | flops 1629879552 | bytes 29756416 | tf_op jit(solution)/shard_map/hqd,kd->hqk/dot_general | solution.py:46
  241.1 12.5 %fusion.1 = f32[3,256]{1,0:T(4,128)S(1)} fusion(f32[3,256,8192]{2,1,0:T(8,128)} %get-tuple-element.16, f32[3,256]{1,0:T(4,128)S(1)} %broadcast_maximum_fusion, pred[256,8192]{1,0:T(8,128)(4,1)S(1)} %fusion.11), kind=kLoop, calls=%fused_computation.6 | loop fusion | flops 31456512 | bytes 27269120 | tf_op jit(solution)/shard_map/reduce_sum | solution.py:62
  253.6 11.8 %fusion.20 = bf16[256,3,128]{0,2,1:T(8,128)(2,1)S(1)} fusion(bf16[8192,2,128]{0,2,1:T(8,128)(2,1)S(1)} %copy-done.5, f32[3,256,8192]{2,1,0:T(8,128)} %get-tuple-element.16, f32[3,256]{1,0:T(4,128)S(1)} %broadcast_maximum_fusion, pred[256,8192]{1,0:T(8,128)(4,1)S(1)} %fusion.11, f32[256,3]{0,1:T(4,128)S(1)} %bitcast.108), kind=kOutput, calls=%fused_computation.34 | convolution fusion | flops 1635975168 | bytes 29564928 | tf_op jit(solution)/shard_map/hqk,kd->hqd/dot_general | solution.py:63
  265.4 32.7 %all-gather.11.cloned.1.call-done = bf16[384,1536]{0,1:T(8,128)(2,1)} async-done(((bf16[384,48]{0,1:T(8,128)(2,1)}), bf16[384,1536]{0,1:T(8,128)(2,1)}) %all-gather.11.cloned.1.call-update) | async-done | bytes 1179664 | tf_op jit(solution)/shard_map/all_gather | solution.py:115
  301.8 9.0 %reduce-window.6 = s32[32,8,128]{2,1,0:T(8,128)S(1)} reduce-window(s32[32,8,128]{2,1,0:T(8,128)S(1)} %fusion.38, s32[]{:T(128)} %constant.26.clone.1), window={size=1x1x128 pad=0_0x0_0x127_0}, to_apply=%region_4.5 | reduce-window | flops 4161536 | bytes 262148 | tf_op jit(solution)/shard_map/reduce-window
  311.7 7.7 %reduce-scatter.7.cloned.1.call-done = bf16[384,256]{1,0:T(8,128)(2,1)} async-done(((bf16[1536,256]{1,0:T(8,128)(2,1)}), bf16[384,256]{1,0:T(8,128)(2,1)}) %reduce-scatter.7.cloned.1.call-update) | async-done | bytes 196624
  320.7 5.3 psum.7
  326.1 9.5 %all_gather.23 = bf16[256,1536]{1,0:T(8,128)(2,1)S(1)} all-gather(bf16[256,384]{1,0:T(8,128)(2,1)S(1)} %fusion.27), channel_id=1, replica_groups=mesh['seq'=32,'mp'=4] {'mp'}, dimensions={1}, use_global_device_ids=true | all-gather | bytes 983040 | tf_op jit(solution)/shard_map/all_gather | solution.py:133
  335.5 19.7 %scatter_custom_fusion = bf16[2048,1536]{1,0:T(8,128)(2,1)} fusion(s32[1024]{0:T(1024)S(1)} %bitcast.105, bf16[256,1536]{1,0:T(8,128)(2,1)S(1)} %all_gather.23, s32[1024]{0:T(1024)S(1)} %broadcast_clamp_fusion.1, bf16[]{:T(256)} %constant.75.clone.1), kind=kCustom, calls=%fused_computation.19 | custom fusion | bytes 6291458 | tf_op jit(solution)/shard_map/scatter | solution.py:137
  355.3 82.6 %all_to_all.10 = bf16[32,64,1536]{2,1,0:T(8,128)(2,1)S(1)} all-to-all(bf16[32,64,1536]{2,1,0:T(8,128)(2,1)} %bitcast.93), channel_id=1, replica_groups=mesh['seq'=32,'mp'=4] {'seq'}, dimensions={0} | all-to-all | bytes 12582912 | tf_op jit(solution)/shard_map/all_to_all | solution.py:139
  440.5 3.2 fusion.24
  443.7 12.3 %convert_bitcast_fusion = bf16[32,1,64,1536]{3,2,0,1:T(8,128)(2,1)} fusion(f32[32,64,192]{2,1,0:T(8,128)} %fusion.24, bf16[32,64,1536]{2,1,0:T(8,128)(2,1)} %copy-done.1, bf16[1,192,1536]{2,1,0:T(8,128)(2,1)S(1)} %copy-done, bf16[1,192,1536]{2,1,0:T(8,128)(2,1)S(1)} %copy-done.7), kind=kOutput, calls=%fused_computation.18 | convolution fusion | flops 2420244480 | bytes 15335424 | tf_op jit(solution)/shard_map/secf,efd->secd/dot_general | solution.py:152
  456.0 18.4 %copy.58 = bf16[32,1,64,1536]{2,0,1,3:T(8,128)(2,1)} copy(bf16[32,1,64,1536]{3,2,0,1:T(8,128)(2,1)} %convert_bitcast_fusion) | data formatting | bytes 12582912
  474.4 17.9 %reshape.397 = bf16[1536,2048]{1,0:T(8,128)(2,1)} reshape(bf16[1536,1,32,64]{3,2,1,0:T(8,128)(2,1)} %bitcast.91) | data formatting | bytes 12582912
  492.3 61.5 %reduce-scatter.9.cloned.1.call-done = bf16[384,2048]{1,0:T(8,128)(2,1)} async-done(((bf16[1536,2048]{1,0:T(8,128)(2,1)}), bf16[384,2048]{1,0:T(8,128)(2,1)}) %reduce-scatter.9.cloned.1.call-update) | async-done | bytes 1572880
  553.9 5.7 reshape.398
  559.6 5.5 copy.59
  565.0 9.1 %all-to-all-start.1 = ((bf16[32,64,384]{2,1,0:T(8,128)(2,1)}), bf16[32,64,384]{2,1,0:T(8,128)(2,1)S(1)}, u32[]{:S(2)}, u32[]{:S(2)}) async-start(bf16[32,64,384]{2,1,0:T(8,128)(2,1)} %bitcast.95), calls=%async_computation.1 | async-start | bytes 3145728 | tf_op jit(solution)/shard_map/all_to_all | solution.py:159
  574.3 22.2 %all-to-all-done.1 = bf16[32,64,384]{2,1,0:T(8,128)(2,1)S(1)} async-done(((bf16[32,64,384]{2,1,0:T(8,128)(2,1)}), bf16[32,64,384]{2,1,0:T(8,128)(2,1)S(1)}, u32[]{:S(2)}, u32[]{:S(2)}) %all-to-all-start.1) | async-done | bytes 1572896 | tf_op jit(solution)/shard_map/all_to_all | solution.py:159
  596.5 3.9 gather_fusion
  (82 shorter events, 29.4 us)
Async XLA Ops:
  6.5 437.2 %copy-start = (bf16[1,192,1536]{2,1,0:T(8,128)(2,1)S(1)}, bf16[1,192,1536]{2,1,0:T(8,128)(2,1)}, u32[]{:S(2)}) copy-start(bf16[1,192,1536]{2,1,0:T(8,128)(2,1)} %param.19) | copy-start | bytes 1769476
  6.5 74.0 %all-gather.7.cloned.1.call-start = ((), (), s32[]{:S(2)}) async-start(), calls=%async_computation.5 | async-start | bytes 1622016 | tf_op jit(solution)/shard_map/all_gather | solution.py:84
  7.3 140.3 %all-gather.5.cloned.1.call-start = ((), (), s32[]{:S(2)}) async-start(), calls=%async_computation.4 | async-start | bytes 1216512 | tf_op jit(solution)/shard_map/all_gather | solution.py:81
  8.0 220.9 %all-gather.9.cloned.1.call-start = ((), (), s32[]{:S(2)}) async-start(), calls=%async_computation.6 | async-start | bytes 4325376 | tf_op jit(solution)/shard_map/all_gather | solution.py:105
  83.9 214.3 %all-gather.11.cloned.1.call-start = ((), (), s32[]{:S(2)}) async-start(), calls=%async_computation.7 | async-start | bytes 1216512 | tf_op jit(solution)/shard_map/all_gather | solution.py:115
  84.4 235.0 %reduce-scatter.7.cloned.1.call-start = ((), (), s32[]{:S(2)}) async-start(), calls=%async_computation.8 | async-start | bytes 983040
  241.1 12.5 %copy-start.5 = (bf16[8192,2,128]{0,2,1:T(8,128)(2,1)S(1)}, bf16[8192,2,128]{0,2,1:T(8,128)(2,1)}, u32[]{:S(2)}) copy-start(bf16[8192,2,128]{0,2,1:T(8,128)(2,1)} %all-gather.9.cloned.1.call-done) | copy-start | bytes 12582916
  265.4 36.0 %copy-start.4 = (s32[256,4]{0,1:T(4,128)S(1)}, s32[256,4]{0,1:T(4,128)}, u32[]{:S(2)}) copy-start(s32[256,4]{0,1:T(4,128)} %param.15) | copy-start | bytes 12292
  265.4 55.1 %copy-start.2 = (bf16[256,384]{1,0:T(8,128)(2,1)S(1)}, bf16[256,384]{1,0:T(8,128)(2,1)}, u32[]{:S(2)}) copy-start(bf16[256,384]{1,0:T(8,128)(2,1)} %param.10) | copy-start | bytes 589828
  301.2 252.7 %reduce-scatter.9.cloned.1.call-start = ((), (), s32[]{:S(2)}) async-start(), calls=%async_computation.9 | async-start | bytes 7864320
  355.2 85.3 %copy-start.6 = (bf16[1,192,1536]{2,1,0:T(8,128)(2,1)S(1)}, bf16[1,192,1536]{2,1,0:T(8,128)(2,1)}, u32[]{:S(2)}) copy-start(bf16[1,192,1536]{2,1,0:T(8,128)(2,1)} %param.17) | copy-start | bytes 1769476
  437.9 2.7 copy-start.1
  440.5 3.2 copy-start.7
  559.5 14.6 %copy-start.3 = (f32[256,4]{0,1:T(4,128)S(1)}, f32[256,4]{0,1:T(4,128)}, u32[]{:S(2)}) copy-start(f32[256,4]{0,1:T(4,128)} %param.16) | copy-start | bytes 12292
  565.0 31.5 %all-to-all-start.1 = ((bf16[32,64,384]{2,1,0:T(8,128)(2,1)}), bf16[32,64,384]{2,1,0:T(8,128)(2,1)S(1)}, u32[]{:S(2)}, u32[]{:S(2)}) async-start(bf16[32,64,384]{2,1,0:T(8,128)(2,1)} %bitcast.95), calls=%async_computation.1 | async-start | bytes 3145728 | tf_op jit(solution)/shard_map/all_to_all | solution.py:159
Sparse Core Ops, SparseCore 0:
  10.4 70.0 all-gather.6
  83.5 64.0 all-gather.4
  150.4 78.4 all-gather.8
  231.7 66.4 all-gather.10
  301.3 18.0 reduce-scatter.6
  492.5 61.3 reduce-scatter.8
where the time goes:
time: 620 us; the launch traced here: 610 us
  waiting for transfers between devices  318 us (51%)
  blocking collectives  108 us (17%)
  local copies, waits for them, and re-layouts  81 us (13%)
  matrix products  45.2 us (7%)
  other arithmetic  32.8 us (5%)
  between operations  15.5 us (2%)
  starting transfers between devices  9.46 us (2%)
    all_to_all x1, blocking collectives, local(): lax.all_to_all(buffer.reshape(experts, capacity, full_rows.shape[1]), 'se...  82.6 us
    all_gather x1, waiting for transfers between devices, local(): lax.all_gather(kv_own, 'seq', axis=0, tiled=True)  75.6 us
    unnamed x8, waiting for transfers between devices  71.2 us
    all_gather x1, waiting for transfers between devices, local(): lax.all_gather(wkv, 'seq', axis=0, tiled=True)  58.6 us
    all_gather x1, waiting for transfers between devices, local(): lax.all_gather(wq, 'seq', axis=0, tiled=True)  57.8 us
    unnamed x25, local copies, waits for them, and re-layouts  53.8 us
    all_gather x1, waiting for transfers between devices, local(): lax.all_gather(wo, 'seq', axis=1, tiled=True)  32.7 us
    all_to_all x1, waiting for transfers between devices, local(): lax.all_to_all(summed.reshape(seq_count * local_experts, capacity, featur...  22.2 us
  transfers between devices with their start and end apart: 7, of which 7 were waited for; matrix products, arithmetic and copies ran while one was open for 10% of the time, Pallas kernels for 0%

commit v1 on v0

v1 whole, which is shorter than its diff:
```python
import math

import jax
import jax.numpy as jnp
from jax import lax
from jax.sharding import PartitionSpec as P

D = 1536
HQ = 12
KVH = 2
HD = 128
WINDOW = 4096


ROPE_BASE = 1500000.0
EPSILON = 1e-06


def prompt_ids(index, lengths):
    first_end = lengths[0]
    second_end = lengths[0] + lengths[1]
    prompt = (index >= first_end).astype(jnp.int32) + (index >= second_end).astype(jnp.int32)
    begin = jnp.where(index >= second_end, second_end, jnp.where(index >= first_end, first_end, 0))
    return (prompt, index - begin)


def rotary(values, position):
    half_dim = values.shape[-1] // 2
    freqs = jnp.exp(
        jnp.arange(half_dim, dtype=jnp.float32) * (-2.0 * math.log(ROPE_BASE) / values.shape[-1])
    )
    angles = position.astype(jnp.float32)[:, None] * freqs[None, :]
    cosine = jnp.cos(angles)[:, None, :]
    sine = jnp.sin(angles)[:, None, :]
    front = values[..., :half_dim]
    latter = values[..., half_dim:]
    return jnp.concatenate(
        [front * cosine - latter * sine, latter * cosine + front * sine], axis=-1
    )


def gather_seq(piece, count):
    rows = piece.shape[0]
    spread = jnp.broadcast_to(piece[None], (count,) + piece.shape).reshape(
        count * rows, piece.shape[1]
    )
    return lax.all_to_all(spread, "seq", 0, 0, tiled=True)


def local(
    hidden_in, wq, wkv, wo, lengths, routes, gate_logits, expert_gate, expert_up, expert_down
):
    tok_rows = hidden_in.shape[0]
    seq_index = lax.axis_index("seq")
    mp_index = lax.axis_index("mp")
    seq_count = lax.axis_size("seq")
    mp_count = lax.axis_size("mp")
    heads_here = wq.shape[1] // HD
    q_cols = heads_here * HD
    kv_group = mp_index * heads_here // (HQ // KVH)

    expert_all = lax.all_gather(
        jnp.concatenate([expert_gate, expert_up, expert_down], axis=0), "mp", axis=1, tiled=True
    )

    key_cols = lax.dynamic_slice_in_dim(wkv, kv_group * HD, HD, 1)
    value_cols = lax.dynamic_slice_in_dim(wkv, KVH * HD + kv_group * HD, HD, 1)
    piece = jnp.concatenate([wq, key_cols, value_cols, wo.T], axis=1)
    weights = gather_seq(piece, seq_count)
    w_qkv = weights[:, : q_cols + 2 * HD]
    wo_rows = weights[:, q_cols + 2 * HD :]

    whole = lax.all_gather(hidden_in, "mp", axis=1, tiled=True)
    whole_f = whole.astype(jnp.float32)
    normed = (
        whole_f * lax.rsqrt(jnp.sum(whole_f * whole_f, axis=-1, keepdims=True) / D + EPSILON)
    ).astype(jnp.bfloat16)
    lin = jnp.dot(normed, w_qkv, preferred_element_type=jnp.float32)
    own_index = seq_index * tok_rows + jnp.arange(tok_rows, dtype=jnp.int32)
    _, own_pos = prompt_ids(own_index, lengths)
    queries = (
        rotary(lin[:, :q_cols].reshape(tok_rows, heads_here, HD), own_pos)
        .astype(jnp.bfloat16)
        .transpose(1, 0, 2)
    )
    key_own = rotary(lin[:, q_cols : q_cols + HD].reshape(tok_rows, 1, HD), own_pos)[:, 0, :]
    value_own = lin[:, q_cols + HD :]
    kv_own = jnp.concatenate([key_own.astype(jnp.bfloat16), value_own.astype(jnp.bfloat16)], axis=1)

    back = min((WINDOW - 1 + tok_rows - 1) // tok_rows, seq_count - 1)
    blocks = []
    for k in range(back, 0, -1):
        blocks.append(lax.ppermute(kv_own, "seq", [(i, i + k) for i in range(seq_count - k)]))
    blocks.append(kv_own)
    kv_win = jnp.concatenate(blocks, axis=0)
    key_rows = kv_win[:, :HD]
    value_rows = kv_win[:, HD:].astype(jnp.float32)
    key_index = (seq_index - back) * tok_rows + jnp.arange((back + 1) * tok_rows, dtype=jnp.int32)

    scores = jnp.einsum(
        "hqd,kd->hqk", queries, key_rows, preferred_element_type=jnp.float32
    ) * HD ** (-0.5)
    query_prompt, _ = prompt_ids(own_index, lengths)
    key_prompt, _ = prompt_ids(key_index, lengths)
    spacing = own_index[:, None] - key_index[None, :]
    allowed = (
        (query_prompt[:, None] == key_prompt[None, :])
        & (spacing >= 0)
        & (spacing < WINDOW)
        & (key_index[None, :] >= 0)
    )[None]
    masked = jnp.where(allowed, scores, -1e30)
    peak = jnp.max(masked, axis=-1)
    probs = jnp.where(allowed, jnp.exp(masked - peak[..., None]), 0.0)
    total = jnp.sum(probs, axis=-1)
    accum = jnp.einsum("hqk,kd->hqd", probs, value_rows)
    attended = (
        (accum / total[..., None])
        .transpose(1, 0, 2)
        .reshape(tok_rows, q_cols)
        .astype(jnp.bfloat16)
    )
    partial_out = lax.dot_general(
        attended, wo_rows, (((1,), (1,)), ((), ())), preferred_element_type=jnp.float32
    )
    attn_mine = lax.psum_scatter(
        partial_out.astype(jnp.bfloat16), "mp", scatter_dimension=1, tiled=True
    ).astype(jnp.float32)
    residual = (hidden_in.astype(jnp.float32) + attn_mine).astype(jnp.bfloat16)
    residual_f = residual.astype(jnp.float32)
    square_sum = lax.psum(jnp.sum(residual_f * residual_f, axis=-1), "mp")
    moe_local = (residual_f * lax.rsqrt(square_sum / D + EPSILON)[:, None]).astype(jnp.bfloat16)

    local_experts = expert_gate.shape[0]
    experts = seq_count * local_experts
    top_count = routes.shape[1]
    capacity = 2 * tok_rows * top_count // experts
    part_cap = capacity // mp_count
    flat_ids = routes.reshape(-1)
    one_hot = (flat_ids[:, None] == jnp.arange(experts, dtype=jnp.int32)[None, :]).astype(jnp.int32)
    earlier_count = jnp.sum((jnp.cumsum(one_hot, axis=0) - one_hot) * one_hot, axis=1)
    mine = (earlier_count // part_cap) == mp_index
    slot_index = flat_ids * part_cap + earlier_count % part_cap
    send_index = jnp.where(mine, slot_index, experts * part_cap)
    source_row = jnp.arange(tok_rows * top_count, dtype=jnp.int32) // top_count
    full_rows = lax.all_gather(moe_local, "mp", axis=1, tiled=True)
    buffer = (
        jnp.zeros((experts * part_cap, D), jnp.bfloat16)
        .at[send_index]
        .set(full_rows[source_row], mode="drop")
    )
    arrived = lax.all_to_all(buffer, "seq", 0, 0, tiled=True)
    hidden_units = expert_all.shape[1]
    w_gate = expert_all[0]
    w_up = expert_all[1]
    w_down = expert_all[2]
    gate_act = lax.dot_general(
        arrived, w_gate, (((1,), (1,)), ((), ())), preferred_element_type=jnp.float32
    )
    up_act = lax.dot_general(
        arrived, w_up, (((1,), (1,)), ((), ())), preferred_element_type=jnp.float32
    )
    active = (jnp.maximum(gate_act, 0.0) * up_act).astype(jnp.bfloat16)
    result = jnp.dot(active, w_down, preferred_element_type=jnp.float32).astype(jnp.bfloat16)
    returned = lax.all_to_all(result, "seq", 0, 0, tiled=True)

    gate_weights = jax.nn.softmax(gate_logits, axis=-1)
    picked_back = returned[jnp.where(mine, slot_index, 0)].astype(jnp.float32)
    share = jnp.where(mine, gate_weights.reshape(-1), 0.0)
    weighted = picked_back * share[:, None]
    partial_moe = jnp.sum(weighted.reshape(tok_rows, top_count, D), axis=1)
    swapped = lax.all_to_all(partial_moe.astype(jnp.bfloat16), "mp", 1, 0, tiled=True)
    moe_total = jnp.sum(
        swapped.reshape(mp_count, tok_rows, D // mp_count).astype(jnp.float32), axis=0
    )
    del hidden_units
    return (residual_f + moe_total).astype(jnp.bfloat16)


def solution(mesh):
    return jax.shard_map(
        local,
        mesh=mesh,
        in_specs=(
            P("seq", "mp"),
            P("seq", "mp"),
            P("seq", None),
            P("mp", "seq"),
            P(),
            P("seq", None),
            P("seq", None),
            P("seq", "mp", None),
            P("seq", "mp", None),
            P("seq", "mp", None),
        ),
        out_specs=P("seq", "mp"),
        check_vma=False,
    )
```

time: 620 us -> 357 us (0.58)
  waiting for transfers between devices: 318 us -> 59.3 us
  starting transfers between devices: 9.46 us -> 71.5 us
  local copies, waits for them, and re-layouts: 81 us -> 41.8 us
  matrix products: 45.2 us -> 27.5 us
    all_gather x4 -> x1, waiting for transfers between devices: 225 us -> 21.1 us  [local(): lax.all_gather(jnp.concatenate([expert_gate, expert_up, expert_down], axi...]
    unnamed x8 -> x3, waiting for transfers between devices: 71.2 us -> 11.4 us
    ppermute x0 -> x16, starting transfers between devices: none -> 50.6 us  [local(): lax.ppermute(kv_own, 'seq', [(i, i + k) for i in range(seq_count - k)])]
    unnamed x25 -> x37, local copies, waits for them, and re-layouts: 53.8 us -> 7.74 us
    all_to_all x1 -> x2, blocking collectives: 82.6 us -> 49.7 us  [the longest x1 36 us: local(): arrived = lax.all_to_all(buffer, 'seq', 0, 0, tiled=True)]
    all_gather x1, blocking collectives: 10.2 us -> 36.9 us  [local(): whole = lax.all_gather(hidden_in, 'mp', axis=1, tiled=True)]
    dot_general x7 -> x6, matrix products: 45.2 us -> 27.5 us  [the longest x1 6.86 us: local(): accum = jnp.einsum('hqk,kd->hqd', probs, value_rows)]
    all_to_all x1 -> x2, starting transfers between devices: 9.09 us -> 20.8 us  [the longest x1 11.6 us: gather_seq(): return lax.all_to_all(spread, 'seq', 0, 0, tiled=True)]
  transfers between devices with their start and end apart: 7 -> 20, of which waited for: 7 -> 4; matrix products, arithmetic and copies ran while one was open for 10% -> 11% of each run, Pallas kernels for 0% -> 0%
where the time goes in v1:
time: 357 us; the launch traced here: 351 us
  blocking collectives  102 us (29%)
  starting transfers between devices  71.5 us (20%)
  waiting for transfers between devices  59.3 us (17%)
  local copies, waits for them, and re-layouts  41.8 us (12%)
  other arithmetic  33.7 us (9%)
  matrix products  27.5 us (8%)
  between operations  15.8 us (4%)
    ppermute x16, starting transfers between devices, local(): lax.ppermute(kv_own, 'seq', [(i, i + k) for i in range(seq_count - k)])  50.6 us
    all_gather x1, blocking collectives, local(): whole = lax.all_gather(hidden_in, 'mp', axis=1, tiled=True)  36.9 us
    all_to_all x1, blocking collectives, local(): arrived = lax.all_to_all(buffer, 'seq', 0, 0, tiled=True)  36 us
    all_to_all x1, waiting for transfers between devices, local(): returned = lax.all_to_all(result, 'seq', 0, 0, tiled=True)  24.2 us
    all_gather x1, waiting for transfers between devices, local(): lax.all_gather(jnp.concatenate([expert_gate, expert_up, expert_down], axi...  21.1 us
    scatter x1, local copies, waits for them, and re-layouts, local(): buffer = jnp.zeros((experts * part_cap, D), jnp.bfloat16).at[send_index]....  16.3 us
    all_to_all x1, blocking collectives, local(): lax.all_to_all(partial_moe.astype(jnp.bfloat16), 'mp', 1, 0, tiled=True)  13.7 us
    all_to_all x1, starting transfers between devices, gather_seq(): return lax.all_to_all(spread, 'seq', 0, 0, tiled=True)  11.6 us
  transfers between devices with their start and end apart: 20, of which 4 were waited for; matrix products, arithmetic and copies ran while one was open for 11% of the time, Pallas kernels for 0%

profile of v1, /device:TPU:1, one launch (start us, length us, event | category | flops | bytes accessed | tf_op | source)
XLA Modules:
  0.0 351.2 jit_solution(2576738332656312989)
XLA Ops:
  10.1 11.6 %all-to-all-start = ((bf16[32,48,1024]{2,1,0:T(8,128)(2,1)}), bf16[32,48,1024]{2,1,0:T(8,128)(2,1)}, u32[]{:S(2)}, u32[]{:S(2)}) async-start(bf16[32,48,1024]{2,1,0:T(8,128)(2,1)} %broadcast_in_dim.38), calls=%async_computation | async-start | bytes 6291456 | tf_op jit(solution)/shard_map/all_to_all | solution.py:47
  25.4 36.9 %all_gather.9 = bf16[256,1536]{1,0:T(8,128)(2,1)S(1)} all-gather(bf16[256,384]{1,0:T(8,128)(2,1)S(1)} %copy-done), channel_id=1, replica_groups=mesh['seq'=32,'mp'=4] {'mp'}, dimensions={1}, use_global_device_ids=true | all-gather | bytes 983040 | tf_op jit(solution)/shard_map/all_gather | solution.py:73
  67.6 5.4 %collective-permute-start = (bf16[256,256]{0,1:T(8,128)(2,1)S(1)}, bf16[256,256]{0,1:T(8,128)(2,1)}, u32[]{:S(2)}, u32[]{:S(2)}) collective-permute-start(bf16[256,256]{0,1:T(8,128)(2,1)S(1)} %pad_maximum_fusion.1), channel_id=1, source_target_pairs={{0,64},{4,68},{8,72},{12,76},{16,80},{20,84},{24,88},{28,92},{32,9... | collective-permute-start | bytes 393224 | tf_op jit(solution)/shard_map/ppermute | solution.py:93
  73.0 10.5 %collective-permute-start.1 = (bf16[256,256]{0,1:T(8,128)(2,1)S(1)}, bf16[256,256]{0,1:T(8,128)(2,1)}, u32[]{:S(2)}, u32[]{:S(2)}) collective-permute-start(bf16[256,256]{0,1:T(8,128)(2,1)S(1)} %pad_maximum_fusion.1), channel_id=1, source_target_pairs={{0,60},{4,64},{8,68},{12,72},{16,76},{20,80},{24,84},{28,88},{32,9... | collective-permute-start | bytes 393224 | tf_op jit(solution)/shard_map/ppermute | solution.py:93
  100.6 5.7 %collective-permute-start.9 = (bf16[256,256]{0,1:T(8,128)(2,1)S(1)}, bf16[256,256]{0,1:T(8,128)(2,1)S(1)}, u32[]{:S(2)}, u32[]{:S(2)}) collective-permute-start(bf16[256,256]{0,1:T(8,128)(2,1)S(1)} %pad_maximum_fusion.1), channel_id=1, source_target_pairs={{0,28},{4,32},{8,36},{12,40},{16,44},{20,48},{24,52},{28,56},{32,6... | collective-permute-start | bytes 393224 | tf_op jit(solution)/shard_map/ppermute | solution.py:93
  108.6 4.0 %collective-permute-start.11 = (bf16[256,256]{0,1:T(8,128)(2,1)S(1)}, bf16[256,256]{0,1:T(8,128)(2,1)S(1)}, u32[]{:S(2)}, u32[]{:S(2)}) collective-permute-start(bf16[256,256]{0,1:T(8,128)(2,1)S(1)} %pad_maximum_fusion.1), channel_id=1, source_target_pairs={{0,20},{4,24},{8,28},{12,32},{16,36},{20,40},{24,44},{28,48},{32,5... | collective-permute-start | bytes 393224 | tf_op jit(solution)/shard_map/ppermute | solution.py:93
  113.9 4.6 %collective-permute-start.13 = (bf16[256,256]{0,1:T(8,128)(2,1)S(1)}, bf16[256,256]{0,1:T(8,128)(2,1)S(1)}, u32[]{:S(2)}, u32[]{:S(2)}) collective-permute-start(bf16[256,256]{0,1:T(8,128)(2,1)S(1)} %pad_maximum_fusion.1), channel_id=1, source_target_pairs={{0,12},{4,16},{8,20},{12,24},{16,28},{20,32},{24,36},{28,40},{32,4... | collective-permute-start | bytes 393224 | tf_op jit(solution)/shard_map/ppermute | solution.py:93
  126.5 6.4 %fusion = (f32[3,256]{1,0:T(4,128)S(1)}, f32[3,256,4352]{2,1,0:T(8,128)}) fusion(pred[256,4352]{1,0:T(8,128)(4,1)S(1)} %fusion.10, bf16[4352,256]{0,1:T(8,128)(2,1)S(1)} %constant_dynamic-update-slice_fusion, bf16[256,3,64]{2,0,1:T(8,128)(2,1)S(1)} %get-tuple-element.9, bf16[256,3,64]{2,0,1:T(8,128)(2,1)S(1)} %get-tuple-element.8), kind=kOutput, calls=%fused_computation.5 | convolution fusion | flops 866057472 | bytes 15993856 | tf_op jit(solution)/shard_map/hqd,kd->hqk/dot_general | solution.py:100
  132.9 9.0 %fusion.1 = f32[3,256]{1,0:T(4,128)S(1)} fusion(f32[3,256,4352]{2,1,0:T(8,128)} %get-tuple-element.21, f32[3,256]{1,0:T(4,128)S(1)} %get-tuple-element.20, pred[256,4352]{1,0:T(8,128)(4,1)S(1)} %fusion.10), kind=kLoop, calls=%fused_computation.6 | loop fusion | flops 16710912 | bytes 14489600 | tf_op jit(solution)/shard_map/reduce_sum | solution.py:115
  141.9 6.9 %fusion.23 = bf16[256,3,128]{0,2,1:T(8,128)(2,1)S(1)} fusion(bf16[4352,256]{0,1:T(8,128)(2,1)S(1)} %constant_dynamic-update-slice_fusion, f32[3,256,4352]{2,1,0:T(8,128)} %get-tuple-element.21, f32[3,256]{1,0:T(4,128)S(1)} %get-tuple-element.20, pred[256,4352]{1,0:T(8,128)(4,1)S(1)} %fusion.10, f32[256,3]{0,1:T(4,128)S(1)} %bitcast.93), kind=kOutput, calls=%fused_computation.43 | convolution fusion | flops 869203968 | bytes 15802368 | tf_op jit(solution)/shard_map/hqk,kd->hqd/dot_general | solution.py:116
  154.2 9.0 %reduce-window.6 = s32[32,8,128]{2,1,0:T(8,128)S(1)} reduce-window(s32[32,8,128]{2,1,0:T(8,128)S(1)} %fusion.36, s32[]{:T(128)} %constant.82.clone.1), window={size=1x1x128 pad=0_0x0_0x127_0}, to_apply=%region_4.5 | reduce-window | flops 4161536 | bytes 262148 | tf_op jit(solution)/shard_map/reduce-window
  164.1 11.4 %reduce-scatter.4.cloned.1.call-done = bf16[384,256]{1,0:T(8,128)(2,1)} async-done(((bf16[1536,256]{1,0:T(8,128)(2,1)}), bf16[384,256]{1,0:T(8,128)(2,1)}) %reduce-scatter.4.cloned.1.call-update) | async-done | bytes 196624
  176.7 5.1 %psum.7 = f32[256]{0:T(256)S(1)} all-reduce(f32[256]{0:T(256)S(1)} %fusion.28), channel_id=1, replica_groups=mesh['seq'=32,'mp'=4] {'mp'}, use_global_device_ids=true, to_apply=%region_8.9 | all-reduce | flops 256 | bytes 2048 | tf_op jit(solution)/shard_map/psum | solution.py:131
  182.0 9.9 %all_gather.10 = bf16[256,1536]{1,0:T(8,128)(2,1)S(1)} all-gather(bf16[256,384]{1,0:T(8,128)(2,1)S(1)} %fusion.29), channel_id=1, replica_groups=mesh['seq'=32,'mp'=4] {'mp'}, dimensions={1}, use_global_device_ids=true | all-gather | bytes 983040 | tf_op jit(solution)/shard_map/all_gather | solution.py:146
  191.9 16.3 %scatter_custom_fusion = bf16[512,1536]{1,0:T(8,128)(2,1)S(1)} fusion(s32[1024]{0:T(1024)S(1)} %bitcast.94, bf16[256,1536]{1,0:T(8,128)(2,1)S(1)} %all_gather.10, s32[1024]{0:T(1024)S(1)} %broadcast_clamp_fusion.1, bf16[]{:T(256)} %constant.99.clone.1), kind=kCustom, calls=%fused_computation.19 | custom fusion | bytes 1572866 | tf_op jit(solution)/shard_map/scatter | solution.py:150
  208.2 36.0 %all_to_all.43 = bf16[32,16,1536]{2,1,0:T(8,128)(2,1)S(1)} all-to-all(bf16[32,16,1536]{2,1,0:T(8,128)(2,1)S(1)} %bitcast.79), channel_id=1, replica_groups=mesh['seq'=32,'mp'=4] {'seq'}, dimensions={0} | all-to-all | bytes 3145728 | tf_op jit(solution)/shard_map/all_to_all | solution.py:152
  244.2 21.1 %all-gather.2.cloned.1.call-done = bf16[3,768,1536]{2,1,0:T(8,128)(2,1)} async-done(((bf16[3,192,1536]{2,1,0:T(8,128)(2,1)}), bf16[3,768,1536]{2,1,0:T(8,128)(2,1)}) %all-gather.2.cloned.1.call-update) | async-done | bytes 7077904 | tf_op jit(solution)/shard_map/all_gather | solution.py:62
  268.4 6.8 %convolution_convert_fusion = bf16[512,1536]{1,0:T(8,128)(2,1)} fusion(bf16[3,768,1536]{2,1,0:T(8,128)(2,1)} %all-gather.2.cloned.1.call-done, f32[512,768]{1,0:T(8,128)S(1)} %fusion.13, bf16[512,1536]{1,0:T(8,128)(2,1)S(1)} %bitcast.83), kind=kOutput, calls=%fused_computation.21 | convolution fusion | flops 2417885184 | bytes 9437184 | tf_op jit(solution)/shard_map/dot_general | solution.py:164
  275.2 9.2 %all-to-all-start.2 = ((bf16[32,16,1536]{2,1,0:T(8,128)(2,1)}), bf16[32,16,1536]{2,1,0:T(8,128)(2,1)S(1)}, u32[]{:S(2)}, u32[]{:S(2)}) async-start(bf16[32,16,1536]{2,1,0:T(8,128)(2,1)} %bitcast.23), calls=%async_computation.2 | async-start | bytes 3145728 | tf_op jit(solution)/shard_map/all_to_all | solution.py:165
  284.8 24.2 %all-to-all-done.2 = bf16[32,16,1536]{2,1,0:T(8,128)(2,1)S(1)} async-done(((bf16[32,16,1536]{2,1,0:T(8,128)(2,1)}), bf16[32,16,1536]{2,1,0:T(8,128)(2,1)S(1)}, u32[]{:S(2)}, u32[]{:S(2)}) %all-to-all-start.2) | async-done | bytes 1572896 | tf_op jit(solution)/shard_map/all_to_all | solution.py:165
  309.0 5.6 %gather_fusion = bf16[1024,1536]{1,0:T(8,128)(2,1)} fusion(bf16[512,1536]{1,0:T(8,128)(2,1)S(1)} %bitcast.78, s32[1024]{0:T(1024)S(1)} %broadcast_clamp_fusion), kind=kCustom, calls=%fused_computation.1 | custom fusion | bytes 6295552 | tf_op jit(solution)/shard_map/gather | solution.py:168
  314.7 6.7 %reshape.440 = f32[256,4,1536]{2,1,0:T(4,128)} reshape(bf16[1024,1536]{1,0:T(8,128)(2,1)} %gather_fusion) | data formatting | bytes 9437184 | tf_op jit(solution)/shard_map/convert_element_type | solution.py:168
  321.3 7.4 %multiply_reduce_fusion = bf16[256,1536]{1,0:T(8,128)(2,1)S(1)} fusion(f32[256,4,1536]{2,1,0:T(4,128)} %reshape.440, f32[256,4]{1,0:T(8,128)S(1)} %copy.97), kind=kLoop, calls=%fused_computation.15 | loop fusion | flops 2752512 | bytes 7081984 | tf_op jit(solution)/shard_map/reduce_sum | solution.py:171
  329.4 13.7 %all_to_all.44 = bf16[256,4,384]{2,0,1:T(8,128)(2,1)S(1)} all-to-all(bf16[256,4,384]{2,0,1:T(8,128)(2,1)S(1)} %copy.99), channel_id=1, replica_groups=mesh['seq'=32,'mp'=4] {'mp'}, dimensions={1} | all-to-all | bytes 1572864 | tf_op jit(solution)/shard_map/all_to_all | solution.py:172
  (127 shorter events, 52.0 us)
Async XLA Ops:
  10.1 11.7 %copy-start.6 = (s32[3]{0:T(128)S(1)}, s32[3]{0:T(128)}, u32[]{:S(2)}) copy-start(s32[3]{0:T(128)} %param.14) | copy-start | bytes 40
  10.1 15.3 %copy-start = (bf16[256,384]{1,0:T(8,128)(2,1)S(1)}, bf16[256,384]{1,0:T(8,128)(2,1)}, u32[]{:S(2)}) copy-start(bf16[256,384]{1,0:T(8,128)(2,1)} %param.10) | copy-start | bytes 589828
  10.1 54.5 %all-to-all-start = ((bf16[32,48,1024]{2,1,0:T(8,128)(2,1)}), bf16[32,48,1024]{2,1,0:T(8,128)(2,1)}, u32[]{:S(2)}, u32[]{:S(2)}) async-start(bf16[32,48,1024]{2,1,0:T(8,128)(2,1)} %broadcast_in_dim.38), calls=%async_computation | async-start | bytes 6291456 | tf_op jit(solution)/shard_map/all_to_all | solution.py:47
  21.7 153.7 %reduce-scatter.4.cloned.1.call-start = ((), (), s32[]{:S(2)}) async-start(), calls=%async_computation.6 | async-start | bytes 983040
  67.6 23.1 %collective-permute-start = (bf16[256,256]{0,1:T(8,128)(2,1)S(1)}, bf16[256,256]{0,1:T(8,128)(2,1)}, u32[]{:S(2)}, u32[]{:S(2)}) collective-permute-start(bf16[256,256]{0,1:T(8,128)(2,1)S(1)} %pad_maximum_fusion.1), channel_id=1, source_target_pairs={{0,64},{4,68},{8,72},{12,76},{16,80},{20,84},{24,88},{28,92},{32,9... | collective-permute-start | bytes 393224 | tf_op jit(solution)/shard_map/ppermute | solution.py:93
  73.0 20.0 %collective-permute-start.1 = (bf16[256,256]{0,1:T(8,128)(2,1)S(1)}, bf16[256,256]{0,1:T(8,128)(2,1)}, u32[]{:S(2)}, u32[]{:S(2)}) collective-permute-start(bf16[256,256]{0,1:T(8,128)(2,1)S(1)} %pad_maximum_fusion.1), channel_id=1, source_target_pairs={{0,60},{4,64},{8,68},{12,72},{16,76},{20,80},{24,84},{28,88},{32,9... | collective-permute-start | bytes 393224 | tf_op jit(solution)/shard_map/ppermute | solution.py:93
  83.5 11.7 %collective-permute-start.2 = (bf16[256,256]{0,1:T(8,128)(2,1)S(1)}, bf16[256,256]{0,1:T(8,128)(2,1)}, u32[]{:S(2)}, u32[]{:S(2)}) collective-permute-start(bf16[256,256]{0,1:T(8,128)(2,1)S(1)} %pad_maximum_fusion.1), channel_id=1, source_target_pairs={{0,56},{4,60},{8,64},{12,68},{16,72},{20,76},{24,80},{28,84},{32,8... | collective-permute-start | bytes 393224 | tf_op jit(solution)/shard_map/ppermute | solution.py:93
  86.2 11.3 %collective-permute-start.3 = (bf16[256,256]{0,1:T(8,128)(2,1)S(1)}, bf16[256,256]{0,1:T(8,128)(2,1)}, u32[]{:S(2)}, u32[]{:S(2)}) collective-permute-start(bf16[256,256]{0,1:T(8,128)(2,1)S(1)} %pad_maximum_fusion.1), channel_id=1, source_target_pairs={{0,52},{4,56},{8,60},{12,64},{16,68},{20,72},{24,76},{28,80},{32,8... | collective-permute-start | bytes 393224 | tf_op jit(solution)/shard_map/ppermute | solution.py:93
  88.1 12.5 %collective-permute-start.4 = (bf16[256,256]{0,1:T(8,128)(2,1)S(1)}, bf16[256,256]{0,1:T(8,128)(2,1)}, u32[]{:S(2)}, u32[]{:S(2)}) collective-permute-start(bf16[256,256]{0,1:T(8,128)(2,1)S(1)} %pad_maximum_fusion.1), channel_id=1, source_target_pairs={{0,48},{4,52},{8,56},{12,60},{16,64},{20,68},{24,72},{28,76},{32,8... | collective-permute-start | bytes 393224 | tf_op jit(solution)/shard_map/ppermute | solution.py:93
  90.8 16.5 %collective-permute-start.5 = (bf16[256,256]{0,1:T(8,128)(2,1)S(1)}, bf16[256,256]{0,1:T(8,128)(2,1)S(1)}, u32[]{:S(2)}, u32[]{:S(2)}) collective-permute-start(bf16[256,256]{0,1:T(8,128)(2,1)S(1)} %pad_maximum_fusion.1), channel_id=1, source_target_pairs={{0,44},{4,48},{8,52},{12,56},{16,60},{20,64},{24,68},{28,72},{32,7... | collective-permute-start | bytes 393224 | tf_op jit(solution)/shard_map/ppermute | solution.py:93
  93.0 15.6 %collective-permute-start.6 = (bf16[256,256]{0,1:T(8,128)(2,1)S(1)}, bf16[256,256]{0,1:T(8,128)(2,1)S(1)}, u32[]{:S(2)}, u32[]{:S(2)}) collective-permute-start(bf16[256,256]{0,1:T(8,128)(2,1)S(1)} %pad_maximum_fusion.1), channel_id=1, source_target_pairs={{0,40},{4,44},{8,48},{12,52},{16,56},{20,60},{24,64},{28,68},{32,7... | collective-permute-start | bytes 393224 | tf_op jit(solution)/shard_map/ppermute | solution.py:93
  95.2 17.4 %collective-permute-start.7 = (bf16[256,256]{0,1:T(8,128)(2,1)S(1)}, bf16[256,256]{0,1:T(8,128)(2,1)S(1)}, u32[]{:S(2)}, u32[]{:S(2)}) collective-permute-start(bf16[256,256]{0,1:T(8,128)(2,1)S(1)} %pad_maximum_fusion.1), channel_id=1, source_target_pairs={{0,36},{4,40},{8,44},{12,48},{16,52},{20,56},{24,60},{28,64},{32,6... | collective-permute-start | bytes 393224 | tf_op jit(solution)/shard_map/ppermute | solution.py:93
  97.5 16.5 %collective-permute-start.8 = (bf16[256,256]{0,1:T(8,128)(2,1)S(1)}, bf16[256,256]{0,1:T(8,128)(2,1)S(1)}, u32[]{:S(2)}, u32[]{:S(2)}) collective-permute-start(bf16[256,256]{0,1:T(8,128)(2,1)S(1)} %pad_maximum_fusion.1), channel_id=1, source_target_pairs={{0,32},{4,36},{8,40},{12,44},{16,48},{20,52},{24,56},{28,60},{32,6... | collective-permute-start | bytes 393224 | tf_op jit(solution)/shard_map/ppermute | solution.py:93
  100.6 18.0 %collective-permute-start.9 = (bf16[256,256]{0,1:T(8,128)(2,1)S(1)}, bf16[256,256]{0,1:T(8,128)(2,1)S(1)}, u32[]{:S(2)}, u32[]{:S(2)}) collective-permute-start(bf16[256,256]{0,1:T(8,128)(2,1)S(1)} %pad_maximum_fusion.1), channel_id=1, source_target_pairs={{0,28},{4,32},{8,36},{12,40},{16,44},{20,48},{24,52},{28,56},{32,6... | collective-permute-start | bytes 393224 | tf_op jit(solution)/shard_map/ppermute | solution.py:93
  107.3 13.0 %collective-permute-start.10 = (bf16[256,256]{0,1:T(8,128)(2,1)S(1)}, bf16[256,256]{0,1:T(8,128)(2,1)S(1)}, u32[]{:S(2)}, u32[]{:S(2)}) collective-permute-start(bf16[256,256]{0,1:T(8,128)(2,1)S(1)} %pad_maximum_fusion.1), channel_id=1, source_target_pairs={{0,24},{4,28},{8,32},{12,36},{16,40},{20,44},{24,48},{28,52},{32,5... | collective-permute-start | bytes 393224 | tf_op jit(solution)/shard_map/ppermute | solution.py:93
  108.6 15.2 %collective-permute-start.11 = (bf16[256,256]{0,1:T(8,128)(2,1)S(1)}, bf16[256,256]{0,1:T(8,128)(2,1)S(1)}, u32[]{:S(2)}, u32[]{:S(2)}) collective-permute-start(bf16[256,256]{0,1:T(8,128)(2,1)S(1)} %pad_maximum_fusion.1), channel_id=1, source_target_pairs={{0,20},{4,24},{8,28},{12,32},{16,36},{20,40},{24,44},{28,48},{32,5... | collective-permute-start | bytes 393224 | tf_op jit(solution)/shard_map/ppermute | solution.py:93
  112.6 11.2 %collective-permute-start.12 = (bf16[256,256]{0,1:T(8,128)(2,1)S(1)}, bf16[256,256]{0,1:T(8,128)(2,1)S(1)}, u32[]{:S(2)}, u32[]{:S(2)}) collective-permute-start(bf16[256,256]{0,1:T(8,128)(2,1)S(1)} %pad_maximum_fusion.1), channel_id=1, source_target_pairs={{0,16},{4,20},{8,24},{12,28},{16,32},{20,36},{24,40},{28,44},{32,4... | collective-permute-start | bytes 393224 | tf_op jit(solution)/shard_map/ppermute | solution.py:93
  113.9 9.9 %collective-permute-start.13 = (bf16[256,256]{0,1:T(8,128)(2,1)S(1)}, bf16[256,256]{0,1:T(8,128)(2,1)S(1)}, u32[]{:S(2)}, u32[]{:S(2)}) collective-permute-start(bf16[256,256]{0,1:T(8,128)(2,1)S(1)} %pad_maximum_fusion.1), channel_id=1, source_target_pairs={{0,12},{4,16},{8,20},{12,24},{16,28},{20,32},{24,36},{28,40},{32,4... | collective-permute-start | bytes 393224 | tf_op jit(solution)/shard_map/ppermute | solution.py:93
  118.6 5.3 %collective-permute-start.14 = (bf16[256,256]{0,1:T(8,128)(2,1)S(1)}, bf16[256,256]{0,1:T(8,128)(2,1)S(1)}, u32[]{:S(2)}, u32[]{:S(2)}) collective-permute-start(bf16[256,256]{0,1:T(8,128)(2,1)S(1)} %pad_maximum_fusion.1), channel_id=1, source_target_pairs={{0,8},{4,12},{8,16},{12,20},{16,24},{20,28},{24,32},{28,36},{32,40... | collective-permute-start | bytes 393224 | tf_op jit(solution)/shard_map/ppermute | solution.py:93
  120.3 6.2 %collective-permute-start.15 = (bf16[256,256]{0,1:T(8,128)(2,1)S(1)}, bf16[256,256]{0,1:T(8,128)(2,1)S(1)}, u32[]{:S(2)}, u32[]{:S(2)}) collective-permute-start(bf16[256,256]{0,1:T(8,128)(2,1)S(1)} %pad_maximum_fusion.1), channel_id=1, source_target_pairs={{0,4},{4,8},{8,12},{12,16},{16,20},{20,24},{24,28},{28,32},{32,36}... | collective-permute-start | bytes 393224 | tf_op jit(solution)/shard_map/ppermute | solution.py:93
  148.8 3.4 copy-start.1
  152.2 113.2 %all-gather.2.cloned.1.call-start = ((), (), s32[]{:S(2)}) async-start(), calls=%async_computation.5 | async-start | bytes 8847360 | tf_op jit(solution)/shard_map/all_gather | solution.py:62
  275.2 9.5 %copy-start.4 = (f32[256,4]{0,1:T(4,128)S(1)}, f32[256,4]{0,1:T(4,128)}, u32[]{:S(2)}) copy-start(f32[256,4]{0,1:T(4,128)} %param.16) | copy-start | bytes 12292
  275.2 33.9 %all-to-all-start.2 = ((bf16[32,16,1536]{2,1,0:T(8,128)(2,1)}), bf16[32,16,1536]{2,1,0:T(8,128)(2,1)S(1)}, u32[]{:S(2)}, u32[]{:S(2)}) async-start(bf16[32,16,1536]{2,1,0:T(8,128)(2,1)} %bitcast.23), calls=%async_computation.2 | async-start | bytes 3145728 | tf_op jit(solution)/shard_map/all_to_all | solution.py:165
  (3 other events, 8.4 us)
Sparse Core Ops, SparseCore 0:
  152.3 23.1 reduce-scatter.3
  177.1 88.1 all-gather.1

commit v2 on v1

--- a/solution.py
+++ b/solution.py
@@ -88,14 +88,41 @@
     kv_own = jnp.concatenate([key_own.astype(jnp.bfloat16), value_own.astype(jnp.bfloat16)], axis=1)
 
     back = min((WINDOW - 1 + tok_rows - 1) // tok_rows, seq_count - 1)
-    blocks = []
-    for k in range(back, 0, -1):
-        blocks.append(lax.ppermute(kv_own, "seq", [(i, i + k) for i in range(seq_count - k)]))
-    blocks.append(kv_own)
-    kv_win = jnp.concatenate(blocks, axis=0)
+    half = (back + 1) // 2
+    core = mp_index % 2
+    fetched = []
+    for j in range(half):
+        pairs = []
+        for s in range(seq_count):
+            for m in range(mp_count):
+                k = 2 * j + 1 + m % 2
+                if s + k < seq_count:
+                    pairs.append((s * mp_count + m, (s + k) * mp_count + m))
+        fetched.append(lax.ppermute(kv_own, ("seq", "mp"), pairs))
+    fetched = jnp.stack(fetched)
+    partner = lax.ppermute(
+        fetched, "mp", [(m, m ^ 1) for m in range(mp_count)]
+    )
+    odd = jnp.where(core == 0, fetched, partner)
+    even = jnp.where(core == 0, partner, fetched)
+    offsets = jnp.concatenate(
+        [
+            2 * jnp.arange(half, dtype=jnp.int32) + 1,
+            2 * jnp.arange(half, dtype=jnp.int32) + 2,
+            jnp.zeros((1,), jnp.int32),
+        ]
+    )
+    kv_win = jnp.concatenate(
+        [odd.reshape(-1, 2 * HD), even.reshape(-1, 2 * HD), kv_own], axis=0
+    )
     key_rows = kv_win[:, :HD]
     value_rows = kv_win[:, HD:].astype(jnp.float32)
-    key_index = (seq_index - back) * tok_rows + jnp.arange((back + 1) * tok_rows, dtype=jnp.int32)
+    key_index = (
+        (seq_index - offsets)[:, None] * tok_rows + jnp.arange(tok_rows, dtype=jnp.int32)[None, :]
+    ).reshape(-1)
+    key_index = jnp.where(
+        jnp.repeat(offsets, tok_rows) <= back, key_index, -1
+    )
 
     scores = jnp.einsum(
         "hqd,kd->hqk", queries, key_rows, preferred_element_type=jnp.float32
@@ -123,13 +150,17 @@
     partial_out = lax.dot_general(
         attended, wo_rows, (((1,), (1,)), ((), ())), preferred_element_type=jnp.float32
     )
-    attn_mine = lax.psum_scatter(
-        partial_out.astype(jnp.bfloat16), "mp", scatter_dimension=1, tiled=True
-    ).astype(jnp.float32)
+    swapped_out = lax.all_to_all(partial_out.astype(jnp.bfloat16), "mp", 1, 0, tiled=True)
+    attn_mine = jnp.sum(
+        swapped_out.reshape(mp_count, tok_rows, D // mp_count).astype(jnp.float32), axis=0
+    )
     residual = (hidden_in.astype(jnp.float32) + attn_mine).astype(jnp.bfloat16)
     residual_f = residual.astype(jnp.float32)
-    square_sum = lax.psum(jnp.sum(residual_f * residual_f, axis=-1), "mp")
-    moe_local = (residual_f * lax.rsqrt(square_sum / D + EPSILON)[:, None]).astype(jnp.bfloat16)
+    residual_rows = lax.all_gather(residual, "mp", axis=1, tiled=True).astype(jnp.float32)
+    full_rows = (
+        residual_rows
+        * lax.rsqrt(jnp.sum(residual_rows * residual_rows, axis=-1, keepdims=True) / D + EPSILON)
+    ).astype(jnp.bfloat16)
 
     local_experts = expert_gate.shape[0]
     experts = seq_count * local_experts
@@ -142,15 +173,11 @@
     mine = (earlier_count // part_cap) == mp_index
     slot_index = flat_ids * part_cap + earlier_count % part_cap
     send_index = jnp.where(mine, slot_index, experts * part_cap)
-    source_row = jnp.arange(tok_rows * top_count, dtype=jnp.int32) // top_count
-    full_rows = lax.all_gather(moe_local, "mp", axis=1, tiled=True)
-    buffer = (
-        jnp.zeros((experts * part_cap, D), jnp.bfloat16)
-        .at[send_index]
-        .set(full_rows[source_row], mode="drop")
-    )
+    slots = jnp.arange(experts * part_cap, dtype=jnp.int32)
+    pick = (send_index[None, :] == slots[:, None]).reshape(experts * part_cap, tok_rows, top_count)
+    select = jnp.sum(pick.astype(jnp.bfloat16), axis=2)
+    buffer = jnp.dot(select, full_rows, preferred_element_type=jnp.float32).astype(jnp.bfloat16)
     arrived = lax.all_to_all(buffer, "seq", 0, 0, tiled=True)
-    hidden_units = expert_all.shape[1]
     w_gate = expert_all[0]
     w_up = expert_all[1]
     w_down = expert_all[2]
@@ -165,15 +192,23 @@
     returned = lax.all_to_all(result, "seq", 0, 0, tiled=True)
 
     gate_weights = jax.nn.softmax(gate_logits, axis=-1)
-    picked_back = returned[jnp.where(mine, slot_index, 0)].astype(jnp.float32)
     share = jnp.where(mine, gate_weights.reshape(-1), 0.0)
-    weighted = picked_back * share[:, None]
-    partial_moe = jnp.sum(weighted.reshape(tok_rows, top_count, D), axis=1)
+    combine = jnp.sum(
+        jnp.where(
+            send_index[:, None] == slots[None, :], share[:, None], 0.0
+        ).reshape(tok_rows, top_count, experts * part_cap),
+        axis=1,
+    )
+    partial_moe = jnp.dot(
+        combine,
+        returned.astype(jnp.float32),
+        precision=lax.Precision.HIGHEST,
+        preferred_element_type=jnp.float32,
+    )
     swapped = lax.all_to_all(partial_moe.astype(jnp.bfloat16), "mp", 1, 0, tiled=True)
     moe_total = jnp.sum(
         swapped.reshape(mp_count, tok_rows, D // mp_count).astype(jnp.float32), axis=0
     )
-    del hidden_units
     return (residual_f + moe_total).astype(jnp.bfloat16)
 
 

time: 357 us -> 285 us (0.80); the launches traced: 351 us -> 284 us
  local copies, waits for them, and re-layouts: 41.8 us -> 11 us
  waiting for transfers between devices: 59.3 us -> 32.5 us
  starting transfers between devices: 71.5 us -> 61.5 us
  blocking collectives: 102 us -> 98.1 us
  matrix products: 27.5 us -> 31.4 us
    all_gather x1, waiting for transfers between devices: 21.1 us -> 0.01 us  [local(): lax.all_gather(jnp.concatenate([expert_gate, expert_up, expert_down], axi...]
    scatter x1 -> x0, local copies, waits for them, and re-layouts: 16.3 us -> none  [local(): buffer = jnp.zeros((experts * part_cap, D), jnp.bfloat16).at[send_index]....]
    unnamed x3 -> x1, waiting for transfers between devices: 11.4 us -> 0.02 us
    all_to_all x0 -> x1, waiting for transfers between devices: none -> 9.97 us  [local(): lax.all_to_all(partial_out.astype(jnp.bfloat16), 'mp', 1, 0, tiled=True)]
    ppermute x16 -> x9, starting transfers between devices: 50.6 us -> 40.8 us  [the longest x8 40.8 us: local(): fetched.append(lax.ppermute(kv_own, ('seq', 'mp'), pairs))]
    convert_element_type x3 -> x0, local copies, waits for them, and re-layouts: 7.3 us -> none  [the longest x1 6.67 us: local(): picked_back = returned[jnp.where(mine, slot_index, 0)].astype(jnp.float32)]
    reduce_sum x2 -> x4, other arithmetic: 7.57 us -> 0.97 us  [the longest x1 0.34 us: local(): jnp.sum(jnp.where(send_index[:, None] == slots[None, :], share[:, None],...]
    gather x1 -> x0, local copies, waits for them, and re-layouts: 5.64 us -> none  [local(): picked_back = returned[jnp.where(mine, slot_index, 0)].astype(jnp.float32)]
  transfers between devices with their start and end apart: 20 -> 13, of which waited for: 4 -> 3; matrix products, arithmetic and copies ran while one was open for 11% -> 20% of each run, Pallas kernels for 0% -> 0%
where the time goes in v2:
time: 285 us; the launch traced here: 284 us
  blocking collectives  98.1 us (34%)
  starting transfers between devices  61.5 us (22%)
  other arithmetic  33.9 us (12%)
  waiting for transfers between devices  32.5 us (11%)
  matrix products  31.4 us (11%)
  between operations  15.3 us (5%)
  local copies, waits for them, and re-layouts  11 us (4%)
    all_gather x1, blocking collectives, local(): whole = lax.all_gather(hidden_in, 'mp', axis=1, tiled=True)  41.7 us
    ppermute x8, starting transfers between devices, local(): fetched.append(lax.ppermute(kv_own, ('seq', 'mp'), pairs))  40.8 us
    all_to_all x1, blocking collectives, local(): arrived = lax.all_to_all(buffer, 'seq', 0, 0, tiled=True)  31.6 us
    all_to_all x1, waiting for transfers between devices, local(): returned = lax.all_to_all(result, 'seq', 0, 0, tiled=True)  20.7 us
    all_to_all x1, blocking collectives, local(): lax.all_to_all(partial_moe.astype(jnp.bfloat16), 'mp', 1, 0, tiled=True)  15.8 us
    another operation x5, other arithmetic  11.5 us
    all_to_all x1, starting transfers between devices, gather_seq(): return lax.all_to_all(spread, 'seq', 0, 0, tiled=True)  11.3 us
    all_to_all x1, waiting for transfers between devices, local(): lax.all_to_all(partial_out.astype(jnp.bfloat16), 'mp', 1, 0, tiled=True)  9.97 us
  transfers between devices with their start and end apart: 13, of which 3 were waited for; matrix products, arithmetic and copies ran while one was open for 20% of the time, Pallas kernels for 0%

profile of v2, /device:TPU:1, one launch (start us, length us, event | category | flops | bytes accessed | tf_op | source)
XLA Modules:
  0.0 283.6 jit_solution(2247942378175176764)
XLA Ops:
  8.1 2.0 broadcast_in_dim.53
  10.1 11.3 %all-to-all-start = ((bf16[32,48,1024]{2,1,0:T(8,128)(2,1)}), bf16[32,48,1024]{2,1,0:T(8,128)(2,1)S(1)}, u32[]{:S(2)}, u32[]{:S(2)}) async-start(bf16[32,48,1024]{2,1,0:T(8,128)(2,1)} %broadcast_in_dim.53), calls=%async_computation | async-start | bytes 6291456 | tf_op jit(solution)/shard_map/all_to_all | solution.py:47
  21.5 2.9 %pad_maximum_fusion.1 = bf16[3,192,1536]{2,1,0:T(8,128)(2,1)} fusion(bf16[1,192,1536]{2,1,0:T(8,128)(2,1)} %param.19, bf16[1,192,1536]{2,1,0:T(8,128)(2,1)} %param.18, bf16[1,192,1536]{2,1,0:T(8,128)(2,1)} %param.17), kind=kLoop, calls=%fused_computation.35 | loop fusion | flops 1769472 | bytes 3538944 | tf_op jit(solution)/shard_map/concatenate | solution.py:63
  27.2 41.7 %all_gather.9 = bf16[256,1536]{1,0:T(8,128)(2,1)S(1)} all-gather(bf16[256,384]{1,0:T(8,128)(2,1)S(1)} %copy-done.5), channel_id=1, replica_groups=mesh['seq'=32,'mp'=4] {'mp'}, dimensions={1}, use_global_device_ids=true | all-gather | bytes 983040 | tf_op jit(solution)/shard_map/all_gather | solution.py:73
  70.4 2.5 fusion.14
  74.4 4.8 %collective-permute-start = (bf16[256,256]{0,1:T(8,128)(2,1)S(1)}, bf16[256,256]{0,1:T(8,128)(2,1)S(1)}, u32[]{:S(2)}, u32[]{:S(2)}) collective-permute-start(bf16[256,256]{0,1:T(8,128)(2,1)S(1)} %pad_maximum_fusion.2), channel_id=1, source_target_pairs={{0,4},{1,9},{2,6},{3,11},{4,8},{5,13},{6,10},{7,15},{8,12},{9,17},... | collective-permute-start | bytes 393224 | tf_op jit(solution)/shard_map/ppermute | solution.py:101
  79.3 4.9 %collective-permute-start.1 = (bf16[256,256]{0,1:T(8,128)(2,1)S(1)}, bf16[256,256]{0,1:T(8,128)(2,1)S(1)}, u32[]{:S(2)}, u32[]{:S(2)}) collective-permute-start(bf16[256,256]{0,1:T(8,128)(2,1)S(1)} %pad_maximum_fusion.2), channel_id=1, source_target_pairs={{0,12},{1,17},{2,14},{3,19},{4,16},{5,21},{6,18},{7,23},{8,20},{9,... | collective-permute-start | bytes 393224 | tf_op jit(solution)/shard_map/ppermute | solution.py:101
  84.2 12.1 %collective-permute-start.2 = (bf16[256,256]{0,1:T(8,128)(2,1)S(1)}, bf16[256,256]{0,1:T(8,128)(2,1)S(1)}, u32[]{:S(2)}, u32[]{:S(2)}) collective-permute-start(bf16[256,256]{0,1:T(8,128)(2,1)S(1)} %pad_maximum_fusion.2), channel_id=1, source_target_pairs={{0,20},{1,25},{2,22},{3,27},{4,24},{5,29},{6,26},{7,31},{8,28},{9,... | collective-permute-start | bytes 393224 | tf_op jit(solution)/shard_map/ppermute | solution.py:101
  97.8 3.7 %collective-permute-start.4 = (bf16[256,256]{0,1:T(8,128)(2,1)S(1)}, bf16[256,256]{0,1:T(8,128)(2,1)S(1)}, u32[]{:S(2)}, u32[]{:S(2)}) collective-permute-start(bf16[256,256]{0,1:T(8,128)(2,1)S(1)} %pad_maximum_fusion.2), channel_id=1, source_target_pairs={{0,36},{1,41},{2,38},{3,43},{4,40},{5,45},{6,42},{7,47},{8,44},{9,... | collective-permute-start | bytes 393224 | tf_op jit(solution)/shard_map/ppermute | solution.py:101
  101.5 4.3 %collective-permute-start.5 = (bf16[256,256]{0,1:T(8,128)(2,1)S(1)}, bf16[256,256]{0,1:T(8,128)(2,1)S(1)}, u32[]{:S(2)}, u32[]{:S(2)}) collective-permute-start(bf16[256,256]{0,1:T(8,128)(2,1)S(1)} %pad_maximum_fusion.2), channel_id=1, source_target_pairs={{0,44},{1,49},{2,46},{3,51},{4,48},{5,53},{6,50},{7,55},{8,52},{9,... | collective-permute-start | bytes 393224 | tf_op jit(solution)/shard_map/ppermute | solution.py:101
  107.9 7.5 %collective-permute-start.7 = (bf16[256,256]{0,1:T(8,128)(2,1)S(1)}, bf16[256,256]{0,1:T(8,128)(2,1)S(1)}, u32[]{:S(2)}, u32[]{:S(2)}) collective-permute-start(bf16[256,256]{0,1:T(8,128)(2,1)S(1)} %pad_maximum_fusion.2), channel_id=1, source_target_pairs={{0,60},{1,65},{2,62},{3,67},{4,64},{5,69},{6,66},{7,71},{8,68},{9,... | collective-permute-start | bytes 393224 | tf_op jit(solution)/shard_map/ppermute | solution.py:101
  119.3 9.2 %reduce-window.6 = s32[32,8,128]{2,1,0:T(8,128)S(1)} reduce-window(s32[32,8,128]{2,1,0:T(8,128)S(1)} %fusion.36, s32[]{:T(128)} %constant.89.clone.1), window={size=1x1x128 pad=0_0x0_0x127_0}, to_apply=%region_4.5 | reduce-window | flops 4161536 | bytes 262148 | tf_op jit(solution)/shard_map/reduce-window
  139.0 6.5 %fusion = (f32[3,256]{1,0:T(4,128)S(1)}, f32[3,256,4352]{2,1,0:T(8,128)}) fusion(pred[256,4352]{1,0:T(8,128)(4,1)S(1)} %fusion.10, bf16[4352,256]{1,0:T(8,128)(2,1)S(1)} %pad_maximum_fusion, bf16[256,3,64]{2,0,1:T(8,128)(2,1)S(1)} %copy-done.8, bf16[256,3,64]{2,0,1:T(8,128)(2,1)S(1)} %copy-done.7), kind=kOutput, calls=%fused_computation.2 | convolution fusion | flops 866057472 | bytes 15993856 | tf_op jit(solution)/shard_map/hqd,kd->hqk/dot_general | solution.py:127
  145.5 9.0 %fusion.1 = f32[3,256]{1,0:T(4,128)S(1)} fusion(f32[3,256,4352]{2,1,0:T(8,128)} %get-tuple-element.22, f32[3,256]{1,0:T(4,128)S(1)} %get-tuple-element.21, pred[256,4352]{1,0:T(8,128)(4,1)S(1)} %fusion.10), kind=kLoop, calls=%fused_computation.3 | loop fusion | flops 16710912 | bytes 14489600 | tf_op jit(solution)/shard_map/reduce_sum | solution.py:142
  154.5 7.0 %fusion.25 = bf16[256,3,128]{0,2,1:T(8,128)(2,1)S(1)} fusion(bf16[4352,256]{1,0:T(8,128)(2,1)S(1)} %pad_maximum_fusion, f32[3,256,4352]{2,1,0:T(8,128)} %get-tuple-element.22, f32[3,256]{1,0:T(4,128)S(1)} %get-tuple-element.21, pred[256,4352]{1,0:T(8,128)(4,1)S(1)} %fusion.10, f32[256,3]{0,1:T(4,128)S(1)} %bitcast.116), kind=kOutput, calls=%fused_computation.52 | convolution fusion | flops 869203968 | bytes 15802368 | tf_op jit(solution)/shard_map/hqk,kd->hqd/dot_general | solution.py:143
  164.4 4.1 %all-to-all-start.1 = ((bf16[256,4,384]{2,0,1:T(8,128)(2,1)}), bf16[256,4,384]{2,0,1:T(8,128)(2,1)S(1)}, u32[]{:S(2)}, u32[]{:S(2)}) async-start(bf16[256,4,384]{2,0,1:T(8,128)(2,1)} %bitcast.99), calls=%async_computation.1 | async-start | bytes 1572864 | tf_op jit(solution)/shard_map/all_to_all | solution.py:153
  169.3 10.0 %all-to-all-done.1 = bf16[256,4,384]{2,0,1:T(8,128)(2,1)S(1)} async-done(((bf16[256,4,384]{2,0,1:T(8,128)(2,1)}), bf16[256,4,384]{2,0,1:T(8,128)(2,1)S(1)}, u32[]{:S(2)}, u32[]{:S(2)}) %all-to-all-start.1) | async-done | bytes 786464 | tf_op jit(solution)/shard_map/all_to_all | solution.py:153
  179.4 8.9 %all_gather.10 = bf16[256,1536]{1,0:T(8,128)(2,1)S(1)} all-gather(bf16[256,384]{1,0:T(8,128)(2,1)S(1)} %add_convert_fusion.1), channel_id=1, replica_groups=mesh['seq'=32,'mp'=4] {'mp'}, dimensions={1}, use_global_device_ids=true | all-gather | bytes 983040 | tf_op jit(solution)/shard_map/all_gather | solution.py:159
  189.3 31.6 %all_to_all.59 = bf16[32,16,1536]{2,1,0:T(8,128)(2,1)S(1)} all-to-all(bf16[32,16,1536]{2,1,0:T(8,128)(2,1)S(1)} %bitcast.100), channel_id=1, replica_groups=mesh['seq'=32,'mp'=4] {'seq'}, dimensions={0} | all-to-all | bytes 3145728 | tf_op jit(solution)/shard_map/all_to_all | solution.py:180
  220.9 4.2 %fusion.11 = f32[512,768]{1,0:T(8,128)} fusion(bf16[512,1536]{1,0:T(8,128)(2,1)S(1)} %bitcast.108, bf16[3,768,1536]{2,1,0:T(8,128)(2,1)} %all-gather.2.cloned.1.call-done), kind=kOutput, calls=%fused_computation.21 | convolution fusion | flops 1207959552 | bytes 5505024 | tf_op jit(solution)/shard_map/dot_general | solution.py:187
  225.1 7.2 %convolution_convert_fusion = bf16[512,1536]{1,0:T(8,128)(2,1)} fusion(bf16[3,768,1536]{2,1,0:T(8,128)(2,1)} %all-gather.2.cloned.1.call-done, f32[512,768]{1,0:T(8,128)} %fusion.11, bf16[512,1536]{1,0:T(8,128)(2,1)S(1)} %bitcast.109), kind=kOutput, calls=%fused_computation.15 | convolution fusion | flops 2417885184 | bytes 9437184 | tf_op jit(solution)/shard_map/dot_general | solution.py:191
  232.3 5.2 %all-to-all-start.3 = ((bf16[32,16,1536]{2,1,0:T(8,128)(2,1)}), bf16[32,16,1536]{2,1,0:T(8,128)(2,1)S(1)}, u32[]{:S(2)}, u32[]{:S(2)}) async-start(bf16[32,16,1536]{2,1,0:T(8,128)(2,1)} %bitcast.30), calls=%async_computation.3 | async-start | bytes 3145728 | tf_op jit(solution)/shard_map/all_to_all | solution.py:192
  238.0 20.7 %all-to-all-done.3 = bf16[32,16,1536]{2,1,0:T(8,128)(2,1)S(1)} async-done(((bf16[32,16,1536]{2,1,0:T(8,128)(2,1)}), bf16[32,16,1536]{2,1,0:T(8,128)(2,1)S(1)}, u32[]{:S(2)}, u32[]{:S(2)}) %all-to-all-start.3) | async-done | bytes 1572896 | tf_op jit(solution)/shard_map/all_to_all | solution.py:192
  260.1 15.8 %all_to_all.60 = bf16[256,4,384]{2,0,1:T(8,128)(2,1)S(1)} all-to-all(bf16[256,4,384]{2,0,1:T(8,128)(2,1)S(1)} %bitcast.106), channel_id=1, replica_groups=mesh['seq'=32,'mp'=4] {'mp'}, dimensions={1} | all-to-all | bytes 1572864 | tf_op jit(solution)/shard_map/all_to_all | solution.py:208
  (114 shorter events, 31.0 us)
Async XLA Ops:
  10.1 60.3 %all-to-all-start = ((bf16[32,48,1024]{2,1,0:T(8,128)(2,1)}), bf16[32,48,1024]{2,1,0:T(8,128)(2,1)S(1)}, u32[]{:S(2)}, u32[]{:S(2)}) async-start(bf16[32,48,1024]{2,1,0:T(8,128)(2,1)} %broadcast_in_dim.53), calls=%async_computation | async-start | bytes 6291456 | tf_op jit(solution)/shard_map/all_to_all | solution.py:47
  21.5 3.2 %copy-start.11 = (s32[3]{0:T(128)S(1)}, s32[3]{0:T(128)}, u32[]{:S(2)}) copy-start(s32[3]{0:T(128)} %param.14) | copy-start | bytes 40
  21.5 5.7 %copy-start.5 = (bf16[256,384]{1,0:T(8,128)(2,1)S(1)}, bf16[256,384]{1,0:T(8,128)(2,1)}, u32[]{:S(2)}) copy-start(bf16[256,384]{1,0:T(8,128)(2,1)} %param.10) | copy-start | bytes 589828
  21.5 199.4 %all-gather.2.cloned.1.call-start = ((), (), s32[]{:S(2)}) async-start(), calls=%async_computation.5 | async-start | bytes 8847360 | tf_op jit(solution)/shard_map/all_gather | solution.py:62
  70.4 2.6 copy-start.1
  73.8 45.1 %copy-start.10 = (s32[256,4]{0,1:T(4,128)S(1)}, s32[256,4]{0,1:T(4,128)}, u32[]{:S(2)}) copy-start(s32[256,4]{0,1:T(4,128)} %param.15) | copy-start | bytes 12292
  74.4 27.1 %collective-permute-start = (bf16[256,256]{0,1:T(8,128)(2,1)S(1)}, bf16[256,256]{0,1:T(8,128)(2,1)S(1)}, u32[]{:S(2)}, u32[]{:S(2)}) collective-permute-start(bf16[256,256]{0,1:T(8,128)(2,1)S(1)} %pad_maximum_fusion.2), channel_id=1, source_target_pairs={{0,4},{1,9},{2,6},{3,11},{4,8},{5,13},{6,10},{7,15},{8,12},{9,17},... | collective-permute-start | bytes 393224 | tf_op jit(solution)/shard_map/ppermute | solution.py:101
  79.3 26.6 %collective-permute-start.1 = (bf16[256,256]{0,1:T(8,128)(2,1)S(1)}, bf16[256,256]{0,1:T(8,128)(2,1)S(1)}, u32[]{:S(2)}, u32[]{:S(2)}) collective-permute-start(bf16[256,256]{0,1:T(8,128)(2,1)S(1)} %pad_maximum_fusion.2), channel_id=1, source_target_pairs={{0,12},{1,17},{2,14},{3,19},{4,16},{5,21},{6,18},{7,23},{8,20},{9,... | collective-permute-start | bytes 393224 | tf_op jit(solution)/shard_map/ppermute | solution.py:101
  84.2 23.6 %collective-permute-start.2 = (bf16[256,256]{0,1:T(8,128)(2,1)S(1)}, bf16[256,256]{0,1:T(8,128)(2,1)S(1)}, u32[]{:S(2)}, u32[]{:S(2)}) collective-permute-start(bf16[256,256]{0,1:T(8,128)(2,1)S(1)} %pad_maximum_fusion.2), channel_id=1, source_target_pairs={{0,20},{1,25},{2,22},{3,27},{4,24},{5,29},{6,26},{7,31},{8,28},{9,... | collective-permute-start | bytes 393224 | tf_op jit(solution)/shard_map/ppermute | solution.py:101
  96.3 19.0 %collective-permute-start.3 = (bf16[256,256]{0,1:T(8,128)(2,1)S(1)}, bf16[256,256]{0,1:T(8,128)(2,1)S(1)}, u32[]{:S(2)}, u32[]{:S(2)}) collective-permute-start(bf16[256,256]{0,1:T(8,128)(2,1)S(1)} %pad_maximum_fusion.2), channel_id=1, source_target_pairs={{0,28},{1,33},{2,30},{3,35},{4,32},{5,37},{6,34},{7,39},{8,36},{9,... | collective-permute-start | bytes 393224 | tf_op jit(solution)/shard_map/ppermute | solution.py:101
  97.8 17.6 %collective-permute-start.4 = (bf16[256,256]{0,1:T(8,128)(2,1)S(1)}, bf16[256,256]{0,1:T(8,128)(2,1)S(1)}, u32[]{:S(2)}, u32[]{:S(2)}) collective-permute-start(bf16[256,256]{0,1:T(8,128)(2,1)S(1)} %pad_maximum_fusion.2), channel_id=1, source_target_pairs={{0,36},{1,41},{2,38},{3,43},{4,40},{5,45},{6,42},{7,47},{8,44},{9,... | collective-permute-start | bytes 393224 | tf_op jit(solution)/shard_map/ppermute | solution.py:101
  101.5 13.9 %collective-permute-start.5 = (bf16[256,256]{0,1:T(8,128)(2,1)S(1)}, bf16[256,256]{0,1:T(8,128)(2,1)S(1)}, u32[]{:S(2)}, u32[]{:S(2)}) collective-permute-start(bf16[256,256]{0,1:T(8,128)(2,1)S(1)} %pad_maximum_fusion.2), channel_id=1, source_target_pairs={{0,44},{1,49},{2,46},{3,51},{4,48},{5,53},{6,50},{7,55},{8,52},{9,... | collective-permute-start | bytes 393224 | tf_op jit(solution)/shard_map/ppermute | solution.py:101
  105.9 9.6 %collective-permute-start.6 = (bf16[256,256]{0,1:T(8,128)(2,1)S(1)}, bf16[256,256]{0,1:T(8,128)(2,1)S(1)}, u32[]{:S(2)}, u32[]{:S(2)}) collective-permute-start(bf16[256,256]{0,1:T(8,128)(2,1)S(1)} %pad_maximum_fusion.2), channel_id=1, source_target_pairs={{0,52},{1,57},{2,54},{3,59},{4,56},{5,61},{6,58},{7,63},{8,60},{9,... | collective-permute-start | bytes 393224 | tf_op jit(solution)/shard_map/ppermute | solution.py:101
  107.9 9.4 %collective-permute-start.7 = (bf16[256,256]{0,1:T(8,128)(2,1)S(1)}, bf16[256,256]{0,1:T(8,128)(2,1)S(1)}, u32[]{:S(2)}, u32[]{:S(2)}) collective-permute-start(bf16[256,256]{0,1:T(8,128)(2,1)S(1)} %pad_maximum_fusion.2), channel_id=1, source_target_pairs={{0,60},{1,65},{2,62},{3,67},{4,64},{5,69},{6,66},{7,71},{8,68},{9,... | collective-permute-start | bytes 393224 | tf_op jit(solution)/shard_map/ppermute | solution.py:101
  115.4 15.4 %slice-start = ((f32[256,640]{1,0:T(8,128)}), f32[256,384]{1,0:T(8,128)S(1)}, s32[]{:S(2)}) async-start(f32[256,640]{1,0:T(8,128)} %copy-done.3), calls=%async_computation.6 | async-start | bytes 786432 | tf_op jit(solution)/shard_map/slice | solution.py:82
  117.3 13.8 %copy-start.4 = (bf16[8,256,256]{1,2,0:T(8,128)(2,1)}, bf16[8,256,256]{1,2,0:T(8,128)(2,1)S(1)}, u32[]{:S(2)}) copy-start(bf16[8,256,256]{1,2,0:T(8,128)(2,1)S(1)} %bitcast_dynamic-update-slice_fusion) | copy-start | bytes 3145732
  117.3 15.9 %collective-permute-start.8 = (bf16[8,256,256]{1,2,0:T(8,128)(2,1)S(1)}, bf16[8,256,256]{1,2,0:T(8,128)(2,1)}, u32[]{:S(2)}, u32[]{:S(2)}) collective-permute-start(bf16[8,256,256]{1,2,0:T(8,128)(2,1)S(1)} %bitcast_dynamic-update-slice_fusion), channel_id=1, source_target_pairs={{0,1},{1,0},{2,3},{3,2},{4,5},{5,4},{6,7},{7,6},{8,9},{9,8},{10,11... | collective-permute-start | bytes 3145736 | tf_op jit(solution)/shard_map/ppermute | solution.py:103
  136.2 1.3 copy-start
  137.5 1.5 copy-start.7
  137.5 1.5 copy-start.8
  164.4 15.0 %copy-start.6 = (bf16[256,384]{1,0:T(8,128)(2,1)S(1)}, bf16[256,384]{1,0:T(8,128)(2,1)}, u32[]{:S(2)}) copy-start(bf16[256,384]{1,0:T(8,128)(2,1)} %param.10) | copy-start | bytes 589828
  164.4 14.9 %all-to-all-start.1 = ((bf16[256,4,384]{2,0,1:T(8,128)(2,1)}), bf16[256,4,384]{2,0,1:T(8,128)(2,1)S(1)}, u32[]{:S(2)}, u32[]{:S(2)}) async-start(bf16[256,4,384]{2,0,1:T(8,128)(2,1)} %bitcast.99), calls=%async_computation.1 | async-start | bytes 1572864 | tf_op jit(solution)/shard_map/all_to_all | solution.py:153
  232.3 5.2 %copy-start.9 = (f32[256,4]{0,1:T(4,128)S(1)}, f32[256,4]{0,1:T(4,128)}, u32[]{:S(2)}) copy-start(f32[256,4]{0,1:T(4,128)} %param.16) | copy-start | bytes 12292
  232.3 26.3 %all-to-all-start.3 = ((bf16[32,16,1536]{2,1,0:T(8,128)(2,1)}), bf16[32,16,1536]{2,1,0:T(8,128)(2,1)S(1)}, u32[]{:S(2)}, u32[]{:S(2)}) async-start(bf16[32,16,1536]{2,1,0:T(8,128)(2,1)} %bitcast.30), calls=%async_computation.3 | async-start | bytes 3145728 | tf_op jit(solution)/shard_map/all_to_all | solution.py:192
  (2 other events, 1.7 us)
Sparse Core Ops, SparseCore 0:
  24.6 99.6 all-gather.1

commit v3 on v2

--- a/solution.py
+++ b/solution.py
@@ -59,9 +59,18 @@
     q_cols = heads_here * HD
     kv_group = mp_index * heads_here // (HQ // KVH)
 
-    expert_all = lax.all_gather(
-        jnp.concatenate([expert_gate, expert_up, expert_down], axis=0), "mp", axis=1, tiled=True
-    )
+    whole = lax.all_gather(hidden_in, "mp", axis=1, tiled=True)
+    expert_own, whole = lax.optimization_barrier(
+        (jnp.concatenate([expert_gate, expert_up, expert_down], axis=0), whole)
+    )
+    mp_count_static = lax.axis_size("mp")
+    across = lax.ppermute(expert_own, "mp", [(m, m ^ 2) for m in range(mp_count_static)])
+    beside = lax.ppermute(
+        jnp.concatenate([expert_own, across], axis=1),
+        "mp",
+        [(m, m ^ 1) for m in range(mp_count_static)],
+    )
+    expert_all = jnp.concatenate([expert_own, across, beside], axis=1)
 
     key_cols = lax.dynamic_slice_in_dim(wkv, kv_group * HD, HD, 1)
     value_cols = lax.dynamic_slice_in_dim(wkv, KVH * HD + kv_group * HD, HD, 1)
@@ -70,7 +79,6 @@
     w_qkv = weights[:, : q_cols + 2 * HD]
     wo_rows = weights[:, q_cols + 2 * HD :]
 
-    whole = lax.all_gather(hidden_in, "mp", axis=1, tiled=True)
     whole_f = whole.astype(jnp.float32)
     normed = (
         whole_f * lax.rsqrt(jnp.sum(whole_f * whole_f, axis=-1, keepdims=True) / D + EPSILON)
@@ -169,7 +177,12 @@
     part_cap = capacity // mp_count
     flat_ids = routes.reshape(-1)
     one_hot = (flat_ids[:, None] == jnp.arange(experts, dtype=jnp.int32)[None, :]).astype(jnp.int32)
-    earlier_count = jnp.sum((jnp.cumsum(one_hot, axis=0) - one_hot) * one_hot, axis=1)
+    pair_count = tok_rows * top_count
+    before = (
+        jnp.arange(pair_count, dtype=jnp.int32)[:, None] > jnp.arange(pair_count, dtype=jnp.int32)[None, :]
+    ).astype(jnp.bfloat16)
+    earlier_all = jnp.dot(before, one_hot.astype(jnp.bfloat16), preferred_element_type=jnp.float32)
+    earlier_count = jnp.sum(earlier_all.astype(jnp.int32) * one_hot, axis=1)
     mine = (earlier_count // part_cap) == mp_index
     slot_index = flat_ids * part_cap + earlier_count % part_cap
     send_index = jnp.where(mine, slot_index, experts * part_cap)

time: 285 us -> 301 us (1.056)
  blocking collectives: 98.1 us -> 64.3 us
  local copies, waits for them, and re-layouts: 11 us -> 43.3 us
  between operations: 15.3 us -> 1.6 us
  starting transfers between devices: 61.5 us -> 74.4 us
  waiting for transfers between devices: 32.5 us -> 43.1 us
  other arithmetic: 33.9 us -> 39.7 us
    all_to_all x1 -> x0, blocking collectives: 31.6 us -> none  [local(): arrived = lax.all_to_all(buffer, 'seq', 0, 0, tiled=True)]
    all_to_all x0 -> x1, waiting for transfers between devices: none -> 16.2 us  [local(): arrived = lax.all_to_all(buffer, 'seq', 0, 0, tiled=True)]
    unnamed x36 -> x40, local copies, waits for them, and re-layouts: 2.25 us -> 17 us
    all_to_all x0 -> x1, starting transfers between devices: none -> 11.1 us  [local(): arrived = lax.all_to_all(buffer, 'seq', 0, 0, tiled=True)]
    another operation x5 -> x2, other arithmetic: 11.5 us -> 3.23 us
    ppermute x8, starting transfers between devices: 40.8 us -> 35 us  [local(): fetched.append(lax.ppermute(kv_own, ('seq', 'mp'), pairs))]
    all_to_all x1, waiting for transfers between devices: 9.97 us -> 5.72 us  [local(): lax.all_to_all(partial_out.astype(jnp.bfloat16), 'mp', 1, 0, tiled=True)]
    concatenate x0 -> x1, local copies, waits for them, and re-layouts: none -> 4.01 us  [local(): expert_all = jnp.concatenate([expert_own, across, beside], axis=1)]
  transfers between devices with their start and end apart: 13 -> 15, of which waited for: 3 -> 4; matrix products, arithmetic and copies ran while one was open for 20% -> 33% of each run, Pallas kernels for 0% -> 0%
where the time goes in v3:
time: 301 us; the launch traced here: 299 us
  starting transfers between devices  74.4 us (25%)
  blocking collectives  64.3 us (21%)
  local copies, waits for them, and re-layouts  43.3 us (14%)
  waiting for transfers between devices  43.1 us (14%)
  other arithmetic  39.7 us (13%)
  matrix products  32.6 us (11%)
    all_gather x1, blocking collectives, local(): whole = lax.all_gather(hidden_in, 'mp', axis=1, tiled=True)  39.7 us
    ppermute x8, starting transfers between devices, local(): fetched.append(lax.ppermute(kv_own, ('seq', 'mp'), pairs))  35 us
    all_to_all x1, waiting for transfers between devices, local(): returned = lax.all_to_all(result, 'seq', 0, 0, tiled=True)  20.9 us
    unnamed x40, local copies, waits for them, and re-layouts  17 us
    all_to_all x1, waiting for transfers between devices, local(): arrived = lax.all_to_all(buffer, 'seq', 0, 0, tiled=True)  16.2 us
    all_to_all x1, blocking collectives, local(): lax.all_to_all(partial_moe.astype(jnp.bfloat16), 'mp', 1, 0, tiled=True)  15.7 us
    all_to_all x1, starting transfers between devices, gather_seq(): return lax.all_to_all(spread, 'seq', 0, 0, tiled=True)  11.6 us
    all_to_all x1, starting transfers between devices, local(): arrived = lax.all_to_all(buffer, 'seq', 0, 0, tiled=True)  11.1 us
  transfers between devices with their start and end apart: 15, of which 4 were waited for; matrix products, arithmetic and copies ran while one was open for 33% of the time, Pallas kernels for 0%

profile of v3, /device:TPU:1, one launch (start us, length us, event | category | flops | bytes accessed | tf_op | source)
XLA Modules:
  0.0 299.0 jit_solution(10469244090912610157)
XLA Ops:
  3.6 11.6 %all-to-all-start = ((bf16[32,48,1024]{2,1,0:T(8,128)(2,1)}), bf16[32,48,1024]{2,1,0:T(8,128)(2,1)}, u32[]{:S(2)}, u32[]{:S(2)}) async-start(bf16[32,48,1024]{2,1,0:T(8,128)(2,1)} %broadcast_in_dim.53), calls=%async_computation | async-start | bytes 6291456 | tf_op jit(solution)/shard_map/all_to_all | solution.py:47
  16.5 39.7 %all_gather.6 = bf16[256,1536]{1,0:T(8,128)(2,1)} all-gather(bf16[256,384]{1,0:T(8,128)(2,1)S(1)} %copy-done.4), channel_id=1, replica_groups=mesh['seq'=32,'mp'=4] {'mp'}, dimensions={1}, use_global_device_ids=true | all-gather | bytes 983040 | tf_op jit(solution)/shard_map/all_gather | solution.py:62
  56.2 3.1 %collective-permute-start.9 = (bf16[3,192,1536]{2,1,0:T(8,128)(2,1)S(1)}, bf16[3,192,1536]{2,1,0:T(8,128)(2,1)S(1)}, u32[]{:S(2)}, u32[]{:S(2)}) collective-permute-start(bf16[3,192,1536]{2,1,0:T(8,128)(2,1)S(1)} %pad_maximum_fusion.2), channel_id=1, source_target_pairs={{0,2},{1,3},{2,0},{3,1},{4,6},{5,7},{6,4},{7,5},{8,10},{9,11},{10,... | collective-permute-start | bytes 5308424 | tf_op jit(solution)/shard_map/ppermute | solution.py:67
  79.6 6.0 %collective-permute-start = (bf16[256,256]{0,1:T(8,128)(2,1)}, bf16[256,256]{0,1:T(8,128)(2,1)}, u32[]{:S(2)}, u32[]{:S(2)}) collective-permute-start(bf16[256,256]{0,1:T(8,128)(2,1)} %pad_maximum_fusion.3), channel_id=1, source_target_pairs={{0,4},{1,9},{2,6},{3,11},{4,8},{5,13},{6,10},{7,15},{8,12},{9,17},... | collective-permute-start | bytes 393224 | tf_op jit(solution)/shard_map/ppermute | solution.py:109
  85.6 3.3 %fusion.10 = pred[256,4352]{1,0:T(8,128)(4,1)} fusion(s32[4352]{0:T(1024)} %select_n.125, s32[256]{0:T(256)} %iota_add_fusion, s32[4352]{0:T(1024)} %convert_add_fusion, s32[256]{0:T(256)S(1)} %get-tuple-element.28, pred[4352]{0:T(1024)(128)(4,1)S(1)} %broadcast_compare_fusion), kind=kLoop, calls=%fused_computation.14 | loop fusion | flops 7798784 | bytes 1155328 | tf_op jit(solution)/shard_map/and | solution.py:142
  90.8 8.0 %collective-permute-start.2 = (bf16[256,256]{0,1:T(8,128)(2,1)}, bf16[256,256]{0,1:T(8,128)(2,1)S(1)}, u32[]{:S(2)}, u32[]{:S(2)}) collective-permute-start(bf16[256,256]{0,1:T(8,128)(2,1)} %pad_maximum_fusion.3), channel_id=1, source_target_pairs={{0,20},{1,25},{2,22},{3,27},{4,24},{5,29},{6,26},{7,31},{8,28},{9,... | collective-permute-start | bytes 393224 | tf_op jit(solution)/shard_map/ppermute | solution.py:109
  100.9 5.7 %collective-permute-start.4 = (bf16[256,256]{0,1:T(8,128)(2,1)}, bf16[256,256]{0,1:T(8,128)(2,1)S(1)}, u32[]{:S(2)}, u32[]{:S(2)}) collective-permute-start(bf16[256,256]{0,1:T(8,128)(2,1)} %pad_maximum_fusion.3), channel_id=1, source_target_pairs={{0,36},{1,41},{2,38},{3,43},{4,40},{5,45},{6,42},{7,47},{8,44},{9,... | collective-permute-start | bytes 393224 | tf_op jit(solution)/shard_map/ppermute | solution.py:109
  108.2 5.0 %collective-permute-start.5 = (bf16[256,256]{0,1:T(8,128)(2,1)}, bf16[256,256]{0,1:T(8,128)(2,1)S(1)}, u32[]{:S(2)}, u32[]{:S(2)}) collective-permute-start(bf16[256,256]{0,1:T(8,128)(2,1)} %pad_maximum_fusion.3), channel_id=1, source_target_pairs={{0,44},{1,49},{2,46},{3,51},{4,48},{5,53},{6,50},{7,55},{8,52},{9,... | collective-permute-start | bytes 393224 | tf_op jit(solution)/shard_map/ppermute | solution.py:109
  117.5 3.4 %collective-permute-start.7 = (bf16[256,256]{0,1:T(8,128)(2,1)}, bf16[256,256]{0,1:T(8,128)(2,1)S(1)}, u32[]{:S(2)}, u32[]{:S(2)}) collective-permute-start(bf16[256,256]{0,1:T(8,128)(2,1)} %pad_maximum_fusion.3), channel_id=1, source_target_pairs={{0,60},{1,65},{2,62},{3,67},{4,64},{5,69},{6,66},{7,71},{8,68},{9,... | collective-permute-start | bytes 393224 | tf_op jit(solution)/shard_map/ppermute | solution.py:109
  124.5 3.4 %collective-permute-start.8 = (bf16[8,256,256]{1,2,0:T(8,128)(2,1)}, bf16[8,256,256]{1,2,0:T(8,128)(2,1)}, u32[]{:S(2)}, u32[]{:S(2)}) collective-permute-start(bf16[8,256,256]{1,2,0:T(8,128)(2,1)} %bitcast_dynamic-update-slice_fusion), channel_id=1, source_target_pairs={{0,1},{1,0},{2,3},{3,2},{4,5},{5,4},{6,7},{7,6},{8,9},{9,8},{10,11... | collective-permute-start | bytes 3145736 | tf_op jit(solution)/shard_map/ppermute | solution.py:111
  154.2 6.4 %fusion = (f32[3,256]{1,0:T(4,128)S(1)}, f32[3,256,4352]{2,1,0:T(8,128)}) fusion(pred[256,4352]{1,0:T(8,128)(4,1)S(1)} %copy-done, bf16[4352,256]{1,0:T(8,128)(2,1)S(1)} %pad_maximum_fusion.1, bf16[256,3,64]{2,0,1:T(8,128)(2,1)S(1)} %copy-done.9, bf16[256,3,64]{2,0,1:T(8,128)(2,1)S(1)} %copy-done.8), kind=kOutput, calls=%fused_computation.2 | convolution fusion | flops 866057472 | bytes 15993856 | tf_op jit(solution)/shard_map/hqd,kd->hqk/dot_general | solution.py:135
  160.6 9.0 %fusion.1 = f32[3,256]{1,0:T(4,128)S(1)} fusion(f32[3,256,4352]{2,1,0:T(8,128)} %get-tuple-element.26, f32[3,256]{1,0:T(4,128)S(1)} %get-tuple-element.25, pred[256,4352]{1,0:T(8,128)(4,1)S(1)} %copy-done), kind=kLoop, calls=%fused_computation.3 | loop fusion | flops 16710912 | bytes 14489600 | tf_op jit(solution)/shard_map/reduce_sum | solution.py:150
  169.7 7.0 %fusion.29 = bf16[256,3,128]{0,2,1:T(8,128)(2,1)S(1)} fusion(bf16[4352,256]{1,0:T(8,128)(2,1)S(1)} %pad_maximum_fusion.1, f32[3,256,4352]{2,1,0:T(8,128)} %get-tuple-element.26, f32[3,256]{1,0:T(4,128)S(1)} %get-tuple-element.25, pred[256,4352]{1,0:T(8,128)(4,1)S(1)} %copy-done, f32[256,3]{0,1:T(4,128)S(1)} %bitcast.93), kind=kOutput, calls=%fused_computation.58 | convolution fusion | flops 869203968 | bytes 15802368 | tf_op jit(solution)/shard_map/hqk,kd->hqd/dot_general | solution.py:151
  179.6 4.7 %all-to-all-start.1 = ((bf16[256,4,384]{2,0,1:T(8,128)(2,1)}), bf16[256,4,384]{2,0,1:T(8,128)(2,1)}, u32[]{:S(2)}, u32[]{:S(2)}) async-start(bf16[256,4,384]{2,0,1:T(8,128)(2,1)} %bitcast.86), calls=%async_computation.1 | async-start | bytes 1572864 | tf_op jit(solution)/shard_map/all_to_all | solution.py:161
  189.4 5.7 %all-to-all-done.1 = bf16[256,4,384]{2,0,1:T(8,128)(2,1)} async-done(((bf16[256,4,384]{2,0,1:T(8,128)(2,1)}), bf16[256,4,384]{2,0,1:T(8,128)(2,1)}, u32[]{:S(2)}, u32[]{:S(2)}) %all-to-all-start.1) | async-done | bytes 786464 | tf_op jit(solution)/shard_map/all_to_all | solution.py:161
  198.1 8.9 %all_gather.7 = bf16[256,1536]{1,0:T(8,128)(2,1)S(1)} all-gather(bf16[256,384]{1,0:T(8,128)(2,1)S(1)} %add_convert_fusion.1), channel_id=1, replica_groups=mesh['seq'=32,'mp'=4] {'mp'}, dimensions={1}, use_global_device_ids=true | all-gather | bytes 983040 | tf_op jit(solution)/shard_map/all_gather | solution.py:167
  209.2 11.1 %all-to-all-start.2 = ((bf16[32,16,1536]{2,1,0:T(8,128)(2,1)}), bf16[32,16,1536]{2,1,0:T(8,128)(2,1)}, u32[]{:S(2)}, u32[]{:S(2)}) async-start(bf16[32,16,1536]{2,1,0:T(8,128)(2,1)} %bitcast.82), calls=%async_computation.2 | async-start | bytes 3145728 | tf_op jit(solution)/shard_map/all_to_all | solution.py:193
  223.0 4.0 %constant_dynamic-update-slice_fusion = bf16[3,768,1536]{2,1,0:T(8,128)(2,1)} fusion(bf16[3,768,1536]{2,1,0:T(8,128)(2,1)} %constant_dynamic-update-slice_fusion.1, bf16[3,384,1536]{2,1,0:T(8,128)(2,1)} %collective-permute-done.10), kind=kLoop, calls=%fused_computation.98 | loop fusion | bytes 7077888 | tf_op jit(solution)/shard_map/concatenate | solution.py:73
  227.0 16.2 %all-to-all-done.2 = bf16[32,16,1536]{2,1,0:T(8,128)(2,1)} async-done(((bf16[32,16,1536]{2,1,0:T(8,128)(2,1)}), bf16[32,16,1536]{2,1,0:T(8,128)(2,1)}, u32[]{:S(2)}, u32[]{:S(2)}) %all-to-all-start.2) | async-done | bytes 1572896 | tf_op jit(solution)/shard_map/all_to_all | solution.py:193
  243.2 3.6 %fusion.12 = f32[512,768]{1,0:T(8,128)S(1)} fusion(bf16[512,1536]{1,0:T(8,128)(2,1)} %bitcast.24, bf16[3,768,1536]{2,1,0:T(8,128)(2,1)} %constant_dynamic-update-slice_fusion), kind=kOutput, calls=%fused_computation.24 | convolution fusion | flops 1207959552 | bytes 5505024 | tf_op jit(solution)/shard_map/dot_general | solution.py:200
  246.8 7.2 %convolution_convert_fusion = bf16[512,1536]{1,0:T(8,128)(2,1)} fusion(bf16[3,768,1536]{2,1,0:T(8,128)(2,1)} %constant_dynamic-update-slice_fusion, f32[512,768]{1,0:T(8,128)S(1)} %fusion.12, bf16[512,1536]{1,0:T(8,128)(2,1)} %bitcast.24), kind=kOutput, calls=%fused_computation.18 | convolution fusion | flops 2417885184 | bytes 9437184 | tf_op jit(solution)/shard_map/dot_general | solution.py:204
  254.0 5.6 %all-to-all-start.3 = ((bf16[32,16,1536]{2,1,0:T(8,128)(2,1)}), bf16[32,16,1536]{2,1,0:T(8,128)(2,1)S(1)}, u32[]{:S(2)}, u32[]{:S(2)}) async-start(bf16[32,16,1536]{2,1,0:T(8,128)(2,1)} %bitcast.28), calls=%async_computation.3 | async-start | bytes 3145728 | tf_op jit(solution)/shard_map/all_to_all | solution.py:205
  260.0 20.9 %all-to-all-done.3 = bf16[32,16,1536]{2,1,0:T(8,128)(2,1)S(1)} async-done(((bf16[32,16,1536]{2,1,0:T(8,128)(2,1)}), bf16[32,16,1536]{2,1,0:T(8,128)(2,1)S(1)}, u32[]{:S(2)}, u32[]{:S(2)}) %all-to-all-start.3) | async-done | bytes 1572896 | tf_op jit(solution)/shard_map/all_to_all | solution.py:205
  282.4 15.7 %all_to_all.59 = bf16[256,4,384]{2,0,1:T(8,128)(2,1)S(1)} all-to-all(bf16[256,4,384]{2,0,1:T(8,128)(2,1)S(1)} %bitcast.87), channel_id=1, replica_groups=mesh['seq'=32,'mp'=4] {'mp'}, dimensions={1} | all-to-all | bytes 1572864 | tf_op jit(solution)/shard_map/all_to_all | solution.py:221
  (112 shorter events, 82.2 us)
Async XLA Ops:
  3.6 11.6 %copy-start.5 = (bf16[1,192,1536]{2,1,0:T(8,128)(2,1)S(1)}, bf16[1,192,1536]{2,1,0:T(8,128)(2,1)}, u32[]{:S(2)}) copy-start(bf16[1,192,1536]{2,1,0:T(8,128)(2,1)} %param.19) | copy-start | bytes 1769476
  3.6 11.6 %copy-start.6 = (bf16[1,192,1536]{2,1,0:T(8,128)(2,1)S(1)}, bf16[1,192,1536]{2,1,0:T(8,128)(2,1)}, u32[]{:S(2)}) copy-start(bf16[1,192,1536]{2,1,0:T(8,128)(2,1)} %param.18) | copy-start | bytes 1769476
  3.6 66.0 %all-to-all-start = ((bf16[32,48,1024]{2,1,0:T(8,128)(2,1)}), bf16[32,48,1024]{2,1,0:T(8,128)(2,1)}, u32[]{:S(2)}, u32[]{:S(2)}) async-start(bf16[32,48,1024]{2,1,0:T(8,128)(2,1)} %broadcast_in_dim.53), calls=%async_computation | async-start | bytes 6291456 | tf_op jit(solution)/shard_map/all_to_all | solution.py:47
  15.2 46.2 %copy-start.12 = (s32[3]{0:T(128)S(1)}, s32[3]{0:T(128)}, u32[]{:S(2)}) copy-start(s32[3]{0:T(128)} %param.14) | copy-start | bytes 40
  56.2 73.6 %collective-permute-start.9 = (bf16[3,192,1536]{2,1,0:T(8,128)(2,1)S(1)}, bf16[3,192,1536]{2,1,0:T(8,128)(2,1)S(1)}, u32[]{:S(2)}, u32[]{:S(2)}) collective-permute-start(bf16[3,192,1536]{2,1,0:T(8,128)(2,1)S(1)} %pad_maximum_fusion.2), channel_id=1, source_target_pairs={{0,2},{1,3},{2,0},{3,1},{4,6},{5,7},{6,4},{7,5},{8,10},{9,11},{10,... | collective-permute-start | bytes 5308424 | tf_op jit(solution)/shard_map/ppermute | solution.py:67
  79.6 21.3 %collective-permute-start = (bf16[256,256]{0,1:T(8,128)(2,1)}, bf16[256,256]{0,1:T(8,128)(2,1)}, u32[]{:S(2)}, u32[]{:S(2)}) collective-permute-start(bf16[256,256]{0,1:T(8,128)(2,1)} %pad_maximum_fusion.3), channel_id=1, source_target_pairs={{0,4},{1,9},{2,6},{3,11},{4,8},{5,13},{6,10},{7,15},{8,12},{9,17},... | collective-permute-start | bytes 393224 | tf_op jit(solution)/shard_map/ppermute | solution.py:109
  88.9 19.3 %collective-permute-start.1 = (bf16[256,256]{0,1:T(8,128)(2,1)}, bf16[256,256]{0,1:T(8,128)(2,1)S(1)}, u32[]{:S(2)}, u32[]{:S(2)}) collective-permute-start(bf16[256,256]{0,1:T(8,128)(2,1)} %pad_maximum_fusion.3), channel_id=1, source_target_pairs={{0,12},{1,17},{2,14},{3,19},{4,16},{5,21},{6,18},{7,23},{8,20},{9,... | collective-permute-start | bytes 393224 | tf_op jit(solution)/shard_map/ppermute | solution.py:109
  90.8 23.1 %collective-permute-start.2 = (bf16[256,256]{0,1:T(8,128)(2,1)}, bf16[256,256]{0,1:T(8,128)(2,1)S(1)}, u32[]{:S(2)}, u32[]{:S(2)}) collective-permute-start(bf16[256,256]{0,1:T(8,128)(2,1)} %pad_maximum_fusion.3), channel_id=1, source_target_pairs={{0,20},{1,25},{2,22},{3,27},{4,24},{5,29},{6,26},{7,31},{8,28},{9,... | collective-permute-start | bytes 393224 | tf_op jit(solution)/shard_map/ppermute | solution.py:109
  98.8 18.8 %collective-permute-start.3 = (bf16[256,256]{0,1:T(8,128)(2,1)}, bf16[256,256]{0,1:T(8,128)(2,1)S(1)}, u32[]{:S(2)}, u32[]{:S(2)}) collective-permute-start(bf16[256,256]{0,1:T(8,128)(2,1)} %pad_maximum_fusion.3), channel_id=1, source_target_pairs={{0,28},{1,33},{2,30},{3,35},{4,32},{5,37},{6,34},{7,39},{8,36},{9,... | collective-permute-start | bytes 393224 | tf_op jit(solution)/shard_map/ppermute | solution.py:109
  100.9 20.7 %collective-permute-start.4 = (bf16[256,256]{0,1:T(8,128)(2,1)}, bf16[256,256]{0,1:T(8,128)(2,1)S(1)}, u32[]{:S(2)}, u32[]{:S(2)}) collective-permute-start(bf16[256,256]{0,1:T(8,128)(2,1)} %pad_maximum_fusion.3), channel_id=1, source_target_pairs={{0,36},{1,41},{2,38},{3,43},{4,40},{5,45},{6,42},{7,47},{8,44},{9,... | collective-permute-start | bytes 393224 | tf_op jit(solution)/shard_map/ppermute | solution.py:109
  108.2 14.1 %collective-permute-start.5 = (bf16[256,256]{0,1:T(8,128)(2,1)}, bf16[256,256]{0,1:T(8,128)(2,1)S(1)}, u32[]{:S(2)}, u32[]{:S(2)}) collective-permute-start(bf16[256,256]{0,1:T(8,128)(2,1)} %pad_maximum_fusion.3), channel_id=1, source_target_pairs={{0,44},{1,49},{2,46},{3,51},{4,48},{5,53},{6,50},{7,55},{8,52},{9,... | collective-permute-start | bytes 393224 | tf_op jit(solution)/shard_map/ppermute | solution.py:109
  113.9 9.1 %collective-permute-start.6 = (bf16[256,256]{0,1:T(8,128)(2,1)}, bf16[256,256]{0,1:T(8,128)(2,1)S(1)}, u32[]{:S(2)}, u32[]{:S(2)}) collective-permute-start(bf16[256,256]{0,1:T(8,128)(2,1)} %pad_maximum_fusion.3), channel_id=1, source_target_pairs={{0,52},{1,57},{2,54},{3,59},{4,56},{5,61},{6,58},{7,63},{8,60},{9,... | collective-permute-start | bytes 393224 | tf_op jit(solution)/shard_map/ppermute | solution.py:109
  117.5 6.3 %collective-permute-start.7 = (bf16[256,256]{0,1:T(8,128)(2,1)}, bf16[256,256]{0,1:T(8,128)(2,1)S(1)}, u32[]{:S(2)}, u32[]{:S(2)}) collective-permute-start(bf16[256,256]{0,1:T(8,128)(2,1)} %pad_maximum_fusion.3), channel_id=1, source_target_pairs={{0,60},{1,65},{2,62},{3,67},{4,64},{5,69},{6,66},{7,71},{8,68},{9,... | collective-permute-start | bytes 393224 | tf_op jit(solution)/shard_map/ppermute | solution.py:109
  124.5 20.2 %collective-permute-start.8 = (bf16[8,256,256]{1,2,0:T(8,128)(2,1)}, bf16[8,256,256]{1,2,0:T(8,128)(2,1)}, u32[]{:S(2)}, u32[]{:S(2)}) collective-permute-start(bf16[8,256,256]{1,2,0:T(8,128)(2,1)} %bitcast_dynamic-update-slice_fusion), channel_id=1, source_target_pairs={{0,1},{1,0},{2,3},{3,2},{4,5},{5,4},{6,7},{7,6},{8,9},{9,8},{10,11... | collective-permute-start | bytes 3145736 | tf_op jit(solution)/shard_map/ppermute | solution.py:111
  131.8 91.3 %collective-permute-start.10 = (bf16[3,384,1536]{2,1,0:T(8,128)(2,1)}, bf16[3,384,1536]{2,1,0:T(8,128)(2,1)}, u32[]{:S(2)}, u32[]{:S(2)}) collective-permute-start(bf16[3,384,1536]{2,1,0:T(8,128)(2,1)} %pad_maximum_fusion), channel_id=1, source_target_pairs={{0,1},{1,0},{2,3},{3,2},{4,5},{5,4},{6,7},{7,6},{8,9},{9,8},{10,11... | collective-permute-start | bytes 10616840 | tf_op jit(solution)/shard_map/ppermute | solution.py:68
  152.2 2.0 copy-start.8
  152.2 2.0 copy-start.9
  176.7 7.6 %copy-start.11 = (s32[256,4]{0,1:T(4,128)S(1)}, s32[256,4]{0,1:T(4,128)}, u32[]{:S(2)}) copy-start(s32[256,4]{0,1:T(4,128)} %param.15) | copy-start | bytes 12292
  179.6 15.5 %all-to-all-start.1 = ((bf16[256,4,384]{2,0,1:T(8,128)(2,1)}), bf16[256,4,384]{2,0,1:T(8,128)(2,1)}, u32[]{:S(2)}, u32[]{:S(2)}) async-start(bf16[256,4,384]{2,0,1:T(8,128)(2,1)} %bitcast.86), calls=%async_computation.1 | async-start | bytes 1572864 | tf_op jit(solution)/shard_map/all_to_all | solution.py:161
  195.1 12.1 %copy-start.3 = (bf16[512,256]{1,0:T(8,128)(2,1)S(1)}, bf16[512,256]{1,0:T(8,128)(2,1)}, u32[]{:S(2)}) copy-start(bf16[512,256]{1,0:T(8,128)(2,1)} %fusion.27) | copy-start | bytes 786436
  209.2 34.1 %all-to-all-start.2 = ((bf16[32,16,1536]{2,1,0:T(8,128)(2,1)}), bf16[32,16,1536]{2,1,0:T(8,128)(2,1)}, u32[]{:S(2)}, u32[]{:S(2)}) async-start(bf16[32,16,1536]{2,1,0:T(8,128)(2,1)} %bitcast.82), calls=%async_computation.2 | async-start | bytes 3145728 | tf_op jit(solution)/shard_map/all_to_all | solution.py:193
  254.0 5.6 %copy-start.10 = (f32[256,4]{0,1:T(4,128)S(1)}, f32[256,4]{0,1:T(4,128)}, u32[]{:S(2)}) copy-start(f32[256,4]{0,1:T(4,128)} %param.16) | copy-start | bytes 12292
  254.0 26.9 %all-to-all-start.3 = ((bf16[32,16,1536]{2,1,0:T(8,128)(2,1)}), bf16[32,16,1536]{2,1,0:T(8,128)(2,1)S(1)}, u32[]{:S(2)}, u32[]{:S(2)}) async-start(bf16[32,16,1536]{2,1,0:T(8,128)(2,1)} %bitcast.28), calls=%async_computation.3 | async-start | bytes 3145728 | tf_op jit(solution)/shard_map/all_to_all | solution.py:205
  282.3 15.9 %copy-start.2 = (bf16[256,384]{1,0:T(8,128)(2,1)S(1)}, bf16[256,384]{1,0:T(8,128)(2,1)}, u32[]{:S(2)}) copy-start(bf16[256,384]{1,0:T(8,128)(2,1)} %copy-done.1) | copy-start | bytes 589828
  (4 other events, 4.8 us)

commit v4 on v2

--- a/solution.py
+++ b/solution.py
@@ -156,58 +156,68 @@
     )
     residual = (hidden_in.astype(jnp.float32) + attn_mine).astype(jnp.bfloat16)
     residual_f = residual.astype(jnp.float32)
-    residual_rows = lax.all_gather(residual, "mp", axis=1, tiled=True).astype(jnp.float32)
-    full_rows = (
-        residual_rows
-        * lax.rsqrt(jnp.sum(residual_rows * residual_rows, axis=-1, keepdims=True) / D + EPSILON)
-    ).astype(jnp.bfloat16)
 
     local_experts = expert_gate.shape[0]
     experts = seq_count * local_experts
     top_count = routes.shape[1]
     capacity = 2 * tok_rows * top_count // experts
     part_cap = capacity // mp_count
+    pair_count = tok_rows * top_count
     flat_ids = routes.reshape(-1)
     one_hot = (flat_ids[:, None] == jnp.arange(experts, dtype=jnp.int32)[None, :]).astype(jnp.int32)
-    earlier_count = jnp.sum((jnp.cumsum(one_hot, axis=0) - one_hot) * one_hot, axis=1)
-    mine = (earlier_count // part_cap) == mp_index
-    slot_index = flat_ids * part_cap + earlier_count % part_cap
-    send_index = jnp.where(mine, slot_index, experts * part_cap)
-    slots = jnp.arange(experts * part_cap, dtype=jnp.int32)
-    pick = (send_index[None, :] == slots[:, None]).reshape(experts * part_cap, tok_rows, top_count)
+    before = (
+        jnp.arange(pair_count, dtype=jnp.int32)[:, None]
+        > jnp.arange(pair_count, dtype=jnp.int32)[None, :]
+    ).astype(jnp.bfloat16)
+    earlier_all = jnp.dot(before, one_hot.astype(jnp.bfloat16), preferred_element_type=jnp.float32)
+    earlier_count = jnp.sum(earlier_all.astype(jnp.int32) * one_hot, axis=1)
+    slot_index = flat_ids * capacity + earlier_count
+    slots = jnp.arange(experts * capacity, dtype=jnp.int32)
+    pick = (slot_index[None, :] == slots[:, None]).reshape(experts * capacity, tok_rows, top_count)
     select = jnp.sum(pick.astype(jnp.bfloat16), axis=2)
-    buffer = jnp.dot(select, full_rows, preferred_element_type=jnp.float32).astype(jnp.bfloat16)
-    arrived = lax.all_to_all(buffer, "seq", 0, 0, tiled=True)
+    buffer = jnp.dot(select, residual, preferred_element_type=jnp.float32).astype(jnp.bfloat16)
+    arrived = lax.all_to_all(buffer, ("seq", "mp"), 0, 0, tiled=True)
+    feat = D // mp_count
+    arrived_rows = (
+        arrived.reshape(seq_count, mp_count, part_cap, feat)
+        .transpose(0, 2, 1, 3)
+        .reshape(seq_count * part_cap, D)
+        .astype(jnp.float32)
+    )
+    moe_in = (
+        arrived_rows
+        * lax.rsqrt(jnp.sum(arrived_rows * arrived_rows, axis=-1, keepdims=True) / D + EPSILON)
+    ).astype(jnp.bfloat16)
     w_gate = expert_all[0]
     w_up = expert_all[1]
     w_down = expert_all[2]
     gate_act = lax.dot_general(
-        arrived, w_gate, (((1,), (1,)), ((), ())), preferred_element_type=jnp.float32
+        moe_in, w_gate, (((1,), (1,)), ((), ())), preferred_element_type=jnp.float32
     )
     up_act = lax.dot_general(
-        arrived, w_up, (((1,), (1,)), ((), ())), preferred_element_type=jnp.float32
+        moe_in, w_up, (((1,), (1,)), ((), ())), preferred_element_type=jnp.float32
     )
     active = (jnp.maximum(gate_act, 0.0) * up_act).astype(jnp.bfloat16)
     result = jnp.dot(active, w_down, preferred_element_type=jnp.float32).astype(jnp.bfloat16)
-    returned = lax.all_to_all(result, "seq", 0, 0, tiled=True)
+    outgoing = (
+        result.reshape(seq_count, part_cap, mp_count, feat)
+        .transpose(0, 2, 1, 3)
+        .reshape(seq_count * mp_count * part_cap, feat)
+    )
+    returned = lax.all_to_all(outgoing, ("seq", "mp"), 0, 0, tiled=True)
 
     gate_weights = jax.nn.softmax(gate_logits, axis=-1)
-    share = jnp.where(mine, gate_weights.reshape(-1), 0.0)
     combine = jnp.sum(
         jnp.where(
-            send_index[:, None] == slots[None, :], share[:, None], 0.0
-        ).reshape(tok_rows, top_count, experts * part_cap),
+            slot_index[:, None] == slots[None, :], gate_weights.reshape(-1)[:, None], 0.0
+        ).reshape(tok_rows, top_count, experts * capacity),
         axis=1,
     )
-    partial_moe = jnp.dot(
+    moe_total = jnp.dot(
         combine,
         returned.astype(jnp.float32),
         precision=lax.Precision.HIGHEST,
         preferred_element_type=jnp.float32,
-    )
-    swapped = lax.all_to_all(partial_moe.astype(jnp.bfloat16), "mp", 1, 0, tiled=True)
-    moe_total = jnp.sum(
-        swapped.reshape(mp_count, tok_rows, D // mp_count).astype(jnp.float32), axis=0
     )
     return (residual_f + moe_total).astype(jnp.bfloat16)
 

time: 285 us -> 263 us (0.923)
  blocking collectives: 98.1 us -> 75.2 us
  other arithmetic: 33.9 us -> 26.2 us
  local copies, waits for them, and re-layouts: 11 us -> 15.4 us
  matrix products: 31.4 us -> 34.5 us
    all_to_all x2 -> x1, blocking collectives: 47.4 us -> 33.6 us  [local(): arrived = lax.all_to_all(buffer, ('seq', 'mp'), 0, 0, tiled=True)]
    another operation x5 -> x2, other arithmetic: 11.5 us -> 2.14 us
    all_gather x1 -> x0, blocking collectives: 8.94 us -> none  [local(): lax.all_gather(residual, 'mp', axis=1, tiled=True).astype(jnp.float32)]
    reshape x0 -> x2, local copies, waits for them, and re-layouts: none -> 4.41 us  [local(): result.reshape(seq_count, part_cap, mp_count, feat).transpose(0, 2, 1, 3)]
where the time goes in v4:
time: 263 us; the launch traced here: 261 us
  blocking collectives  75.2 us (29%)
  starting transfers between devices  61.7 us (23%)
  matrix products  34.5 us (13%)
  waiting for transfers between devices  33.1 us (13%)
  other arithmetic  26.2 us (10%)
  local copies, waits for them, and re-layouts  15.4 us (6%)
  between operations  15.3 us (6%)
    all_gather x1, blocking collectives, local(): whole = lax.all_gather(hidden_in, 'mp', axis=1, tiled=True)  41.7 us
    ppermute x8, starting transfers between devices, local(): fetched.append(lax.ppermute(kv_own, ('seq', 'mp'), pairs))  40.7 us
    all_to_all x1, blocking collectives, local(): arrived = lax.all_to_all(buffer, ('seq', 'mp'), 0, 0, tiled=True)  33.6 us
    all_to_all x1, waiting for transfers between devices, local(): returned = lax.all_to_all(outgoing, ('seq', 'mp'), 0, 0, tiled=True)  22.9 us
    all_to_all x1, starting transfers between devices, gather_seq(): return lax.all_to_all(spread, 'seq', 0, 0, tiled=True)  11.3 us
    reduce_sum x1, other arithmetic, local(): total = jnp.sum(probs, axis=-1)  9.02 us
    all_to_all x1, waiting for transfers between devices, local(): lax.all_to_all(partial_out.astype(jnp.bfloat16), 'mp', 1, 0, tiled=True)  8.38 us
    dot_general x1, matrix products, local(): jnp.dot(active, w_down, preferred_element_type=jnp.float32)  7.18 us
  transfers between devices with their start and end apart: 13, of which 3 were waited for; matrix products, arithmetic and copies ran while one was open for 20% of the time, Pallas kernels for 0%

profile of v4, /device:TPU:1, one launch (start us, length us, event | category | flops | bytes accessed | tf_op | source)
XLA Modules:
  0.0 261.5 jit_solution(17124637981531215132)
XLA Ops:
  8.1 2.0 broadcast_in_dim.45
  10.1 11.3 %all-to-all-start = ((bf16[32,48,1024]{2,1,0:T(8,128)(2,1)}), bf16[32,48,1024]{2,1,0:T(8,128)(2,1)S(1)}, u32[]{:S(2)}, u32[]{:S(2)}) async-start(bf16[32,48,1024]{2,1,0:T(8,128)(2,1)} %broadcast_in_dim.45), calls=%async_computation | async-start | bytes 6291456 | tf_op jit(solution)/shard_map/all_to_all | solution.py:47
  21.5 2.9 %pad_maximum_fusion.1 = bf16[3,192,1536]{2,1,0:T(8,128)(2,1)} fusion(bf16[1,192,1536]{2,1,0:T(8,128)(2,1)} %param.19, bf16[1,192,1536]{2,1,0:T(8,128)(2,1)} %param.18, bf16[1,192,1536]{2,1,0:T(8,128)(2,1)} %param.17), kind=kLoop, calls=%fused_computation.39 | loop fusion | flops 1769472 | bytes 3538944 | tf_op jit(solution)/shard_map/concatenate | solution.py:63
  27.2 41.7 %all_gather.6 = bf16[256,1536]{1,0:T(8,128)(2,1)S(1)} all-gather(bf16[256,384]{1,0:T(8,128)(2,1)S(1)} %copy-done.3), channel_id=1, replica_groups=mesh['seq'=32,'mp'=4] {'mp'}, dimensions={1}, use_global_device_ids=true | all-gather | bytes 983040 | tf_op jit(solution)/shard_map/all_gather | solution.py:73
  70.4 2.6 fusion.18
  74.4 4.8 %collective-permute-start = (bf16[256,256]{0,1:T(8,128)(2,1)S(1)}, bf16[256,256]{0,1:T(8,128)(2,1)S(1)}, u32[]{:S(2)}, u32[]{:S(2)}) collective-permute-start(bf16[256,256]{0,1:T(8,128)(2,1)S(1)} %pad_maximum_fusion.2), channel_id=1, source_target_pairs={{0,4},{1,9},{2,6},{3,11},{4,8},{5,13},{6,10},{7,15},{8,12},{9,17},... | collective-permute-start | bytes 393224 | tf_op jit(solution)/shard_map/ppermute | solution.py:101
  79.3 5.0 %collective-permute-start.1 = (bf16[256,256]{0,1:T(8,128)(2,1)S(1)}, bf16[256,256]{0,1:T(8,128)(2,1)S(1)}, u32[]{:S(2)}, u32[]{:S(2)}) collective-permute-start(bf16[256,256]{0,1:T(8,128)(2,1)S(1)} %pad_maximum_fusion.2), channel_id=1, source_target_pairs={{0,12},{1,17},{2,14},{3,19},{4,16},{5,21},{6,18},{7,23},{8,20},{9,... | collective-permute-start | bytes 393224 | tf_op jit(solution)/shard_map/ppermute | solution.py:101
  84.2 12.1 %collective-permute-start.2 = (bf16[256,256]{0,1:T(8,128)(2,1)S(1)}, bf16[256,256]{0,1:T(8,128)(2,1)S(1)}, u32[]{:S(2)}, u32[]{:S(2)}) collective-permute-start(bf16[256,256]{0,1:T(8,128)(2,1)S(1)} %pad_maximum_fusion.2), channel_id=1, source_target_pairs={{0,20},{1,25},{2,22},{3,27},{4,24},{5,29},{6,26},{7,31},{8,28},{9,... | collective-permute-start | bytes 393224 | tf_op jit(solution)/shard_map/ppermute | solution.py:101
  97.8 3.7 %collective-permute-start.4 = (bf16[256,256]{0,1:T(8,128)(2,1)S(1)}, bf16[256,256]{0,1:T(8,128)(2,1)S(1)}, u32[]{:S(2)}, u32[]{:S(2)}) collective-permute-start(bf16[256,256]{0,1:T(8,128)(2,1)S(1)} %pad_maximum_fusion.2), channel_id=1, source_target_pairs={{0,36},{1,41},{2,38},{3,43},{4,40},{5,45},{6,42},{7,47},{8,44},{9,... | collective-permute-start | bytes 393224 | tf_op jit(solution)/shard_map/ppermute | solution.py:101
  101.5 4.3 %collective-permute-start.5 = (bf16[256,256]{0,1:T(8,128)(2,1)S(1)}, bf16[256,256]{0,1:T(8,128)(2,1)S(1)}, u32[]{:S(2)}, u32[]{:S(2)}) collective-permute-start(bf16[256,256]{0,1:T(8,128)(2,1)S(1)} %pad_maximum_fusion.2), channel_id=1, source_target_pairs={{0,44},{1,49},{2,46},{3,51},{4,48},{5,53},{6,50},{7,55},{8,52},{9,... | collective-permute-start | bytes 393224 | tf_op jit(solution)/shard_map/ppermute | solution.py:101
  105.9 2.1 collective-permute-start.6
  108.0 7.3 %collective-permute-start.7 = (bf16[256,256]{0,1:T(8,128)(2,1)S(1)}, bf16[256,256]{0,1:T(8,128)(2,1)S(1)}, u32[]{:S(2)}, u32[]{:S(2)}) collective-permute-start(bf16[256,256]{0,1:T(8,128)(2,1)S(1)} %pad_maximum_fusion.2), channel_id=1, source_target_pairs={{0,60},{1,65},{2,62},{3,67},{4,64},{5,69},{6,66},{7,71},{8,68},{9,... | collective-permute-start | bytes 393224 | tf_op jit(solution)/shard_map/ppermute | solution.py:101
  128.7 6.4 %fusion = (f32[3,256]{1,0:T(4,128)S(1)}, f32[3,256,4352]{2,1,0:T(8,128)}) fusion(pred[256,4352]{1,0:T(8,128)(4,1)S(1)} %fusion.11, bf16[4352,256]{1,0:T(8,128)(2,1)S(1)} %pad_maximum_fusion, bf16[256,3,64]{2,0,1:T(8,128)(2,1)S(1)} %copy-done.7, bf16[256,3,64]{2,0,1:T(8,128)(2,1)S(1)} %copy-done.6), kind=kOutput, calls=%fused_computation.2 | convolution fusion | flops 866057472 | bytes 15993856 | tf_op jit(solution)/shard_map/hqd,kd->hqk/dot_general | solution.py:127
  135.1 9.0 %fusion.1 = f32[3,256]{1,0:T(4,128)S(1)} fusion(f32[3,256,4352]{2,1,0:T(8,128)} %get-tuple-element.22, f32[3,256]{1,0:T(4,128)S(1)} %get-tuple-element.21, pred[256,4352]{1,0:T(8,128)(4,1)S(1)} %fusion.11), kind=kLoop, calls=%fused_computation.3 | loop fusion | flops 16710912 | bytes 14489600 | tf_op jit(solution)/shard_map/reduce_sum | solution.py:142
  144.1 7.0 %fusion.31 = bf16[256,3,128]{0,2,1:T(8,128)(2,1)S(1)} fusion(bf16[4352,256]{1,0:T(8,128)(2,1)S(1)} %pad_maximum_fusion, f32[3,256,4352]{2,1,0:T(8,128)} %get-tuple-element.22, f32[3,256]{1,0:T(4,128)S(1)} %get-tuple-element.21, pred[256,4352]{1,0:T(8,128)(4,1)S(1)} %fusion.11, f32[256,3]{0,1:T(4,128)S(1)} %bitcast.100), kind=kOutput, calls=%fused_computation.58 | convolution fusion | flops 869203968 | bytes 15802368 | tf_op jit(solution)/shard_map/hqk,kd->hqd/dot_general | solution.py:143
  154.0 4.0 %all-to-all-start.1 = ((bf16[256,4,384]{2,0,1:T(8,128)(2,1)}), bf16[256,4,384]{2,0,1:T(8,128)(2,1)S(1)}, u32[]{:S(2)}, u32[]{:S(2)}) async-start(bf16[256,4,384]{2,0,1:T(8,128)(2,1)} %bitcast.86), calls=%async_computation.1 | async-start | bytes 1572864 | tf_op jit(solution)/shard_map/all_to_all | solution.py:153
  160.3 8.4 %all-to-all-done.1 = bf16[256,4,384]{2,0,1:T(8,128)(2,1)S(1)} async-done(((bf16[256,4,384]{2,0,1:T(8,128)(2,1)}), bf16[256,4,384]{2,0,1:T(8,128)(2,1)S(1)}, u32[]{:S(2)}, u32[]{:S(2)}) %all-to-all-start.1) | async-done | bytes 786464 | tf_op jit(solution)/shard_map/all_to_all | solution.py:153
  169.5 33.6 %all_to_all.43 = bf16[128,16,384]{2,1,0:T(8,128)(2,1)S(1)} all-to-all(bf16[128,16,384]{2,1,0:T(8,128)(2,1)S(1)} %bitcast.88), channel_id=1, replica_groups=mesh['seq'=32,'mp'=4] {'seq','mp'}, dimensions={0} | all-to-all | bytes 3145728 | tf_op jit(solution)/shard_map/all_to_all | solution.py:179
  204.9 4.3 %fusion.16 = f32[512,768]{1,0:T(8,128)} fusion(bf16[512,1536]{1,0:T(8,128)(2,1)S(1)} %bitcast.94, bf16[3,768,1536]{2,1,0:T(8,128)(2,1)} %all-gather.2.cloned.1.call-done), kind=kOutput, calls=%fused_computation.31 | convolution fusion | flops 1207959552 | bytes 5505024 | tf_op jit(solution)/shard_map/dot_general | solution.py:197
  209.2 7.2 %convolution_convert_fusion = bf16[512,1536]{1,0:T(8,128)(2,1)} fusion(bf16[3,768,1536]{2,1,0:T(8,128)(2,1)} %all-gather.2.cloned.1.call-done, f32[512,768]{1,0:T(8,128)} %fusion.16, bf16[512,1536]{1,0:T(8,128)(2,1)S(1)} %bitcast.95), kind=kOutput, calls=%fused_computation.26 | convolution fusion | flops 2417885184 | bytes 9437184 | tf_op jit(solution)/shard_map/dot_general | solution.py:201
  216.4 3.0 %reshape.378 = bf16[32,16,4,384]{3,2,1,0:T(4,128)(2,1)S(1)} reshape(bf16[512,1536]{1,0:T(8,128)(2,1)} %convolution_convert_fusion) | data formatting | bytes 3145728 | tf_op jit(solution)/shard_map/reshape | solution.py:203
  220.8 5.6 %all-to-all-start.3 = ((bf16[128,16,384]{2,1,0:T(8,128)(2,1)}), bf16[128,16,384]{2,1,0:T(8,128)(2,1)}, u32[]{:S(2)}, u32[]{:S(2)}) async-start(bf16[128,16,384]{2,1,0:T(8,128)(2,1)} %bitcast.31), calls=%async_computation.3 | async-start | bytes 3145728 | tf_op jit(solution)/shard_map/all_to_all | solution.py:207
  227.8 22.9 %all-to-all-done.3 = bf16[128,16,384]{2,1,0:T(8,128)(2,1)} async-done(((bf16[128,16,384]{2,1,0:T(8,128)(2,1)}), bf16[128,16,384]{2,1,0:T(8,128)(2,1)}, u32[]{:S(2)}, u32[]{:S(2)}) %all-to-all-start.3) | async-done | bytes 1572896 | tf_op jit(solution)/shard_map/all_to_all | solution.py:207
  250.7 3.9 %fusion.25 = bf16[256,384]{1,0:T(8,128)(2,1)} fusion(f32[256,2048]{1,0:T(8,128)S(1)} %select_reduce_fusion, bf16[2048,384]{1,0:T(8,128)(2,1)} %bitcast.32, f32[256,384]{1,0:T(8,128)S(1)} %convert_reduce_fusion, bf16[256,384]{1,0:T(8,128)(2,1)S(1)} %copy-done.3), kind=kOutput, calls=%fused_computation.48 | convolution fusion | flops 2416508928 | bytes 4456448 | tf_op jit(solution)/shard_map/dot_general | solution.py:216
  (102 shorter events, 31.3 us)
Async XLA Ops:
  10.1 60.3 %all-to-all-start = ((bf16[32,48,1024]{2,1,0:T(8,128)(2,1)}), bf16[32,48,1024]{2,1,0:T(8,128)(2,1)S(1)}, u32[]{:S(2)}, u32[]{:S(2)}) async-start(bf16[32,48,1024]{2,1,0:T(8,128)(2,1)} %broadcast_in_dim.45), calls=%async_computation | async-start | bytes 6291456 | tf_op jit(solution)/shard_map/all_to_all | solution.py:47
  21.4 3.2 %copy-start.10 = (s32[3]{0:T(128)S(1)}, s32[3]{0:T(128)}, u32[]{:S(2)}) copy-start(s32[3]{0:T(128)} %param.14) | copy-start | bytes 40
  21.4 5.7 %copy-start.3 = (bf16[256,384]{1,0:T(8,128)(2,1)S(1)}, bf16[256,384]{1,0:T(8,128)(2,1)}, u32[]{:S(2)}) copy-start(bf16[256,384]{1,0:T(8,128)(2,1)} %param.10) | copy-start | bytes 589828
  21.5 183.5 %all-gather.2.cloned.1.call-start = ((), (), s32[]{:S(2)}) async-start(), calls=%async_computation.4 | async-start | bytes 8847360 | tf_op jit(solution)/shard_map/all_gather | solution.py:62
  68.8 0.9 copy-start.2
  70.4 2.6 copy-start.1
  74.4 27.1 %collective-permute-start = (bf16[256,256]{0,1:T(8,128)(2,1)S(1)}, bf16[256,256]{0,1:T(8,128)(2,1)S(1)}, u32[]{:S(2)}, u32[]{:S(2)}) collective-permute-start(bf16[256,256]{0,1:T(8,128)(2,1)S(1)} %pad_maximum_fusion.2), channel_id=1, source_target_pairs={{0,4},{1,9},{2,6},{3,11},{4,8},{5,13},{6,10},{7,15},{8,12},{9,17},... | collective-permute-start | bytes 393224 | tf_op jit(solution)/shard_map/ppermute | solution.py:101
  79.3 26.7 %collective-permute-start.1 = (bf16[256,256]{0,1:T(8,128)(2,1)S(1)}, bf16[256,256]{0,1:T(8,128)(2,1)S(1)}, u32[]{:S(2)}, u32[]{:S(2)}) collective-permute-start(bf16[256,256]{0,1:T(8,128)(2,1)S(1)} %pad_maximum_fusion.2), channel_id=1, source_target_pairs={{0,12},{1,17},{2,14},{3,19},{4,16},{5,21},{6,18},{7,23},{8,20},{9,... | collective-permute-start | bytes 393224 | tf_op jit(solution)/shard_map/ppermute | solution.py:101
  84.2 23.8 %collective-permute-start.2 = (bf16[256,256]{0,1:T(8,128)(2,1)S(1)}, bf16[256,256]{0,1:T(8,128)(2,1)S(1)}, u32[]{:S(2)}, u32[]{:S(2)}) collective-permute-start(bf16[256,256]{0,1:T(8,128)(2,1)S(1)} %pad_maximum_fusion.2), channel_id=1, source_target_pairs={{0,20},{1,25},{2,22},{3,27},{4,24},{5,29},{6,26},{7,31},{8,28},{9,... | collective-permute-start | bytes 393224 | tf_op jit(solution)/shard_map/ppermute | solution.py:101
  96.3 19.0 %collective-permute-start.3 = (bf16[256,256]{0,1:T(8,128)(2,1)S(1)}, bf16[256,256]{0,1:T(8,128)(2,1)S(1)}, u32[]{:S(2)}, u32[]{:S(2)}) collective-permute-start(bf16[256,256]{0,1:T(8,128)(2,1)S(1)} %pad_maximum_fusion.2), channel_id=1, source_target_pairs={{0,28},{1,33},{2,30},{3,35},{4,32},{5,37},{6,34},{7,39},{8,36},{9,... | collective-permute-start | bytes 393224 | tf_op jit(solution)/shard_map/ppermute | solution.py:101
  97.8 17.6 %collective-permute-start.4 = (bf16[256,256]{0,1:T(8,128)(2,1)S(1)}, bf16[256,256]{0,1:T(8,128)(2,1)S(1)}, u32[]{:S(2)}, u32[]{:S(2)}) collective-permute-start(bf16[256,256]{0,1:T(8,128)(2,1)S(1)} %pad_maximum_fusion.2), channel_id=1, source_target_pairs={{0,36},{1,41},{2,38},{3,43},{4,40},{5,45},{6,42},{7,47},{8,44},{9,... | collective-permute-start | bytes 393224 | tf_op jit(solution)/shard_map/ppermute | solution.py:101
  101.5 13.9 %collective-permute-start.5 = (bf16[256,256]{0,1:T(8,128)(2,1)S(1)}, bf16[256,256]{0,1:T(8,128)(2,1)S(1)}, u32[]{:S(2)}, u32[]{:S(2)}) collective-permute-start(bf16[256,256]{0,1:T(8,128)(2,1)S(1)} %pad_maximum_fusion.2), channel_id=1, source_target_pairs={{0,44},{1,49},{2,46},{3,51},{4,48},{5,53},{6,50},{7,55},{8,52},{9,... | collective-permute-start | bytes 393224 | tf_op jit(solution)/shard_map/ppermute | solution.py:101
  105.9 14.4 %slice-start = ((f32[256,640]{1,0:T(8,128)}), f32[256,384]{1,0:T(8,128)S(1)}, s32[]{:S(2)}) async-start(f32[256,640]{1,0:T(8,128)} %copy-done.4), calls=%async_computation.5 | async-start | bytes 786432 | tf_op jit(solution)/shard_map/slice | solution.py:82
  105.9 9.5 %collective-permute-start.6 = (bf16[256,256]{0,1:T(8,128)(2,1)S(1)}, bf16[256,256]{0,1:T(8,128)(2,1)S(1)}, u32[]{:S(2)}, u32[]{:S(2)}) collective-permute-start(bf16[256,256]{0,1:T(8,128)(2,1)S(1)} %pad_maximum_fusion.2), channel_id=1, source_target_pairs={{0,52},{1,57},{2,54},{3,59},{4,56},{5,61},{6,58},{7,63},{8,60},{9,... | collective-permute-start | bytes 393224 | tf_op jit(solution)/shard_map/ppermute | solution.py:101
  108.0 9.2 %collective-permute-start.7 = (bf16[256,256]{0,1:T(8,128)(2,1)S(1)}, bf16[256,256]{0,1:T(8,128)(2,1)S(1)}, u32[]{:S(2)}, u32[]{:S(2)}) collective-permute-start(bf16[256,256]{0,1:T(8,128)(2,1)S(1)} %pad_maximum_fusion.2), channel_id=1, source_target_pairs={{0,60},{1,65},{2,62},{3,67},{4,64},{5,69},{6,66},{7,71},{8,68},{9,... | collective-permute-start | bytes 393224 | tf_op jit(solution)/shard_map/ppermute | solution.py:101
  117.3 3.4 %copy-start.5 = (bf16[8,256,256]{1,2,0:T(8,128)(2,1)}, bf16[8,256,256]{1,2,0:T(8,128)(2,1)S(1)}, u32[]{:S(2)}) copy-start(bf16[8,256,256]{1,2,0:T(8,128)(2,1)S(1)} %bitcast_dynamic-update-slice_fusion) | copy-start | bytes 3145732
  117.3 5.4 %collective-permute-start.8 = (bf16[8,256,256]{1,2,0:T(8,128)(2,1)S(1)}, bf16[8,256,256]{1,2,0:T(8,128)(2,1)}, u32[]{:S(2)}, u32[]{:S(2)}) collective-permute-start(bf16[8,256,256]{1,2,0:T(8,128)(2,1)S(1)} %bitcast_dynamic-update-slice_fusion), channel_id=1, source_target_pairs={{0,1},{1,0},{2,3},{3,2},{4,5},{5,4},{6,7},{7,6},{8,9},{9,8},{10,11... | collective-permute-start | bytes 3145736 | tf_op jit(solution)/shard_map/ppermute | solution.py:103
  125.9 1.3 copy-start
  127.2 1.4 copy-start.6
  127.2 1.4 copy-start.7
  151.1 6.8 %copy-start.9 = (s32[256,4]{0,1:T(4,128)S(1)}, s32[256,4]{0,1:T(4,128)}, u32[]{:S(2)}) copy-start(s32[256,4]{0,1:T(4,128)} %param.15) | copy-start | bytes 12292
  154.0 14.7 %all-to-all-start.1 = ((bf16[256,4,384]{2,0,1:T(8,128)(2,1)}), bf16[256,4,384]{2,0,1:T(8,128)(2,1)S(1)}, u32[]{:S(2)}, u32[]{:S(2)}) async-start(bf16[256,4,384]{2,0,1:T(8,128)(2,1)} %bitcast.86), calls=%async_computation.1 | async-start | bytes 1572864 | tf_op jit(solution)/shard_map/all_to_all | solution.py:153
  220.8 5.6 %copy-start.8 = (f32[256,4]{0,1:T(4,128)S(1)}, f32[256,4]{0,1:T(4,128)}, u32[]{:S(2)}) copy-start(f32[256,4]{0,1:T(4,128)} %param.16) | copy-start | bytes 12292
  220.8 30.0 %all-to-all-start.3 = ((bf16[128,16,384]{2,1,0:T(8,128)(2,1)}), bf16[128,16,384]{2,1,0:T(8,128)(2,1)}, u32[]{:S(2)}, u32[]{:S(2)}) async-start(bf16[128,16,384]{2,1,0:T(8,128)(2,1)} %bitcast.31), calls=%async_computation.3 | async-start | bytes 3145728 | tf_op jit(solution)/shard_map/all_to_all | solution.py:207
  (1 other events, 0.8 us)
Sparse Core Ops, SparseCore 0:
  24.6 99.6 all-gather.1

commit v5 on v4

--- a/solution.py
+++ b/solution.py
@@ -63,12 +63,10 @@
         jnp.concatenate([expert_gate, expert_up, expert_down], axis=0), "mp", axis=1, tiled=True
     )
 
-    key_cols = lax.dynamic_slice_in_dim(wkv, kv_group * HD, HD, 1)
-    value_cols = lax.dynamic_slice_in_dim(wkv, KVH * HD + kv_group * HD, HD, 1)
-    piece = jnp.concatenate([wq, key_cols, value_cols, wo.T], axis=1)
-    weights = gather_seq(piece, seq_count)
-    w_qkv = weights[:, : q_cols + 2 * HD]
-    wo_rows = weights[:, q_cols + 2 * HD :]
+    core = mp_index % 2
+    kv_col = jnp.where(core == 0, kv_group * HD, KVH * HD + kv_group * HD)
+    kv_cols = lax.dynamic_slice_in_dim(wkv, kv_col, HD, 1)
+    w_qkv = gather_seq(jnp.concatenate([wq, kv_cols], axis=1), seq_count)
 
     whole = lax.all_gather(hidden_in, "mp", axis=1, tiled=True)
     whole_f = whole.astype(jnp.float32)
@@ -76,6 +74,8 @@
         whole_f * lax.rsqrt(jnp.sum(whole_f * whole_f, axis=-1, keepdims=True) / D + EPSILON)
     ).astype(jnp.bfloat16)
     lin = jnp.dot(normed, w_qkv, preferred_element_type=jnp.float32)
+    wo_piece, lin = lax.optimization_barrier((wo.T, lin))
+    wo_rows = gather_seq(wo_piece, seq_count)
     own_index = seq_index * tok_rows + jnp.arange(tok_rows, dtype=jnp.int32)
     _, own_pos = prompt_ids(own_index, lengths)
     queries = (
@@ -83,13 +83,17 @@
         .astype(jnp.bfloat16)
         .transpose(1, 0, 2)
     )
-    key_own = rotary(lin[:, q_cols : q_cols + HD].reshape(tok_rows, 1, HD), own_pos)[:, 0, :]
-    value_own = lin[:, q_cols + HD :]
-    kv_own = jnp.concatenate([key_own.astype(jnp.bfloat16), value_own.astype(jnp.bfloat16)], axis=1)
+    kv_lin = lin[:, q_cols:]
+    kv_mine = jnp.where(
+        core == 0, rotary(kv_lin.reshape(tok_rows, 1, HD), own_pos)[:, 0, :], kv_lin
+    ).astype(jnp.bfloat16)
+    kv_other = lax.ppermute(kv_mine, "mp", [(m, m ^ 1) for m in range(mp_count)])
+    key_own = jnp.where(core == 0, kv_mine, kv_other)
+    value_own = jnp.where(core == 0, kv_other, kv_mine)
+    kv_own = jnp.concatenate([key_own, value_own], axis=1)
 
     back = min((WINDOW - 1 + tok_rows - 1) // tok_rows, seq_count - 1)
     half = (back + 1) // 2
-    core = mp_index % 2
     fetched = []
     for j in range(half):
         pairs = []

time: 263 us -> 243 us (0.924)
  blocking collectives: 75.2 us -> 56.1 us
  starting transfers between devices: 61.7 us -> 66.5 us
  matrix products: 34.5 us -> 31.2 us
    all_gather x1, blocking collectives: 41.7 us -> 22 us  [local(): whole = lax.all_gather(hidden_in, 'mp', axis=1, tiled=True)]
    all_to_all x1 -> x2, starting transfers between devices: 11.3 us -> 22.5 us  [gather_seq(): return lax.all_to_all(spread, 'seq', 0, 0, tiled=True)]
    ppermute x8, starting transfers between devices: 40.7 us -> 34 us  [local(): fetched.append(lax.ppermute(kv_own, ('seq', 'mp'), pairs))]
    unnamed x35 -> x27, local copies, waits for them, and re-layouts: 2.52 us -> 6.19 us
    select_n x2 -> x0, local copies, waits for them, and re-layouts: 2.81 us -> none  [the longest x1 1.5 us: local(): odd = jnp.where(core == 0, fetched, partner)]
  transfers between devices with their start and end apart: 13 -> 15, of which waited for: 3 -> 3; matrix products, arithmetic and copies ran while one was open for 20% -> 21% of each run, Pallas kernels for 0% -> 0%
where the time goes in v5:
time: 243 us; the launch traced here: 242 us
  starting transfers between devices  66.5 us (27%)
  blocking collectives  56.1 us (23%)
  waiting for transfers between devices  31.9 us (13%)
  matrix products  31.2 us (13%)
  other arithmetic  24.5 us (10%)
  local copies, waits for them, and re-layouts  16.6 us (7%)
  between operations  15.1 us (6%)
    all_to_all x1, blocking collectives, local(): arrived = lax.all_to_all(buffer, ('seq', 'mp'), 0, 0, tiled=True)  34.1 us
    ppermute x8, starting transfers between devices, local(): fetched.append(lax.ppermute(kv_own, ('seq', 'mp'), pairs))  34 us
    all_to_all x1, waiting for transfers between devices, local(): returned = lax.all_to_all(outgoing, ('seq', 'mp'), 0, 0, tiled=True)  22.9 us
    all_to_all x2, starting transfers between devices, gather_seq(): return lax.all_to_all(spread, 'seq', 0, 0, tiled=True)  22.5 us
    all_gather x1, blocking collectives, local(): whole = lax.all_gather(hidden_in, 'mp', axis=1, tiled=True)  22 us
    reduce_sum x1, other arithmetic, local(): total = jnp.sum(probs, axis=-1)  9.02 us
    all_to_all x1, waiting for transfers between devices, local(): lax.all_to_all(partial_out.astype(jnp.bfloat16), 'mp', 1, 0, tiled=True)  8.38 us
    dot_general x1, matrix products, local(): jnp.dot(active, w_down, preferred_element_type=jnp.float32)  7.18 us
  transfers between devices with their start and end apart: 15, of which 3 were waited for; matrix products, arithmetic and copies ran while one was open for 21% of the time, Pallas kernels for 0%

profile of v5, /device:TPU:1, one launch (start us, length us, event | category | flops | bytes accessed | tf_op | source)
XLA Modules:
  0.0 241.8 jit_solution(15356082634708065352)
XLA Ops:
  9.5 11.3 %all-to-all-start = ((bf16[32,48,512]{2,1,0:T(8,128)(2,1)}), bf16[32,48,512]{2,1,0:T(8,128)(2,1)S(1)}, u32[]{:S(2)}, u32[]{:S(2)}) async-start(bf16[32,48,512]{2,1,0:T(8,128)(2,1)} %broadcast_in_dim.47), calls=%async_computation | async-start | bytes 3145728 | tf_op jit(solution)/shard_map/all_to_all | solution.py:47
  20.9 2.5 %pad_maximum_fusion = bf16[3,192,1536]{2,1,0:T(8,128)(2,1)} fusion(bf16[1,192,1536]{2,1,0:T(8,128)(2,1)S(1)} %copy-done.2, bf16[1,192,1536]{2,1,0:T(8,128)(2,1)S(1)} %copy-done.3, bf16[1,192,1536]{2,1,0:T(8,128)(2,1)} %param.17), kind=kLoop, calls=%fused_computation.37 | loop fusion | flops 1769472 | bytes 3538944 | tf_op jit(solution)/shard_map/concatenate | solution.py:63
  26.0 22.0 %all_gather.6 = bf16[256,1536]{1,0:T(8,128)(2,1)S(1)} all-gather(bf16[256,384]{1,0:T(8,128)(2,1)S(1)} %copy-done.1), channel_id=1, replica_groups=mesh['seq'=32,'mp'=4] {'mp'}, dimensions={1}, use_global_device_ids=true | all-gather | bytes 983040 | tf_op jit(solution)/shard_map/all_gather | solution.py:71
  51.0 5.1 %collective-permute-start.1 = (bf16[256,256]{1,0:T(8,128)(2,1)S(1)}, bf16[256,256]{1,0:T(8,128)(2,1)S(1)}, u32[]{:S(2)}, u32[]{:S(2)}) collective-permute-start(bf16[256,256]{1,0:T(8,128)(2,1)S(1)} %pad_maximum_fusion.1), channel_id=1, source_target_pairs={{0,4},{1,9},{2,6},{3,11},{4,8},{5,13},{6,10},{7,15},{8,12},{9,17},... | collective-permute-start | bytes 393224 | tf_op jit(solution)/shard_map/ppermute | solution.py:105
  56.7 5.0 %collective-permute-start.2 = (bf16[256,256]{1,0:T(8,128)(2,1)S(1)}, bf16[256,256]{1,0:T(8,128)(2,1)S(1)}, u32[]{:S(2)}, u32[]{:S(2)}) collective-permute-start(bf16[256,256]{1,0:T(8,128)(2,1)S(1)} %pad_maximum_fusion.1), channel_id=1, source_target_pairs={{0,12},{1,17},{2,14},{3,19},{4,16},{5,21},{6,18},{7,23},{8,20},{9,... | collective-permute-start | bytes 393224 | tf_op jit(solution)/shard_map/ppermute | solution.py:105
  61.7 8.5 %collective-permute-start.3 = (bf16[256,256]{1,0:T(8,128)(2,1)S(1)}, bf16[256,256]{1,0:T(8,128)(2,1)S(1)}, u32[]{:S(2)}, u32[]{:S(2)}) collective-permute-start(bf16[256,256]{1,0:T(8,128)(2,1)S(1)} %pad_maximum_fusion.1), channel_id=1, source_target_pairs={{0,20},{1,25},{2,22},{3,27},{4,24},{5,29},{6,26},{7,31},{8,28},{9,... | collective-permute-start | bytes 393224 | tf_op jit(solution)/shard_map/ppermute | solution.py:105
  70.3 2.1 collective-permute-start.4
  72.4 2.1 collective-permute-start.5
  74.5 4.3 %collective-permute-start.6 = (bf16[256,256]{1,0:T(8,128)(2,1)S(1)}, bf16[256,256]{1,0:T(8,128)(2,1)S(1)}, u32[]{:S(2)}, u32[]{:S(2)}) collective-permute-start(bf16[256,256]{1,0:T(8,128)(2,1)S(1)} %pad_maximum_fusion.1), channel_id=1, source_target_pairs={{0,44},{1,49},{2,46},{3,51},{4,48},{5,53},{6,50},{7,55},{8,52},{9,... | collective-permute-start | bytes 393224 | tf_op jit(solution)/shard_map/ppermute | solution.py:105
  79.5 1.9 collective-permute-start.7
  82.1 4.9 %collective-permute-start.8 = (bf16[256,256]{1,0:T(8,128)(2,1)S(1)}, bf16[256,256]{1,0:T(8,128)(2,1)S(1)}, u32[]{:S(2)}, u32[]{:S(2)}) collective-permute-start(bf16[256,256]{1,0:T(8,128)(2,1)S(1)} %pad_maximum_fusion.1), channel_id=1, source_target_pairs={{0,60},{1,65},{2,62},{3,67},{4,64},{5,69},{6,66},{7,71},{8,68},{9,... | collective-permute-start | bytes 393224 | tf_op jit(solution)/shard_map/ppermute | solution.py:105
  95.9 11.1 %all-to-all-start.1 = ((bf16[32,48,384]{2,1,0:T(8,128)(2,1)}), bf16[32,48,384]{2,1,0:T(8,128)(2,1)S(1)}, u32[]{:S(2)}, u32[]{:S(2)}) async-start(bf16[32,48,384]{2,1,0:T(8,128)(2,1)} %broadcast_in_dim.51), calls=%async_computation.1 | async-start | bytes 2359296 | tf_op jit(solution)/shard_map/all_to_all | solution.py:47
  110.0 6.4 %fusion = (f32[3,256]{1,0:T(4,128)S(1)}, f32[3,256,4352]{2,1,0:T(8,128)}) fusion(pred[256,4352]{1,0:T(8,128)(4,1)S(1)} %fusion.11, bf16[4352,256]{1,0:T(8,128)(2,1)S(1)} %maximum_maximum_fusion, bf16[256,3,64]{2,0,1:T(8,128)(2,1)S(1)} %get-tuple-element.14, bf16[256,3,64]{2,0,1:T(8,128)(2,1)S(1)} %get-tuple-element.13), kind=kOutput, calls=%fused_computation.2 | convolution fusion | flops 866057472 | bytes 15993856 | tf_op jit(solution)/shard_map/hqd,kd->hqk/dot_general | solution.py:131
  116.4 9.0 %fusion.1 = f32[3,256]{1,0:T(4,128)S(1)} fusion(f32[3,256,4352]{2,1,0:T(8,128)} %get-tuple-element.26, f32[3,256]{1,0:T(4,128)S(1)} %get-tuple-element.25, pred[256,4352]{1,0:T(8,128)(4,1)S(1)} %fusion.11), kind=kLoop, calls=%fused_computation.3 | loop fusion | flops 16710912 | bytes 14489600 | tf_op jit(solution)/shard_map/reduce_sum | solution.py:146
  125.4 7.0 %fusion.28 = bf16[256,3,128]{0,2,1:T(8,128)(2,1)S(1)} fusion(bf16[4352,256]{1,0:T(8,128)(2,1)S(1)} %maximum_maximum_fusion, f32[3,256,4352]{2,1,0:T(8,128)} %get-tuple-element.26, f32[3,256]{1,0:T(4,128)S(1)} %get-tuple-element.25, pred[256,4352]{1,0:T(8,128)(4,1)S(1)} %fusion.11, f32[256,3]{0,1:T(4,128)S(1)} %bitcast.108), kind=kOutput, calls=%fused_computation.55 | convolution fusion | flops 869203968 | bytes 15802368 | tf_op jit(solution)/shard_map/hqk,kd->hqd/dot_general | solution.py:147
  134.0 3.7 %all-to-all-start.2 = ((bf16[256,4,384]{2,0,1:T(8,128)(2,1)}), bf16[256,4,384]{2,0,1:T(8,128)(2,1)S(1)}, u32[]{:S(2)}, u32[]{:S(2)}) async-start(bf16[256,4,384]{2,0,1:T(8,128)(2,1)} %bitcast.94), calls=%async_computation.2 | async-start | bytes 1572864 | tf_op jit(solution)/shard_map/all_to_all | solution.py:157
  140.2 8.4 %all-to-all-done.2 = bf16[256,4,384]{2,0,1:T(8,128)(2,1)S(1)} async-done(((bf16[256,4,384]{2,0,1:T(8,128)(2,1)}), bf16[256,4,384]{2,0,1:T(8,128)(2,1)S(1)}, u32[]{:S(2)}, u32[]{:S(2)}) %all-to-all-start.2) | async-done | bytes 786464 | tf_op jit(solution)/shard_map/all_to_all | solution.py:157
  149.4 34.1 %all_to_all.52 = bf16[128,16,384]{2,1,0:T(8,128)(2,1)S(1)} all-to-all(bf16[128,16,384]{2,1,0:T(8,128)(2,1)S(1)} %bitcast.96), channel_id=1, replica_groups=mesh['seq'=32,'mp'=4] {'seq','mp'}, dimensions={0} | all-to-all | bytes 3145728 | tf_op jit(solution)/shard_map/all_to_all | solution.py:183
  185.3 4.2 %fusion.16 = f32[512,768]{1,0:T(8,128)} fusion(bf16[512,1536]{1,0:T(8,128)(2,1)S(1)} %bitcast.103, bf16[3,768,1536]{2,1,0:T(8,128)(2,1)} %all-gather.2.cloned.1.call-done), kind=kOutput, calls=%fused_computation.31 | convolution fusion | flops 1207959552 | bytes 5505024 | tf_op jit(solution)/shard_map/dot_general | solution.py:201
  189.5 7.2 %convolution_convert_fusion = bf16[512,1536]{1,0:T(8,128)(2,1)} fusion(bf16[3,768,1536]{2,1,0:T(8,128)(2,1)} %all-gather.2.cloned.1.call-done, f32[512,768]{1,0:T(8,128)} %fusion.16, bf16[512,1536]{1,0:T(8,128)(2,1)S(1)} %bitcast.104), kind=kOutput, calls=%fused_computation.26 | convolution fusion | flops 2417885184 | bytes 9437184 | tf_op jit(solution)/shard_map/dot_general | solution.py:205
  196.7 3.0 %reshape.382 = bf16[32,16,4,384]{3,2,1,0:T(4,128)(2,1)S(1)} reshape(bf16[512,1536]{1,0:T(8,128)(2,1)} %convolution_convert_fusion) | data formatting | bytes 3145728 | tf_op jit(solution)/shard_map/reshape | solution.py:207
  201.1 5.6 %all-to-all-start.4 = ((bf16[128,16,384]{2,1,0:T(8,128)(2,1)}), bf16[128,16,384]{2,1,0:T(8,128)(2,1)}, u32[]{:S(2)}, u32[]{:S(2)}) async-start(bf16[128,16,384]{2,1,0:T(8,128)(2,1)} %bitcast.32), calls=%async_computation.4 | async-start | bytes 3145728 | tf_op jit(solution)/shard_map/all_to_all | solution.py:211
  208.2 22.9 %all-to-all-done.4 = bf16[128,16,384]{2,1,0:T(8,128)(2,1)} async-done(((bf16[128,16,384]{2,1,0:T(8,128)(2,1)}), bf16[128,16,384]{2,1,0:T(8,128)(2,1)}, u32[]{:S(2)}, u32[]{:S(2)}) %all-to-all-start.4) | async-done | bytes 1572896 | tf_op jit(solution)/shard_map/all_to_all | solution.py:211
  231.1 3.9 %fusion.22 = bf16[256,384]{1,0:T(8,128)(2,1)} fusion(f32[256,2048]{1,0:T(8,128)S(1)} %select_reduce_fusion, bf16[2048,384]{1,0:T(8,128)(2,1)} %bitcast.33, f32[256,384]{1,0:T(8,128)S(1)} %convert_reduce_fusion, bf16[256,384]{1,0:T(8,128)(2,1)S(1)} %copy-done.1), kind=kOutput, calls=%fused_computation.45 | convolution fusion | flops 2416508928 | bytes 4456448 | tf_op jit(solution)/shard_map/dot_general | solution.py:220
  (95 shorter events, 30.3 us)
Async XLA Ops:
  6.5 0.8 copy-start
  8.1 12.8 %copy-start.2 = (bf16[1,192,1536]{2,1,0:T(8,128)(2,1)S(1)}, bf16[1,192,1536]{2,1,0:T(8,128)(2,1)}, u32[]{:S(2)}) copy-start(bf16[1,192,1536]{2,1,0:T(8,128)(2,1)} %param.19) | copy-start | bytes 1769476
  8.1 12.8 %copy-start.3 = (bf16[1,192,1536]{2,1,0:T(8,128)(2,1)S(1)}, bf16[1,192,1536]{2,1,0:T(8,128)(2,1)}, u32[]{:S(2)}) copy-start(bf16[1,192,1536]{2,1,0:T(8,128)(2,1)} %param.18) | copy-start | bytes 1769476
  9.5 38.8 %all-to-all-start = ((bf16[32,48,512]{2,1,0:T(8,128)(2,1)}), bf16[32,48,512]{2,1,0:T(8,128)(2,1)S(1)}, u32[]{:S(2)}, u32[]{:S(2)}) async-start(bf16[32,48,512]{2,1,0:T(8,128)(2,1)} %broadcast_in_dim.47), calls=%async_computation | async-start | bytes 3145728 | tf_op jit(solution)/shard_map/all_to_all | solution.py:47
  20.8 2.8 %copy-start.7 = (s32[3]{0:T(128)S(1)}, s32[3]{0:T(128)}, u32[]{:S(2)}) copy-start(s32[3]{0:T(128)} %param.14) | copy-start | bytes 40
  20.8 5.2 %copy-start.1 = (bf16[256,384]{1,0:T(8,128)(2,1)S(1)}, bf16[256,384]{1,0:T(8,128)(2,1)}, u32[]{:S(2)}) copy-start(bf16[256,384]{1,0:T(8,128)(2,1)} %param.10) | copy-start | bytes 589828
  20.8 164.4 %all-gather.2.cloned.1.call-start = ((), (), s32[]{:S(2)}) async-start(), calls=%async_computation.5 | async-start | bytes 8847360 | tf_op jit(solution)/shard_map/all_gather | solution.py:62
  49.6 1.3 collective-permute-start
  51.0 23.5 %collective-permute-start.1 = (bf16[256,256]{1,0:T(8,128)(2,1)S(1)}, bf16[256,256]{1,0:T(8,128)(2,1)S(1)}, u32[]{:S(2)}, u32[]{:S(2)}) collective-permute-start(bf16[256,256]{1,0:T(8,128)(2,1)S(1)} %pad_maximum_fusion.1), channel_id=1, source_target_pairs={{0,4},{1,9},{2,6},{3,11},{4,8},{5,13},{6,10},{7,15},{8,12},{9,17},... | collective-permute-start | bytes 393224 | tf_op jit(solution)/shard_map/ppermute | solution.py:105
  56.7 22.8 %collective-permute-start.2 = (bf16[256,256]{1,0:T(8,128)(2,1)S(1)}, bf16[256,256]{1,0:T(8,128)(2,1)S(1)}, u32[]{:S(2)}, u32[]{:S(2)}) collective-permute-start(bf16[256,256]{1,0:T(8,128)(2,1)S(1)} %pad_maximum_fusion.1), channel_id=1, source_target_pairs={{0,12},{1,17},{2,14},{3,19},{4,16},{5,21},{6,18},{7,23},{8,20},{9,... | collective-permute-start | bytes 393224 | tf_op jit(solution)/shard_map/ppermute | solution.py:105
  61.7 20.4 %collective-permute-start.3 = (bf16[256,256]{1,0:T(8,128)(2,1)S(1)}, bf16[256,256]{1,0:T(8,128)(2,1)S(1)}, u32[]{:S(2)}, u32[]{:S(2)}) collective-permute-start(bf16[256,256]{1,0:T(8,128)(2,1)S(1)} %pad_maximum_fusion.1), channel_id=1, source_target_pairs={{0,20},{1,25},{2,22},{3,27},{4,24},{5,29},{6,26},{7,31},{8,28},{9,... | collective-permute-start | bytes 393224 | tf_op jit(solution)/shard_map/ppermute | solution.py:105
  70.3 17.4 %collective-permute-start.4 = (bf16[256,256]{1,0:T(8,128)(2,1)S(1)}, bf16[256,256]{1,0:T(8,128)(2,1)S(1)}, u32[]{:S(2)}, u32[]{:S(2)}) collective-permute-start(bf16[256,256]{1,0:T(8,128)(2,1)S(1)} %pad_maximum_fusion.1), channel_id=1, source_target_pairs={{0,28},{1,33},{2,30},{3,35},{4,32},{5,37},{6,34},{7,39},{8,36},{9,... | collective-permute-start | bytes 393224 | tf_op jit(solution)/shard_map/ppermute | solution.py:105
  72.4 15.9 %collective-permute-start.5 = (bf16[256,256]{1,0:T(8,128)(2,1)S(1)}, bf16[256,256]{1,0:T(8,128)(2,1)S(1)}, u32[]{:S(2)}, u32[]{:S(2)}) collective-permute-start(bf16[256,256]{1,0:T(8,128)(2,1)S(1)} %pad_maximum_fusion.1), channel_id=1, source_target_pairs={{0,36},{1,41},{2,38},{3,43},{4,40},{5,45},{6,42},{7,47},{8,44},{9,... | collective-permute-start | bytes 393224 | tf_op jit(solution)/shard_map/ppermute | solution.py:105
  74.5 14.5 %collective-permute-start.6 = (bf16[256,256]{1,0:T(8,128)(2,1)S(1)}, bf16[256,256]{1,0:T(8,128)(2,1)S(1)}, u32[]{:S(2)}, u32[]{:S(2)}) collective-permute-start(bf16[256,256]{1,0:T(8,128)(2,1)S(1)} %pad_maximum_fusion.1), channel_id=1, source_target_pairs={{0,44},{1,49},{2,46},{3,51},{4,48},{5,53},{6,50},{7,55},{8,52},{9,... | collective-permute-start | bytes 393224 | tf_op jit(solution)/shard_map/ppermute | solution.py:105
  79.5 10.1 %collective-permute-start.7 = (bf16[256,256]{1,0:T(8,128)(2,1)S(1)}, bf16[256,256]{1,0:T(8,128)(2,1)S(1)}, u32[]{:S(2)}, u32[]{:S(2)}) collective-permute-start(bf16[256,256]{1,0:T(8,128)(2,1)S(1)} %pad_maximum_fusion.1), channel_id=1, source_target_pairs={{0,52},{1,57},{2,54},{3,59},{4,56},{5,61},{6,58},{7,63},{8,60},{9,... | collective-permute-start | bytes 393224 | tf_op jit(solution)/shard_map/ppermute | solution.py:105
  82.1 8.2 %collective-permute-start.8 = (bf16[256,256]{1,0:T(8,128)(2,1)S(1)}, bf16[256,256]{1,0:T(8,128)(2,1)S(1)}, u32[]{:S(2)}, u32[]{:S(2)}) collective-permute-start(bf16[256,256]{1,0:T(8,128)(2,1)S(1)} %pad_maximum_fusion.1), channel_id=1, source_target_pairs={{0,60},{1,65},{2,62},{3,67},{4,64},{5,69},{6,66},{7,71},{8,68},{9,... | collective-permute-start | bytes 393224 | tf_op jit(solution)/shard_map/ppermute | solution.py:105
  91.0 17.2 %collective-permute-start.9 = (bf16[8,256,256]{2,1,0:T(8,128)(2,1)}, bf16[8,256,256]{2,1,0:T(8,128)(2,1)}, u32[]{:S(2)}, u32[]{:S(2)}) collective-permute-start(bf16[8,256,256]{2,1,0:T(8,128)(2,1)} %bitcast_dynamic-update-slice_fusion), channel_id=1, source_target_pairs={{0,1},{1,0},{2,3},{3,2},{4,5},{5,4},{6,7},{7,6},{8,9},{9,8},{10,11... | collective-permute-start | bytes 3145736 | tf_op jit(solution)/shard_map/ppermute | solution.py:107
  91.4 3.4 %copy-start.4 = (bf16[384,48]{0,1:T(8,128)(2,1)S(1)}, bf16[384,48]{0,1:T(8,128)(2,1)}, u32[]{:S(2)}) copy-start(bf16[384,48]{0,1:T(8,128)(2,1)} %param.13) | copy-start | bytes 110596
  95.9 36.5 %all-to-all-start.1 = ((bf16[32,48,384]{2,1,0:T(8,128)(2,1)}), bf16[32,48,384]{2,1,0:T(8,128)(2,1)S(1)}, u32[]{:S(2)}, u32[]{:S(2)}) async-start(bf16[32,48,384]{2,1,0:T(8,128)(2,1)} %broadcast_in_dim.51), calls=%async_computation.1 | async-start | bytes 2359296 | tf_op jit(solution)/shard_map/all_to_all | solution.py:47
  132.5 5.3 %copy-start.6 = (s32[256,4]{0,1:T(4,128)S(1)}, s32[256,4]{0,1:T(4,128)}, u32[]{:S(2)}) copy-start(s32[256,4]{0,1:T(4,128)} %param.15) | copy-start | bytes 12292
  134.0 14.5 %all-to-all-start.2 = ((bf16[256,4,384]{2,0,1:T(8,128)(2,1)}), bf16[256,4,384]{2,0,1:T(8,128)(2,1)S(1)}, u32[]{:S(2)}, u32[]{:S(2)}) async-start(bf16[256,4,384]{2,0,1:T(8,128)(2,1)} %bitcast.94), calls=%async_computation.2 | async-start | bytes 1572864 | tf_op jit(solution)/shard_map/all_to_all | solution.py:157
  201.1 5.6 %copy-start.5 = (f32[256,4]{0,1:T(4,128)S(1)}, f32[256,4]{0,1:T(4,128)}, u32[]{:S(2)}) copy-start(f32[256,4]{0,1:T(4,128)} %param.16) | copy-start | bytes 12292
  201.1 30.0 %all-to-all-start.4 = ((bf16[128,16,384]{2,1,0:T(8,128)(2,1)}), bf16[128,16,384]{2,1,0:T(8,128)(2,1)}, u32[]{:S(2)}, u32[]{:S(2)}) async-start(bf16[128,16,384]{2,1,0:T(8,128)(2,1)} %bitcast.32), calls=%async_computation.4 | async-start | bytes 3145728 | tf_op jit(solution)/shard_map/all_to_all | solution.py:211
Sparse Core Ops, SparseCore 0:
  23.6 85.0 all-gather.1

commit v6 on v5

--- a/solution.py
+++ b/solution.py
@@ -75,7 +75,7 @@
     ).astype(jnp.bfloat16)
     lin = jnp.dot(normed, w_qkv, preferred_element_type=jnp.float32)
     wo_piece, lin = lax.optimization_barrier((wo.T, lin))
-    wo_rows = gather_seq(wo_piece, seq_count)
+    wo_cols = lax.all_to_all(gather_seq(wo_piece, seq_count), "mp", 0, 1, tiled=True)
     own_index = seq_index * tok_rows + jnp.arange(tok_rows, dtype=jnp.int32)
     _, own_pos = prompt_ids(own_index, lengths)
     queries = (
@@ -151,12 +151,9 @@
         .reshape(tok_rows, q_cols)
         .astype(jnp.bfloat16)
     )
-    partial_out = lax.dot_general(
-        attended, wo_rows, (((1,), (1,)), ((), ())), preferred_element_type=jnp.float32
-    )
-    swapped_out = lax.all_to_all(partial_out.astype(jnp.bfloat16), "mp", 1, 0, tiled=True)
-    attn_mine = jnp.sum(
-        swapped_out.reshape(mp_count, tok_rows, D // mp_count).astype(jnp.float32), axis=0
+    attended_rows = lax.all_gather(attended, "mp", axis=1, tiled=True)
+    attn_mine = lax.dot_general(
+        attended_rows, wo_cols, (((1,), (1,)), ((), ())), preferred_element_type=jnp.float32
     )
     residual = (hidden_in.astype(jnp.float32) + attn_mine).astype(jnp.bfloat16)
     residual_f = residual.astype(jnp.float32)

time: 243 us -> 252 us (1.037)
  starting transfers between devices: 66.5 us -> 76.9 us
  blocking collectives: 56.1 us -> 64.8 us
  waiting for transfers between devices: 31.9 us -> 23.4 us
    ppermute x8, starting transfers between devices: 34 us -> 43.3 us  [local(): fetched.append(lax.ppermute(kv_own, ('seq', 'mp'), pairs))]
    all_gather x0 -> x1, blocking collectives: none -> 8.89 us  [local(): attended_rows = lax.all_gather(attended, 'mp', axis=1, tiled=True)]
    all_to_all x1, waiting for transfers between devices: 8.38 us -> 0.01 us  [local(): lax.all_to_all(gather_seq(wo_piece, seq_count), 'mp', 0, 1, tiled=True)]
    reshape x2, local copies, waits for them, and re-layouts: 4.42 us -> 1.83 us  [local(): result.reshape(seq_count, part_cap, mp_count, feat).transpose(0, 2, 1, 3)]
    unnamed x27 -> x45, local copies, waits for them, and re-layouts: 6.19 us -> 7.48 us
  transfers between devices with their start and end apart: 15 -> 15, of which waited for: 3 -> 2; matrix products, arithmetic and copies ran while one was open for 21% -> 20% of each run, Pallas kernels for 0% -> 0%
where the time goes in v6:
time: 252 us; the launch traced here: 251 us
  starting transfers between devices  76.9 us (31%)
  blocking collectives  64.8 us (26%)
  matrix products  31.3 us (12%)
  waiting for transfers between devices  23.4 us (9%)
  other arithmetic  23.3 us (9%)
  local copies, waits for them, and re-layouts  15.9 us (6%)
  between operations  15.3 us (6%)
    ppermute x8, starting transfers between devices, local(): fetched.append(lax.ppermute(kv_own, ('seq', 'mp'), pairs))  43.3 us
    all_to_all x1, blocking collectives, local(): arrived = lax.all_to_all(buffer, ('seq', 'mp'), 0, 0, tiled=True)  33.5 us
    all_to_all x1, waiting for transfers between devices, local(): returned = lax.all_to_all(outgoing, ('seq', 'mp'), 0, 0, tiled=True)  22.9 us
    all_to_all x2, starting transfers between devices, gather_seq(): return lax.all_to_all(spread, 'seq', 0, 0, tiled=True)  22.5 us
    all_gather x1, blocking collectives, local(): whole = lax.all_gather(hidden_in, 'mp', axis=1, tiled=True)  22.4 us
    reduce_sum x1, other arithmetic, local(): total = jnp.sum(probs, axis=-1)  9.02 us
    all_gather x1, blocking collectives, local(): attended_rows = lax.all_gather(attended, 'mp', axis=1, tiled=True)  8.89 us
    unnamed x45, local copies, waits for them, and re-layouts  7.48 us
  transfers between devices with their start and end apart: 15, of which 2 were waited for; matrix products, arithmetic and copies ran while one was open for 20% of the time, Pallas kernels for 0%

profile of v6, /device:TPU:1, one launch (start us, length us, event | category | flops | bytes accessed | tf_op | source)
XLA Modules:
  0.0 250.9 jit_solution(6778000539454713452)
XLA Ops:
  9.5 11.3 %all-to-all-start = ((bf16[32,48,512]{2,1,0:T(8,128)(2,1)}), bf16[32,48,512]{2,1,0:T(8,128)(2,1)S(1)}, u32[]{:S(2)}, u32[]{:S(2)}) async-start(bf16[32,48,512]{2,1,0:T(8,128)(2,1)} %broadcast_in_dim.47), calls=%async_computation | async-start | bytes 3145728 | tf_op jit(solution)/shard_map/all_to_all | solution.py:47
  25.8 22.4 %all_gather.9 = bf16[256,1536]{1,0:T(8,128)(2,1)S(1)} all-gather(bf16[256,384]{1,0:T(8,128)(2,1)} %param.10), channel_id=1, replica_groups=mesh['seq'=32,'mp'=4] {'mp'}, dimensions={1}, use_global_device_ids=true | all-gather | bytes 983040 | tf_op jit(solution)/shard_map/all_gather | solution.py:71
  52.6 5.1 %collective-permute-start.1 = (bf16[256,256]{1,0:T(8,128)(2,1)S(1)}, bf16[256,256]{1,0:T(8,128)(2,1)S(1)}, u32[]{:S(2)}, u32[]{:S(2)}) collective-permute-start(bf16[256,256]{1,0:T(8,128)(2,1)S(1)} %pad_maximum_fusion.1), channel_id=1, source_target_pairs={{0,4},{1,9},{2,6},{3,11},{4,8},{5,13},{6,10},{7,15},{8,12},{9,17},... | collective-permute-start | bytes 393224 | tf_op jit(solution)/shard_map/ppermute | solution.py:105
  59.6 11.1 %all-to-all-start.1 = ((bf16[32,48,384]{2,1,0:T(8,128)(2,1)}), bf16[32,48,384]{2,1,0:T(8,128)(2,1)}, u32[]{:S(2)}, u32[]{:S(2)}) async-start(bf16[32,48,384]{2,1,0:T(8,128)(2,1)} %broadcast_in_dim.51), calls=%async_computation.1 | async-start | bytes 2359296 | tf_op jit(solution)/shard_map/all_to_all | solution.py:47
  70.8 4.6 %collective-permute-start.2 = (bf16[256,256]{1,0:T(8,128)(2,1)S(1)}, bf16[256,256]{1,0:T(8,128)(2,1)S(1)}, u32[]{:S(2)}, u32[]{:S(2)}) collective-permute-start(bf16[256,256]{1,0:T(8,128)(2,1)S(1)} %pad_maximum_fusion.1), channel_id=1, source_target_pairs={{0,12},{1,17},{2,14},{3,19},{4,16},{5,21},{6,18},{7,23},{8,20},{9,... | collective-permute-start | bytes 393224 | tf_op jit(solution)/shard_map/ppermute | solution.py:105
  75.4 5.5 %collective-permute-start.3 = (bf16[256,256]{1,0:T(8,128)(2,1)S(1)}, bf16[256,256]{1,0:T(8,128)(2,1)S(1)}, u32[]{:S(2)}, u32[]{:S(2)}) collective-permute-start(bf16[256,256]{1,0:T(8,128)(2,1)S(1)} %pad_maximum_fusion.1), channel_id=1, source_target_pairs={{0,20},{1,25},{2,22},{3,27},{4,24},{5,29},{6,26},{7,31},{8,28},{9,... | collective-permute-start | bytes 393224 | tf_op jit(solution)/shard_map/ppermute | solution.py:105
  80.9 3.1 %collective-permute-start.4 = (bf16[256,256]{1,0:T(8,128)(2,1)S(1)}, bf16[256,256]{1,0:T(8,128)(2,1)S(1)}, u32[]{:S(2)}, u32[]{:S(2)}) collective-permute-start(bf16[256,256]{1,0:T(8,128)(2,1)S(1)} %pad_maximum_fusion.1), channel_id=1, source_target_pairs={{0,28},{1,33},{2,30},{3,35},{4,32},{5,37},{6,34},{7,39},{8,36},{9,... | collective-permute-start | bytes 393224 | tf_op jit(solution)/shard_map/ppermute | solution.py:105
  84.0 2.9 %collective-permute-start.5 = (bf16[256,256]{1,0:T(8,128)(2,1)S(1)}, bf16[256,256]{1,0:T(8,128)(2,1)S(1)}, u32[]{:S(2)}, u32[]{:S(2)}) collective-permute-start(bf16[256,256]{1,0:T(8,128)(2,1)S(1)} %pad_maximum_fusion.1), channel_id=1, source_target_pairs={{0,36},{1,41},{2,38},{3,43},{4,40},{5,45},{6,42},{7,47},{8,44},{9,... | collective-permute-start | bytes 393224 | tf_op jit(solution)/shard_map/ppermute | solution.py:105
  86.8 4.3 %collective-permute-start.6 = (bf16[256,256]{1,0:T(8,128)(2,1)S(1)}, bf16[256,256]{1,0:T(8,128)(2,1)S(1)}, u32[]{:S(2)}, u32[]{:S(2)}) collective-permute-start(bf16[256,256]{1,0:T(8,128)(2,1)S(1)} %pad_maximum_fusion.1), channel_id=1, source_target_pairs={{0,44},{1,49},{2,46},{3,51},{4,48},{5,53},{6,50},{7,55},{8,52},{9,... | collective-permute-start | bytes 393224 | tf_op jit(solution)/shard_map/ppermute | solution.py:105
  92.3 14.8 %collective-permute-start.7 = (bf16[256,256]{1,0:T(8,128)(2,1)S(1)}, bf16[256,256]{1,0:T(8,128)(2,1)S(1)}, u32[]{:S(2)}, u32[]{:S(2)}) collective-permute-start(bf16[256,256]{1,0:T(8,128)(2,1)S(1)} %pad_maximum_fusion.1), channel_id=1, source_target_pairs={{0,52},{1,57},{2,54},{3,59},{4,56},{5,61},{6,58},{7,63},{8,60},{9,... | collective-permute-start | bytes 393224 | tf_op jit(solution)/shard_map/ppermute | solution.py:105
  107.7 3.1 %collective-permute-start.8 = (bf16[256,256]{1,0:T(8,128)(2,1)S(1)}, bf16[256,256]{1,0:T(8,128)(2,1)S(1)}, u32[]{:S(2)}, u32[]{:S(2)}) collective-permute-start(bf16[256,256]{1,0:T(8,128)(2,1)S(1)} %pad_maximum_fusion.1), channel_id=1, source_target_pairs={{0,60},{1,65},{2,62},{3,67},{4,64},{5,69},{6,66},{7,71},{8,68},{9,... | collective-permute-start | bytes 393224 | tf_op jit(solution)/shard_map/ppermute | solution.py:105
  120.9 3.7 %all-to-all-start.2 = ((bf16[4,384,384]{2,1,0:T(8,128)(2,1)}), bf16[4,384,384]{2,1,0:T(8,128)(2,1)S(1)}, u32[]{:S(2)}, u32[]{:S(2)}) async-start(bf16[4,384,384]{2,1,0:T(8,128)(2,1)} %bitcast.23), calls=%async_computation.2 | async-start | bytes 2359296 | tf_op jit(solution)/shard_map/all_to_all | solution.py:78
  124.6 1.7 broadcast_select_fusion.1
  127.4 6.4 %fusion = (f32[3,256]{1,0:T(4,128)S(1)}, f32[3,256,4352]{2,1,0:T(8,128)}) fusion(pred[256,4352]{1,0:T(8,128)(4,1)S(1)} %fusion.11, bf16[4352,256]{1,0:T(8,128)(2,1)S(1)} %maximum_maximum_fusion, bf16[256,3,64]{2,0,1:T(8,128)(2,1)S(1)} %copy-done.12, bf16[256,3,64]{2,0,1:T(8,128)(2,1)S(1)} %copy-done.11), kind=kOutput, calls=%fused_computation.2 | convolution fusion | flops 866057472 | bytes 15993856 | tf_op jit(solution)/shard_map/hqd,kd->hqk/dot_general | solution.py:131
  133.8 9.0 %fusion.1 = f32[3,256]{1,0:T(4,128)S(1)} fusion(f32[3,256,4352]{2,1,0:T(8,128)} %get-tuple-element.26, f32[3,256]{1,0:T(4,128)S(1)} %get-tuple-element.25, pred[256,4352]{1,0:T(8,128)(4,1)S(1)} %fusion.11), kind=kLoop, calls=%fused_computation.3 | loop fusion | flops 16710912 | bytes 14489600 | tf_op jit(solution)/shard_map/reduce_sum | solution.py:146
  142.8 7.0 %fusion.29 = bf16[256,3,128]{0,2,1:T(8,128)(2,1)S(1)} fusion(bf16[4352,256]{1,0:T(8,128)(2,1)S(1)} %maximum_maximum_fusion, f32[3,256,4352]{2,1,0:T(8,128)} %get-tuple-element.26, f32[3,256]{1,0:T(4,128)S(1)} %get-tuple-element.25, pred[256,4352]{1,0:T(8,128)(4,1)S(1)} %fusion.11, f32[256,3]{0,1:T(4,128)S(1)} %bitcast.107), kind=kOutput, calls=%fused_computation.55 | convolution fusion | flops 869203968 | bytes 15802368 | tf_op jit(solution)/shard_map/hqk,kd->hqd/dot_general | solution.py:147
  149.8 8.9 %all_gather.10 = bf16[256,1536]{0,1:T(8,128)(2,1)S(1)} all-gather(bf16[256,384]{0,1:T(8,128)(2,1)S(1)} %bitcast.105), channel_id=1, replica_groups=mesh['seq'=32,'mp'=4] {'mp'}, dimensions={1}, use_global_device_ids=true | all-gather | bytes 983040 | tf_op jit(solution)/shard_map/all_gather | solution.py:154
  160.2 1.9 fusion.23
  162.8 33.5 %all_to_all.55 = bf16[128,16,384]{2,1,0:T(8,128)(2,1)S(1)} all-to-all(bf16[128,16,384]{2,1,0:T(8,128)(2,1)S(1)} %bitcast.96), channel_id=1, replica_groups=mesh['seq'=32,'mp'=4] {'seq','mp'}, dimensions={0} | all-to-all | bytes 3145728 | tf_op jit(solution)/shard_map/all_to_all | solution.py:180
  198.1 4.2 %fusion.16 = f32[512,768]{1,0:T(8,128)} fusion(bf16[512,1536]{1,0:T(8,128)(2,1)S(1)} %bitcast.101, bf16[3,768,1536]{2,1,0:T(8,128)(2,1)} %all-gather.2.cloned.1.call-done), kind=kOutput, calls=%fused_computation.30 | convolution fusion | flops 1207959552 | bytes 5505024 | tf_op jit(solution)/shard_map/dot_general | solution.py:198
  202.3 6.0 %convolution_convert_fusion = bf16[512,1536]{1,0:T(8,128)(2,1)S(1)} fusion(bf16[3,768,1536]{2,1,0:T(8,128)(2,1)} %all-gather.2.cloned.1.call-done, f32[512,768]{1,0:T(8,128)} %fusion.16, bf16[512,1536]{1,0:T(8,128)(2,1)S(1)} %bitcast.102), kind=kOutput, calls=%fused_computation.26 | convolution fusion | flops 2417885184 | bytes 9437184 | tf_op jit(solution)/shard_map/dot_general | solution.py:202
  210.2 5.6 %all-to-all-start.4 = ((bf16[128,16,384]{2,1,0:T(8,128)(2,1)}), bf16[128,16,384]{2,1,0:T(8,128)(2,1)}, u32[]{:S(2)}, u32[]{:S(2)}) async-start(bf16[128,16,384]{2,1,0:T(8,128)(2,1)} %bitcast.34), calls=%async_computation.4 | async-start | bytes 3145728 | tf_op jit(solution)/shard_map/all_to_all | solution.py:208
  217.2 22.9 %all-to-all-done.4 = bf16[128,16,384]{2,1,0:T(8,128)(2,1)} async-done(((bf16[128,16,384]{2,1,0:T(8,128)(2,1)}), bf16[128,16,384]{2,1,0:T(8,128)(2,1)}, u32[]{:S(2)}, u32[]{:S(2)}) %all-to-all-start.4) | async-done | bytes 1572896 | tf_op jit(solution)/shard_map/all_to_all | solution.py:208
  240.2 3.9 %fusion.22 = bf16[256,384]{1,0:T(8,128)(2,1)} fusion(f32[256,2048]{1,0:T(8,128)S(1)} %select_reduce_fusion, bf16[2048,384]{1,0:T(8,128)(2,1)} %bitcast.35, bf16[256,384]{1,0:T(8,128)(2,1)S(1)} %fusion.23), kind=kOutput, calls=%fused_computation.44 | convolution fusion | flops 2416214016 | bytes 4063232 | tf_op jit(solution)/shard_map/dot_general | solution.py:217
  (113 shorter events, 32.7 us)
Async XLA Ops:
  8.1 12.8 %copy-start.5 = (bf16[1,192,1536]{2,1,0:T(8,128)(2,1)S(1)}, bf16[1,192,1536]{2,1,0:T(8,128)(2,1)}, u32[]{:S(2)}) copy-start(bf16[1,192,1536]{2,1,0:T(8,128)(2,1)} %param.19) | copy-start | bytes 1769476
  8.1 12.8 %copy-start.6 = (bf16[1,192,1536]{2,1,0:T(8,128)(2,1)S(1)}, bf16[1,192,1536]{2,1,0:T(8,128)(2,1)}, u32[]{:S(2)}) copy-start(bf16[1,192,1536]{2,1,0:T(8,128)(2,1)} %param.18) | copy-start | bytes 1769476
  8.1 12.8 %copy-start.7 = (bf16[1,192,1536]{2,1,0:T(8,128)(2,1)S(1)}, bf16[1,192,1536]{2,1,0:T(8,128)(2,1)}, u32[]{:S(2)}) copy-start(bf16[1,192,1536]{2,1,0:T(8,128)(2,1)} %param.17) | copy-start | bytes 1769476
  9.5 39.6 %all-to-all-start = ((bf16[32,48,512]{2,1,0:T(8,128)(2,1)}), bf16[32,48,512]{2,1,0:T(8,128)(2,1)S(1)}, u32[]{:S(2)}, u32[]{:S(2)}) async-start(bf16[32,48,512]{2,1,0:T(8,128)(2,1)} %broadcast_in_dim.47), calls=%async_computation | async-start | bytes 3145728 | tf_op jit(solution)/shard_map/all_to_all | solution.py:47
  20.8 177.2 %all-gather.2.cloned.1.call-start = ((), (), s32[]{:S(2)}) async-start(), calls=%async_computation.5 | async-start | bytes 8847360 | tf_op jit(solution)/shard_map/all_gather | solution.py:62
  49.1 3.2 %copy-start.15 = (s32[256,4]{0,1:T(4,128)S(1)}, s32[256,4]{0,1:T(4,128)}, u32[]{:S(2)}) copy-start(s32[256,4]{0,1:T(4,128)} %param.15) | copy-start | bytes 12292
  49.7 8.7 %copy-start.13 = (bf16[384,48]{0,1:T(8,128)(2,1)S(1)}, bf16[384,48]{0,1:T(8,128)(2,1)}, u32[]{:S(2)}) copy-start(bf16[384,48]{0,1:T(8,128)(2,1)} %param.13) | copy-start | bytes 110596
  50.4 2.1 collective-permute-start
  52.6 7.1 %copy-start.1 = (bf16[256,128]{1,0:T(8,128)(2,1)}, bf16[256,128]{1,0:T(8,128)(2,1)S(1)}, u32[]{:S(2)}) copy-start(bf16[256,128]{1,0:T(8,128)(2,1)S(1)} %get-tuple-element.19) | copy-start | bytes 196612
  52.6 7.0 %copy-start.3 = (bf16[256,128]{1,0:T(8,128)(2,1)}, bf16[256,128]{1,0:T(8,128)(2,1)S(1)}, u32[]{:S(2)}) copy-start(bf16[256,128]{1,0:T(8,128)(2,1)S(1)} %get-tuple-element.20) | copy-start | bytes 196612
  52.6 34.2 %collective-permute-start.1 = (bf16[256,256]{1,0:T(8,128)(2,1)S(1)}, bf16[256,256]{1,0:T(8,128)(2,1)S(1)}, u32[]{:S(2)}, u32[]{:S(2)}) collective-permute-start(bf16[256,256]{1,0:T(8,128)(2,1)S(1)} %pad_maximum_fusion.1), channel_id=1, source_target_pairs={{0,4},{1,9},{2,6},{3,11},{4,8},{5,13},{6,10},{7,15},{8,12},{9,17},... | collective-permute-start | bytes 393224 | tf_op jit(solution)/shard_map/ppermute | solution.py:105
  59.6 61.3 %all-to-all-start.1 = ((bf16[32,48,384]{2,1,0:T(8,128)(2,1)}), bf16[32,48,384]{2,1,0:T(8,128)(2,1)}, u32[]{:S(2)}, u32[]{:S(2)}) async-start(bf16[32,48,384]{2,1,0:T(8,128)(2,1)} %broadcast_in_dim.51), calls=%async_computation.1 | async-start | bytes 2359296 | tf_op jit(solution)/shard_map/all_to_all | solution.py:47
  70.8 21.5 %collective-permute-start.2 = (bf16[256,256]{1,0:T(8,128)(2,1)S(1)}, bf16[256,256]{1,0:T(8,128)(2,1)S(1)}, u32[]{:S(2)}, u32[]{:S(2)}) collective-permute-start(bf16[256,256]{1,0:T(8,128)(2,1)S(1)} %pad_maximum_fusion.1), channel_id=1, source_target_pairs={{0,12},{1,17},{2,14},{3,19},{4,16},{5,21},{6,18},{7,23},{8,20},{9,... | collective-permute-start | bytes 393224 | tf_op jit(solution)/shard_map/ppermute | solution.py:105
  75.4 32.4 %collective-permute-start.3 = (bf16[256,256]{1,0:T(8,128)(2,1)S(1)}, bf16[256,256]{1,0:T(8,128)(2,1)S(1)}, u32[]{:S(2)}, u32[]{:S(2)}) collective-permute-start(bf16[256,256]{1,0:T(8,128)(2,1)S(1)} %pad_maximum_fusion.1), channel_id=1, source_target_pairs={{0,20},{1,25},{2,22},{3,27},{4,24},{5,29},{6,26},{7,31},{8,28},{9,... | collective-permute-start | bytes 393224 | tf_op jit(solution)/shard_map/ppermute | solution.py:105
  80.9 30.6 %collective-permute-start.4 = (bf16[256,256]{1,0:T(8,128)(2,1)S(1)}, bf16[256,256]{1,0:T(8,128)(2,1)S(1)}, u32[]{:S(2)}, u32[]{:S(2)}) collective-permute-start(bf16[256,256]{1,0:T(8,128)(2,1)S(1)} %pad_maximum_fusion.1), channel_id=1, source_target_pairs={{0,28},{1,33},{2,30},{3,35},{4,32},{5,37},{6,34},{7,39},{8,36},{9,... | collective-permute-start | bytes 393224 | tf_op jit(solution)/shard_map/ppermute | solution.py:105
  84.0 28.2 %collective-permute-start.5 = (bf16[256,256]{1,0:T(8,128)(2,1)S(1)}, bf16[256,256]{1,0:T(8,128)(2,1)S(1)}, u32[]{:S(2)}, u32[]{:S(2)}) collective-permute-start(bf16[256,256]{1,0:T(8,128)(2,1)S(1)} %pad_maximum_fusion.1), channel_id=1, source_target_pairs={{0,36},{1,41},{2,38},{3,43},{4,40},{5,45},{6,42},{7,47},{8,44},{9,... | collective-permute-start | bytes 393224 | tf_op jit(solution)/shard_map/ppermute | solution.py:105
  86.8 26.0 %collective-permute-start.6 = (bf16[256,256]{1,0:T(8,128)(2,1)S(1)}, bf16[256,256]{1,0:T(8,128)(2,1)S(1)}, u32[]{:S(2)}, u32[]{:S(2)}) collective-permute-start(bf16[256,256]{1,0:T(8,128)(2,1)S(1)} %pad_maximum_fusion.1), channel_id=1, source_target_pairs={{0,44},{1,49},{2,46},{3,51},{4,48},{5,53},{6,50},{7,55},{8,52},{9,... | collective-permute-start | bytes 393224 | tf_op jit(solution)/shard_map/ppermute | solution.py:105
  92.3 21.2 %collective-permute-start.7 = (bf16[256,256]{1,0:T(8,128)(2,1)S(1)}, bf16[256,256]{1,0:T(8,128)(2,1)S(1)}, u32[]{:S(2)}, u32[]{:S(2)}) collective-permute-start(bf16[256,256]{1,0:T(8,128)(2,1)S(1)} %pad_maximum_fusion.1), channel_id=1, source_target_pairs={{0,52},{1,57},{2,54},{3,59},{4,56},{5,61},{6,58},{7,63},{8,60},{9,... | collective-permute-start | bytes 393224 | tf_op jit(solution)/shard_map/ppermute | solution.py:105
  107.7 6.4 %collective-permute-start.8 = (bf16[256,256]{1,0:T(8,128)(2,1)S(1)}, bf16[256,256]{1,0:T(8,128)(2,1)S(1)}, u32[]{:S(2)}, u32[]{:S(2)}) collective-permute-start(bf16[256,256]{1,0:T(8,128)(2,1)S(1)} %pad_maximum_fusion.1), channel_id=1, source_target_pairs={{0,60},{1,65},{2,62},{3,67},{4,64},{5,69},{6,66},{7,71},{8,68},{9,... | collective-permute-start | bytes 393224 | tf_op jit(solution)/shard_map/ppermute | solution.py:105
  114.8 9.8 %collective-permute-start.9 = (bf16[8,256,256]{2,1,0:T(8,128)(2,1)}, bf16[8,256,256]{2,1,0:T(8,128)(2,1)}, u32[]{:S(2)}, u32[]{:S(2)}) collective-permute-start(bf16[8,256,256]{2,1,0:T(8,128)(2,1)} %bitcast_dynamic-update-slice_fusion), channel_id=1, source_target_pairs={{0,1},{1,0},{2,3},{3,2},{4,5},{5,4},{6,7},{7,6},{8,9},{9,8},{10,11... | collective-permute-start | bytes 3145736 | tf_op jit(solution)/shard_map/ppermute | solution.py:107
  120.9 37.8 %all-to-all-start.2 = ((bf16[4,384,384]{2,1,0:T(8,128)(2,1)}), bf16[4,384,384]{2,1,0:T(8,128)(2,1)S(1)}, u32[]{:S(2)}, u32[]{:S(2)}) async-start(bf16[4,384,384]{2,1,0:T(8,128)(2,1)} %bitcast.23), calls=%async_computation.2 | async-start | bytes 2359296 | tf_op jit(solution)/shard_map/all_to_all | solution.py:78
  149.8 10.4 %copy-start.10 = (bf16[256,384]{1,0:T(8,128)(2,1)S(1)}, bf16[256,384]{1,0:T(8,128)(2,1)}, u32[]{:S(2)}) copy-start(bf16[256,384]{1,0:T(8,128)(2,1)} %param.10) | copy-start | bytes 589828
  210.2 5.6 %copy-start.14 = (f32[256,4]{0,1:T(4,128)S(1)}, f32[256,4]{0,1:T(4,128)}, u32[]{:S(2)}) copy-start(f32[256,4]{0,1:T(4,128)} %param.16) | copy-start | bytes 12292
  210.2 30.0 %all-to-all-start.4 = ((bf16[128,16,384]{2,1,0:T(8,128)(2,1)}), bf16[128,16,384]{2,1,0:T(8,128)(2,1)}, u32[]{:S(2)}, u32[]{:S(2)}) async-start(bf16[128,16,384]{2,1,0:T(8,128)(2,1)} %bitcast.34), calls=%async_computation.4 | async-start | bytes 3145728 | tf_op jit(solution)/shard_map/all_to_all | solution.py:208
  (8 other events, 9.9 us)
Sparse Core Ops, SparseCore 0:
  23.3 95.3 all-gather.1

commit v7 on v5

--- a/solution.py
+++ b/solution.py
@@ -4,6 +4,8 @@
 import jax.numpy as jnp
 from jax import lax
 from jax.sharding import PartitionSpec as P
+from jax.experimental import pallas as pl
+from jax.experimental.pallas import tpu as pltpu
 
 D = 1536
 HQ = 12
@@ -37,6 +39,67 @@
     return jnp.concatenate(
         [front * cosine - latter * sine, latter * cosine + front * sine], axis=-1
     )
+
+
+def attention_kernel(q_ref, k_ref, v_ref, qi_ref, qp_ref, ki_ref, kp_ref, o_ref, m_sc, l_sc, acc_sc):
+    step = pl.program_id(0)
+
+    @pl.when(step == 0)
+    def _():
+        m_sc[...] = jnp.full(m_sc.shape, -1e30, jnp.float32)
+        l_sc[...] = jnp.zeros(l_sc.shape, jnp.float32)
+        acc_sc[...] = jnp.zeros(acc_sc.shape, jnp.float32)
+
+    scores = lax.dot_general(
+        q_ref[...], k_ref[...], (((1,), (1,)), ((), ())), preferred_element_type=jnp.float32
+    ) * HD ** (-0.5)
+    key_at = ki_ref[...]
+    spacing = qi_ref[...] - key_at
+    allowed = (qp_ref[...] == kp_ref[...]) & (spacing >= 0) & (spacing < WINDOW) & (key_at >= 0)
+    masked = jnp.where(allowed, scores, -1e30)
+    m_old = m_sc[...]
+    m_new = jnp.maximum(m_old, jnp.max(masked, axis=1, keepdims=True))
+    alpha = jnp.exp(m_old - m_new)
+    probs = jnp.where(allowed, jnp.exp(masked - m_new), 0.0)
+    l_sc[...] = alpha * l_sc[...] + jnp.sum(probs, axis=1, keepdims=True)
+    probs_hi = probs.astype(jnp.bfloat16)
+    probs_lo = (probs - probs_hi.astype(jnp.float32)).astype(jnp.bfloat16)
+    values = v_ref[...]
+    mixed = jnp.dot(probs_hi, values, preferred_element_type=jnp.float32) + jnp.dot(
+        probs_lo, values, preferred_element_type=jnp.float32
+    )
+    acc_sc[...] = alpha * acc_sc[...] + mixed
+    m_sc[...] = m_new
+
+    @pl.when(step == pl.num_programs(0) - 1)
+    def _():
+        o_ref[...] = (acc_sc[...] / l_sc[...]).astype(o_ref.dtype)
+
+
+def attention(queries, keys, values, query_at, query_prompt, key_at, key_prompt, chunk):
+    rows = queries.shape[0]
+    steps = keys.shape[0] // chunk
+    full = lambda shape: pl.BlockSpec(shape, lambda j: (0, 0))
+    return pl.pallas_call(
+        attention_kernel,
+        grid=(steps,),
+        in_specs=[
+            full((rows, HD)),
+            pl.BlockSpec((chunk, HD), lambda j: (j, 0)),
+            pl.BlockSpec((chunk, HD), lambda j: (j, 0)),
+            full((rows, 1)),
+            full((rows, 1)),
+            pl.BlockSpec((1, chunk), lambda j: (0, j)),
+            pl.BlockSpec((1, chunk), lambda j: (0, j)),
+        ],
+        out_specs=full((rows, HD)),
+        out_shape=jax.ShapeDtypeStruct((rows, HD), jnp.bfloat16),
+        scratch_shapes=[
+            pltpu.VMEM((rows, 1), jnp.float32),
+            pltpu.VMEM((rows, 1), jnp.float32),
+            pltpu.VMEM((rows, HD), jnp.float32),
+        ],
+    )(queries, keys, values, query_at, query_prompt, key_at, key_prompt)
 
 
 def gather_seq(piece, count):
@@ -117,39 +180,33 @@
         ]
     )
     kv_win = jnp.concatenate(
-        [odd.reshape(-1, 2 * HD), even.reshape(-1, 2 * HD), kv_own], axis=0
-    )
-    key_rows = kv_win[:, :HD]
-    value_rows = kv_win[:, HD:].astype(jnp.float32)
+        [
+            odd.reshape(-1, 2 * HD),
+            even.reshape(-1, 2 * HD),
+            kv_own,
+            jnp.zeros((tok_rows, 2 * HD), jnp.bfloat16),
+        ],
+        axis=0,
+    )
     key_index = (
         (seq_index - offsets)[:, None] * tok_rows + jnp.arange(tok_rows, dtype=jnp.int32)[None, :]
     ).reshape(-1)
-    key_index = jnp.where(
-        jnp.repeat(offsets, tok_rows) <= back, key_index, -1
-    )
-
-    scores = jnp.einsum(
-        "hqd,kd->hqk", queries, key_rows, preferred_element_type=jnp.float32
-    ) * HD ** (-0.5)
+    key_index = jnp.where(jnp.repeat(offsets, tok_rows) <= back, key_index, -1)
+    key_index = jnp.concatenate([key_index, jnp.full((tok_rows,), -1, jnp.int32)])
     query_prompt, _ = prompt_ids(own_index, lengths)
     key_prompt, _ = prompt_ids(key_index, lengths)
-    spacing = own_index[:, None] - key_index[None, :]
-    allowed = (
-        (query_prompt[:, None] == key_prompt[None, :])
-        & (spacing >= 0)
-        & (spacing < WINDOW)
-        & (key_index[None, :] >= 0)
-    )[None]
-    masked = jnp.where(allowed, scores, -1e30)
-    peak = jnp.max(masked, axis=-1)
-    probs = jnp.where(allowed, jnp.exp(masked - peak[..., None]), 0.0)
-    total = jnp.sum(probs, axis=-1)
-    accum = jnp.einsum("hqk,kd->hqd", probs, value_rows)
+    mixed = attention(
+        queries.reshape(heads_here * tok_rows, HD),
+        kv_win[:, :HD],
+        kv_win[:, HD:],
+        jnp.tile(own_index, heads_here)[:, None],
+        jnp.tile(query_prompt, heads_here)[:, None],
+        key_index[None, :],
+        key_prompt[None, :],
+        3 * tok_rows,
+    )
     attended = (
-        (accum / total[..., None])
-        .transpose(1, 0, 2)
-        .reshape(tok_rows, q_cols)
-        .astype(jnp.bfloat16)
+        mixed.reshape(heads_here, tok_rows, HD).transpose(1, 0, 2).reshape(tok_rows, q_cols)
     )
     partial_out = lax.dot_general(
         attended, wo_rows, (((1,), (1,)), ((), ())), preferred_element_type=jnp.float32

time: 243 us -> 248 us (1.021)
  Pallas kernels: 0 us -> 19.1 us
  matrix products: 31.2 us -> 17.9 us
  other arithmetic: 24.5 us -> 18.3 us
  waiting for transfers between devices: 31.9 us -> 35.7 us
  local copies, waits for them, and re-layouts: 16.6 us -> 19.8 us
    pallas_call x0 -> x1, Pallas kernels: none -> 19.1 us  [attention(): pl.pallas_call(attention_kernel, grid=(steps,), in_specs=[full((rows, HD)...]
    dot_general x2 -> x0, matrix products: 13.4 us -> none  [the longest x1 7 us: local(): accum = jnp.einsum('hqk,kd->hqd', probs, value_rows)]
    reduce_sum x1 -> x0, other arithmetic: 9.02 us -> none  [local(): total = jnp.sum(probs, axis=-1)]
    concatenate x1, other arithmetic: 0.16 us -> 8.47 us  [local(): jnp.concatenate([odd.reshape(-1, 2 * HD), even.reshape(-1, 2 * HD), kv_ow...]
    ppermute x8, waiting for transfers between devices: 0.02 us -> 3.24 us  [local(): fetched.append(lax.ppermute(kv_own, ('seq', 'mp'), pairs))]
    unnamed x27 -> x43, local copies, waits for them, and re-layouts: 6.19 us -> 5.38 us
  transfers between devices with their start and end apart: 15 -> 15, of which waited for: 3 -> 4; matrix products, arithmetic and copies ran while one was open for 21% -> 13% of each run, Pallas kernels for 0% -> 8%
where the time goes in v7:
time: 248 us; the launch traced here: 247 us
  starting transfers between devices  65.4 us (26%)
  blocking collectives  55.2 us (22%)
  waiting for transfers between devices  35.7 us (14%)
  local copies, waits for them, and re-layouts  19.8 us (8%)
  Pallas kernels  19.1 us (8%)
  other arithmetic  18.3 us (7%)
  matrix products  17.9 us (7%)
  between operations  15.3 us (6%)
    all_to_all x1, blocking collectives, local(): arrived = lax.all_to_all(buffer, ('seq', 'mp'), 0, 0, tiled=True)  34.1 us
    ppermute x8, starting transfers between devices, local(): fetched.append(lax.ppermute(kv_own, ('seq', 'mp'), pairs))  32.1 us
    all_to_all x1, waiting for transfers between devices, local(): returned = lax.all_to_all(outgoing, ('seq', 'mp'), 0, 0, tiled=True)  22.9 us
    all_to_all x2, starting transfers between devices, gather_seq(): return lax.all_to_all(spread, 'seq', 0, 0, tiled=True)  21.6 us
    all_gather x1, blocking collectives, local(): whole = lax.all_gather(hidden_in, 'mp', axis=1, tiled=True)  21.1 us
    pallas_call x1, Pallas kernels, attention(): pl.pallas_call(attention_kernel, grid=(steps,), in_specs=[full((rows, HD)...  19.1 us
    concatenate x1, other arithmetic, local(): jnp.concatenate([odd.reshape(-1, 2 * HD), even.reshape(-1, 2 * HD), kv_ow...  8.47 us
    all_to_all x1, waiting for transfers between devices, local(): lax.all_to_all(partial_out.astype(jnp.bfloat16), 'mp', 1, 0, tiled=True)  8.38 us
  transfers between devices with their start and end apart: 15, of which 4 were waited for; matrix products, arithmetic and copies ran while one was open for 13% of the time, Pallas kernels for 8%

profile of v7, /device:TPU:1, one launch (start us, length us, event | category | flops | bytes accessed | tf_op | source)
XLA Modules:
  0.0 246.5 jit_solution(3839971856850720459)
XLA Ops:
  9.4 11.5 %all-to-all-start = ((bf16[32,48,512]{2,1,0:T(8,128)(2,1)}), bf16[32,48,512]{2,1,0:T(8,128)(2,1)S(1)}, u32[]{:S(2)}, u32[]{:S(2)}) async-start(bf16[32,48,512]{2,1,0:T(8,128)(2,1)} %broadcast_in_dim.32), calls=%async_computation | async-start | bytes 3145728 | tf_op jit(solution)/shard_map/all_to_all | solution.py:110
  21.0 2.5 %pad_maximum_fusion = bf16[3,192,1536]{2,1,0:T(8,128)(2,1)} fusion(bf16[1,192,1536]{2,1,0:T(8,128)(2,1)S(1)} %copy-done.8, bf16[1,192,1536]{2,1,0:T(8,128)(2,1)S(1)} %copy-done.9, bf16[1,192,1536]{2,1,0:T(8,128)(2,1)} %param.17), kind=kLoop, calls=%fused_computation.22 | loop fusion | flops 1769472 | bytes 3538944 | tf_op jit(solution)/shard_map/concatenate | solution.py:126
  26.8 21.1 %all_gather.6 = bf16[256,1536]{1,0:T(8,128)(2,1)S(1)} all-gather(bf16[256,384]{1,0:T(8,128)(2,1)S(1)} %copy-done.1), channel_id=1, replica_groups=mesh['seq'=32,'mp'=4] {'mp'}, dimensions={1}, use_global_device_ids=true | all-gather | bytes 983040 | tf_op jit(solution)/shard_map/all_gather | solution.py:134
  51.7 5.5 %collective-permute-start.1 = (bf16[256,256]{1,0:T(8,128)(2,1)S(1)}, bf16[256,256]{1,0:T(8,128)(2,1)S(1)}, u32[]{:S(2)}, u32[]{:S(2)}) collective-permute-start(bf16[256,256]{1,0:T(8,128)(2,1)S(1)} %pad_maximum_fusion.1), channel_id=1, source_target_pairs={{0,4},{1,9},{2,6},{3,11},{4,8},{5,13},{6,10},{7,15},{8,12},{9,17},... | collective-permute-start | bytes 393224 | tf_op jit(solution)/shard_map/ppermute | solution.py:168
  59.1 5.1 %collective-permute-start.2 = (bf16[256,256]{1,0:T(8,128)(2,1)S(1)}, bf16[256,256]{1,0:T(8,128)(2,1)S(1)}, u32[]{:S(2)}, u32[]{:S(2)}) collective-permute-start(bf16[256,256]{1,0:T(8,128)(2,1)S(1)} %pad_maximum_fusion.1), channel_id=1, source_target_pairs={{0,12},{1,17},{2,14},{3,19},{4,16},{5,21},{6,18},{7,23},{8,20},{9,... | collective-permute-start | bytes 393224 | tf_op jit(solution)/shard_map/ppermute | solution.py:168
  64.3 8.4 %collective-permute-start.3 = (bf16[256,256]{1,0:T(8,128)(2,1)S(1)}, bf16[256,256]{1,0:T(8,128)(2,1)S(1)}, u32[]{:S(2)}, u32[]{:S(2)}) collective-permute-start(bf16[256,256]{1,0:T(8,128)(2,1)S(1)} %pad_maximum_fusion.1), channel_id=1, source_target_pairs={{0,20},{1,25},{2,22},{3,27},{4,24},{5,29},{6,26},{7,31},{8,28},{9,... | collective-permute-start | bytes 393224 | tf_op jit(solution)/shard_map/ppermute | solution.py:168
  72.7 2.1 collective-permute-start.4
  74.8 2.2 collective-permute-start.5
  77.0 4.3 %collective-permute-start.6 = (bf16[256,256]{1,0:T(8,128)(2,1)S(1)}, bf16[256,256]{1,0:T(8,128)(2,1)S(1)}, u32[]{:S(2)}, u32[]{:S(2)}) collective-permute-start(bf16[256,256]{1,0:T(8,128)(2,1)S(1)} %pad_maximum_fusion.1), channel_id=1, source_target_pairs={{0,44},{1,49},{2,46},{3,51},{4,48},{5,53},{6,50},{7,55},{8,52},{9,... | collective-permute-start | bytes 393224 | tf_op jit(solution)/shard_map/ppermute | solution.py:168
  83.3 2.5 %collective-permute-start.8 = (bf16[256,256]{1,0:T(8,128)(2,1)S(1)}, bf16[256,256]{1,0:T(8,128)(2,1)S(1)}, u32[]{:S(2)}, u32[]{:S(2)}) collective-permute-start(bf16[256,256]{1,0:T(8,128)(2,1)S(1)} %pad_maximum_fusion.1), channel_id=1, source_target_pairs={{0,60},{1,65},{2,62},{3,67},{4,64},{5,69},{6,66},{7,71},{8,68},{9,... | collective-permute-start | bytes 393224 | tf_op jit(solution)/shard_map/ppermute | solution.py:168
  86.0 3.2 %collective-permute-done.8 = bf16[256,256]{1,0:T(8,128)(2,1)S(1)} collective-permute-done((bf16[256,256]{1,0:T(8,128)(2,1)S(1)}, bf16[256,256]{1,0:T(8,128)(2,1)S(1)}, u32[]{:S(2)}, u32[]{:S(2)}) %collective-permute-start.8) | collective-permute-done | bytes 131104 | tf_op jit(solution)/shard_map/ppermute | solution.py:168
  89.2 2.1 collective-permute-start.9
  95.9 10.1 %all-to-all-start.1 = ((bf16[32,48,384]{2,1,0:T(8,128)(2,1)}), bf16[32,48,384]{2,1,0:T(8,128)(2,1)S(1)}, u32[]{:S(2)}, u32[]{:S(2)}) async-start(bf16[32,48,384]{2,1,0:T(8,128)(2,1)} %broadcast_in_dim.39), calls=%async_computation.1 | async-start | bytes 2359296 | tf_op jit(solution)/shard_map/all_to_all | solution.py:110
  106.9 8.5 %maximum_maximum_fusion = bf16[4608,256]{1,0:T(8,128)(2,1)S(1)} fusion(bf16[256,128]{1,0:T(8,128)(2,1)S(1)} %copy-done.7, bf16[256,128]{1,0:T(8,128)(2,1)S(1)} %copy-done.5, bf16[2048,256]{1,0:T(8,128)(2,1)S(1)} %bitcast.92, bf16[2048,256]{1,0:T(8,128)(2,1)S(1)} %bitcast.91, bf16[4608]{0:T(1024)(128)(2,1)S(1)} %pad.11.clone), kind=kLoop, calls=%fused_computation.19 | loop fusion | flops 11796480 | bytes 4596736 | tf_op jit(solution)/shard_map/concatenate | solution.py:182
  116.9 19.1 %shard_map.100 = bf16[768,128]{1,0:T(8,128)(2,1)} custom-call(bf16[768,128]{1,0:T(8,128)(2,1)} %bitcast.101, bf16[4608,128]{1,0:T(8,128)(2,1)} %get-tuple-element.12.k_ref, bf16[4608,128]{1,0:T(8,128)(2,1)} %get-tuple-element.11.v_ref, s32[768,1]{1,0:T(8,128)} %bitcast.99, s32[768,1]{1,0:T(8,128)} %bitcast.98, s32[1,4608]{1,0:T(1,128)} %broadcast_in_dim.37.ki_ref, ...), custom_call_target="tpu_custom_call" | custom-call | tf_op jit(solution)/shard_map/pallas_call | solution.py:83
  138.7 3.8 %all-to-all-start.2 = ((bf16[256,4,384]{2,0,1:T(8,128)(2,1)}), bf16[256,4,384]{2,0,1:T(8,128)(2,1)S(1)}, u32[]{:S(2)}, u32[]{:S(2)}) async-start(bf16[256,4,384]{2,0,1:T(8,128)(2,1)} %bitcast.86), calls=%async_computation.2 | async-start | bytes 1572864 | tf_op jit(solution)/shard_map/all_to_all | solution.py:214
  144.8 8.4 %all-to-all-done.2 = bf16[256,4,384]{2,0,1:T(8,128)(2,1)S(1)} async-done(((bf16[256,4,384]{2,0,1:T(8,128)(2,1)}), bf16[256,4,384]{2,0,1:T(8,128)(2,1)S(1)}, u32[]{:S(2)}, u32[]{:S(2)}) %all-to-all-start.2) | async-done | bytes 786464 | tf_op jit(solution)/shard_map/all_to_all | solution.py:214
  154.0 34.1 %all_to_all.52 = bf16[128,16,384]{2,1,0:T(8,128)(2,1)S(1)} all-to-all(bf16[128,16,384]{2,1,0:T(8,128)(2,1)S(1)} %bitcast.88), channel_id=1, replica_groups=mesh['seq'=32,'mp'=4] {'seq','mp'}, dimensions={0} | all-to-all | bytes 3145728 | tf_op jit(solution)/shard_map/all_to_all | solution.py:240
  189.9 4.3 %fusion.5 = f32[512,768]{1,0:T(8,128)} fusion(bf16[512,1536]{1,0:T(8,128)(2,1)S(1)} %bitcast.95, bf16[3,768,1536]{2,1,0:T(8,128)(2,1)} %all-gather.2.cloned.1.call-done), kind=kOutput, calls=%fused_computation.16 | convolution fusion | flops 1207959552 | bytes 5505024 | tf_op jit(solution)/shard_map/dot_general | solution.py:258
  194.2 7.2 %convolution_convert_fusion = bf16[512,1536]{1,0:T(8,128)(2,1)} fusion(bf16[3,768,1536]{2,1,0:T(8,128)(2,1)} %all-gather.2.cloned.1.call-done, f32[512,768]{1,0:T(8,128)} %fusion.5, bf16[512,1536]{1,0:T(8,128)(2,1)S(1)} %bitcast.96), kind=kOutput, calls=%fused_computation.11 | convolution fusion | flops 2417885184 | bytes 9437184 | tf_op jit(solution)/shard_map/dot_general | solution.py:262
  201.4 3.0 %reshape.281 = bf16[32,16,4,384]{3,2,1,0:T(4,128)(2,1)S(1)} reshape(bf16[512,1536]{1,0:T(8,128)(2,1)} %convolution_convert_fusion) | data formatting | bytes 3145728 | tf_op jit(solution)/shard_map/reshape | solution.py:264
  205.8 5.6 %all-to-all-start.4 = ((bf16[128,16,384]{2,1,0:T(8,128)(2,1)}), bf16[128,16,384]{2,1,0:T(8,128)(2,1)}, u32[]{:S(2)}, u32[]{:S(2)}) async-start(bf16[128,16,384]{2,1,0:T(8,128)(2,1)} %bitcast.31), calls=%async_computation.4 | async-start | bytes 3145728 | tf_op jit(solution)/shard_map/all_to_all | solution.py:268
  212.9 22.9 %all-to-all-done.4 = bf16[128,16,384]{2,1,0:T(8,128)(2,1)} async-done(((bf16[128,16,384]{2,1,0:T(8,128)(2,1)}), bf16[128,16,384]{2,1,0:T(8,128)(2,1)}, u32[]{:S(2)}, u32[]{:S(2)}) %all-to-all-start.4) | async-done | bytes 1572896 | tf_op jit(solution)/shard_map/all_to_all | solution.py:268
  235.8 3.9 %fusion.10 = bf16[256,384]{1,0:T(8,128)(2,1)} fusion(f32[256,2048]{1,0:T(8,128)S(1)} %select_reduce_fusion, bf16[2048,384]{1,0:T(8,128)(2,1)} %bitcast.32, f32[256,384]{1,0:T(8,128)S(1)} %convert_reduce_fusion, bf16[256,384]{1,0:T(8,128)(2,1)S(1)} %copy-done.1), kind=kOutput, calls=%fused_computation.29 | convolution fusion | flops 2416508928 | bytes 4456448 | tf_op jit(solution)/shard_map/dot_general | solution.py:277
  (114 shorter events, 30.0 us)
Async XLA Ops:
  9.4 11.5 %copy-start.8 = (bf16[1,192,1536]{2,1,0:T(8,128)(2,1)S(1)}, bf16[1,192,1536]{2,1,0:T(8,128)(2,1)}, u32[]{:S(2)}) copy-start(bf16[1,192,1536]{2,1,0:T(8,128)(2,1)} %param.19) | copy-start | bytes 1769476
  9.4 11.5 %copy-start.9 = (bf16[1,192,1536]{2,1,0:T(8,128)(2,1)S(1)}, bf16[1,192,1536]{2,1,0:T(8,128)(2,1)}, u32[]{:S(2)}) copy-start(bf16[1,192,1536]{2,1,0:T(8,128)(2,1)} %param.18) | copy-start | bytes 1769476
  9.4 38.7 %all-to-all-start = ((bf16[32,48,512]{2,1,0:T(8,128)(2,1)}), bf16[32,48,512]{2,1,0:T(8,128)(2,1)S(1)}, u32[]{:S(2)}, u32[]{:S(2)}) async-start(bf16[32,48,512]{2,1,0:T(8,128)(2,1)} %broadcast_in_dim.32), calls=%async_computation | async-start | bytes 3145728 | tf_op jit(solution)/shard_map/all_to_all | solution.py:110
  20.9 169.0 %all-gather.2.cloned.1.call-start = ((), (), s32[]{:S(2)}) async-start(), calls=%async_computation.5 | async-start | bytes 8847360 | tf_op jit(solution)/shard_map/all_gather | solution.py:125
  23.5 3.2 %copy-start.1 = (bf16[256,384]{1,0:T(8,128)(2,1)S(1)}, bf16[256,384]{1,0:T(8,128)(2,1)}, u32[]{:S(2)}) copy-start(bf16[256,384]{1,0:T(8,128)(2,1)} %param.10) | copy-start | bytes 589828
  49.7 1.3 collective-permute-start
  51.7 42.0 %copy-start.3 = (f32[256,512]{1,0:T(8,128)S(1)}, f32[256,512]{1,0:T(8,128)}, u32[]{:S(2)}) copy-start(f32[256,512]{1,0:T(8,128)} %copy-done.2) | copy-start | bytes 1572868
  51.7 25.3 %collective-permute-start.1 = (bf16[256,256]{1,0:T(8,128)(2,1)S(1)}, bf16[256,256]{1,0:T(8,128)(2,1)S(1)}, u32[]{:S(2)}, u32[]{:S(2)}) collective-permute-start(bf16[256,256]{1,0:T(8,128)(2,1)S(1)} %pad_maximum_fusion.1), channel_id=1, source_target_pairs={{0,4},{1,9},{2,6},{3,11},{4,8},{5,13},{6,10},{7,15},{8,12},{9,17},... | collective-permute-start | bytes 393224 | tf_op jit(solution)/shard_map/ppermute | solution.py:168
  59.1 22.2 %collective-permute-start.2 = (bf16[256,256]{1,0:T(8,128)(2,1)S(1)}, bf16[256,256]{1,0:T(8,128)(2,1)S(1)}, u32[]{:S(2)}, u32[]{:S(2)}) collective-permute-start(bf16[256,256]{1,0:T(8,128)(2,1)S(1)} %pad_maximum_fusion.1), channel_id=1, source_target_pairs={{0,12},{1,17},{2,14},{3,19},{4,16},{5,21},{6,18},{7,23},{8,20},{9,... | collective-permute-start | bytes 393224 | tf_op jit(solution)/shard_map/ppermute | solution.py:168
  64.3 19.1 %collective-permute-start.3 = (bf16[256,256]{1,0:T(8,128)(2,1)S(1)}, bf16[256,256]{1,0:T(8,128)(2,1)S(1)}, u32[]{:S(2)}, u32[]{:S(2)}) collective-permute-start(bf16[256,256]{1,0:T(8,128)(2,1)S(1)} %pad_maximum_fusion.1), channel_id=1, source_target_pairs={{0,20},{1,25},{2,22},{3,27},{4,24},{5,29},{6,26},{7,31},{8,28},{9,... | collective-permute-start | bytes 393224 | tf_op jit(solution)/shard_map/ppermute | solution.py:168
  72.7 13.2 %collective-permute-start.4 = (bf16[256,256]{1,0:T(8,128)(2,1)S(1)}, bf16[256,256]{1,0:T(8,128)(2,1)S(1)}, u32[]{:S(2)}, u32[]{:S(2)}) collective-permute-start(bf16[256,256]{1,0:T(8,128)(2,1)S(1)} %pad_maximum_fusion.1), channel_id=1, source_target_pairs={{0,28},{1,33},{2,30},{3,35},{4,32},{5,37},{6,34},{7,39},{8,36},{9,... | collective-permute-start | bytes 393224 | tf_op jit(solution)/shard_map/ppermute | solution.py:168
  74.8 11.1 %collective-permute-start.5 = (bf16[256,256]{1,0:T(8,128)(2,1)S(1)}, bf16[256,256]{1,0:T(8,128)(2,1)S(1)}, u32[]{:S(2)}, u32[]{:S(2)}) collective-permute-start(bf16[256,256]{1,0:T(8,128)(2,1)S(1)} %pad_maximum_fusion.1), channel_id=1, source_target_pairs={{0,36},{1,41},{2,38},{3,43},{4,40},{5,45},{6,42},{7,47},{8,44},{9,... | collective-permute-start | bytes 393224 | tf_op jit(solution)/shard_map/ppermute | solution.py:168
  77.0 8.9 %collective-permute-start.6 = (bf16[256,256]{1,0:T(8,128)(2,1)S(1)}, bf16[256,256]{1,0:T(8,128)(2,1)S(1)}, u32[]{:S(2)}, u32[]{:S(2)}) collective-permute-start(bf16[256,256]{1,0:T(8,128)(2,1)S(1)} %pad_maximum_fusion.1), channel_id=1, source_target_pairs={{0,44},{1,49},{2,46},{3,51},{4,48},{5,53},{6,50},{7,55},{8,52},{9,... | collective-permute-start | bytes 393224 | tf_op jit(solution)/shard_map/ppermute | solution.py:168
  81.4 4.6 %collective-permute-start.7 = (bf16[256,256]{1,0:T(8,128)(2,1)S(1)}, bf16[256,256]{1,0:T(8,128)(2,1)S(1)}, u32[]{:S(2)}, u32[]{:S(2)}) collective-permute-start(bf16[256,256]{1,0:T(8,128)(2,1)S(1)} %pad_maximum_fusion.1), channel_id=1, source_target_pairs={{0,52},{1,57},{2,54},{3,59},{4,56},{5,61},{6,58},{7,63},{8,60},{9,... | collective-permute-start | bytes 393224 | tf_op jit(solution)/shard_map/ppermute | solution.py:168
  83.3 5.9 %collective-permute-start.8 = (bf16[256,256]{1,0:T(8,128)(2,1)S(1)}, bf16[256,256]{1,0:T(8,128)(2,1)S(1)}, u32[]{:S(2)}, u32[]{:S(2)}) collective-permute-start(bf16[256,256]{1,0:T(8,128)(2,1)S(1)} %pad_maximum_fusion.1), channel_id=1, source_target_pairs={{0,60},{1,65},{2,62},{3,67},{4,64},{5,69},{6,66},{7,71},{8,68},{9,... | collective-permute-start | bytes 393224 | tf_op jit(solution)/shard_map/ppermute | solution.py:168
  89.2 16.8 %collective-permute-start.9 = (bf16[8,256,256]{2,1,0:T(8,128)(2,1)S(1)}, bf16[8,256,256]{2,1,0:T(8,128)(2,1)S(1)}, u32[]{:S(2)}, u32[]{:S(2)}) collective-permute-start(bf16[8,256,256]{2,1,0:T(8,128)(2,1)S(1)} %bitcast_dynamic-update-slice_fusion), channel_id=1, source_target_pairs={{0,1},{1,0},{2,3},{3,2},{4,5},{5,4},{6,7},{7,6},{8,9},{9,8},{10,11... | collective-permute-start | bytes 3145736 | tf_op jit(solution)/shard_map/ppermute | solution.py:170
  92.4 2.4 copy-start.10
  95.9 41.1 %all-to-all-start.1 = ((bf16[32,48,384]{2,1,0:T(8,128)(2,1)}), bf16[32,48,384]{2,1,0:T(8,128)(2,1)S(1)}, u32[]{:S(2)}, u32[]{:S(2)}) async-start(bf16[32,48,384]{2,1,0:T(8,128)(2,1)} %broadcast_in_dim.39), calls=%async_computation.1 | async-start | bytes 2359296 | tf_op jit(solution)/shard_map/all_to_all | solution.py:110
  106.0 0.8 copy-start.5
  106.0 0.9 copy-start.7
  137.7 4.8 %copy-start.12 = (s32[256,4]{0,1:T(4,128)S(1)}, s32[256,4]{0,1:T(4,128)}, u32[]{:S(2)}) copy-start(s32[256,4]{0,1:T(4,128)} %param.15) | copy-start | bytes 12292
  138.7 14.6 %all-to-all-start.2 = ((bf16[256,4,384]{2,0,1:T(8,128)(2,1)}), bf16[256,4,384]{2,0,1:T(8,128)(2,1)S(1)}, u32[]{:S(2)}, u32[]{:S(2)}) async-start(bf16[256,4,384]{2,0,1:T(8,128)(2,1)} %bitcast.86), calls=%async_computation.2 | async-start | bytes 1572864 | tf_op jit(solution)/shard_map/all_to_all | solution.py:214
  205.8 5.6 %copy-start.11 = (f32[256,4]{0,1:T(4,128)S(1)}, f32[256,4]{0,1:T(4,128)}, u32[]{:S(2)}) copy-start(f32[256,4]{0,1:T(4,128)} %param.16) | copy-start | bytes 12292
  205.8 30.0 %all-to-all-start.4 = ((bf16[128,16,384]{2,1,0:T(8,128)(2,1)}), bf16[128,16,384]{2,1,0:T(8,128)(2,1)}, u32[]{:S(2)}, u32[]{:S(2)}) async-start(bf16[128,16,384]{2,1,0:T(8,128)(2,1)} %bitcast.31), calls=%async_computation.4 | async-start | bytes 3145728 | tf_op jit(solution)/shard_map/all_to_all | solution.py:268
  (5 other events, 3.5 us)
Sparse Core Ops, SparseCore 0:
  23.7 82.4 all-gather.1

commit v8 on v5

--- a/solution.py
+++ b/solution.py
@@ -1,9 +1,12 @@
+import functools
 import math
 
 import jax
 import jax.numpy as jnp
 from jax import lax
 from jax.sharding import PartitionSpec as P
+from jax.experimental import pallas as pl
+from jax.experimental.pallas import tpu as pltpu
 
 D = 1536
 HQ = 12
@@ -37,6 +40,89 @@
     return jnp.concatenate(
         [front * cosine - latter * sine, latter * cosine + front * sine], axis=-1
     )
+
+
+def attention_kernel(
+    half, q_ref, fetched_ref, partner_ref, own_ref, qi_ref, qp_ref, ki_ref, kp_ref, o_ref, m_sc, l_sc,
+    acc_sc
+):
+    step = pl.program_id(0)
+
+    @pl.when(step == 0)
+    def _():
+        m_sc[...] = jnp.full(m_sc.shape, -1e30, jnp.float32)
+        l_sc[...] = jnp.zeros(l_sc.shape, jnp.float32)
+        acc_sc[...] = jnp.zeros(acc_sc.shape, jnp.float32)
+
+    heads, rows, _ = q_ref.shape
+    key_at = ki_ref[0]
+    spacing = qi_ref[...] - key_at
+    allowed = (qp_ref[...] == kp_ref[0]) & (spacing >= 0) & (spacing < WINDOW) & (key_at >= 0)
+
+    def update(block):
+        keys = block[:, :HD]
+        values = block[:, HD:]
+        scores = lax.dot_general(
+            q_ref[...].reshape(heads * rows, HD), keys, (((1,), (1,)), ((), ())),
+            preferred_element_type=jnp.float32,
+        ).reshape(heads, rows, -1) * HD ** (-0.5)
+        masked = jnp.where(allowed[None], scores, -1e30)
+        m_old = m_sc[...]
+        m_new = jnp.maximum(m_old, jnp.max(masked, axis=2, keepdims=True))
+        alpha = jnp.exp(m_old - m_new)
+        probs = jnp.where(allowed[None], jnp.exp(masked - m_new), 0.0)
+        l_sc[...] = alpha * l_sc[...] + jnp.sum(probs, axis=2, keepdims=True)
+        mixed = jnp.dot(
+            probs.reshape(heads * rows, -1).astype(jnp.bfloat16), values,
+            preferred_element_type=jnp.float32,
+        ).reshape(heads, rows, HD)
+        acc_sc[...] = alpha * acc_sc[...] + mixed
+        m_sc[...] = m_new
+
+    @pl.when(step < half)
+    def _():
+        update(fetched_ref[0])
+
+    @pl.when((step >= half) & (step < 2 * half))
+    def _():
+        update(partner_ref[0])
+
+    @pl.when(step == 2 * half)
+    def _():
+        update(own_ref[...])
+
+    @pl.when(step == pl.num_programs(0) - 1)
+    def _():
+        o_ref[...] = (acc_sc[...] / l_sc[...]).astype(o_ref.dtype)
+
+
+def attention(queries, fetched, partner, own, query_at, query_prompt, key_at, key_prompt):
+    heads, rows, _ = queries.shape
+    half, block, width = fetched.shape
+    last = half - 1
+    return pl.pallas_call(
+        functools.partial(attention_kernel, half),
+        grid=(2 * half + 1,),
+        in_specs=[
+            pl.BlockSpec((heads, rows, HD), lambda j: (0, 0, 0)),
+            pl.BlockSpec((1, block, width), lambda j: (jnp.minimum(j, last), 0, 0)),
+            pl.BlockSpec(
+                (1, block, width), lambda j: (jnp.minimum(jnp.maximum(j - half, 0), last), 0, 0)
+            ),
+            pl.BlockSpec((block, width), lambda j: (0, 0)),
+            pl.BlockSpec((rows, 1), lambda j: (0, 0)),
+            pl.BlockSpec((rows, 1), lambda j: (0, 0)),
+            pl.BlockSpec((1, 1, block), lambda j: (j, 0, 0)),
+            pl.BlockSpec((1, 1, block), lambda j: (j, 0, 0)),
+        ],
+        out_specs=pl.BlockSpec((heads, rows, HD), lambda j: (0, 0, 0)),
+        out_shape=jax.ShapeDtypeStruct((heads, rows, HD), jnp.bfloat16),
+        scratch_shapes=[
+            pltpu.VMEM((heads, rows, 1), jnp.float32),
+            pltpu.VMEM((heads, rows, 1), jnp.float32),
+            pltpu.VMEM((heads, rows, HD), jnp.float32),
+        ],
+    )(queries, fetched, partner, own, query_at, query_prompt, key_at, key_prompt)
 
 
 def gather_seq(piece, count):
@@ -107,50 +193,26 @@
     partner = lax.ppermute(
         fetched, "mp", [(m, m ^ 1) for m in range(mp_count)]
     )
-    odd = jnp.where(core == 0, fetched, partner)
-    even = jnp.where(core == 0, partner, fetched)
-    offsets = jnp.concatenate(
-        [
-            2 * jnp.arange(half, dtype=jnp.int32) + 1,
-            2 * jnp.arange(half, dtype=jnp.int32) + 2,
-            jnp.zeros((1,), jnp.int32),
-        ]
-    )
-    kv_win = jnp.concatenate(
-        [odd.reshape(-1, 2 * HD), even.reshape(-1, 2 * HD), kv_own], axis=0
-    )
-    key_rows = kv_win[:, :HD]
-    value_rows = kv_win[:, HD:].astype(jnp.float32)
+    fetch_offsets = 2 * jnp.arange(half, dtype=jnp.int32) + 1 + core
+    partner_offsets = 2 * jnp.arange(half, dtype=jnp.int32) + 2 - core
+    offsets = jnp.concatenate([fetch_offsets, partner_offsets, jnp.zeros((1,), jnp.int32)])
     key_index = (
         (seq_index - offsets)[:, None] * tok_rows + jnp.arange(tok_rows, dtype=jnp.int32)[None, :]
-    ).reshape(-1)
-    key_index = jnp.where(
-        jnp.repeat(offsets, tok_rows) <= back, key_index, -1
-    )
-
-    scores = jnp.einsum(
-        "hqd,kd->hqk", queries, key_rows, preferred_element_type=jnp.float32
-    ) * HD ** (-0.5)
+    )
+    key_index = jnp.where((offsets <= back)[:, None], key_index, -1)
     query_prompt, _ = prompt_ids(own_index, lengths)
     key_prompt, _ = prompt_ids(key_index, lengths)
-    spacing = own_index[:, None] - key_index[None, :]
-    allowed = (
-        (query_prompt[:, None] == key_prompt[None, :])
-        & (spacing >= 0)
-        & (spacing < WINDOW)
-        & (key_index[None, :] >= 0)
-    )[None]
-    masked = jnp.where(allowed, scores, -1e30)
-    peak = jnp.max(masked, axis=-1)
-    probs = jnp.where(allowed, jnp.exp(masked - peak[..., None]), 0.0)
-    total = jnp.sum(probs, axis=-1)
-    accum = jnp.einsum("hqk,kd->hqd", probs, value_rows)
-    attended = (
-        (accum / total[..., None])
-        .transpose(1, 0, 2)
-        .reshape(tok_rows, q_cols)
-        .astype(jnp.bfloat16)
-    )
+    mixed = attention(
+        queries,
+        fetched,
+        partner,
+        kv_own,
+        own_index[:, None],
+        query_prompt[:, None],
+        key_index[:, None, :],
+        key_prompt[:, None, :],
+    )
+    attended = mixed.transpose(1, 0, 2).reshape(tok_rows, q_cols)
     partial_out = lax.dot_general(
         attended, wo_rows, (((1,), (1,)), ((), ())), preferred_element_type=jnp.float32
     )

time: 243 us -> 275 us (1.13)
  Pallas kernels: 0 us -> 38.4 us
  matrix products: 31.2 us -> 17.9 us
  other arithmetic: 24.5 us -> 14.3 us
  starting transfers between devices: 66.5 us -> 75.7 us
  blocking collectives: 56.1 us -> 64.4 us
  local copies, waits for them, and re-layouts: 16.6 us -> 12.6 us
  waiting for transfers between devices: 31.9 us -> 34.9 us
    pallas_call x0 -> x1, Pallas kernels: none -> 38.4 us  [attention(): pl.pallas_call(functools.partial(attention_kernel, half), grid=(2 * half...]
    dot_general x2 -> x0, matrix products: 13.4 us -> none  [the longest x1 7 us: local(): accum = jnp.einsum('hqk,kd->hqd', probs, value_rows)]
    ppermute x8, starting transfers between devices: 34 us -> 43.2 us  [local(): fetched.append(lax.ppermute(kv_own, ('seq', 'mp'), pairs))]
    reduce_sum x1 -> x0, other arithmetic: 9.02 us -> none  [local(): total = jnp.sum(probs, axis=-1)]
    all_gather x1, blocking collectives: 22 us -> 28.9 us  [local(): whole = lax.all_gather(hidden_in, 'mp', axis=1, tiled=True)]
    unnamed x27 -> x33, local copies, waits for them, and re-layouts: 6.19 us -> 1.71 us
  transfers between devices with their start and end apart: 15 -> 15, of which waited for: 3 -> 5; matrix products, arithmetic and copies ran while one was open for 21% -> 8% of each run, Pallas kernels for 0% -> 14%
where the time goes in v8:
time: 275 us; the launch traced here: 274 us
  starting transfers between devices  75.7 us (28%)
  blocking collectives  64.4 us (23%)
  Pallas kernels  38.4 us (14%)
  waiting for transfers between devices  34.9 us (13%)
  matrix products  17.9 us (7%)
  between operations  15.3 us (6%)
  other arithmetic  14.3 us (5%)
  local copies, waits for them, and re-layouts  12.6 us (5%)
    ppermute x8, starting transfers between devices, local(): fetched.append(lax.ppermute(kv_own, ('seq', 'mp'), pairs))  43.2 us
    pallas_call x1, Pallas kernels, attention(): pl.pallas_call(functools.partial(attention_kernel, half), grid=(2 * half...  38.4 us
    all_to_all x1, blocking collectives, local(): arrived = lax.all_to_all(buffer, ('seq', 'mp'), 0, 0, tiled=True)  35.6 us
    all_gather x1, blocking collectives, local(): whole = lax.all_gather(hidden_in, 'mp', axis=1, tiled=True)  28.9 us
    all_to_all x1, waiting for transfers between devices, local(): returned = lax.all_to_all(outgoing, ('seq', 'mp'), 0, 0, tiled=True)  22.9 us
    all_to_all x2, starting transfers between devices, gather_seq(): return lax.all_to_all(spread, 'seq', 0, 0, tiled=True)  20.1 us
    all_to_all x1, waiting for transfers between devices, local(): lax.all_to_all(partial_out.astype(jnp.bfloat16), 'mp', 1, 0, tiled=True)  8.19 us
    dot_general x1, matrix products, local(): jnp.dot(active, w_down, preferred_element_type=jnp.float32)  7.21 us
  transfers between devices with their start and end apart: 15, of which 5 were waited for; matrix products, arithmetic and copies ran while one was open for 8% of the time, Pallas kernels for 14%

profile of v8, /device:TPU:1, one launch (start us, length us, event | category | flops | bytes accessed | tf_op | source)
XLA Modules:
  0.0 273.6 jit_solution(7540040486584184237)
XLA Ops:
  6.5 2.9 %pad_maximum_fusion = bf16[3,192,1536]{2,1,0:T(8,128)(2,1)} fusion(bf16[1,192,1536]{2,1,0:T(8,128)(2,1)} %param.19, bf16[1,192,1536]{2,1,0:T(8,128)(2,1)} %param.18, bf16[1,192,1536]{2,1,0:T(8,128)(2,1)} %param.17), kind=kLoop, calls=%fused_computation.21 | loop fusion | flops 1769472 | bytes 3538944 | tf_op jit(solution)/shard_map/concatenate | solution.py:149
  11.6 11.5 %all-to-all-start = ((bf16[32,48,512]{2,1,0:T(8,128)(2,1)}), bf16[32,48,512]{2,1,0:T(8,128)(2,1)S(1)}, u32[]{:S(2)}, u32[]{:S(2)}) async-start(bf16[32,48,512]{2,1,0:T(8,128)(2,1)} %broadcast_in_dim.28), calls=%async_computation | async-start | bytes 3145728 | tf_op jit(solution)/shard_map/all_to_all | solution.py:133
  25.8 28.9 %all_gather.6 = bf16[256,1536]{1,0:T(8,128)(2,1)S(1)} all-gather(bf16[256,384]{1,0:T(8,128)(2,1)S(1)} %copy-done.1), channel_id=1, replica_groups=mesh['seq'=32,'mp'=4] {'mp'}, dimensions={1}, use_global_device_ids=true | all-gather | bytes 983040 | tf_op jit(solution)/shard_map/all_gather | solution.py:157
  57.8 4.8 %collective-permute-start.1 = (bf16[256,256]{1,0:T(8,128)(2,1)S(1)}, bf16[256,256]{1,0:T(8,128)(2,1)S(1)}, u32[]{:S(2)}, u32[]{:S(2)}) collective-permute-start(bf16[256,256]{1,0:T(8,128)(2,1)S(1)} %pad_maximum_fusion.1.own_ref), channel_id=1, source_target_pairs={{0,4},{1,9},{2,6},{3,11},{4,8},{5,13},{6,10},{7,15},{8,12},{9,17},... | collective-permute-start | bytes 393224 | tf_op jit(solution)/shard_map/ppermute | solution.py:191
  65.2 8.6 %all-to-all-start.1 = ((bf16[32,48,384]{2,1,0:T(8,128)(2,1)}), bf16[32,48,384]{2,1,0:T(8,128)(2,1)S(1)}, u32[]{:S(2)}, u32[]{:S(2)}) async-start(bf16[32,48,384]{2,1,0:T(8,128)(2,1)} %broadcast_in_dim.36), calls=%async_computation.1 | async-start | bytes 2359296 | tf_op jit(solution)/shard_map/all_to_all | solution.py:133
  73.8 4.8 %collective-permute-start.2 = (bf16[256,256]{1,0:T(8,128)(2,1)S(1)}, bf16[256,256]{1,0:T(8,128)(2,1)S(1)}, u32[]{:S(2)}, u32[]{:S(2)}) collective-permute-start(bf16[256,256]{1,0:T(8,128)(2,1)S(1)} %pad_maximum_fusion.1.own_ref), channel_id=1, source_target_pairs={{0,12},{1,17},{2,14},{3,19},{4,16},{5,21},{6,18},{7,23},{8,20},{9,... | collective-permute-start | bytes 393224 | tf_op jit(solution)/shard_map/ppermute | solution.py:191
  78.6 5.5 %collective-permute-start.3 = (bf16[256,256]{1,0:T(8,128)(2,1)S(1)}, bf16[256,256]{1,0:T(8,128)(2,1)S(1)}, u32[]{:S(2)}, u32[]{:S(2)}) collective-permute-start(bf16[256,256]{1,0:T(8,128)(2,1)S(1)} %pad_maximum_fusion.1.own_ref), channel_id=1, source_target_pairs={{0,20},{1,25},{2,22},{3,27},{4,24},{5,29},{6,26},{7,31},{8,28},{9,... | collective-permute-start | bytes 393224 | tf_op jit(solution)/shard_map/ppermute | solution.py:191
  84.1 3.1 %collective-permute-start.4 = (bf16[256,256]{1,0:T(8,128)(2,1)S(1)}, bf16[256,256]{1,0:T(8,128)(2,1)S(1)}, u32[]{:S(2)}, u32[]{:S(2)}) collective-permute-start(bf16[256,256]{1,0:T(8,128)(2,1)S(1)} %pad_maximum_fusion.1.own_ref), channel_id=1, source_target_pairs={{0,28},{1,33},{2,30},{3,35},{4,32},{5,37},{6,34},{7,39},{8,36},{9,... | collective-permute-start | bytes 393224 | tf_op jit(solution)/shard_map/ppermute | solution.py:191
  87.2 2.9 %collective-permute-start.5 = (bf16[256,256]{1,0:T(8,128)(2,1)S(1)}, bf16[256,256]{1,0:T(8,128)(2,1)S(1)}, u32[]{:S(2)}, u32[]{:S(2)}) collective-permute-start(bf16[256,256]{1,0:T(8,128)(2,1)S(1)} %pad_maximum_fusion.1.own_ref), channel_id=1, source_target_pairs={{0,36},{1,41},{2,38},{3,43},{4,40},{5,45},{6,42},{7,47},{8,44},{9,... | collective-permute-start | bytes 393224 | tf_op jit(solution)/shard_map/ppermute | solution.py:191
  90.1 4.3 %collective-permute-start.6 = (bf16[256,256]{1,0:T(8,128)(2,1)S(1)}, bf16[256,256]{1,0:T(8,128)(2,1)S(1)}, u32[]{:S(2)}, u32[]{:S(2)}) collective-permute-start(bf16[256,256]{1,0:T(8,128)(2,1)S(1)} %pad_maximum_fusion.1.own_ref), channel_id=1, source_target_pairs={{0,44},{1,49},{2,46},{3,51},{4,48},{5,53},{6,50},{7,55},{8,52},{9,... | collective-permute-start | bytes 393224 | tf_op jit(solution)/shard_map/ppermute | solution.py:191
  95.4 14.8 %collective-permute-start.7 = (bf16[256,256]{1,0:T(8,128)(2,1)S(1)}, bf16[256,256]{1,0:T(8,128)(2,1)S(1)}, u32[]{:S(2)}, u32[]{:S(2)}) collective-permute-start(bf16[256,256]{1,0:T(8,128)(2,1)S(1)} %pad_maximum_fusion.1.own_ref), channel_id=1, source_target_pairs={{0,52},{1,57},{2,54},{3,59},{4,56},{5,61},{6,58},{7,63},{8,60},{9,... | collective-permute-start | bytes 393224 | tf_op jit(solution)/shard_map/ppermute | solution.py:191
  110.2 3.1 %collective-permute-start.8 = (bf16[256,256]{1,0:T(8,128)(2,1)S(1)}, bf16[256,256]{1,0:T(8,128)(2,1)S(1)}, u32[]{:S(2)}, u32[]{:S(2)}) collective-permute-start(bf16[256,256]{1,0:T(8,128)(2,1)S(1)} %pad_maximum_fusion.1.own_ref), channel_id=1, source_target_pairs={{0,60},{1,65},{2,62},{3,67},{4,64},{5,69},{6,66},{7,71},{8,68},{9,... | collective-permute-start | bytes 393224 | tf_op jit(solution)/shard_map/ppermute | solution.py:191
  113.5 1.8 collective-permute-done.8
  115.3 2.9 %collective-permute-start.9 = (bf16[8,256,256]{2,1,0:T(8,128)(2,1)S(1)}, bf16[8,256,256]{2,1,0:T(8,128)(2,1)}, u32[]{:S(2)}, u32[]{:S(2)}) collective-permute-start(bf16[8,256,256]{2,1,0:T(8,128)(2,1)S(1)} %bitcast_dynamic-update-slice_fusion.fetched_ref), channel_id=1, source_target_pairs={{0,1},{1,0},{2,3},{3,2},{4,5},{5,4},{6,7},{7,6},{8,9},{9,8},{10,11... | collective-permute-start | bytes 3145736 | tf_op jit(solution)/shard_map/ppermute | solution.py:193
  123.3 38.4 %shard_map.100 = bf16[3,256,128]{2,1,0:T(8,128)(2,1)} custom-call(bf16[3,256,128]{2,1,0:T(8,128)(2,1)} %maximum_bitcast_fusion.q_ref, bf16[8,256,256]{2,1,0:T(8,128)(2,1)} %copy-done.2, bf16[8,256,256]{2,1,0:T(8,128)(2,1)} %collective-permute-done.9.partner_ref, bf16[256,256]{1,0:T(8,128)(2,1)} %copy-done.5, s32[256,1]{1,0:T(8,128)} %get-tuple-element.28.qi_ref, ...), custom_call_target="tpu_custom_call" | custom-call | tf_op jit(solution)/shard_map/pallas_call | solution.py:103
  164.4 3.7 %all-to-all-start.2 = ((bf16[256,4,384]{2,0,1:T(8,128)(2,1)}), bf16[256,4,384]{2,0,1:T(8,128)(2,1)S(1)}, u32[]{:S(2)}, u32[]{:S(2)}) async-start(bf16[256,4,384]{2,0,1:T(8,128)(2,1)} %bitcast.71), calls=%async_computation.2 | async-start | bytes 1572864 | tf_op jit(solution)/shard_map/all_to_all | solution.py:219
  170.5 8.2 %all-to-all-done.2 = bf16[256,4,384]{2,0,1:T(8,128)(2,1)S(1)} async-done(((bf16[256,4,384]{2,0,1:T(8,128)(2,1)}), bf16[256,4,384]{2,0,1:T(8,128)(2,1)S(1)}, u32[]{:S(2)}, u32[]{:S(2)}) %all-to-all-start.2) | async-done | bytes 786464 | tf_op jit(solution)/shard_map/all_to_all | solution.py:219
  179.5 35.6 %all_to_all.52 = bf16[128,16,384]{2,1,0:T(8,128)(2,1)S(1)} all-to-all(bf16[128,16,384]{2,1,0:T(8,128)(2,1)S(1)} %bitcast.73), channel_id=1, replica_groups=mesh['seq'=32,'mp'=4] {'seq','mp'}, dimensions={0} | all-to-all | bytes 3145728 | tf_op jit(solution)/shard_map/all_to_all | solution.py:245
  216.9 4.3 %fusion.5 = f32[512,768]{1,0:T(8,128)} fusion(bf16[512,1536]{1,0:T(8,128)(2,1)S(1)} %bitcast.78, bf16[3,768,1536]{2,1,0:T(8,128)(2,1)} %all-gather.2.cloned.1.call-done), kind=kOutput, calls=%fused_computation.16 | convolution fusion | flops 1207959552 | bytes 5505024 | tf_op jit(solution)/shard_map/dot_general | solution.py:263
  221.2 7.2 %convolution_convert_fusion = bf16[512,1536]{1,0:T(8,128)(2,1)} fusion(bf16[3,768,1536]{2,1,0:T(8,128)(2,1)} %all-gather.2.cloned.1.call-done, f32[512,768]{1,0:T(8,128)} %fusion.5, bf16[512,1536]{1,0:T(8,128)(2,1)S(1)} %bitcast.79), kind=kOutput, calls=%fused_computation.11 | convolution fusion | flops 2417885184 | bytes 9437184 | tf_op jit(solution)/shard_map/dot_general | solution.py:267
  228.4 3.0 %reshape.383 = bf16[32,16,4,384]{3,2,1,0:T(4,128)(2,1)S(1)} reshape(bf16[512,1536]{1,0:T(8,128)(2,1)} %convolution_convert_fusion) | data formatting | bytes 3145728 | tf_op jit(solution)/shard_map/reshape | solution.py:269
  232.8 5.6 %all-to-all-start.4 = ((bf16[128,16,384]{2,1,0:T(8,128)(2,1)}), bf16[128,16,384]{2,1,0:T(8,128)(2,1)}, u32[]{:S(2)}, u32[]{:S(2)}) async-start(bf16[128,16,384]{2,1,0:T(8,128)(2,1)} %bitcast.27), calls=%async_computation.4 | async-start | bytes 3145728 | tf_op jit(solution)/shard_map/all_to_all | solution.py:273
  239.9 22.9 %all-to-all-done.4 = bf16[128,16,384]{2,1,0:T(8,128)(2,1)} async-done(((bf16[128,16,384]{2,1,0:T(8,128)(2,1)}), bf16[128,16,384]{2,1,0:T(8,128)(2,1)}, u32[]{:S(2)}, u32[]{:S(2)}) %all-to-all-start.4) | async-done | bytes 1572896 | tf_op jit(solution)/shard_map/all_to_all | solution.py:273
  262.8 3.9 %fusion.10 = bf16[256,384]{1,0:T(8,128)(2,1)} fusion(f32[256,2048]{1,0:T(8,128)S(1)} %select_reduce_fusion, bf16[2048,384]{1,0:T(8,128)(2,1)} %bitcast.28, f32[256,384]{1,0:T(8,128)S(1)} %convert_reduce_fusion, bf16[256,384]{1,0:T(8,128)(2,1)S(1)} %copy-done.1), kind=kOutput, calls=%fused_computation.28 | convolution fusion | flops 2416508928 | bytes 4456448 | tf_op jit(solution)/shard_map/dot_general | solution.py:282
  (95 shorter events, 25.7 us)
Async XLA Ops:
  6.5 3.0 %copy-start = (bf16[48,512]{1,0:T(8,128)(2,1)S(1)}, bf16[48,512]{1,0:T(8,128)(2,1)}, u32[]{:S(2)}) copy-start(bf16[48,512]{1,0:T(8,128)(2,1)} %param.12) | copy-start | bytes 147460
  6.5 210.3 %all-gather.2.cloned.1.call-start = ((), (), s32[]{:S(2)}) async-start(), calls=%async_computation.5 | async-start | bytes 8847360 | tf_op jit(solution)/shard_map/all_gather | solution.py:148
  11.6 11.5 %copy-start.10 = (s32[3]{0:T(128)S(1)}, s32[3]{0:T(128)}, u32[]{:S(2)}) copy-start(s32[3]{0:T(128)} %param.14) | copy-start | bytes 40
  11.6 14.2 %copy-start.1 = (bf16[256,384]{1,0:T(8,128)(2,1)S(1)}, bf16[256,384]{1,0:T(8,128)(2,1)}, u32[]{:S(2)}) copy-start(bf16[256,384]{1,0:T(8,128)(2,1)} %param.10) | copy-start | bytes 589828
  11.6 43.3 %all-to-all-start = ((bf16[32,48,512]{2,1,0:T(8,128)(2,1)}), bf16[32,48,512]{2,1,0:T(8,128)(2,1)S(1)}, u32[]{:S(2)}, u32[]{:S(2)}) async-start(bf16[32,48,512]{2,1,0:T(8,128)(2,1)} %broadcast_in_dim.28), calls=%async_computation | async-start | bytes 3145728 | tf_op jit(solution)/shard_map/all_to_all | solution.py:133
  55.5 8.5 %copy-start.6 = (bf16[384,48]{0,1:T(8,128)(2,1)S(1)}, bf16[384,48]{0,1:T(8,128)(2,1)}, u32[]{:S(2)}) copy-start(bf16[384,48]{0,1:T(8,128)(2,1)} %param.13) | copy-start | bytes 110596
  56.4 1.3 collective-permute-start
  57.8 52.4 %copy-start.5 = (bf16[256,256]{1,0:T(8,128)(2,1)}, bf16[256,256]{1,0:T(8,128)(2,1)S(1)}, u32[]{:S(2)}) copy-start(bf16[256,256]{1,0:T(8,128)(2,1)S(1)} %pad_maximum_fusion.1.own_ref) | copy-start | bytes 393220
  57.8 32.2 %collective-permute-start.1 = (bf16[256,256]{1,0:T(8,128)(2,1)S(1)}, bf16[256,256]{1,0:T(8,128)(2,1)S(1)}, u32[]{:S(2)}, u32[]{:S(2)}) collective-permute-start(bf16[256,256]{1,0:T(8,128)(2,1)S(1)} %pad_maximum_fusion.1.own_ref), channel_id=1, source_target_pairs={{0,4},{1,9},{2,6},{3,11},{4,8},{5,13},{6,10},{7,15},{8,12},{9,17},... | collective-permute-start | bytes 393224 | tf_op jit(solution)/shard_map/ppermute | solution.py:191
  65.2 97.6 %all-to-all-start.1 = ((bf16[32,48,384]{2,1,0:T(8,128)(2,1)}), bf16[32,48,384]{2,1,0:T(8,128)(2,1)S(1)}, u32[]{:S(2)}, u32[]{:S(2)}) async-start(bf16[32,48,384]{2,1,0:T(8,128)(2,1)} %broadcast_in_dim.36), calls=%async_computation.1 | async-start | bytes 2359296 | tf_op jit(solution)/shard_map/all_to_all | solution.py:133
  73.8 47.1 %copy-start.4 = (f32[256,512]{1,0:T(8,128)S(1)}, f32[256,512]{1,0:T(8,128)}, u32[]{:S(2)}) copy-start(f32[256,512]{1,0:T(8,128)} %copy-done.3) | copy-start | bytes 1572868
  73.8 21.6 %collective-permute-start.2 = (bf16[256,256]{1,0:T(8,128)(2,1)S(1)}, bf16[256,256]{1,0:T(8,128)(2,1)S(1)}, u32[]{:S(2)}, u32[]{:S(2)}) collective-permute-start(bf16[256,256]{1,0:T(8,128)(2,1)S(1)} %pad_maximum_fusion.1.own_ref), channel_id=1, source_target_pairs={{0,12},{1,17},{2,14},{3,19},{4,16},{5,21},{6,18},{7,23},{8,20},{9,... | collective-permute-start | bytes 393224 | tf_op jit(solution)/shard_map/ppermute | solution.py:191
  78.6 31.6 %collective-permute-start.3 = (bf16[256,256]{1,0:T(8,128)(2,1)S(1)}, bf16[256,256]{1,0:T(8,128)(2,1)S(1)}, u32[]{:S(2)}, u32[]{:S(2)}) collective-permute-start(bf16[256,256]{1,0:T(8,128)(2,1)S(1)} %pad_maximum_fusion.1.own_ref), channel_id=1, source_target_pairs={{0,20},{1,25},{2,22},{3,27},{4,24},{5,29},{6,26},{7,31},{8,28},{9,... | collective-permute-start | bytes 393224 | tf_op jit(solution)/shard_map/ppermute | solution.py:191
  84.1 29.3 %collective-permute-start.4 = (bf16[256,256]{1,0:T(8,128)(2,1)S(1)}, bf16[256,256]{1,0:T(8,128)(2,1)S(1)}, u32[]{:S(2)}, u32[]{:S(2)}) collective-permute-start(bf16[256,256]{1,0:T(8,128)(2,1)S(1)} %pad_maximum_fusion.1.own_ref), channel_id=1, source_target_pairs={{0,28},{1,33},{2,30},{3,35},{4,32},{5,37},{6,34},{7,39},{8,36},{9,... | collective-permute-start | bytes 393224 | tf_op jit(solution)/shard_map/ppermute | solution.py:191
  87.2 26.2 %collective-permute-start.5 = (bf16[256,256]{1,0:T(8,128)(2,1)S(1)}, bf16[256,256]{1,0:T(8,128)(2,1)S(1)}, u32[]{:S(2)}, u32[]{:S(2)}) collective-permute-start(bf16[256,256]{1,0:T(8,128)(2,1)S(1)} %pad_maximum_fusion.1.own_ref), channel_id=1, source_target_pairs={{0,36},{1,41},{2,38},{3,43},{4,40},{5,45},{6,42},{7,47},{8,44},{9,... | collective-permute-start | bytes 393224 | tf_op jit(solution)/shard_map/ppermute | solution.py:191
  90.1 23.3 %collective-permute-start.6 = (bf16[256,256]{1,0:T(8,128)(2,1)S(1)}, bf16[256,256]{1,0:T(8,128)(2,1)S(1)}, u32[]{:S(2)}, u32[]{:S(2)}) collective-permute-start(bf16[256,256]{1,0:T(8,128)(2,1)S(1)} %pad_maximum_fusion.1.own_ref), channel_id=1, source_target_pairs={{0,44},{1,49},{2,46},{3,51},{4,48},{5,53},{6,50},{7,55},{8,52},{9,... | collective-permute-start | bytes 393224 | tf_op jit(solution)/shard_map/ppermute | solution.py:191
  95.4 18.1 %collective-permute-start.7 = (bf16[256,256]{1,0:T(8,128)(2,1)S(1)}, bf16[256,256]{1,0:T(8,128)(2,1)S(1)}, u32[]{:S(2)}, u32[]{:S(2)}) collective-permute-start(bf16[256,256]{1,0:T(8,128)(2,1)S(1)} %pad_maximum_fusion.1.own_ref), channel_id=1, source_target_pairs={{0,52},{1,57},{2,54},{3,59},{4,56},{5,61},{6,58},{7,63},{8,60},{9,... | collective-permute-start | bytes 393224 | tf_op jit(solution)/shard_map/ppermute | solution.py:191
  110.2 5.0 %collective-permute-start.8 = (bf16[256,256]{1,0:T(8,128)(2,1)S(1)}, bf16[256,256]{1,0:T(8,128)(2,1)S(1)}, u32[]{:S(2)}, u32[]{:S(2)}) collective-permute-start(bf16[256,256]{1,0:T(8,128)(2,1)S(1)} %pad_maximum_fusion.1.own_ref), channel_id=1, source_target_pairs={{0,60},{1,65},{2,62},{3,67},{4,64},{5,69},{6,66},{7,71},{8,68},{9,... | collective-permute-start | bytes 393224 | tf_op jit(solution)/shard_map/ppermute | solution.py:191
  115.3 6.0 %copy-start.2 = (bf16[8,256,256]{2,1,0:T(8,128)(2,1)}, bf16[8,256,256]{2,1,0:T(8,128)(2,1)S(1)}, u32[]{:S(2)}) copy-start(bf16[8,256,256]{2,1,0:T(8,128)(2,1)S(1)} %bitcast_dynamic-update-slice_fusion.fetched_ref) | copy-start | bytes 3145732
  115.3 8.0 %collective-permute-start.9 = (bf16[8,256,256]{2,1,0:T(8,128)(2,1)S(1)}, bf16[8,256,256]{2,1,0:T(8,128)(2,1)}, u32[]{:S(2)}, u32[]{:S(2)}) collective-permute-start(bf16[8,256,256]{2,1,0:T(8,128)(2,1)S(1)} %bitcast_dynamic-update-slice_fusion.fetched_ref), channel_id=1, source_target_pairs={{0,1},{1,0},{2,3},{3,2},{4,5},{5,4},{6,7},{7,6},{8,9},{9,8},{10,11... | collective-permute-start | bytes 3145736 | tf_op jit(solution)/shard_map/ppermute | solution.py:193
  163.4 4.7 %copy-start.9 = (s32[256,4]{0,1:T(4,128)S(1)}, s32[256,4]{0,1:T(4,128)}, u32[]{:S(2)}) copy-start(s32[256,4]{0,1:T(4,128)} %param.15) | copy-start | bytes 12292
  164.4 14.3 %all-to-all-start.2 = ((bf16[256,4,384]{2,0,1:T(8,128)(2,1)}), bf16[256,4,384]{2,0,1:T(8,128)(2,1)S(1)}, u32[]{:S(2)}, u32[]{:S(2)}) async-start(bf16[256,4,384]{2,0,1:T(8,128)(2,1)} %bitcast.71), calls=%async_computation.2 | async-start | bytes 1572864 | tf_op jit(solution)/shard_map/all_to_all | solution.py:219
  232.8 5.6 %copy-start.8 = (f32[256,4]{0,1:T(4,128)S(1)}, f32[256,4]{0,1:T(4,128)}, u32[]{:S(2)}) copy-start(f32[256,4]{0,1:T(4,128)} %param.16) | copy-start | bytes 12292
  232.8 30.0 %all-to-all-start.4 = ((bf16[128,16,384]{2,1,0:T(8,128)(2,1)}), bf16[128,16,384]{2,1,0:T(8,128)(2,1)}, u32[]{:S(2)}, u32[]{:S(2)}) async-start(bf16[128,16,384]{2,1,0:T(8,128)(2,1)} %bitcast.27), calls=%async_computation.4 | async-start | bytes 3145728 | tf_op jit(solution)/shard_map/all_to_all | solution.py:273
  (2 other events, 1.6 us)
Sparse Core Ops, SparseCore 0:
  9.6 111.3 all-gather.1

commit v9 on v8

--- a/solution.py
+++ b/solution.py
@@ -43,53 +43,54 @@
 
 
 def attention_kernel(
-    half, q_ref, fetched_ref, partner_ref, own_ref, qi_ref, qp_ref, ki_ref, kp_ref, o_ref, m_sc, l_sc,
-    acc_sc
+    pairs, heads, q_ref, fetched_ref, partner_ref, own_ref, qi_ref, qp_ref, ki_ref, kp_ref, o_ref,
+    m_sc, l_sc, acc_sc
 ):
     step = pl.program_id(0)
 
     @pl.when(step == 0)
     def _():
-        m_sc[...] = jnp.full(m_sc.shape, -1e30, jnp.float32)
+        m_sc[...] = jnp.full(m_sc.shape, -1e29, jnp.float32)
         l_sc[...] = jnp.zeros(l_sc.shape, jnp.float32)
         acc_sc[...] = jnp.zeros(acc_sc.shape, jnp.float32)
 
-    heads, rows, _ = q_ref.shape
+    rows = qi_ref.shape[0]
     key_at = ki_ref[0]
     spacing = qi_ref[...] - key_at
     allowed = (qp_ref[...] == kp_ref[0]) & (spacing >= 0) & (spacing < WINDOW) & (key_at >= 0)
 
-    def update(block):
+    def update(block, allowed):
         keys = block[:, :HD]
         values = block[:, HD:]
         scores = lax.dot_general(
-            q_ref[...].reshape(heads * rows, HD), keys, (((1,), (1,)), ((), ())),
-            preferred_element_type=jnp.float32,
-        ).reshape(heads, rows, -1) * HD ** (-0.5)
-        masked = jnp.where(allowed[None], scores, -1e30)
+            q_ref[...], keys, (((1,), (1,)), ((), ())), preferred_element_type=jnp.float32
+        ) * HD ** (-0.5)
+        masked = jnp.concatenate(
+            [jnp.where(allowed, scores[h * rows : (h + 1) * rows], -1e30) for h in range(heads)],
+            axis=0,
+        )
         m_old = m_sc[...]
-        m_new = jnp.maximum(m_old, jnp.max(masked, axis=2, keepdims=True))
+        m_new = jnp.maximum(m_old, jnp.max(masked, axis=1, keepdims=True))
         alpha = jnp.exp(m_old - m_new)
-        probs = jnp.where(allowed[None], jnp.exp(masked - m_new), 0.0)
-        l_sc[...] = alpha * l_sc[...] + jnp.sum(probs, axis=2, keepdims=True)
-        mixed = jnp.dot(
-            probs.reshape(heads * rows, -1).astype(jnp.bfloat16), values,
-            preferred_element_type=jnp.float32,
-        ).reshape(heads, rows, HD)
+        probs = jnp.exp(masked - m_new)
+        l_sc[...] = alpha * l_sc[...] + jnp.sum(probs, axis=1, keepdims=True)
+        mixed = jnp.dot(probs.astype(jnp.bfloat16), values, preferred_element_type=jnp.float32)
         acc_sc[...] = alpha * acc_sc[...] + mixed
         m_sc[...] = m_new
 
-    @pl.when(step < half)
-    def _():
-        update(fetched_ref[0])
-
-    @pl.when((step >= half) & (step < 2 * half))
-    def _():
-        update(partner_ref[0])
-
-    @pl.when(step == 2 * half)
-    def _():
-        update(own_ref[...])
+    width = fetched_ref.shape[2]
+
+    @pl.when(step < pairs)
+    def _():
+        update(fetched_ref[...].reshape(-1, width), allowed)
+
+    @pl.when((step >= pairs) & (step < 2 * pairs))
+    def _():
+        update(partner_ref[...].reshape(-1, width), allowed)
+
+    @pl.when(step == 2 * pairs)
+    def _():
+        update(own_ref[...], allowed[:, : own_ref.shape[0]])
 
     @pl.when(step == pl.num_programs(0) - 1)
     def _():
@@ -99,30 +100,34 @@
 def attention(queries, fetched, partner, own, query_at, query_prompt, key_at, key_prompt):
     heads, rows, _ = queries.shape
     half, block, width = fetched.shape
-    last = half - 1
+    pairs = half // 2
+    last = pairs - 1
     return pl.pallas_call(
-        functools.partial(attention_kernel, half),
-        grid=(2 * half + 1,),
+        functools.partial(attention_kernel, pairs, heads),
+        grid=(2 * pairs + 1,),
         in_specs=[
-            pl.BlockSpec((heads, rows, HD), lambda j: (0, 0, 0)),
-            pl.BlockSpec((1, block, width), lambda j: (jnp.minimum(j, last), 0, 0)),
+            pl.BlockSpec((heads * rows, HD), lambda j: (0, 0)),
+            pl.BlockSpec((2, block, width), lambda j: (jnp.minimum(j, last), 0, 0)),
             pl.BlockSpec(
-                (1, block, width), lambda j: (jnp.minimum(jnp.maximum(j - half, 0), last), 0, 0)
+                (2, block, width), lambda j: (jnp.minimum(jnp.maximum(j - pairs, 0), last), 0, 0)
             ),
             pl.BlockSpec((block, width), lambda j: (0, 0)),
             pl.BlockSpec((rows, 1), lambda j: (0, 0)),
             pl.BlockSpec((rows, 1), lambda j: (0, 0)),
-            pl.BlockSpec((1, 1, block), lambda j: (j, 0, 0)),
-            pl.BlockSpec((1, 1, block), lambda j: (j, 0, 0)),
+            pl.BlockSpec((1, 1, 2 * block), lambda j: (j, 0, 0)),
+            pl.BlockSpec((1, 1, 2 * block), lambda j: (j, 0, 0)),
         ],
-        out_specs=pl.BlockSpec((heads, rows, HD), lambda j: (0, 0, 0)),
-        out_shape=jax.ShapeDtypeStruct((heads, rows, HD), jnp.bfloat16),
+        out_specs=pl.BlockSpec((heads * rows, HD), lambda j: (0, 0)),
+        out_shape=jax.ShapeDtypeStruct((heads * rows, HD), jnp.bfloat16),
         scratch_shapes=[
-            pltpu.VMEM((heads, rows, 1), jnp.float32),
-            pltpu.VMEM((heads, rows, 1), jnp.float32),
-            pltpu.VMEM((heads, rows, HD), jnp.float32),
+            pltpu.VMEM((heads * rows, 1), jnp.float32),
+            pltpu.VMEM((heads * rows, 1), jnp.float32),
+            pltpu.VMEM((heads * rows, HD), jnp.float32),
         ],
-    )(queries, fetched, partner, own, query_at, query_prompt, key_at, key_prompt)
+    )(
+        queries.reshape(heads * rows, HD), fetched, partner, own, query_at, query_prompt, key_at,
+        key_prompt,
+    ).reshape(heads, rows, HD)
 
 
 def gather_seq(piece, count):
@@ -200,6 +205,9 @@
         (seq_index - offsets)[:, None] * tok_rows + jnp.arange(tok_rows, dtype=jnp.int32)[None, :]
     )
     key_index = jnp.where((offsets <= back)[:, None], key_index, -1)
+    key_index = jnp.concatenate(
+        [key_index, jnp.full((1, tok_rows), -1, jnp.int32)], axis=0
+    ).reshape(half + 1, 1, 2 * tok_rows)
     query_prompt, _ = prompt_ids(own_index, lengths)
     key_prompt, _ = prompt_ids(key_index, lengths)
     mixed = attention(
@@ -209,8 +217,8 @@
         kv_own,
         own_index[:, None],
         query_prompt[:, None],
-        key_index[:, None, :],
-        key_prompt[:, None, :],
+        key_index,
+        key_prompt,
     )
     attended = mixed.transpose(1, 0, 2).reshape(tok_rows, q_cols)
     partial_out = lax.dot_general(

time: 275 us -> 258 us (0.938)
  Pallas kernels: 38.4 us -> 23 us
  other arithmetic: 14.3 us -> 11.1 us
    pallas_call x1, Pallas kernels: 38.4 us -> 23 us  [attention(): pl.pallas_call(functools.partial(attention_kernel, pairs, heads), grid=(2...]
  transfers between devices with their start and end apart: 15 -> 15, of which waited for: 5 -> 5; matrix products, arithmetic and copies ran while one was open for 8% -> 8% of each run, Pallas kernels for 14% -> 9%
where the time goes in v9:
time: 258 us; the launch traced here: 257 us
  starting transfers between devices  75.6 us (29%)
  blocking collectives  64.7 us (25%)
  waiting for transfers between devices  35 us (14%)
  Pallas kernels  23 us (9%)
  matrix products  17.9 us (7%)
  between operations  15.2 us (6%)
  local copies, waits for them, and re-layouts  14.1 us (5%)
  other arithmetic  11.1 us (4%)
    ppermute x8, starting transfers between devices, local(): fetched.append(lax.ppermute(kv_own, ('seq', 'mp'), pairs))  43.1 us
    all_to_all x1, blocking collectives, local(): arrived = lax.all_to_all(buffer, ('seq', 'mp'), 0, 0, tiled=True)  35.6 us
    all_gather x1, blocking collectives, local(): whole = lax.all_gather(hidden_in, 'mp', axis=1, tiled=True)  29.1 us
    pallas_call x1, Pallas kernels, attention(): pl.pallas_call(functools.partial(attention_kernel, pairs, heads), grid=(2...  23 us
    all_to_all x1, waiting for transfers between devices, local(): returned = lax.all_to_all(outgoing, ('seq', 'mp'), 0, 0, tiled=True)  22.9 us
    all_to_all x2, starting transfers between devices, gather_seq(): return lax.all_to_all(spread, 'seq', 0, 0, tiled=True)  20.1 us
    all_to_all x1, waiting for transfers between devices, local(): lax.all_to_all(partial_out.astype(jnp.bfloat16), 'mp', 1, 0, tiled=True)  8.19 us
    dot_general x1, matrix products, local(): jnp.dot(active, w_down, preferred_element_type=jnp.float32)  7.23 us
  transfers between devices with their start and end apart: 15, of which 5 were waited for; matrix products, arithmetic and copies ran while one was open for 8% of the time, Pallas kernels for 9%

profile of v9, /device:TPU:1, one launch (start us, length us, event | category | flops | bytes accessed | tf_op | source)
XLA Modules:
  0.0 256.6 jit_solution(14474545710674137451)
XLA Ops:
  6.5 2.9 %pad_maximum_fusion = bf16[3,192,1536]{2,1,0:T(8,128)(2,1)} fusion(bf16[1,192,1536]{2,1,0:T(8,128)(2,1)} %param.19, bf16[1,192,1536]{2,1,0:T(8,128)(2,1)} %param.18, bf16[1,192,1536]{2,1,0:T(8,128)(2,1)} %param.17), kind=kLoop, calls=%fused_computation.21 | loop fusion | flops 1769472 | bytes 3538944 | tf_op jit(solution)/shard_map/concatenate | solution.py:154
  11.6 11.5 %all-to-all-start = ((bf16[32,48,512]{2,1,0:T(8,128)(2,1)}), bf16[32,48,512]{2,1,0:T(8,128)(2,1)S(1)}, u32[]{:S(2)}, u32[]{:S(2)}) async-start(bf16[32,48,512]{2,1,0:T(8,128)(2,1)} %broadcast_in_dim.28), calls=%async_computation | async-start | bytes 3145728 | tf_op jit(solution)/shard_map/all_to_all | solution.py:138
  25.5 29.1 %all_gather.6 = bf16[256,1536]{1,0:T(8,128)(2,1)S(1)} all-gather(bf16[256,384]{1,0:T(8,128)(2,1)S(1)} %copy-done.1), channel_id=1, replica_groups=mesh['seq'=32,'mp'=4] {'mp'}, dimensions={1}, use_global_device_ids=true | all-gather | bytes 983040 | tf_op jit(solution)/shard_map/all_gather | solution.py:162
  57.8 4.8 %collective-permute-start.1 = (bf16[256,256]{1,0:T(8,128)(2,1)S(1)}, bf16[256,256]{1,0:T(8,128)(2,1)S(1)}, u32[]{:S(2)}, u32[]{:S(2)}) collective-permute-start(bf16[256,256]{1,0:T(8,128)(2,1)S(1)} %pad_maximum_fusion.1.own_ref), channel_id=1, source_target_pairs={{0,4},{1,9},{2,6},{3,11},{4,8},{5,13},{6,10},{7,15},{8,12},{9,17},... | collective-permute-start | bytes 393224 | tf_op jit(solution)/shard_map/ppermute | solution.py:196
  63.7 8.6 %all-to-all-start.1 = ((bf16[32,48,384]{2,1,0:T(8,128)(2,1)}), bf16[32,48,384]{2,1,0:T(8,128)(2,1)S(1)}, u32[]{:S(2)}, u32[]{:S(2)}) async-start(bf16[32,48,384]{2,1,0:T(8,128)(2,1)} %broadcast_in_dim.36), calls=%async_computation.1 | async-start | bytes 2359296 | tf_op jit(solution)/shard_map/all_to_all | solution.py:138
  72.4 4.6 %collective-permute-start.2 = (bf16[256,256]{1,0:T(8,128)(2,1)S(1)}, bf16[256,256]{1,0:T(8,128)(2,1)S(1)}, u32[]{:S(2)}, u32[]{:S(2)}) collective-permute-start(bf16[256,256]{1,0:T(8,128)(2,1)S(1)} %pad_maximum_fusion.1.own_ref), channel_id=1, source_target_pairs={{0,12},{1,17},{2,14},{3,19},{4,16},{5,21},{6,18},{7,23},{8,20},{9,... | collective-permute-start | bytes 393224 | tf_op jit(solution)/shard_map/ppermute | solution.py:196
  77.0 5.5 %collective-permute-start.3 = (bf16[256,256]{1,0:T(8,128)(2,1)S(1)}, bf16[256,256]{1,0:T(8,128)(2,1)S(1)}, u32[]{:S(2)}, u32[]{:S(2)}) collective-permute-start(bf16[256,256]{1,0:T(8,128)(2,1)S(1)} %pad_maximum_fusion.1.own_ref), channel_id=1, source_target_pairs={{0,20},{1,25},{2,22},{3,27},{4,24},{5,29},{6,26},{7,31},{8,28},{9,... | collective-permute-start | bytes 393224 | tf_op jit(solution)/shard_map/ppermute | solution.py:196
  82.5 3.1 %collective-permute-start.4 = (bf16[256,256]{1,0:T(8,128)(2,1)S(1)}, bf16[256,256]{1,0:T(8,128)(2,1)S(1)}, u32[]{:S(2)}, u32[]{:S(2)}) collective-permute-start(bf16[256,256]{1,0:T(8,128)(2,1)S(1)} %pad_maximum_fusion.1.own_ref), channel_id=1, source_target_pairs={{0,28},{1,33},{2,30},{3,35},{4,32},{5,37},{6,34},{7,39},{8,36},{9,... | collective-permute-start | bytes 393224 | tf_op jit(solution)/shard_map/ppermute | solution.py:196
  85.6 2.9 %collective-permute-start.5 = (bf16[256,256]{1,0:T(8,128)(2,1)S(1)}, bf16[256,256]{1,0:T(8,128)(2,1)S(1)}, u32[]{:S(2)}, u32[]{:S(2)}) collective-permute-start(bf16[256,256]{1,0:T(8,128)(2,1)S(1)} %pad_maximum_fusion.1.own_ref), channel_id=1, source_target_pairs={{0,36},{1,41},{2,38},{3,43},{4,40},{5,45},{6,42},{7,47},{8,44},{9,... | collective-permute-start | bytes 393224 | tf_op jit(solution)/shard_map/ppermute | solution.py:196
  88.5 4.3 %collective-permute-start.6 = (bf16[256,256]{1,0:T(8,128)(2,1)S(1)}, bf16[256,256]{1,0:T(8,128)(2,1)S(1)}, u32[]{:S(2)}, u32[]{:S(2)}) collective-permute-start(bf16[256,256]{1,0:T(8,128)(2,1)S(1)} %pad_maximum_fusion.1.own_ref), channel_id=1, source_target_pairs={{0,44},{1,49},{2,46},{3,51},{4,48},{5,53},{6,50},{7,55},{8,52},{9,... | collective-permute-start | bytes 393224 | tf_op jit(solution)/shard_map/ppermute | solution.py:196
  93.9 14.8 %collective-permute-start.7 = (bf16[256,256]{1,0:T(8,128)(2,1)S(1)}, bf16[256,256]{1,0:T(8,128)(2,1)S(1)}, u32[]{:S(2)}, u32[]{:S(2)}) collective-permute-start(bf16[256,256]{1,0:T(8,128)(2,1)S(1)} %pad_maximum_fusion.1.own_ref), channel_id=1, source_target_pairs={{0,52},{1,57},{2,54},{3,59},{4,56},{5,61},{6,58},{7,63},{8,60},{9,... | collective-permute-start | bytes 393224 | tf_op jit(solution)/shard_map/ppermute | solution.py:196
  108.8 3.1 %collective-permute-start.8 = (bf16[256,256]{1,0:T(8,128)(2,1)S(1)}, bf16[256,256]{1,0:T(8,128)(2,1)S(1)}, u32[]{:S(2)}, u32[]{:S(2)}) collective-permute-start(bf16[256,256]{1,0:T(8,128)(2,1)S(1)} %pad_maximum_fusion.1.own_ref), channel_id=1, source_target_pairs={{0,60},{1,65},{2,62},{3,67},{4,64},{5,69},{6,66},{7,71},{8,68},{9,... | collective-permute-start | bytes 393224 | tf_op jit(solution)/shard_map/ppermute | solution.py:196
  112.0 1.8 collective-permute-done.8
  113.9 2.9 %collective-permute-start.9 = (bf16[8,256,256]{2,1,0:T(8,128)(2,1)S(1)}, bf16[8,256,256]{2,1,0:T(8,128)(2,1)}, u32[]{:S(2)}, u32[]{:S(2)}) collective-permute-start(bf16[8,256,256]{2,1,0:T(8,128)(2,1)S(1)} %bitcast_dynamic-update-slice_fusion.fetched_ref), channel_id=1, source_target_pairs={{0,1},{1,0},{2,3},{3,2},{4,5},{5,4},{6,7},{7,6},{8,9},{9,8},{10,11... | collective-permute-start | bytes 3145736 | tf_op jit(solution)/shard_map/ppermute | solution.py:198
  121.8 23.0 %shard_map.100 = bf16[768,128]{1,0:T(8,128)(2,1)} custom-call(bf16[768,128]{1,0:T(8,128)(2,1)} %bitcast.84, bf16[8,256,256]{2,1,0:T(8,128)(2,1)} %copy-done.2, bf16[8,256,256]{2,1,0:T(8,128)(2,1)} %collective-permute-done.9.partner_ref, bf16[256,256]{1,0:T(8,128)(2,1)} %copy-done.4, s32[256,1]{1,0:T(8,128)} %get-tuple-element.24.qi_ref, ...), custom_call_target="tpu_custom_call" | custom-call | tf_op jit(solution)/shard_map/pallas_call | solution.py:105
  147.5 3.7 %all-to-all-start.2 = ((bf16[256,4,384]{2,0,1:T(8,128)(2,1)}), bf16[256,4,384]{2,0,1:T(8,128)(2,1)S(1)}, u32[]{:S(2)}, u32[]{:S(2)}) async-start(bf16[256,4,384]{2,0,1:T(8,128)(2,1)} %bitcast.74), calls=%async_computation.2 | async-start | bytes 1572864 | tf_op jit(solution)/shard_map/all_to_all | solution.py:227
  153.5 8.2 %all-to-all-done.2 = bf16[256,4,384]{2,0,1:T(8,128)(2,1)S(1)} async-done(((bf16[256,4,384]{2,0,1:T(8,128)(2,1)}), bf16[256,4,384]{2,0,1:T(8,128)(2,1)S(1)}, u32[]{:S(2)}, u32[]{:S(2)}) %all-to-all-start.2) | async-done | bytes 786464 | tf_op jit(solution)/shard_map/all_to_all | solution.py:227
  162.6 35.6 %all_to_all.52 = bf16[128,16,384]{2,1,0:T(8,128)(2,1)S(1)} all-to-all(bf16[128,16,384]{2,1,0:T(8,128)(2,1)S(1)} %bitcast.76), channel_id=1, replica_groups=mesh['seq'=32,'mp'=4] {'seq','mp'}, dimensions={0} | all-to-all | bytes 3145728 | tf_op jit(solution)/shard_map/all_to_all | solution.py:253
  199.9 4.3 %fusion.5 = f32[512,768]{1,0:T(8,128)} fusion(bf16[512,1536]{1,0:T(8,128)(2,1)S(1)} %bitcast.81, bf16[3,768,1536]{2,1,0:T(8,128)(2,1)} %all-gather.2.cloned.1.call-done), kind=kOutput, calls=%fused_computation.16 | convolution fusion | flops 1207959552 | bytes 5505024 | tf_op jit(solution)/shard_map/dot_general | solution.py:271
  204.3 7.2 %convolution_convert_fusion = bf16[512,1536]{1,0:T(8,128)(2,1)} fusion(bf16[3,768,1536]{2,1,0:T(8,128)(2,1)} %all-gather.2.cloned.1.call-done, f32[512,768]{1,0:T(8,128)} %fusion.5, bf16[512,1536]{1,0:T(8,128)(2,1)S(1)} %bitcast.82), kind=kOutput, calls=%fused_computation.11 | convolution fusion | flops 2417885184 | bytes 9437184 | tf_op jit(solution)/shard_map/dot_general | solution.py:275
  211.5 3.0 %reshape.329 = bf16[32,16,4,384]{3,2,1,0:T(4,128)(2,1)S(1)} reshape(bf16[512,1536]{1,0:T(8,128)(2,1)} %convolution_convert_fusion) | data formatting | bytes 3145728 | tf_op jit(solution)/shard_map/reshape | solution.py:277
  215.9 5.6 %all-to-all-start.4 = ((bf16[128,16,384]{2,1,0:T(8,128)(2,1)}), bf16[128,16,384]{2,1,0:T(8,128)(2,1)}, u32[]{:S(2)}, u32[]{:S(2)}) async-start(bf16[128,16,384]{2,1,0:T(8,128)(2,1)} %bitcast.29), calls=%async_computation.4 | async-start | bytes 3145728 | tf_op jit(solution)/shard_map/all_to_all | solution.py:281
  223.0 22.9 %all-to-all-done.4 = bf16[128,16,384]{2,1,0:T(8,128)(2,1)} async-done(((bf16[128,16,384]{2,1,0:T(8,128)(2,1)}), bf16[128,16,384]{2,1,0:T(8,128)(2,1)}, u32[]{:S(2)}, u32[]{:S(2)}) %all-to-all-start.4) | async-done | bytes 1572896 | tf_op jit(solution)/shard_map/all_to_all | solution.py:281
  245.9 3.9 %fusion.10 = bf16[256,384]{1,0:T(8,128)(2,1)} fusion(f32[256,2048]{1,0:T(8,128)S(1)} %select_reduce_fusion, bf16[2048,384]{1,0:T(8,128)(2,1)} %bitcast.30, f32[256,384]{1,0:T(8,128)S(1)} %convert_reduce_fusion, bf16[256,384]{1,0:T(8,128)(2,1)S(1)} %copy-done.1), kind=kOutput, calls=%fused_computation.28 | convolution fusion | flops 2416508928 | bytes 4456448 | tf_op jit(solution)/shard_map/dot_general | solution.py:290
  (96 shorter events, 24.1 us)
Async XLA Ops:
  6.5 3.0 %copy-start = (bf16[48,512]{1,0:T(8,128)(2,1)S(1)}, bf16[48,512]{1,0:T(8,128)(2,1)}, u32[]{:S(2)}) copy-start(bf16[48,512]{1,0:T(8,128)(2,1)} %param.12) | copy-start | bytes 147460
  6.5 193.4 %all-gather.2.cloned.1.call-start = ((), (), s32[]{:S(2)}) async-start(), calls=%async_computation.5 | async-start | bytes 8847360 | tf_op jit(solution)/shard_map/all_gather | solution.py:153
  11.6 11.5 %copy-start.10 = (s32[3]{0:T(128)S(1)}, s32[3]{0:T(128)}, u32[]{:S(2)}) copy-start(s32[3]{0:T(128)} %param.14) | copy-start | bytes 40
  11.6 13.9 %copy-start.1 = (bf16[256,384]{1,0:T(8,128)(2,1)S(1)}, bf16[256,384]{1,0:T(8,128)(2,1)}, u32[]{:S(2)}) copy-start(bf16[256,384]{1,0:T(8,128)(2,1)} %param.10) | copy-start | bytes 589828
  11.6 43.3 %all-to-all-start = ((bf16[32,48,512]{2,1,0:T(8,128)(2,1)}), bf16[32,48,512]{2,1,0:T(8,128)(2,1)S(1)}, u32[]{:S(2)}, u32[]{:S(2)}) async-start(bf16[32,48,512]{2,1,0:T(8,128)(2,1)} %broadcast_in_dim.28), calls=%async_computation | async-start | bytes 3145728 | tf_op jit(solution)/shard_map/all_to_all | solution.py:138
  54.9 7.7 %copy-start.6 = (bf16[384,48]{0,1:T(8,128)(2,1)S(1)}, bf16[384,48]{0,1:T(8,128)(2,1)}, u32[]{:S(2)}) copy-start(bf16[384,48]{0,1:T(8,128)(2,1)} %param.13) | copy-start | bytes 110596
  56.4 1.3 collective-permute-start
  57.8 51.0 %copy-start.4 = (bf16[256,256]{1,0:T(8,128)(2,1)}, bf16[256,256]{1,0:T(8,128)(2,1)S(1)}, u32[]{:S(2)}) copy-start(bf16[256,256]{1,0:T(8,128)(2,1)S(1)} %pad_maximum_fusion.1.own_ref) | copy-start | bytes 393220
  57.8 30.7 %collective-permute-start.1 = (bf16[256,256]{1,0:T(8,128)(2,1)S(1)}, bf16[256,256]{1,0:T(8,128)(2,1)S(1)}, u32[]{:S(2)}, u32[]{:S(2)}) collective-permute-start(bf16[256,256]{1,0:T(8,128)(2,1)S(1)} %pad_maximum_fusion.1.own_ref), channel_id=1, source_target_pairs={{0,4},{1,9},{2,6},{3,11},{4,8},{5,13},{6,10},{7,15},{8,12},{9,17},... | collective-permute-start | bytes 393224 | tf_op jit(solution)/shard_map/ppermute | solution.py:196
  63.7 82.1 %all-to-all-start.1 = ((bf16[32,48,384]{2,1,0:T(8,128)(2,1)}), bf16[32,48,384]{2,1,0:T(8,128)(2,1)S(1)}, u32[]{:S(2)}, u32[]{:S(2)}) async-start(bf16[32,48,384]{2,1,0:T(8,128)(2,1)} %broadcast_in_dim.36), calls=%async_computation.1 | async-start | bytes 2359296 | tf_op jit(solution)/shard_map/all_to_all | solution.py:138
  72.4 21.6 %collective-permute-start.2 = (bf16[256,256]{1,0:T(8,128)(2,1)S(1)}, bf16[256,256]{1,0:T(8,128)(2,1)S(1)}, u32[]{:S(2)}, u32[]{:S(2)}) collective-permute-start(bf16[256,256]{1,0:T(8,128)(2,1)S(1)} %pad_maximum_fusion.1.own_ref), channel_id=1, source_target_pairs={{0,12},{1,17},{2,14},{3,19},{4,16},{5,21},{6,18},{7,23},{8,20},{9,... | collective-permute-start | bytes 393224 | tf_op jit(solution)/shard_map/ppermute | solution.py:196
  77.0 31.8 %collective-permute-start.3 = (bf16[256,256]{1,0:T(8,128)(2,1)S(1)}, bf16[256,256]{1,0:T(8,128)(2,1)S(1)}, u32[]{:S(2)}, u32[]{:S(2)}) collective-permute-start(bf16[256,256]{1,0:T(8,128)(2,1)S(1)} %pad_maximum_fusion.1.own_ref), channel_id=1, source_target_pairs={{0,20},{1,25},{2,22},{3,27},{4,24},{5,29},{6,26},{7,31},{8,28},{9,... | collective-permute-start | bytes 393224 | tf_op jit(solution)/shard_map/ppermute | solution.py:196
  82.5 29.4 %collective-permute-start.4 = (bf16[256,256]{1,0:T(8,128)(2,1)S(1)}, bf16[256,256]{1,0:T(8,128)(2,1)S(1)}, u32[]{:S(2)}, u32[]{:S(2)}) collective-permute-start(bf16[256,256]{1,0:T(8,128)(2,1)S(1)} %pad_maximum_fusion.1.own_ref), channel_id=1, source_target_pairs={{0,28},{1,33},{2,30},{3,35},{4,32},{5,37},{6,34},{7,39},{8,36},{9,... | collective-permute-start | bytes 393224 | tf_op jit(solution)/shard_map/ppermute | solution.py:196
  85.6 26.3 %collective-permute-start.5 = (bf16[256,256]{1,0:T(8,128)(2,1)S(1)}, bf16[256,256]{1,0:T(8,128)(2,1)S(1)}, u32[]{:S(2)}, u32[]{:S(2)}) collective-permute-start(bf16[256,256]{1,0:T(8,128)(2,1)S(1)} %pad_maximum_fusion.1.own_ref), channel_id=1, source_target_pairs={{0,36},{1,41},{2,38},{3,43},{4,40},{5,45},{6,42},{7,47},{8,44},{9,... | collective-permute-start | bytes 393224 | tf_op jit(solution)/shard_map/ppermute | solution.py:196
  88.5 23.5 %collective-permute-start.6 = (bf16[256,256]{1,0:T(8,128)(2,1)S(1)}, bf16[256,256]{1,0:T(8,128)(2,1)S(1)}, u32[]{:S(2)}, u32[]{:S(2)}) collective-permute-start(bf16[256,256]{1,0:T(8,128)(2,1)S(1)} %pad_maximum_fusion.1.own_ref), channel_id=1, source_target_pairs={{0,44},{1,49},{2,46},{3,51},{4,48},{5,53},{6,50},{7,55},{8,52},{9,... | collective-permute-start | bytes 393224 | tf_op jit(solution)/shard_map/ppermute | solution.py:196
  93.9 18.1 %collective-permute-start.7 = (bf16[256,256]{1,0:T(8,128)(2,1)S(1)}, bf16[256,256]{1,0:T(8,128)(2,1)S(1)}, u32[]{:S(2)}, u32[]{:S(2)}) collective-permute-start(bf16[256,256]{1,0:T(8,128)(2,1)S(1)} %pad_maximum_fusion.1.own_ref), channel_id=1, source_target_pairs={{0,52},{1,57},{2,54},{3,59},{4,56},{5,61},{6,58},{7,63},{8,60},{9,... | collective-permute-start | bytes 393224 | tf_op jit(solution)/shard_map/ppermute | solution.py:196
  108.8 5.0 %collective-permute-start.8 = (bf16[256,256]{1,0:T(8,128)(2,1)S(1)}, bf16[256,256]{1,0:T(8,128)(2,1)S(1)}, u32[]{:S(2)}, u32[]{:S(2)}) collective-permute-start(bf16[256,256]{1,0:T(8,128)(2,1)S(1)} %pad_maximum_fusion.1.own_ref), channel_id=1, source_target_pairs={{0,60},{1,65},{2,62},{3,67},{4,64},{5,69},{6,66},{7,71},{8,68},{9,... | collective-permute-start | bytes 393224 | tf_op jit(solution)/shard_map/ppermute | solution.py:196
  113.8 7.1 %copy-start.2 = (bf16[8,256,256]{2,1,0:T(8,128)(2,1)}, bf16[8,256,256]{2,1,0:T(8,128)(2,1)S(1)}, u32[]{:S(2)}) copy-start(bf16[8,256,256]{2,1,0:T(8,128)(2,1)S(1)} %bitcast_dynamic-update-slice_fusion.fetched_ref) | copy-start | bytes 3145732
  113.9 7.9 %collective-permute-start.9 = (bf16[8,256,256]{2,1,0:T(8,128)(2,1)S(1)}, bf16[8,256,256]{2,1,0:T(8,128)(2,1)}, u32[]{:S(2)}, u32[]{:S(2)}) collective-permute-start(bf16[8,256,256]{2,1,0:T(8,128)(2,1)S(1)} %bitcast_dynamic-update-slice_fusion.fetched_ref), channel_id=1, source_target_pairs={{0,1},{1,0},{2,3},{3,2},{4,5},{5,4},{6,7},{7,6},{8,9},{9,8},{10,11... | collective-permute-start | bytes 3145736 | tf_op jit(solution)/shard_map/ppermute | solution.py:198
  116.9 4.9 %copy-start.5 = (s32[9,1,512]{2,1,0:T(1,128)}, s32[9,1,512]{2,1,0:T(1,128)S(1)}, u32[]{:S(2)}) copy-start(s32[9,1,512]{2,1,0:T(1,128)S(1)} %reshape.326.ki_ref) | copy-start | bytes 55300
  146.5 4.7 %copy-start.9 = (s32[256,4]{0,1:T(4,128)S(1)}, s32[256,4]{0,1:T(4,128)}, u32[]{:S(2)}) copy-start(s32[256,4]{0,1:T(4,128)} %param.15) | copy-start | bytes 12292
  147.5 14.3 %all-to-all-start.2 = ((bf16[256,4,384]{2,0,1:T(8,128)(2,1)}), bf16[256,4,384]{2,0,1:T(8,128)(2,1)S(1)}, u32[]{:S(2)}, u32[]{:S(2)}) async-start(bf16[256,4,384]{2,0,1:T(8,128)(2,1)} %bitcast.74), calls=%async_computation.2 | async-start | bytes 1572864 | tf_op jit(solution)/shard_map/all_to_all | solution.py:227
  215.9 5.6 %copy-start.8 = (f32[256,4]{0,1:T(4,128)S(1)}, f32[256,4]{0,1:T(4,128)}, u32[]{:S(2)}) copy-start(f32[256,4]{0,1:T(4,128)} %param.16) | copy-start | bytes 12292
  215.9 30.0 %all-to-all-start.4 = ((bf16[128,16,384]{2,1,0:T(8,128)(2,1)}), bf16[128,16,384]{2,1,0:T(8,128)(2,1)}, u32[]{:S(2)}, u32[]{:S(2)}) async-start(bf16[128,16,384]{2,1,0:T(8,128)(2,1)} %bitcast.29), calls=%async_computation.4 | async-start | bytes 3145728 | tf_op jit(solution)/shard_map/all_to_all | solution.py:281
  (2 other events, 1.6 us)
Sparse Core Ops, SparseCore 0:
  9.6 111.3 all-gather.1

commit v10 on v5

--- a/solution.py
+++ b/solution.py
@@ -74,8 +74,7 @@
         whole_f * lax.rsqrt(jnp.sum(whole_f * whole_f, axis=-1, keepdims=True) / D + EPSILON)
     ).astype(jnp.bfloat16)
     lin = jnp.dot(normed, w_qkv, preferred_element_type=jnp.float32)
-    wo_piece, lin = lax.optimization_barrier((wo.T, lin))
-    wo_rows = gather_seq(wo_piece, seq_count)
+    wo_rows = lax.all_gather(wo.T, "seq", axis=0, tiled=True)
     own_index = seq_index * tok_rows + jnp.arange(tok_rows, dtype=jnp.int32)
     _, own_pos = prompt_ids(own_index, lengths)
     queries = (

time: 243 us -> 250 us (1.029)
  waiting for transfers between devices: 31.9 us -> 54.6 us
  starting transfers between devices: 66.5 us -> 55.3 us
  local copies, waits for them, and re-layouts: 16.6 us -> 9.52 us
    all_to_all x2 -> x1, starting transfers between devices: 22.5 us -> 11.3 us  [gather_seq(): return lax.all_to_all(spread, 'seq', 0, 0, tiled=True)]
    all_to_all x1, waiting for transfers between devices: 8.38 us -> 16.8 us  [local(): lax.all_to_all(partial_out.astype(jnp.bfloat16), 'mp', 1, 0, tiled=True)]
    all_gather x1, waiting for transfers between devices: 0.02 us -> 7.63 us  [local(): lax.all_gather(jnp.concatenate([expert_gate, expert_up, expert_down], axi...]
    ppermute x8, waiting for transfers between devices: 0.02 us -> 6.12 us  [local(): fetched.append(lax.ppermute(kv_own, ('seq', 'mp'), pairs))]
    ppermute x8, starting transfers between devices: 34 us -> 28.2 us  [local(): fetched.append(lax.ppermute(kv_own, ('seq', 'mp'), pairs))]
    unnamed x27 -> x25, local copies, waits for them, and re-layouts: 6.19 us -> 0.87 us
    all_to_all x1, blocking collectives: 34.1 us -> 38.1 us  [local(): arrived = lax.all_to_all(buffer, ('seq', 'mp'), 0, 0, tiled=True)]
    all_to_all x1, starting transfers between devices: 5.56 us -> 9.09 us  [local(): returned = lax.all_to_all(outgoing, ('seq', 'mp'), 0, 0, tiled=True)]
  transfers between devices with their start and end apart: 15 -> 15, of which waited for: 3 -> 6; matrix products, arithmetic and copies ran while one was open for 21% -> 19% of each run, Pallas kernels for 0% -> 0%
where the time goes in v10:
time: 250 us; the launch traced here: 249 us
  blocking collectives  57 us (23%)
  starting transfers between devices  55.3 us (22%)
  waiting for transfers between devices  54.6 us (22%)
  matrix products  32.5 us (13%)
  other arithmetic  24.7 us (10%)
  between operations  15.2 us (6%)
  local copies, waits for them, and re-layouts  9.52 us (4%)
    all_to_all x1, blocking collectives, local(): arrived = lax.all_to_all(buffer, ('seq', 'mp'), 0, 0, tiled=True)  38.1 us
    ppermute x8, starting transfers between devices, local(): fetched.append(lax.ppermute(kv_own, ('seq', 'mp'), pairs))  28.2 us
    all_to_all x1, waiting for transfers between devices, local(): returned = lax.all_to_all(outgoing, ('seq', 'mp'), 0, 0, tiled=True)  22.8 us
    all_gather x1, blocking collectives, local(): whole = lax.all_gather(hidden_in, 'mp', axis=1, tiled=True)  18.9 us
    all_to_all x1, waiting for transfers between devices, local(): lax.all_to_all(partial_out.astype(jnp.bfloat16), 'mp', 1, 0, tiled=True)  16.8 us
    all_to_all x1, starting transfers between devices, gather_seq(): return lax.all_to_all(spread, 'seq', 0, 0, tiled=True)  11.3 us
    reduce_sum x1, other arithmetic, local(): total = jnp.sum(probs, axis=-1)  9.61 us
    all_to_all x1, starting transfers between devices, local(): returned = lax.all_to_all(outgoing, ('seq', 'mp'), 0, 0, tiled=True)  9.09 us
  transfers between devices with their start and end apart: 15, of which 6 were waited for; matrix products, arithmetic and copies ran while one was open for 19% of the time, Pallas kernels for 0%

profile of v10, /device:TPU:1, one launch (start us, length us, event | category | flops | bytes accessed | tf_op | source)
XLA Modules:
  0.0 248.7 jit_solution(9750314692322336725)
XLA Ops:
  9.5 11.3 %all-to-all-start = ((bf16[32,48,512]{2,1,0:T(8,128)(2,1)}), bf16[32,48,512]{2,1,0:T(8,128)(2,1)S(1)}, u32[]{:S(2)}, u32[]{:S(2)}) async-start(bf16[32,48,512]{2,1,0:T(8,128)(2,1)} %broadcast_in_dim.45), calls=%async_computation | async-start | bytes 3145728 | tf_op jit(solution)/shard_map/all_to_all | solution.py:47
  20.9 2.5 %pad_maximum_fusion = bf16[3,192,1536]{2,1,0:T(8,128)(2,1)} fusion(bf16[1,192,1536]{2,1,0:T(8,128)(2,1)S(1)} %copy-done.2, bf16[1,192,1536]{2,1,0:T(8,128)(2,1)S(1)} %copy-done.3, bf16[1,192,1536]{2,1,0:T(8,128)(2,1)} %param.17), kind=kLoop, calls=%fused_computation.37 | loop fusion | flops 1769472 | bytes 3538944 | tf_op jit(solution)/shard_map/concatenate | solution.py:63
  26.0 18.9 %all_gather.9 = bf16[256,1536]{1,0:T(8,128)(2,1)S(1)} all-gather(bf16[256,384]{1,0:T(8,128)(2,1)S(1)} %copy-done.1), channel_id=1, replica_groups=mesh['seq'=32,'mp'=4] {'mp'}, dimensions={1}, use_global_device_ids=true | all-gather | bytes 983040 | tf_op jit(solution)/shard_map/all_gather | solution.py:71
  47.8 4.8 %collective-permute-start.1 = (bf16[256,256]{1,0:T(8,128)(2,1)S(1)}, bf16[256,256]{1,0:T(8,128)(2,1)S(1)}, u32[]{:S(2)}, u32[]{:S(2)}) collective-permute-start(bf16[256,256]{1,0:T(8,128)(2,1)S(1)} %pad_maximum_fusion.1), channel_id=1, source_target_pairs={{0,4},{1,9},{2,6},{3,11},{4,8},{5,13},{6,10},{7,15},{8,12},{9,17},... | collective-permute-start | bytes 393224 | tf_op jit(solution)/shard_map/ppermute | solution.py:104
  53.2 5.6 %collective-permute-start.2 = (bf16[256,256]{1,0:T(8,128)(2,1)S(1)}, bf16[256,256]{1,0:T(8,128)(2,1)S(1)}, u32[]{:S(2)}, u32[]{:S(2)}) collective-permute-start(bf16[256,256]{1,0:T(8,128)(2,1)S(1)} %pad_maximum_fusion.1), channel_id=1, source_target_pairs={{0,12},{1,17},{2,14},{3,19},{4,16},{5,21},{6,18},{7,23},{8,20},{9,... | collective-permute-start | bytes 393224 | tf_op jit(solution)/shard_map/ppermute | solution.py:104
  58.8 5.9 %collective-permute-start.3 = (bf16[256,256]{1,0:T(8,128)(2,1)S(1)}, bf16[256,256]{1,0:T(8,128)(2,1)S(1)}, u32[]{:S(2)}, u32[]{:S(2)}) collective-permute-start(bf16[256,256]{1,0:T(8,128)(2,1)S(1)} %pad_maximum_fusion.1), channel_id=1, source_target_pairs={{0,20},{1,25},{2,22},{3,27},{4,24},{5,29},{6,26},{7,31},{8,28},{9,... | collective-permute-start | bytes 393224 | tf_op jit(solution)/shard_map/ppermute | solution.py:104
  67.1 2.8 %collective-permute-start.5 = (bf16[256,256]{1,0:T(8,128)(2,1)S(1)}, bf16[256,256]{1,0:T(8,128)(2,1)S(1)}, u32[]{:S(2)}, u32[]{:S(2)}) collective-permute-start(bf16[256,256]{1,0:T(8,128)(2,1)S(1)} %pad_maximum_fusion.1), channel_id=1, source_target_pairs={{0,36},{1,41},{2,38},{3,43},{4,40},{5,45},{6,42},{7,47},{8,44},{9,... | collective-permute-start | bytes 393224 | tf_op jit(solution)/shard_map/ppermute | solution.py:104
  72.3 3.0 %collective-permute-start.7 = (bf16[256,256]{1,0:T(8,128)(2,1)S(1)}, bf16[256,256]{1,0:T(8,128)(2,1)S(1)}, u32[]{:S(2)}, u32[]{:S(2)}) collective-permute-start(bf16[256,256]{1,0:T(8,128)(2,1)S(1)} %pad_maximum_fusion.1), channel_id=1, source_target_pairs={{0,52},{1,57},{2,54},{3,59},{4,56},{5,61},{6,58},{7,63},{8,60},{9,... | collective-permute-start | bytes 393224 | tf_op jit(solution)/shard_map/ppermute | solution.py:104
  76.9 2.6 %collective-permute-done.7 = bf16[256,256]{1,0:T(8,128)(2,1)S(1)} collective-permute-done((bf16[256,256]{1,0:T(8,128)(2,1)S(1)}, bf16[256,256]{1,0:T(8,128)(2,1)S(1)}, u32[]{:S(2)}, u32[]{:S(2)}) %collective-permute-start.7) | collective-permute-done | bytes 131104 | tf_op jit(solution)/shard_map/ppermute | solution.py:104
  79.5 3.5 %collective-permute-done.8 = bf16[256,256]{1,0:T(8,128)(2,1)S(1)} collective-permute-done((bf16[256,256]{1,0:T(8,128)(2,1)S(1)}, bf16[256,256]{1,0:T(8,128)(2,1)S(1)}, u32[]{:S(2)}, u32[]{:S(2)}) %collective-permute-start.8) | collective-permute-done | bytes 131104 | tf_op jit(solution)/shard_map/ppermute | solution.py:104
  83.0 2.6 %collective-permute-start.9 = (bf16[8,256,256]{2,1,0:T(8,128)(2,1)S(1)}, bf16[8,256,256]{2,1,0:T(8,128)(2,1)}, u32[]{:S(2)}, u32[]{:S(2)}) collective-permute-start(bf16[8,256,256]{2,1,0:T(8,128)(2,1)S(1)} %bitcast_dynamic-update-slice_fusion), channel_id=1, source_target_pairs={{0,1},{1,0},{2,3},{3,2},{4,5},{5,4},{6,7},{7,6},{8,9},{9,8},{10,11... | collective-permute-start | bytes 3145736 | tf_op jit(solution)/shard_map/ppermute | solution.py:106
  91.6 6.4 %fusion = (f32[3,256]{1,0:T(4,128)S(1)}, f32[3,256,4352]{2,1,0:T(8,128)}) fusion(pred[256,4352]{1,0:T(8,128)(4,1)S(1)} %fusion.11, bf16[4352,256]{1,0:T(8,128)(2,1)S(1)} %maximum_maximum_fusion, bf16[256,3,64]{2,0,1:T(8,128)(2,1)S(1)} %get-tuple-element.10, bf16[256,3,64]{2,0,1:T(8,128)(2,1)S(1)} %get-tuple-element.9), kind=kOutput, calls=%fused_computation.2 | convolution fusion | flops 866057472 | bytes 15993856 | tf_op jit(solution)/shard_map/hqd,kd->hqk/dot_general | solution.py:130
  98.1 9.6 %fusion.1 = f32[3,256]{1,0:T(4,128)S(1)} fusion(f32[3,256,4352]{2,1,0:T(8,128)} %get-tuple-element.22, f32[3,256]{1,0:T(4,128)S(1)} %get-tuple-element.21, pred[256,4352]{1,0:T(8,128)(4,1)S(1)} %fusion.11), kind=kLoop, calls=%fused_computation.3 | loop fusion | flops 16710912 | bytes 14489600 | tf_op jit(solution)/shard_map/reduce_sum | solution.py:145
  107.7 7.0 %fusion.28 = bf16[256,3,128]{0,2,1:T(8,128)(2,1)S(1)} fusion(bf16[4352,256]{1,0:T(8,128)(2,1)S(1)} %maximum_maximum_fusion, f32[3,256,4352]{2,1,0:T(8,128)} %get-tuple-element.22, f32[3,256]{1,0:T(4,128)S(1)} %get-tuple-element.21, pred[256,4352]{1,0:T(8,128)(4,1)S(1)} %fusion.11, f32[256,3]{0,1:T(4,128)S(1)} %bitcast.106), kind=kOutput, calls=%fused_computation.55 | convolution fusion | flops 869203968 | bytes 15802368 | tf_op jit(solution)/shard_map/hqk,kd->hqd/dot_general | solution.py:146
  117.6 3.7 %all-to-all-start.1 = ((bf16[256,4,384]{2,0,1:T(8,128)(2,1)}), bf16[256,4,384]{2,0,1:T(8,128)(2,1)S(1)}, u32[]{:S(2)}, u32[]{:S(2)}) async-start(bf16[256,4,384]{2,0,1:T(8,128)(2,1)} %bitcast.93), calls=%async_computation.1 | async-start | bytes 1572864 | tf_op jit(solution)/shard_map/all_to_all | solution.py:156
  123.7 16.8 %all-to-all-done.1 = bf16[256,4,384]{2,0,1:T(8,128)(2,1)S(1)} async-done(((bf16[256,4,384]{2,0,1:T(8,128)(2,1)}), bf16[256,4,384]{2,0,1:T(8,128)(2,1)S(1)}, u32[]{:S(2)}, u32[]{:S(2)}) %all-to-all-start.1) | async-done | bytes 786464 | tf_op jit(solution)/shard_map/all_to_all | solution.py:156
  141.3 38.1 %all_to_all.43 = bf16[128,16,384]{2,1,0:T(8,128)(2,1)S(1)} all-to-all(bf16[128,16,384]{2,1,0:T(8,128)(2,1)S(1)} %bitcast.95), channel_id=1, replica_groups=mesh['seq'=32,'mp'=4] {'seq','mp'}, dimensions={0} | all-to-all | bytes 3145728 | tf_op jit(solution)/shard_map/all_to_all | solution.py:182
  181.2 7.6 %all-gather.5.cloned.1.call-done = bf16[3,768,1536]{2,1,0:T(8,128)(2,1)} async-done(((bf16[3,192,1536]{2,1,0:T(8,128)(2,1)}), bf16[3,768,1536]{2,1,0:T(8,128)(2,1)}) %all-gather.5.cloned.1.call-update) | async-done | bytes 7077904 | tf_op jit(solution)/shard_map/all_gather | solution.py:62
  188.8 4.2 %fusion.16 = f32[512,768]{1,0:T(8,128)} fusion(bf16[512,1536]{1,0:T(8,128)(2,1)S(1)} %bitcast.101, bf16[3,768,1536]{2,1,0:T(8,128)(2,1)} %all-gather.5.cloned.1.call-done), kind=kOutput, calls=%fused_computation.31 | convolution fusion | flops 1207959552 | bytes 5505024 | tf_op jit(solution)/shard_map/dot_general | solution.py:200
  193.0 7.2 %convolution_convert_fusion = bf16[512,1536]{1,0:T(8,128)(2,1)} fusion(bf16[3,768,1536]{2,1,0:T(8,128)(2,1)} %all-gather.5.cloned.1.call-done, f32[512,768]{1,0:T(8,128)} %fusion.16, bf16[512,1536]{1,0:T(8,128)(2,1)S(1)} %bitcast.102), kind=kOutput, calls=%fused_computation.26 | convolution fusion | flops 2417885184 | bytes 9437184 | tf_op jit(solution)/shard_map/dot_general | solution.py:204
  200.2 3.0 %reshape.377 = bf16[32,16,4,384]{3,2,1,0:T(4,128)(2,1)S(1)} reshape(bf16[512,1536]{1,0:T(8,128)(2,1)} %convolution_convert_fusion) | data formatting | bytes 3145728 | tf_op jit(solution)/shard_map/reshape | solution.py:206
  204.6 9.1 %all-to-all-start.3 = ((bf16[128,16,384]{2,1,0:T(8,128)(2,1)}), bf16[128,16,384]{2,1,0:T(8,128)(2,1)}, u32[]{:S(2)}, u32[]{:S(2)}) async-start(bf16[128,16,384]{2,1,0:T(8,128)(2,1)} %bitcast.31), calls=%async_computation.3 | async-start | bytes 3145728 | tf_op jit(solution)/shard_map/all_to_all | solution.py:210
  215.2 22.8 %all-to-all-done.3 = bf16[128,16,384]{2,1,0:T(8,128)(2,1)} async-done(((bf16[128,16,384]{2,1,0:T(8,128)(2,1)}), bf16[128,16,384]{2,1,0:T(8,128)(2,1)}, u32[]{:S(2)}, u32[]{:S(2)}) %all-to-all-start.3) | async-done | bytes 1572896 | tf_op jit(solution)/shard_map/all_to_all | solution.py:210
  238.0 3.9 %fusion.22 = bf16[256,384]{1,0:T(8,128)(2,1)} fusion(f32[256,2048]{1,0:T(8,128)S(1)} %select_reduce_fusion, bf16[2048,384]{1,0:T(8,128)(2,1)} %bitcast.32, f32[256,384]{1,0:T(8,128)S(1)} %convert_reduce_fusion, bf16[256,384]{1,0:T(8,128)(2,1)S(1)} %copy-done.1), kind=kOutput, calls=%fused_computation.45 | convolution fusion | flops 2416508928 | bytes 4456448 | tf_op jit(solution)/shard_map/dot_general | solution.py:219
  (93 shorter events, 30.7 us)
Async XLA Ops:
  6.5 0.8 copy-start
  6.5 108.2 %all-gather.3.cloned.1.call-start = ((), (), s32[]{:S(2)}) async-start(), calls=%async_computation.4 | async-start | bytes 1216512 | tf_op jit(solution)/shard_map/all_gather | solution.py:77
  8.1 12.8 %copy-start.2 = (bf16[1,192,1536]{2,1,0:T(8,128)(2,1)S(1)}, bf16[1,192,1536]{2,1,0:T(8,128)(2,1)}, u32[]{:S(2)}) copy-start(bf16[1,192,1536]{2,1,0:T(8,128)(2,1)} %param.19) | copy-start | bytes 1769476
  8.1 12.8 %copy-start.3 = (bf16[1,192,1536]{2,1,0:T(8,128)(2,1)S(1)}, bf16[1,192,1536]{2,1,0:T(8,128)(2,1)}, u32[]{:S(2)}) copy-start(bf16[1,192,1536]{2,1,0:T(8,128)(2,1)} %param.18) | copy-start | bytes 1769476
  9.5 35.7 %all-to-all-start = ((bf16[32,48,512]{2,1,0:T(8,128)(2,1)}), bf16[32,48,512]{2,1,0:T(8,128)(2,1)S(1)}, u32[]{:S(2)}, u32[]{:S(2)}) async-start(bf16[32,48,512]{2,1,0:T(8,128)(2,1)} %broadcast_in_dim.45), calls=%async_computation | async-start | bytes 3145728 | tf_op jit(solution)/shard_map/all_to_all | solution.py:47
  20.8 2.8 %copy-start.6 = (s32[3]{0:T(128)S(1)}, s32[3]{0:T(128)}, u32[]{:S(2)}) copy-start(s32[3]{0:T(128)} %param.14) | copy-start | bytes 40
  20.8 5.2 %copy-start.1 = (bf16[256,384]{1,0:T(8,128)(2,1)S(1)}, bf16[256,384]{1,0:T(8,128)(2,1)}, u32[]{:S(2)}) copy-start(bf16[256,384]{1,0:T(8,128)(2,1)} %param.10) | copy-start | bytes 589828
  20.8 168.0 %all-gather.5.cloned.1.call-start = ((), (), s32[]{:S(2)}) async-start(), calls=%async_computation.5 | async-start | bytes 8847360 | tf_op jit(solution)/shard_map/all_gather | solution.py:62
  46.5 1.3 collective-permute-start
  47.8 22.1 %collective-permute-start.1 = (bf16[256,256]{1,0:T(8,128)(2,1)S(1)}, bf16[256,256]{1,0:T(8,128)(2,1)S(1)}, u32[]{:S(2)}, u32[]{:S(2)}) collective-permute-start(bf16[256,256]{1,0:T(8,128)(2,1)S(1)} %pad_maximum_fusion.1), channel_id=1, source_target_pairs={{0,4},{1,9},{2,6},{3,11},{4,8},{5,13},{6,10},{7,15},{8,12},{9,17},... | collective-permute-start | bytes 393224 | tf_op jit(solution)/shard_map/ppermute | solution.py:104
  53.2 19.1 %collective-permute-start.2 = (bf16[256,256]{1,0:T(8,128)(2,1)S(1)}, bf16[256,256]{1,0:T(8,128)(2,1)S(1)}, u32[]{:S(2)}, u32[]{:S(2)}) collective-permute-start(bf16[256,256]{1,0:T(8,128)(2,1)S(1)} %pad_maximum_fusion.1), channel_id=1, source_target_pairs={{0,12},{1,17},{2,14},{3,19},{4,16},{5,21},{6,18},{7,23},{8,20},{9,... | collective-permute-start | bytes 393224 | tf_op jit(solution)/shard_map/ppermute | solution.py:104
  58.8 16.5 %collective-permute-start.3 = (bf16[256,256]{1,0:T(8,128)(2,1)S(1)}, bf16[256,256]{1,0:T(8,128)(2,1)S(1)}, u32[]{:S(2)}, u32[]{:S(2)}) collective-permute-start(bf16[256,256]{1,0:T(8,128)(2,1)S(1)} %pad_maximum_fusion.1), channel_id=1, source_target_pairs={{0,20},{1,25},{2,22},{3,27},{4,24},{5,29},{6,26},{7,31},{8,28},{9,... | collective-permute-start | bytes 393224 | tf_op jit(solution)/shard_map/ppermute | solution.py:104
  64.7 12.1 %collective-permute-start.4 = (bf16[256,256]{1,0:T(8,128)(2,1)S(1)}, bf16[256,256]{1,0:T(8,128)(2,1)S(1)}, u32[]{:S(2)}, u32[]{:S(2)}) collective-permute-start(bf16[256,256]{1,0:T(8,128)(2,1)S(1)} %pad_maximum_fusion.1), channel_id=1, source_target_pairs={{0,28},{1,33},{2,30},{3,35},{4,32},{5,37},{6,34},{7,39},{8,36},{9,... | collective-permute-start | bytes 393224 | tf_op jit(solution)/shard_map/ppermute | solution.py:104
  67.1 9.7 %collective-permute-start.5 = (bf16[256,256]{1,0:T(8,128)(2,1)S(1)}, bf16[256,256]{1,0:T(8,128)(2,1)S(1)}, u32[]{:S(2)}, u32[]{:S(2)}) collective-permute-start(bf16[256,256]{1,0:T(8,128)(2,1)S(1)} %pad_maximum_fusion.1), channel_id=1, source_target_pairs={{0,36},{1,41},{2,38},{3,43},{4,40},{5,45},{6,42},{7,47},{8,44},{9,... | collective-permute-start | bytes 393224 | tf_op jit(solution)/shard_map/ppermute | solution.py:104
  69.9 6.9 %collective-permute-start.6 = (bf16[256,256]{1,0:T(8,128)(2,1)S(1)}, bf16[256,256]{1,0:T(8,128)(2,1)S(1)}, u32[]{:S(2)}, u32[]{:S(2)}) collective-permute-start(bf16[256,256]{1,0:T(8,128)(2,1)S(1)} %pad_maximum_fusion.1), channel_id=1, source_target_pairs={{0,44},{1,49},{2,46},{3,51},{4,48},{5,53},{6,50},{7,55},{8,52},{9,... | collective-permute-start | bytes 393224 | tf_op jit(solution)/shard_map/ppermute | solution.py:104
  72.3 7.2 %collective-permute-start.7 = (bf16[256,256]{1,0:T(8,128)(2,1)S(1)}, bf16[256,256]{1,0:T(8,128)(2,1)S(1)}, u32[]{:S(2)}, u32[]{:S(2)}) collective-permute-start(bf16[256,256]{1,0:T(8,128)(2,1)S(1)} %pad_maximum_fusion.1), channel_id=1, source_target_pairs={{0,52},{1,57},{2,54},{3,59},{4,56},{5,61},{6,58},{7,63},{8,60},{9,... | collective-permute-start | bytes 393224 | tf_op jit(solution)/shard_map/ppermute | solution.py:104
  75.3 7.7 %collective-permute-start.8 = (bf16[256,256]{1,0:T(8,128)(2,1)S(1)}, bf16[256,256]{1,0:T(8,128)(2,1)S(1)}, u32[]{:S(2)}, u32[]{:S(2)}) collective-permute-start(bf16[256,256]{1,0:T(8,128)(2,1)S(1)} %pad_maximum_fusion.1), channel_id=1, source_target_pairs={{0,60},{1,65},{2,62},{3,67},{4,64},{5,69},{6,66},{7,71},{8,68},{9,... | collective-permute-start | bytes 393224 | tf_op jit(solution)/shard_map/ppermute | solution.py:104
  83.0 7.1 %collective-permute-start.9 = (bf16[8,256,256]{2,1,0:T(8,128)(2,1)S(1)}, bf16[8,256,256]{2,1,0:T(8,128)(2,1)}, u32[]{:S(2)}, u32[]{:S(2)}) collective-permute-start(bf16[8,256,256]{2,1,0:T(8,128)(2,1)S(1)} %bitcast_dynamic-update-slice_fusion), channel_id=1, source_target_pairs={{0,1},{1,0},{2,3},{3,2},{4,5},{5,4},{6,7},{7,6},{8,9},{9,8},{10,11... | collective-permute-start | bytes 3145736 | tf_op jit(solution)/shard_map/ppermute | solution.py:106
  114.7 6.6 %copy-start.5 = (s32[256,4]{0,1:T(4,128)S(1)}, s32[256,4]{0,1:T(4,128)}, u32[]{:S(2)}) copy-start(s32[256,4]{0,1:T(4,128)} %param.15) | copy-start | bytes 12292
  117.6 22.9 %all-to-all-start.1 = ((bf16[256,4,384]{2,0,1:T(8,128)(2,1)}), bf16[256,4,384]{2,0,1:T(8,128)(2,1)S(1)}, u32[]{:S(2)}, u32[]{:S(2)}) async-start(bf16[256,4,384]{2,0,1:T(8,128)(2,1)} %bitcast.93), calls=%async_computation.1 | async-start | bytes 1572864 | tf_op jit(solution)/shard_map/all_to_all | solution.py:156
  204.6 9.1 %copy-start.4 = (f32[256,4]{0,1:T(4,128)S(1)}, f32[256,4]{0,1:T(4,128)}, u32[]{:S(2)}) copy-start(f32[256,4]{0,1:T(4,128)} %param.16) | copy-start | bytes 12292
  204.6 33.4 %all-to-all-start.3 = ((bf16[128,16,384]{2,1,0:T(8,128)(2,1)}), bf16[128,16,384]{2,1,0:T(8,128)(2,1)}, u32[]{:S(2)}, u32[]{:S(2)}) async-start(bf16[128,16,384]{2,1,0:T(8,128)(2,1)} %bitcast.31), calls=%async_computation.3 | async-start | bytes 3145728 | tf_op jit(solution)/shard_map/all_to_all | solution.py:210
Sparse Core Ops, SparseCore 0:
  10.3 82.6 all-gather.2
  94.7 94.0 all-gather.4

commit v11 on v10

--- a/solution.py
+++ b/solution.py
@@ -59,9 +59,8 @@
     q_cols = heads_here * HD
     kv_group = mp_index * heads_here // (HQ // KVH)
 
-    expert_all = lax.all_gather(
-        jnp.concatenate([expert_gate, expert_up, expert_down], axis=0), "mp", axis=1, tiled=True
-    )
+    expert_own = jnp.concatenate([expert_gate, expert_up, expert_down], axis=0)
+    across = lax.ppermute(expert_own, "mp", [(m, m ^ 2) for m in range(mp_count)])
 
     core = mp_index % 2
     kv_col = jnp.where(core == 0, kv_group * HD, KVH * HD + kv_group * HD)
@@ -74,6 +73,11 @@
         whole_f * lax.rsqrt(jnp.sum(whole_f * whole_f, axis=-1, keepdims=True) / D + EPSILON)
     ).astype(jnp.bfloat16)
     lin = jnp.dot(normed, w_qkv, preferred_element_type=jnp.float32)
+    across, lin = lax.optimization_barrier((across, lin))
+    beside = lax.ppermute(
+        jnp.stack([expert_own, across]), "mp", [(m, m ^ 1) for m in range(mp_count)]
+    )
+    expert_pieces = [expert_own, across, beside[0], beside[1]]
     wo_rows = lax.all_gather(wo.T, "seq", axis=0, tiled=True)
     own_index = seq_index * tok_rows + jnp.arange(tok_rows, dtype=jnp.int32)
     _, own_pos = prompt_ids(own_index, lengths)
@@ -191,17 +195,18 @@
         arrived_rows
         * lax.rsqrt(jnp.sum(arrived_rows * arrived_rows, axis=-1, keepdims=True) / D + EPSILON)
     ).astype(jnp.bfloat16)
-    w_gate = expert_all[0]
-    w_up = expert_all[1]
-    w_down = expert_all[2]
-    gate_act = lax.dot_general(
-        moe_in, w_gate, (((1,), (1,)), ((), ())), preferred_element_type=jnp.float32
-    )
-    up_act = lax.dot_general(
-        moe_in, w_up, (((1,), (1,)), ((), ())), preferred_element_type=jnp.float32
-    )
-    active = (jnp.maximum(gate_act, 0.0) * up_act).astype(jnp.bfloat16)
-    result = jnp.dot(active, w_down, preferred_element_type=jnp.float32).astype(jnp.bfloat16)
+    result_f = None
+    for piece in expert_pieces:
+        gate_act = lax.dot_general(
+            moe_in, piece[0], (((1,), (1,)), ((), ())), preferred_element_type=jnp.float32
+        )
+        up_act = lax.dot_general(
+            moe_in, piece[1], (((1,), (1,)), ((), ())), preferred_element_type=jnp.float32
+        )
+        active = (jnp.maximum(gate_act, 0.0) * up_act).astype(jnp.bfloat16)
+        part = jnp.dot(active, piece[2], preferred_element_type=jnp.float32)
+        result_f = part if result_f is None else result_f + part
+    result = result_f.astype(jnp.bfloat16)
     outgoing = (
         result.reshape(seq_count, part_cap, mp_count, feat)
         .transpose(0, 2, 1, 3)

time: 250 us -> 291 us (1.16)
  matrix products: 32.5 us -> 50 us
  local copies, waits for them, and re-layouts: 9.52 us -> 21.4 us
  starting transfers between devices: 55.3 us -> 63.5 us
  blocking collectives: 57 us -> 60.8 us
    all_gather x1, blocking collectives: 18.9 us -> 60.8 us  [local(): whole = lax.all_gather(hidden_in, 'mp', axis=1, tiled=True)]
    all_to_all x1 -> x0, blocking collectives: 38.1 us -> none  [local(): arrived = lax.all_to_all(buffer, ('seq', 'mp'), 0, 0, tiled=True)]
    all_to_all x0 -> x1, waiting for transfers between devices: none -> 19.9 us  [local(): arrived = lax.all_to_all(buffer, ('seq', 'mp'), 0, 0, tiled=True)]
    dot_general x2 -> x8, matrix products: 11.4 us -> 25.2 us  [the longest x4 18.2 us: local(): part = jnp.dot(active, piece[2], preferred_element_type=jnp.float32)]
    unnamed x25 -> x37, local copies, waits for them, and re-layouts: 0.87 us -> 11.3 us
    all_to_all x0 -> x1, starting transfers between devices: none -> 8.92 us  [local(): arrived = lax.all_to_all(buffer, ('seq', 'mp'), 0, 0, tiled=True)]
    all_to_all x1, waiting for transfers between devices: 16.8 us -> 8.19 us  [local(): lax.all_to_all(partial_out.astype(jnp.bfloat16), 'mp', 1, 0, tiled=True)]
    all_gather x1 -> x0, waiting for transfers between devices: 7.63 us -> none  [local(): lax.all_gather(jnp.concatenate([expert_gate, expert_up, expert_down], axi...]
  transfers between devices with their start and end apart: 15 -> 17, of which waited for: 6 -> 5; matrix products, arithmetic and copies ran while one was open for 19% -> 24% of each run, Pallas kernels for 0% -> 0%
where the time goes in v11:
time: 291 us; the launch traced here: 290 us
  starting transfers between devices  63.5 us (22%)
  blocking collectives  60.8 us (21%)
  waiting for transfers between devices  51.7 us (18%)
  matrix products  50 us (17%)
  other arithmetic  27.3 us (9%)
  local copies, waits for them, and re-layouts  21.4 us (7%)
  between operations  15.2 us (5%)
    all_gather x1, blocking collectives, local(): whole = lax.all_gather(hidden_in, 'mp', axis=1, tiled=True)  60.8 us
    ppermute x8, starting transfers between devices, local(): fetched.append(lax.ppermute(kv_own, ('seq', 'mp'), pairs))  29 us
    all_to_all x1, waiting for transfers between devices, local(): returned = lax.all_to_all(outgoing, ('seq', 'mp'), 0, 0, tiled=True)  22.9 us
    all_to_all x1, waiting for transfers between devices, local(): arrived = lax.all_to_all(buffer, ('seq', 'mp'), 0, 0, tiled=True)  19.9 us
    dot_general x4, matrix products, local(): part = jnp.dot(active, piece[2], preferred_element_type=jnp.float32)  18.2 us
    all_to_all x1, starting transfers between devices, gather_seq(): return lax.all_to_all(spread, 'seq', 0, 0, tiled=True)  11.6 us
    unnamed x37, local copies, waits for them, and re-layouts  11.3 us
    reduce_sum x1, other arithmetic, local(): total = jnp.sum(probs, axis=-1)  9.02 us
  transfers between devices with their start and end apart: 17, of which 5 were waited for; matrix products, arithmetic and copies ran while one was open for 24% of the time, Pallas kernels for 0%

profile of v11, /device:TPU:1, one launch (start us, length us, event | category | flops | bytes accessed | tf_op | source)
XLA Modules:
  0.0 289.8 jit_solution(15306206490783953655)
XLA Ops:
  9.4 11.6 %all-to-all-start = ((bf16[32,48,512]{2,1,0:T(8,128)(2,1)}), bf16[32,48,512]{2,1,0:T(8,128)(2,1)}, u32[]{:S(2)}, u32[]{:S(2)}) async-start(bf16[32,48,512]{2,1,0:T(8,128)(2,1)} %broadcast_in_dim.45), calls=%async_computation | async-start | bytes 3145728 | tf_op jit(solution)/shard_map/all_to_all | solution.py:47
  26.9 60.8 %all_gather.6 = bf16[256,1536]{1,0:T(8,128)(2,1)S(1)} all-gather(bf16[256,384]{1,0:T(8,128)(2,1)} %param.10), channel_id=1, replica_groups=mesh['seq'=32,'mp'=4] {'mp'}, dimensions={1}, use_global_device_ids=true | all-gather | bytes 983040 | tf_op jit(solution)/shard_map/all_gather | solution.py:70
  92.0 4.6 %collective-permute-start.2 = (bf16[256,256]{1,0:T(8,128)(2,1)S(1)}, bf16[256,256]{1,0:T(8,128)(2,1)S(1)}, u32[]{:S(2)}, u32[]{:S(2)}) collective-permute-start(bf16[256,256]{1,0:T(8,128)(2,1)S(1)} %pad_maximum_fusion.1), channel_id=1, source_target_pairs={{0,4},{1,9},{2,6},{3,11},{4,8},{5,13},{6,10},{7,15},{8,12},{9,17},... | collective-permute-start | bytes 393224 | tf_op jit(solution)/shard_map/ppermute | solution.py:108
  97.4 6.1 %collective-permute-start.3 = (bf16[256,256]{1,0:T(8,128)(2,1)S(1)}, bf16[256,256]{1,0:T(8,128)(2,1)S(1)}, u32[]{:S(2)}, u32[]{:S(2)}) collective-permute-start(bf16[256,256]{1,0:T(8,128)(2,1)S(1)} %pad_maximum_fusion.1), channel_id=1, source_target_pairs={{0,12},{1,17},{2,14},{3,19},{4,16},{5,21},{6,18},{7,23},{8,20},{9,... | collective-permute-start | bytes 393224 | tf_op jit(solution)/shard_map/ppermute | solution.py:108
  103.4 6.1 %collective-permute-start.4 = (bf16[256,256]{1,0:T(8,128)(2,1)S(1)}, bf16[256,256]{1,0:T(8,128)(2,1)S(1)}, u32[]{:S(2)}, u32[]{:S(2)}) collective-permute-start(bf16[256,256]{1,0:T(8,128)(2,1)S(1)} %pad_maximum_fusion.1), channel_id=1, source_target_pairs={{0,20},{1,25},{2,22},{3,27},{4,24},{5,29},{6,26},{7,31},{8,28},{9,... | collective-permute-start | bytes 393224 | tf_op jit(solution)/shard_map/ppermute | solution.py:108
  112.1 2.6 collective-permute-start.6
  114.6 2.8 collective-permute-start.7
  118.1 2.6 collective-permute-start.8
  141.2 6.4 %fusion = (f32[3,256]{1,0:T(4,128)S(1)}, f32[3,256,4352]{2,1,0:T(8,128)}) fusion(pred[256,4352]{1,0:T(8,128)(4,1)S(1)} %fusion.11, bf16[4352,256]{1,0:T(8,128)(2,1)S(1)} %maximum_maximum_fusion, bf16[256,3,64]{2,0,1:T(8,128)(2,1)S(1)} %get-tuple-element.14, bf16[256,3,64]{2,0,1:T(8,128)(2,1)S(1)} %get-tuple-element.13), kind=kOutput, calls=%fused_computation.2 | convolution fusion | flops 866057472 | bytes 15993856 | tf_op jit(solution)/shard_map/hqd,kd->hqk/dot_general | solution.py:134
  147.7 9.0 %fusion.1 = f32[3,256]{1,0:T(4,128)S(1)} fusion(f32[3,256,4352]{2,1,0:T(8,128)} %get-tuple-element.26, f32[3,256]{1,0:T(4,128)S(1)} %get-tuple-element.25, pred[256,4352]{1,0:T(8,128)(4,1)S(1)} %fusion.11), kind=kLoop, calls=%fused_computation.3 | loop fusion | flops 16710912 | bytes 14489600 | tf_op jit(solution)/shard_map/reduce_sum | solution.py:149
  156.7 7.0 %fusion.36 = bf16[256,3,128]{0,2,1:T(8,128)(2,1)S(1)} fusion(bf16[4352,256]{1,0:T(8,128)(2,1)S(1)} %maximum_maximum_fusion, f32[3,256,4352]{2,1,0:T(8,128)} %get-tuple-element.26, f32[3,256]{1,0:T(4,128)S(1)} %get-tuple-element.25, pred[256,4352]{1,0:T(8,128)(4,1)S(1)} %fusion.11, f32[256,3]{0,1:T(4,128)S(1)} %bitcast.146), kind=kOutput, calls=%fused_computation.66 | convolution fusion | flops 869203968 | bytes 15802368 | tf_op jit(solution)/shard_map/hqk,kd->hqd/dot_general | solution.py:150
  166.6 4.4 %all-to-all-start.1 = ((bf16[256,4,384]{2,0,1:T(8,128)(2,1)}), bf16[256,4,384]{2,0,1:T(8,128)(2,1)}, u32[]{:S(2)}, u32[]{:S(2)}) async-start(bf16[256,4,384]{2,0,1:T(8,128)(2,1)} %bitcast.128), calls=%async_computation.1 | async-start | bytes 1572864 | tf_op jit(solution)/shard_map/all_to_all | solution.py:160
  173.5 8.2 %all-to-all-done.1 = bf16[256,4,384]{2,0,1:T(8,128)(2,1)} async-done(((bf16[256,4,384]{2,0,1:T(8,128)(2,1)}), bf16[256,4,384]{2,0,1:T(8,128)(2,1)}, u32[]{:S(2)}, u32[]{:S(2)}) %all-to-all-start.1) | async-done | bytes 786464 | tf_op jit(solution)/shard_map/all_to_all | solution.py:160
  182.9 3.0 %convolution_convert_fusion = bf16[2048,384]{1,0:T(8,128)(2,1)} fusion(bf16[2048,256]{1,0:T(8,128)(2,1)S(1)} %fusion.12, f32[256,384]{1,0:T(8,128)S(1)} %convert_reduce_fusion, bf16[256,384]{1,0:T(8,128)(2,1)} %param.10), kind=kOutput, calls=%fused_computation.31 | convolution fusion | flops 403734528 | bytes 3211264 | tf_op jit(solution)/shard_map/dot_general | solution.py:185
  186.0 8.9 %all-to-all-start.2 = ((bf16[128,16,384]{2,1,0:T(8,128)(2,1)}), bf16[128,16,384]{2,1,0:T(8,128)(2,1)S(1)}, u32[]{:S(2)}, u32[]{:S(2)}) async-start(bf16[128,16,384]{2,1,0:T(8,128)(2,1)} %bitcast.23), calls=%async_computation.2 | async-start | bytes 3145728 | tf_op jit(solution)/shard_map/all_to_all | solution.py:186
  194.9 3.6 %pad_maximum_fusion = bf16[2,3,192,1536]{3,2,1,0:T(8,128)(2,1)} fusion(bf16[1,3,192,1536]{3,2,1,0:T(8,128)(2,1)S(1)} %bitcast.139, bf16[1,3,192,1536]{3,2,1,0:T(8,128)(2,1)} %bitcast.33), kind=kLoop, calls=%fused_computation.24 | loop fusion | flops 1769472 | bytes 7077888 | tf_op jit(solution)/shard_map/stack | solution.py:78
  199.5 19.9 %all-to-all-done.2 = bf16[128,16,384]{2,1,0:T(8,128)(2,1)S(1)} async-done(((bf16[128,16,384]{2,1,0:T(8,128)(2,1)}), bf16[128,16,384]{2,1,0:T(8,128)(2,1)S(1)}, u32[]{:S(2)}, u32[]{:S(2)}) %all-to-all-start.2) | async-done | bytes 1572896 | tf_op jit(solution)/shard_map/all_to_all | solution.py:186
  224.9 4.3 %fusion.29 = f32[512,1536]{1,0:T(8,128)} fusion(f32[512,192]{0,1:T(8,128)} %convolution_maximum_fusion.3, bf16[512,1536]{1,0:T(8,128)(2,1)S(1)} %bitcast.131, bf16[1,192,1536]{2,1,0:T(8,128)(2,1)} %param.19, bf16[1,192,1536]{2,1,0:T(8,128)(2,1)} %param.18), kind=kOutput, calls=%fused_computation.55 | convolution fusion | flops 604176384 | bytes 6291456 | tf_op jit(solution)/shard_map/dot_general | solution.py:207
  229.2 5.0 %convolution_add_fusion.1 = f32[512,1536]{1,0:T(8,128)} fusion(f32[512,1536]{1,0:T(8,128)} %fusion.29, f32[512,192]{0,1:T(8,128)} %convolution_maximum_fusion.2, bf16[512,1536]{1,0:T(8,128)(2,1)S(1)} %bitcast.132, bf16[3,192,1536]{2,1,0:T(8,128)(2,1)S(1)} %collective-permute-done), kind=kOutput, calls=%fused_computation.27 | convolution fusion | flops 604962816 | bytes 9437184 | tf_op jit(solution)/shard_map/dot_general | solution.py:207
  238.4 4.2 %fusion.30 = f32[512,1536]{1,0:T(8,128)} fusion(f32[512,192]{0,1:T(8,128)S(1)} %fusion.40, bf16[512,1536]{1,0:T(8,128)(2,1)S(1)} %bitcast.135, bf16[2,3,192,1536]{3,2,1,0:T(8,128)(2,1)} %collective-permute-done.11), kind=kOutput, calls=%fused_computation.56 | convolution fusion | flops 604274688 | bytes 6291456 | tf_op jit(solution)/shard_map/dot_general | solution.py:207
  242.6 4.6 %fusion.17 = bf16[512,1536]{1,0:T(8,128)(2,1)S(1)} fusion(f32[512,1536]{1,0:T(8,128)} %fusion.30, f32[512,1536]{1,0:T(8,128)} %convolution_add_fusion.1, f32[512,192]{0,1:T(8,128)} %fusion.41, bf16[512,1536]{1,0:T(8,128)(2,1)S(1)} %bitcast.136, bf16[2,3,192,1536]{3,2,1,0:T(8,128)(2,1)} %collective-permute-done.11), kind=kOutput, calls=%fused_computation.30 | convolution fusion | flops 606633984 | bytes 11010048 | tf_op jit(solution)/shard_map/dot_general | solution.py:207
  249.1 5.6 %all-to-all-start.3 = ((bf16[128,16,384]{2,1,0:T(8,128)(2,1)}), bf16[128,16,384]{2,1,0:T(8,128)(2,1)}, u32[]{:S(2)}, u32[]{:S(2)}) async-start(bf16[128,16,384]{2,1,0:T(8,128)(2,1)} %bitcast.42), calls=%async_computation.3 | async-start | bytes 3145728 | tf_op jit(solution)/shard_map/all_to_all | solution.py:215
  256.2 22.9 %all-to-all-done.3 = bf16[128,16,384]{2,1,0:T(8,128)(2,1)} async-done(((bf16[128,16,384]{2,1,0:T(8,128)(2,1)}), bf16[128,16,384]{2,1,0:T(8,128)(2,1)}, u32[]{:S(2)}, u32[]{:S(2)}) %all-to-all-start.3) | async-done | bytes 1572896 | tf_op jit(solution)/shard_map/all_to_all | solution.py:215
  279.1 3.9 %fusion.24 = bf16[256,384]{1,0:T(8,128)(2,1)} fusion(f32[256,2048]{1,0:T(8,128)S(1)} %select_reduce_fusion, bf16[2048,384]{1,0:T(8,128)(2,1)} %bitcast.43, f32[256,384]{1,0:T(8,128)S(1)} %copy-done.3, bf16[256,384]{1,0:T(8,128)(2,1)S(1)} %copy-done.8), kind=kOutput, calls=%fused_computation.50 | convolution fusion | flops 2416508928 | bytes 4456448 | tf_op jit(solution)/shard_map/dot_general | solution.py:224
  (114 shorter events, 56.6 us)
Async XLA Ops:
  8.1 13.0 %copy-start.6 = (bf16[1,192,1536]{2,1,0:T(8,128)(2,1)S(1)}, bf16[1,192,1536]{2,1,0:T(8,128)(2,1)}, u32[]{:S(2)}) copy-start(bf16[1,192,1536]{2,1,0:T(8,128)(2,1)} %param.17) | copy-start | bytes 1769476
  9.4 12.5 %copy-start.4 = (bf16[1,192,1536]{2,1,0:T(8,128)(2,1)S(1)}, bf16[1,192,1536]{2,1,0:T(8,128)(2,1)}, u32[]{:S(2)}) copy-start(bf16[1,192,1536]{2,1,0:T(8,128)(2,1)} %param.18) | copy-start | bytes 1769476
  9.4 13.4 %copy-start.5 = (bf16[1,192,1536]{2,1,0:T(8,128)(2,1)S(1)}, bf16[1,192,1536]{2,1,0:T(8,128)(2,1)}, u32[]{:S(2)}) copy-start(bf16[1,192,1536]{2,1,0:T(8,128)(2,1)} %param.19) | copy-start | bytes 1769476
  9.4 78.5 %all-to-all-start = ((bf16[32,48,512]{2,1,0:T(8,128)(2,1)}), bf16[32,48,512]{2,1,0:T(8,128)(2,1)}, u32[]{:S(2)}, u32[]{:S(2)}) async-start(bf16[32,48,512]{2,1,0:T(8,128)(2,1)} %broadcast_in_dim.45), calls=%async_computation | async-start | bytes 3145728 | tf_op jit(solution)/shard_map/all_to_all | solution.py:47
  21.1 142.7 %all-gather.2.cloned.1.call-start = ((), (), s32[]{:S(2)}) async-start(), calls=%async_computation.4 | async-start | bytes 1216512 | tf_op jit(solution)/shard_map/all_gather | solution.py:81
  23.6 66.3 %collective-permute-start = (bf16[3,192,1536]{2,1,0:T(8,128)(2,1)}, bf16[3,192,1536]{2,1,0:T(8,128)(2,1)S(1)}, u32[]{:S(2)}, u32[]{:S(2)}) collective-permute-start(bf16[3,192,1536]{2,1,0:T(8,128)(2,1)} %constant_dynamic-update-slice_fusion), channel_id=1, source_target_pairs={{0,2},{1,3},{2,0},{3,1},{4,6},{5,7},{6,4},{7,5},{8,10},{9,11},{10,... | collective-permute-start | bytes 5308424 | tf_op jit(solution)/shard_map/ppermute | solution.py:63
  90.7 1.3 collective-permute-start.1
  92.0 22.6 %collective-permute-start.2 = (bf16[256,256]{1,0:T(8,128)(2,1)S(1)}, bf16[256,256]{1,0:T(8,128)(2,1)S(1)}, u32[]{:S(2)}, u32[]{:S(2)}) collective-permute-start(bf16[256,256]{1,0:T(8,128)(2,1)S(1)} %pad_maximum_fusion.1), channel_id=1, source_target_pairs={{0,4},{1,9},{2,6},{3,11},{4,8},{5,13},{6,10},{7,15},{8,12},{9,17},... | collective-permute-start | bytes 393224 | tf_op jit(solution)/shard_map/ppermute | solution.py:108
  97.4 20.7 %collective-permute-start.3 = (bf16[256,256]{1,0:T(8,128)(2,1)S(1)}, bf16[256,256]{1,0:T(8,128)(2,1)S(1)}, u32[]{:S(2)}, u32[]{:S(2)}) collective-permute-start(bf16[256,256]{1,0:T(8,128)(2,1)S(1)} %pad_maximum_fusion.1), channel_id=1, source_target_pairs={{0,12},{1,17},{2,14},{3,19},{4,16},{5,21},{6,18},{7,23},{8,20},{9,... | collective-permute-start | bytes 393224 | tf_op jit(solution)/shard_map/ppermute | solution.py:108
  103.4 17.9 %collective-permute-start.4 = (bf16[256,256]{1,0:T(8,128)(2,1)S(1)}, bf16[256,256]{1,0:T(8,128)(2,1)S(1)}, u32[]{:S(2)}, u32[]{:S(2)}) collective-permute-start(bf16[256,256]{1,0:T(8,128)(2,1)S(1)} %pad_maximum_fusion.1), channel_id=1, source_target_pairs={{0,20},{1,25},{2,22},{3,27},{4,24},{5,29},{6,26},{7,31},{8,28},{9,... | collective-permute-start | bytes 393224 | tf_op jit(solution)/shard_map/ppermute | solution.py:108
  109.6 14.3 %collective-permute-start.5 = (bf16[256,256]{1,0:T(8,128)(2,1)S(1)}, bf16[256,256]{1,0:T(8,128)(2,1)S(1)}, u32[]{:S(2)}, u32[]{:S(2)}) collective-permute-start(bf16[256,256]{1,0:T(8,128)(2,1)S(1)} %pad_maximum_fusion.1), channel_id=1, source_target_pairs={{0,28},{1,33},{2,30},{3,35},{4,32},{5,37},{6,34},{7,39},{8,36},{9,... | collective-permute-start | bytes 393224 | tf_op jit(solution)/shard_map/ppermute | solution.py:108
  112.1 12.5 %collective-permute-start.6 = (bf16[256,256]{1,0:T(8,128)(2,1)S(1)}, bf16[256,256]{1,0:T(8,128)(2,1)S(1)}, u32[]{:S(2)}, u32[]{:S(2)}) collective-permute-start(bf16[256,256]{1,0:T(8,128)(2,1)S(1)} %pad_maximum_fusion.1), channel_id=1, source_target_pairs={{0,36},{1,41},{2,38},{3,43},{4,40},{5,45},{6,42},{7,47},{8,44},{9,... | collective-permute-start | bytes 393224 | tf_op jit(solution)/shard_map/ppermute | solution.py:108
  114.6 10.6 %collective-permute-start.7 = (bf16[256,256]{1,0:T(8,128)(2,1)S(1)}, bf16[256,256]{1,0:T(8,128)(2,1)S(1)}, u32[]{:S(2)}, u32[]{:S(2)}) collective-permute-start(bf16[256,256]{1,0:T(8,128)(2,1)S(1)} %pad_maximum_fusion.1), channel_id=1, source_target_pairs={{0,44},{1,49},{2,46},{3,51},{4,48},{5,53},{6,50},{7,55},{8,52},{9,... | collective-permute-start | bytes 393224 | tf_op jit(solution)/shard_map/ppermute | solution.py:108
  118.1 7.8 %collective-permute-start.8 = (bf16[256,256]{1,0:T(8,128)(2,1)S(1)}, bf16[256,256]{1,0:T(8,128)(2,1)S(1)}, u32[]{:S(2)}, u32[]{:S(2)}) collective-permute-start(bf16[256,256]{1,0:T(8,128)(2,1)S(1)} %pad_maximum_fusion.1), channel_id=1, source_target_pairs={{0,52},{1,57},{2,54},{3,59},{4,56},{5,61},{6,58},{7,63},{8,60},{9,... | collective-permute-start | bytes 393224 | tf_op jit(solution)/shard_map/ppermute | solution.py:108
  121.3 5.4 %collective-permute-start.9 = (bf16[256,256]{1,0:T(8,128)(2,1)S(1)}, bf16[256,256]{1,0:T(8,128)(2,1)S(1)}, u32[]{:S(2)}, u32[]{:S(2)}) collective-permute-start(bf16[256,256]{1,0:T(8,128)(2,1)S(1)} %pad_maximum_fusion.1), channel_id=1, source_target_pairs={{0,60},{1,65},{2,62},{3,67},{4,64},{5,69},{6,66},{7,71},{8,68},{9,... | collective-permute-start | bytes 393224 | tf_op jit(solution)/shard_map/ppermute | solution.py:108
  127.4 12.0 %collective-permute-start.10 = (bf16[8,256,256]{2,1,0:T(8,128)(2,1)}, bf16[8,256,256]{2,1,0:T(8,128)(2,1)}, u32[]{:S(2)}, u32[]{:S(2)}) collective-permute-start(bf16[8,256,256]{2,1,0:T(8,128)(2,1)} %bitcast_dynamic-update-slice_fusion), channel_id=1, source_target_pairs={{0,1},{1,0},{2,3},{3,2},{4,5},{5,4},{6,7},{7,6},{8,9},{9,8},{10,11... | collective-permute-start | bytes 3145736 | tf_op jit(solution)/shard_map/ppermute | solution.py:110
  165.6 5.4 %copy-start.10 = (s32[256,4]{0,1:T(4,128)S(1)}, s32[256,4]{0,1:T(4,128)}, u32[]{:S(2)}) copy-start(s32[256,4]{0,1:T(4,128)} %param.15) | copy-start | bytes 12292
  166.6 15.0 %all-to-all-start.1 = ((bf16[256,4,384]{2,0,1:T(8,128)(2,1)}), bf16[256,4,384]{2,0,1:T(8,128)(2,1)}, u32[]{:S(2)}, u32[]{:S(2)}) async-start(bf16[256,4,384]{2,0,1:T(8,128)(2,1)} %bitcast.128), calls=%async_computation.1 | async-start | bytes 1572864 | tf_op jit(solution)/shard_map/all_to_all | solution.py:160
  186.0 33.5 %all-to-all-start.2 = ((bf16[128,16,384]{2,1,0:T(8,128)(2,1)}), bf16[128,16,384]{2,1,0:T(8,128)(2,1)S(1)}, u32[]{:S(2)}, u32[]{:S(2)}) async-start(bf16[128,16,384]{2,1,0:T(8,128)(2,1)} %bitcast.23), calls=%async_computation.2 | async-start | bytes 3145728 | tf_op jit(solution)/shard_map/all_to_all | solution.py:186
  198.5 35.8 %collective-permute-start.11 = (bf16[2,3,192,1536]{3,2,1,0:T(8,128)(2,1)}, bf16[2,3,192,1536]{3,2,1,0:T(8,128)(2,1)}, u32[]{:S(2)}, u32[]{:S(2)}) collective-permute-start(bf16[2,3,192,1536]{3,2,1,0:T(8,128)(2,1)} %pad_maximum_fusion), channel_id=1, source_target_pairs={{0,1},{1,0},{2,3},{3,2},{4,5},{5,4},{6,7},{7,6},{8,9},{9,8},{10,11... | collective-permute-start | bytes 10616840 | tf_op jit(solution)/shard_map/ppermute | solution.py:77
  249.1 5.6 %copy-start.9 = (f32[256,4]{0,1:T(4,128)S(1)}, f32[256,4]{0,1:T(4,128)}, u32[]{:S(2)}) copy-start(f32[256,4]{0,1:T(4,128)} %param.16) | copy-start | bytes 12292
  249.1 30.0 %copy-start.3 = (f32[256,384]{1,0:T(8,128)S(1)}, f32[256,384]{1,0:T(8,128)}, u32[]{:S(2)}) copy-start(f32[256,384]{1,0:T(8,128)} %copy-done.2) | copy-start | bytes 1179652
  249.1 30.0 %copy-start.8 = (bf16[256,384]{1,0:T(8,128)(2,1)S(1)}, bf16[256,384]{1,0:T(8,128)(2,1)}, u32[]{:S(2)}) copy-start(bf16[256,384]{1,0:T(8,128)(2,1)} %param.10) | copy-start | bytes 589828
  249.1 30.0 %all-to-all-start.3 = ((bf16[128,16,384]{2,1,0:T(8,128)(2,1)}), bf16[128,16,384]{2,1,0:T(8,128)(2,1)}, u32[]{:S(2)}, u32[]{:S(2)}) async-start(bf16[128,16,384]{2,1,0:T(8,128)(2,1)} %bitcast.42), calls=%async_computation.3 | async-start | bytes 3145728 | tf_op jit(solution)/shard_map/all_to_all | solution.py:215
  (5 other events, 12.0 us)
Sparse Core Ops, SparseCore 0:
  24.8 71.9 all-gather.1

commit v12 on v9

--- a/solution.py
+++ b/solution.py
@@ -43,7 +43,7 @@
 
 
 def attention_kernel(
-    pairs, heads, q_ref, fetched_ref, partner_ref, own_ref, qi_ref, qp_ref, ki_ref, kp_ref, o_ref,
+    pairs, q_ref, fetched_ref, partner_ref, own_ref, qi_ref, qp_ref, ki_ref, kp_ref, o_ref,
     m_sc, l_sc, acc_sc
 ):
     step = pl.program_id(0)
@@ -54,27 +54,26 @@
         l_sc[...] = jnp.zeros(l_sc.shape, jnp.float32)
         acc_sc[...] = jnp.zeros(acc_sc.shape, jnp.float32)
 
-    rows = qi_ref.shape[0]
-    key_at = ki_ref[0]
+    key_at = ki_ref[...]
     spacing = qi_ref[...] - key_at
-    allowed = (qp_ref[...] == kp_ref[0]) & (spacing >= 0) & (spacing < WINDOW) & (key_at >= 0)
+    allowed = (qp_ref[...] == kp_ref[...]) & (spacing >= 0) & (spacing < WINDOW) & (key_at >= 0)
 
     def update(block, allowed):
         keys = block[:, :HD]
         values = block[:, HD:]
         scores = lax.dot_general(
-            q_ref[...], keys, (((1,), (1,)), ((), ())), preferred_element_type=jnp.float32
+            keys, q_ref[...], (((1,), (1,)), ((), ())), preferred_element_type=jnp.float32
         ) * HD ** (-0.5)
-        masked = jnp.concatenate(
-            [jnp.where(allowed, scores[h * rows : (h + 1) * rows], -1e30) for h in range(heads)],
-            axis=0,
-        )
+        masked = jnp.where(allowed, scores, -1e30)
         m_old = m_sc[...]
-        m_new = jnp.maximum(m_old, jnp.max(masked, axis=1, keepdims=True))
+        m_new = jnp.maximum(m_old, jnp.max(masked, axis=0, keepdims=True))
         alpha = jnp.exp(m_old - m_new)
         probs = jnp.exp(masked - m_new)
-        l_sc[...] = alpha * l_sc[...] + jnp.sum(probs, axis=1, keepdims=True)
-        mixed = jnp.dot(probs.astype(jnp.bfloat16), values, preferred_element_type=jnp.float32)
+        l_sc[...] = alpha * l_sc[...] + jnp.sum(probs, axis=0, keepdims=True)
+        mixed = lax.dot_general(
+            values, probs.astype(jnp.bfloat16), (((0,), (0,)), ((), ())),
+            preferred_element_type=jnp.float32,
+        )
         acc_sc[...] = alpha * acc_sc[...] + mixed
         m_sc[...] = m_new
 
@@ -90,7 +89,7 @@
 
     @pl.when(step == 2 * pairs)
     def _():
-        update(own_ref[...], allowed[:, : own_ref.shape[0]])
+        update(own_ref[...], allowed[: own_ref.shape[0]])
 
     @pl.when(step == pl.num_programs(0) - 1)
     def _():
@@ -102,32 +101,35 @@
     half, block, width = fetched.shape
     pairs = half // 2
     last = pairs - 1
-    return pl.pallas_call(
-        functools.partial(attention_kernel, pairs, heads),
+    cols = heads * rows
+    out_t = pl.pallas_call(
+        functools.partial(attention_kernel, pairs),
         grid=(2 * pairs + 1,),
         in_specs=[
-            pl.BlockSpec((heads * rows, HD), lambda j: (0, 0)),
+            pl.BlockSpec((cols, HD), lambda j: (0, 0)),
             pl.BlockSpec((2, block, width), lambda j: (jnp.minimum(j, last), 0, 0)),
             pl.BlockSpec(
                 (2, block, width), lambda j: (jnp.minimum(jnp.maximum(j - pairs, 0), last), 0, 0)
             ),
             pl.BlockSpec((block, width), lambda j: (0, 0)),
-            pl.BlockSpec((rows, 1), lambda j: (0, 0)),
-            pl.BlockSpec((rows, 1), lambda j: (0, 0)),
-            pl.BlockSpec((1, 1, 2 * block), lambda j: (j, 0, 0)),
-            pl.BlockSpec((1, 1, 2 * block), lambda j: (j, 0, 0)),
+            pl.BlockSpec((1, cols), lambda j: (0, 0)),
+            pl.BlockSpec((1, cols), lambda j: (0, 0)),
+            pl.BlockSpec((2 * block, 1), lambda j: (j, 0)),
+            pl.BlockSpec((2 * block, 1), lambda j: (j, 0)),
         ],
-        out_specs=pl.BlockSpec((heads * rows, HD), lambda j: (0, 0)),
-        out_shape=jax.ShapeDtypeStruct((heads * rows, HD), jnp.bfloat16),
+        out_specs=pl.BlockSpec((HD, cols), lambda j: (0, 0)),
+        out_shape=jax.ShapeDtypeStruct((HD, cols), jnp.bfloat16),
         scratch_shapes=[
-            pltpu.VMEM((heads * rows, 1), jnp.float32),
-            pltpu.VMEM((heads * rows, 1), jnp.float32),
-            pltpu.VMEM((heads * rows, HD), jnp.float32),
+            pltpu.VMEM((1, cols), jnp.float32),
+            pltpu.VMEM((1, cols), jnp.float32),
+            pltpu.VMEM((HD, cols), jnp.float32),
         ],
     )(
-        queries.reshape(heads * rows, HD), fetched, partner, own, query_at, query_prompt, key_at,
-        key_prompt,
-    ).reshape(heads, rows, HD)
+        queries.reshape(cols, HD), fetched, partner, own,
+        jnp.tile(query_at, heads)[None, :], jnp.tile(query_prompt, heads)[None, :],
+        key_at.reshape(-1, 1), key_prompt.reshape(-1, 1),
+    )
+    return out_t.T.reshape(heads, rows, HD)
 
 
 def gather_seq(piece, count):
@@ -215,8 +217,8 @@
         fetched,
         partner,
         kv_own,
-        own_index[:, None],
-        query_prompt[:, None],
+        own_index,
+        query_prompt,
         key_index,
         key_prompt,
     )

time: 258 us -> 250 us (0.969)
  blocking collectives: 64.7 us -> 56 us
  Pallas kernels: 23 us -> 19.4 us
  starting transfers between devices: 75.6 us -> 78.6 us
    all_gather x1, blocking collectives: 29.1 us -> 21 us  [local(): whole = lax.all_gather(hidden_in, 'mp', axis=1, tiled=True)]
    pallas_call x1, Pallas kernels: 23 us -> 19.4 us  [attention(): pl.pallas_call(functools.partial(attention_kernel, pairs), grid=(2 * pair...]
  transfers between devices with their start and end apart: 15 -> 15, of which waited for: 5 -> 5; matrix products, arithmetic and copies ran while one was open for 8% -> 9% of each run, Pallas kernels for 9% -> 8%
where the time goes in v12:
time: 250 us; the launch traced here: 249 us
  starting transfers between devices  78.6 us (31%)
  blocking collectives  56 us (22%)
  waiting for transfers between devices  34.5 us (14%)
  Pallas kernels  19.4 us (8%)
  matrix products  17.9 us (7%)
  local copies, waits for them, and re-layouts  15.8 us (6%)
  between operations  15.3 us (6%)
  other arithmetic  11.6 us (5%)
    ppermute x8, starting transfers between devices, local(): fetched.append(lax.ppermute(kv_own, ('seq', 'mp'), pairs))  43.8 us
    all_to_all x1, blocking collectives, local(): arrived = lax.all_to_all(buffer, ('seq', 'mp'), 0, 0, tiled=True)  35 us
    all_to_all x1, waiting for transfers between devices, local(): returned = lax.all_to_all(outgoing, ('seq', 'mp'), 0, 0, tiled=True)  22.9 us
    all_to_all x2, starting transfers between devices, gather_seq(): return lax.all_to_all(spread, 'seq', 0, 0, tiled=True)  22.5 us
    all_gather x1, blocking collectives, local(): whole = lax.all_gather(hidden_in, 'mp', axis=1, tiled=True)  21 us
    pallas_call x1, Pallas kernels, attention(): pl.pallas_call(functools.partial(attention_kernel, pairs), grid=(2 * pair...  19.4 us
    all_to_all x1, waiting for transfers between devices, local(): lax.all_to_all(partial_out.astype(jnp.bfloat16), 'mp', 1, 0, tiled=True)  8.34 us
    dot_general x1, matrix products, local(): jnp.dot(active, w_down, preferred_element_type=jnp.float32)  7.2 us
  transfers between devices with their start and end apart: 15, of which 5 were waited for; matrix products, arithmetic and copies ran while one was open for 9% of the time, Pallas kernels for 8%

profile of v12, /device:TPU:1, one launch (start us, length us, event | category | flops | bytes accessed | tf_op | source)
XLA Modules:
  0.0 249.2 jit_solution(9538478337489377438)
XLA Ops:
  9.5 11.5 %all-to-all-start = ((bf16[32,48,512]{2,1,0:T(8,128)(2,1)}), bf16[32,48,512]{2,1,0:T(8,128)(2,1)S(1)}, u32[]{:S(2)}, u32[]{:S(2)}) async-start(bf16[32,48,512]{2,1,0:T(8,128)(2,1)} %broadcast_in_dim.28), calls=%async_computation | async-start | bytes 3145728 | tf_op jit(solution)/shard_map/all_to_all | solution.py:140
  21.1 2.6 %pad_maximum_fusion = bf16[3,192,1536]{2,1,0:T(8,128)(2,1)} fusion(bf16[1,192,1536]{2,1,0:T(8,128)(2,1)S(1)} %copy-done.6, bf16[1,192,1536]{2,1,0:T(8,128)(2,1)S(1)} %copy-done.7, bf16[1,192,1536]{2,1,0:T(8,128)(2,1)} %param.17), kind=kLoop, calls=%fused_computation.22 | loop fusion | flops 1769472 | bytes 3538944 | tf_op jit(solution)/shard_map/concatenate | solution.py:156
  27.1 21.0 %all_gather.6 = bf16[256,1536]{1,0:T(8,128)(2,1)S(1)} all-gather(bf16[256,384]{1,0:T(8,128)(2,1)S(1)} %copy-done.2), channel_id=1, replica_groups=mesh['seq'=32,'mp'=4] {'mp'}, dimensions={1}, use_global_device_ids=true | all-gather | bytes 983040 | tf_op jit(solution)/shard_map/all_gather | solution.py:164
  51.1 5.4 %collective-permute-start.1 = (bf16[256,256]{1,0:T(8,128)(2,1)S(1)}, bf16[256,256]{1,0:T(8,128)(2,1)S(1)}, u32[]{:S(2)}, u32[]{:S(2)}) collective-permute-start(bf16[256,256]{1,0:T(8,128)(2,1)S(1)} %pad_maximum_fusion.1.own_ref), channel_id=1, source_target_pairs={{0,4},{1,9},{2,6},{3,11},{4,8},{5,13},{6,10},{7,15},{8,12},{9,17},... | collective-permute-start | bytes 393224 | tf_op jit(solution)/shard_map/ppermute | solution.py:198
  56.5 2.5 convert_add_fusion.kp_ref
  60.1 11.0 %all-to-all-start.1 = ((bf16[32,48,384]{2,1,0:T(8,128)(2,1)}), bf16[32,48,384]{2,1,0:T(8,128)(2,1)S(1)}, u32[]{:S(2)}, u32[]{:S(2)}) async-start(bf16[32,48,384]{2,1,0:T(8,128)(2,1)} %broadcast_in_dim.36), calls=%async_computation.1 | async-start | bytes 2359296 | tf_op jit(solution)/shard_map/all_to_all | solution.py:140
  71.2 4.8 %collective-permute-start.2 = (bf16[256,256]{1,0:T(8,128)(2,1)S(1)}, bf16[256,256]{1,0:T(8,128)(2,1)S(1)}, u32[]{:S(2)}, u32[]{:S(2)}) collective-permute-start(bf16[256,256]{1,0:T(8,128)(2,1)S(1)} %pad_maximum_fusion.1.own_ref), channel_id=1, source_target_pairs={{0,12},{1,17},{2,14},{3,19},{4,16},{5,21},{6,18},{7,23},{8,20},{9,... | collective-permute-start | bytes 393224 | tf_op jit(solution)/shard_map/ppermute | solution.py:198
  75.9 5.5 %collective-permute-start.3 = (bf16[256,256]{1,0:T(8,128)(2,1)S(1)}, bf16[256,256]{1,0:T(8,128)(2,1)S(1)}, u32[]{:S(2)}, u32[]{:S(2)}) collective-permute-start(bf16[256,256]{1,0:T(8,128)(2,1)S(1)} %pad_maximum_fusion.1.own_ref), channel_id=1, source_target_pairs={{0,20},{1,25},{2,22},{3,27},{4,24},{5,29},{6,26},{7,31},{8,28},{9,... | collective-permute-start | bytes 393224 | tf_op jit(solution)/shard_map/ppermute | solution.py:198
  81.4 3.1 %collective-permute-start.4 = (bf16[256,256]{1,0:T(8,128)(2,1)S(1)}, bf16[256,256]{1,0:T(8,128)(2,1)S(1)}, u32[]{:S(2)}, u32[]{:S(2)}) collective-permute-start(bf16[256,256]{1,0:T(8,128)(2,1)S(1)} %pad_maximum_fusion.1.own_ref), channel_id=1, source_target_pairs={{0,28},{1,33},{2,30},{3,35},{4,32},{5,37},{6,34},{7,39},{8,36},{9,... | collective-permute-start | bytes 393224 | tf_op jit(solution)/shard_map/ppermute | solution.py:198
  84.5 2.9 %collective-permute-start.5 = (bf16[256,256]{1,0:T(8,128)(2,1)S(1)}, bf16[256,256]{1,0:T(8,128)(2,1)S(1)}, u32[]{:S(2)}, u32[]{:S(2)}) collective-permute-start(bf16[256,256]{1,0:T(8,128)(2,1)S(1)} %pad_maximum_fusion.1.own_ref), channel_id=1, source_target_pairs={{0,36},{1,41},{2,38},{3,43},{4,40},{5,45},{6,42},{7,47},{8,44},{9,... | collective-permute-start | bytes 393224 | tf_op jit(solution)/shard_map/ppermute | solution.py:198
  87.4 4.3 %collective-permute-start.6 = (bf16[256,256]{1,0:T(8,128)(2,1)S(1)}, bf16[256,256]{1,0:T(8,128)(2,1)S(1)}, u32[]{:S(2)}, u32[]{:S(2)}) collective-permute-start(bf16[256,256]{1,0:T(8,128)(2,1)S(1)} %pad_maximum_fusion.1.own_ref), channel_id=1, source_target_pairs={{0,44},{1,49},{2,46},{3,51},{4,48},{5,53},{6,50},{7,55},{8,52},{9,... | collective-permute-start | bytes 393224 | tf_op jit(solution)/shard_map/ppermute | solution.py:198
  92.8 14.7 %collective-permute-start.7 = (bf16[256,256]{1,0:T(8,128)(2,1)S(1)}, bf16[256,256]{1,0:T(8,128)(2,1)S(1)}, u32[]{:S(2)}, u32[]{:S(2)}) collective-permute-start(bf16[256,256]{1,0:T(8,128)(2,1)S(1)} %pad_maximum_fusion.1.own_ref), channel_id=1, source_target_pairs={{0,52},{1,57},{2,54},{3,59},{4,56},{5,61},{6,58},{7,63},{8,60},{9,... | collective-permute-start | bytes 393224 | tf_op jit(solution)/shard_map/ppermute | solution.py:198
  107.6 3.1 %collective-permute-start.8 = (bf16[256,256]{1,0:T(8,128)(2,1)S(1)}, bf16[256,256]{1,0:T(8,128)(2,1)S(1)}, u32[]{:S(2)}, u32[]{:S(2)}) collective-permute-start(bf16[256,256]{1,0:T(8,128)(2,1)S(1)} %pad_maximum_fusion.1.own_ref), channel_id=1, source_target_pairs={{0,60},{1,65},{2,62},{3,67},{4,64},{5,69},{6,66},{7,71},{8,68},{9,... | collective-permute-start | bytes 393224 | tf_op jit(solution)/shard_map/ppermute | solution.py:198
  112.6 2.9 %collective-permute-start.9 = (bf16[8,256,256]{2,1,0:T(8,128)(2,1)S(1)}, bf16[8,256,256]{2,1,0:T(8,128)(2,1)}, u32[]{:S(2)}, u32[]{:S(2)}) collective-permute-start(bf16[8,256,256]{2,1,0:T(8,128)(2,1)S(1)} %bitcast_dynamic-update-slice_fusion.fetched_ref), channel_id=1, source_target_pairs={{0,1},{1,0},{2,3},{3,2},{4,5},{5,4},{6,7},{7,6},{8,9},{9,8},{10,11... | collective-permute-start | bytes 3145736 | tf_op jit(solution)/shard_map/ppermute | solution.py:200
  118.2 19.4 %shard_map.100 = bf16[128,768]{1,0:T(8,128)(2,1)} custom-call(bf16[768,128]{1,0:T(8,128)(2,1)} %bitcast.102, bf16[8,256,256]{2,1,0:T(8,128)(2,1)} %copy-done.3, bf16[8,256,256]{2,1,0:T(8,128)(2,1)} %collective-permute-done.9.partner_ref, bf16[256,256]{1,0:T(8,128)(2,1)} %copy-done.8, s32[1,768]{1,0:T(1,128)} %bitcast.107, s32[1,768]{1,0:T(1,128)} %bitcast.106, ...), custom_call_target="tpu_custom_call" | custom-call | tf_op jit(solution)/shard_map/pallas_call | solution.py:105
  140.4 3.7 %all-to-all-start.2 = ((bf16[256,4,384]{2,0,1:T(8,128)(2,1)}), bf16[256,4,384]{2,0,1:T(8,128)(2,1)S(1)}, u32[]{:S(2)}, u32[]{:S(2)}) async-start(bf16[256,4,384]{2,0,1:T(8,128)(2,1)} %bitcast.89), calls=%async_computation.2 | async-start | bytes 1572864 | tf_op jit(solution)/shard_map/all_to_all | solution.py:229
  146.5 8.3 %all-to-all-done.2 = bf16[256,4,384]{2,0,1:T(8,128)(2,1)S(1)} async-done(((bf16[256,4,384]{2,0,1:T(8,128)(2,1)}), bf16[256,4,384]{2,0,1:T(8,128)(2,1)S(1)}, u32[]{:S(2)}, u32[]{:S(2)}) %all-to-all-start.2) | async-done | bytes 786464 | tf_op jit(solution)/shard_map/all_to_all | solution.py:229
  155.7 35.0 %all_to_all.52 = bf16[128,16,384]{2,1,0:T(8,128)(2,1)S(1)} all-to-all(bf16[128,16,384]{2,1,0:T(8,128)(2,1)S(1)} %bitcast.92), channel_id=1, replica_groups=mesh['seq'=32,'mp'=4] {'seq','mp'}, dimensions={0} | all-to-all | bytes 3145728 | tf_op jit(solution)/shard_map/all_to_all | solution.py:255
  192.5 4.3 %fusion.5 = f32[512,768]{1,0:T(8,128)} fusion(bf16[512,1536]{1,0:T(8,128)(2,1)S(1)} %bitcast.97, bf16[3,768,1536]{2,1,0:T(8,128)(2,1)} %all-gather.2.cloned.1.call-done), kind=kOutput, calls=%fused_computation.16 | convolution fusion | flops 1207959552 | bytes 5505024 | tf_op jit(solution)/shard_map/dot_general | solution.py:273
  196.9 7.2 %convolution_convert_fusion = bf16[512,1536]{1,0:T(8,128)(2,1)} fusion(bf16[3,768,1536]{2,1,0:T(8,128)(2,1)} %all-gather.2.cloned.1.call-done, f32[512,768]{1,0:T(8,128)} %fusion.5, bf16[512,1536]{1,0:T(8,128)(2,1)S(1)} %bitcast.98), kind=kOutput, calls=%fused_computation.11 | convolution fusion | flops 2417885184 | bytes 9437184 | tf_op jit(solution)/shard_map/dot_general | solution.py:277
  204.1 3.0 %reshape.321 = bf16[32,16,4,384]{3,2,1,0:T(4,128)(2,1)S(1)} reshape(bf16[512,1536]{1,0:T(8,128)(2,1)} %convolution_convert_fusion) | data formatting | bytes 3145728 | tf_op jit(solution)/shard_map/reshape | solution.py:279
  208.5 5.6 %all-to-all-start.4 = ((bf16[128,16,384]{2,1,0:T(8,128)(2,1)}), bf16[128,16,384]{2,1,0:T(8,128)(2,1)}, u32[]{:S(2)}, u32[]{:S(2)}) async-start(bf16[128,16,384]{2,1,0:T(8,128)(2,1)} %bitcast.30), calls=%async_computation.4 | async-start | bytes 3145728 | tf_op jit(solution)/shard_map/all_to_all | solution.py:283
  215.5 22.9 %all-to-all-done.4 = bf16[128,16,384]{2,1,0:T(8,128)(2,1)} async-done(((bf16[128,16,384]{2,1,0:T(8,128)(2,1)}), bf16[128,16,384]{2,1,0:T(8,128)(2,1)}, u32[]{:S(2)}, u32[]{:S(2)}) %all-to-all-start.4) | async-done | bytes 1572896 | tf_op jit(solution)/shard_map/all_to_all | solution.py:283
  238.4 3.9 %fusion.10 = bf16[256,384]{1,0:T(8,128)(2,1)} fusion(f32[256,2048]{1,0:T(8,128)S(1)} %select_reduce_fusion, bf16[2048,384]{1,0:T(8,128)(2,1)} %bitcast.31, f32[256,384]{1,0:T(8,128)S(1)} %convert_reduce_fusion, bf16[256,384]{1,0:T(8,128)(2,1)S(1)} %copy-done.2), kind=kOutput, calls=%fused_computation.29 | convolution fusion | flops 2416508928 | bytes 4456448 | tf_op jit(solution)/shard_map/dot_general | solution.py:292
  (106 shorter events, 25.4 us)
Async XLA Ops:
  9.5 11.5 %copy-start.6 = (bf16[1,192,1536]{2,1,0:T(8,128)(2,1)S(1)}, bf16[1,192,1536]{2,1,0:T(8,128)(2,1)}, u32[]{:S(2)}) copy-start(bf16[1,192,1536]{2,1,0:T(8,128)(2,1)} %param.19) | copy-start | bytes 1769476
  9.5 11.5 %copy-start.7 = (bf16[1,192,1536]{2,1,0:T(8,128)(2,1)S(1)}, bf16[1,192,1536]{2,1,0:T(8,128)(2,1)}, u32[]{:S(2)}) copy-start(bf16[1,192,1536]{2,1,0:T(8,128)(2,1)} %param.18) | copy-start | bytes 1769476
  9.5 38.9 %all-to-all-start = ((bf16[32,48,512]{2,1,0:T(8,128)(2,1)}), bf16[32,48,512]{2,1,0:T(8,128)(2,1)S(1)}, u32[]{:S(2)}, u32[]{:S(2)}) async-start(bf16[32,48,512]{2,1,0:T(8,128)(2,1)} %broadcast_in_dim.28), calls=%async_computation | async-start | bytes 3145728 | tf_op jit(solution)/shard_map/all_to_all | solution.py:140
  21.0 171.5 %all-gather.2.cloned.1.call-start = ((), (), s32[]{:S(2)}) async-start(), calls=%async_computation.5 | async-start | bytes 8847360 | tf_op jit(solution)/shard_map/all_gather | solution.py:155
  49.7 1.3 collective-permute-start
  50.7 8.3 %copy-start.1 = (s32[1,4608]{0,1:T(8,128)}, s32[1,4608]{0,1:T(8,128)S(1)}, u32[]{:S(2)}) copy-start(s32[1,4608]{0,1:T(8,128)S(1)} %copy.88) | copy-start | bytes 55300
  51.1 56.5 %copy-start.8 = (bf16[256,256]{1,0:T(8,128)(2,1)}, bf16[256,256]{1,0:T(8,128)(2,1)S(1)}, u32[]{:S(2)}) copy-start(bf16[256,256]{1,0:T(8,128)(2,1)S(1)} %pad_maximum_fusion.1.own_ref) | copy-start | bytes 393220
  51.1 7.9 %copy-start.9 = (bf16[384,48]{0,1:T(8,128)(2,1)S(1)}, bf16[384,48]{0,1:T(8,128)(2,1)}, u32[]{:S(2)}) copy-start(bf16[384,48]{0,1:T(8,128)(2,1)} %param.13) | copy-start | bytes 110596
  51.1 36.3 %collective-permute-start.1 = (bf16[256,256]{1,0:T(8,128)(2,1)S(1)}, bf16[256,256]{1,0:T(8,128)(2,1)S(1)}, u32[]{:S(2)}, u32[]{:S(2)}) collective-permute-start(bf16[256,256]{1,0:T(8,128)(2,1)S(1)} %pad_maximum_fusion.1.own_ref), channel_id=1, source_target_pairs={{0,4},{1,9},{2,6},{3,11},{4,8},{5,13},{6,10},{7,15},{8,12},{9,17},... | collective-permute-start | bytes 393224 | tf_op jit(solution)/shard_map/ppermute | solution.py:198
  60.1 78.7 %all-to-all-start.1 = ((bf16[32,48,384]{2,1,0:T(8,128)(2,1)}), bf16[32,48,384]{2,1,0:T(8,128)(2,1)S(1)}, u32[]{:S(2)}, u32[]{:S(2)}) async-start(bf16[32,48,384]{2,1,0:T(8,128)(2,1)} %broadcast_in_dim.36), calls=%async_computation.1 | async-start | bytes 2359296 | tf_op jit(solution)/shard_map/all_to_all | solution.py:140
  71.1 45.9 %copy-start.5 = (f32[256,512]{1,0:T(8,128)S(1)}, f32[256,512]{1,0:T(8,128)}, u32[]{:S(2)}) copy-start(f32[256,512]{1,0:T(8,128)} %copy-done.4) | copy-start | bytes 1572868
  71.2 21.7 %collective-permute-start.2 = (bf16[256,256]{1,0:T(8,128)(2,1)S(1)}, bf16[256,256]{1,0:T(8,128)(2,1)S(1)}, u32[]{:S(2)}, u32[]{:S(2)}) collective-permute-start(bf16[256,256]{1,0:T(8,128)(2,1)S(1)} %pad_maximum_fusion.1.own_ref), channel_id=1, source_target_pairs={{0,12},{1,17},{2,14},{3,19},{4,16},{5,21},{6,18},{7,23},{8,20},{9,... | collective-permute-start | bytes 393224 | tf_op jit(solution)/shard_map/ppermute | solution.py:198
  75.9 31.6 %collective-permute-start.3 = (bf16[256,256]{1,0:T(8,128)(2,1)S(1)}, bf16[256,256]{1,0:T(8,128)(2,1)S(1)}, u32[]{:S(2)}, u32[]{:S(2)}) collective-permute-start(bf16[256,256]{1,0:T(8,128)(2,1)S(1)} %pad_maximum_fusion.1.own_ref), channel_id=1, source_target_pairs={{0,20},{1,25},{2,22},{3,27},{4,24},{5,29},{6,26},{7,31},{8,28},{9,... | collective-permute-start | bytes 393224 | tf_op jit(solution)/shard_map/ppermute | solution.py:198
  81.4 29.3 %collective-permute-start.4 = (bf16[256,256]{1,0:T(8,128)(2,1)S(1)}, bf16[256,256]{1,0:T(8,128)(2,1)S(1)}, u32[]{:S(2)}, u32[]{:S(2)}) collective-permute-start(bf16[256,256]{1,0:T(8,128)(2,1)S(1)} %pad_maximum_fusion.1.own_ref), channel_id=1, source_target_pairs={{0,28},{1,33},{2,30},{3,35},{4,32},{5,37},{6,34},{7,39},{8,36},{9,... | collective-permute-start | bytes 393224 | tf_op jit(solution)/shard_map/ppermute | solution.py:198
  84.5 26.2 %collective-permute-start.5 = (bf16[256,256]{1,0:T(8,128)(2,1)S(1)}, bf16[256,256]{1,0:T(8,128)(2,1)S(1)}, u32[]{:S(2)}, u32[]{:S(2)}) collective-permute-start(bf16[256,256]{1,0:T(8,128)(2,1)S(1)} %pad_maximum_fusion.1.own_ref), channel_id=1, source_target_pairs={{0,36},{1,41},{2,38},{3,43},{4,40},{5,45},{6,42},{7,47},{8,44},{9,... | collective-permute-start | bytes 393224 | tf_op jit(solution)/shard_map/ppermute | solution.py:198
  87.4 23.3 %collective-permute-start.6 = (bf16[256,256]{1,0:T(8,128)(2,1)S(1)}, bf16[256,256]{1,0:T(8,128)(2,1)S(1)}, u32[]{:S(2)}, u32[]{:S(2)}) collective-permute-start(bf16[256,256]{1,0:T(8,128)(2,1)S(1)} %pad_maximum_fusion.1.own_ref), channel_id=1, source_target_pairs={{0,44},{1,49},{2,46},{3,51},{4,48},{5,53},{6,50},{7,55},{8,52},{9,... | collective-permute-start | bytes 393224 | tf_op jit(solution)/shard_map/ppermute | solution.py:198
  92.8 18.0 %collective-permute-start.7 = (bf16[256,256]{1,0:T(8,128)(2,1)S(1)}, bf16[256,256]{1,0:T(8,128)(2,1)S(1)}, u32[]{:S(2)}, u32[]{:S(2)}) collective-permute-start(bf16[256,256]{1,0:T(8,128)(2,1)S(1)} %pad_maximum_fusion.1.own_ref), channel_id=1, source_target_pairs={{0,52},{1,57},{2,54},{3,59},{4,56},{5,61},{6,58},{7,63},{8,60},{9,... | collective-permute-start | bytes 393224 | tf_op jit(solution)/shard_map/ppermute | solution.py:198
  107.6 5.0 %collective-permute-start.8 = (bf16[256,256]{1,0:T(8,128)(2,1)S(1)}, bf16[256,256]{1,0:T(8,128)(2,1)S(1)}, u32[]{:S(2)}, u32[]{:S(2)}) collective-permute-start(bf16[256,256]{1,0:T(8,128)(2,1)S(1)} %pad_maximum_fusion.1.own_ref), channel_id=1, source_target_pairs={{0,60},{1,65},{2,62},{3,67},{4,64},{5,69},{6,66},{7,71},{8,68},{9,... | collective-permute-start | bytes 393224 | tf_op jit(solution)/shard_map/ppermute | solution.py:198
  112.6 5.5 %copy-start.3 = (bf16[8,256,256]{2,1,0:T(8,128)(2,1)}, bf16[8,256,256]{2,1,0:T(8,128)(2,1)S(1)}, u32[]{:S(2)}) copy-start(bf16[8,256,256]{2,1,0:T(8,128)(2,1)S(1)} %bitcast_dynamic-update-slice_fusion.fetched_ref) | copy-start | bytes 3145732
  112.6 5.5 %collective-permute-start.9 = (bf16[8,256,256]{2,1,0:T(8,128)(2,1)S(1)}, bf16[8,256,256]{2,1,0:T(8,128)(2,1)}, u32[]{:S(2)}, u32[]{:S(2)}) collective-permute-start(bf16[8,256,256]{2,1,0:T(8,128)(2,1)S(1)} %bitcast_dynamic-update-slice_fusion.fetched_ref), channel_id=1, source_target_pairs={{0,1},{1,0},{2,3},{3,2},{4,5},{5,4},{6,7},{7,6},{8,9},{9,8},{10,11... | collective-permute-start | bytes 3145736 | tf_op jit(solution)/shard_map/ppermute | solution.py:200
  139.5 4.7 %copy-start.11 = (s32[256,4]{0,1:T(4,128)S(1)}, s32[256,4]{0,1:T(4,128)}, u32[]{:S(2)}) copy-start(s32[256,4]{0,1:T(4,128)} %param.15) | copy-start | bytes 12292
  140.4 14.4 %all-to-all-start.2 = ((bf16[256,4,384]{2,0,1:T(8,128)(2,1)}), bf16[256,4,384]{2,0,1:T(8,128)(2,1)S(1)}, u32[]{:S(2)}, u32[]{:S(2)}) async-start(bf16[256,4,384]{2,0,1:T(8,128)(2,1)} %bitcast.89), calls=%async_computation.2 | async-start | bytes 1572864 | tf_op jit(solution)/shard_map/all_to_all | solution.py:229
  208.5 5.6 %copy-start.10 = (f32[256,4]{0,1:T(4,128)S(1)}, f32[256,4]{0,1:T(4,128)}, u32[]{:S(2)}) copy-start(f32[256,4]{0,1:T(4,128)} %param.16) | copy-start | bytes 12292
  208.5 30.0 %all-to-all-start.4 = ((bf16[128,16,384]{2,1,0:T(8,128)(2,1)}), bf16[128,16,384]{2,1,0:T(8,128)(2,1)}, u32[]{:S(2)}, u32[]{:S(2)}) async-start(bf16[128,16,384]{2,1,0:T(8,128)(2,1)} %bitcast.30), calls=%async_computation.4 | async-start | bytes 3145728 | tf_op jit(solution)/shard_map/all_to_all | solution.py:283
  (4 other events, 5.8 us)
Sparse Core Ops, SparseCore 0:
  23.8 95.0 all-gather.1

commit v13 on v5

--- a/solution.py
+++ b/solution.py
@@ -142,7 +142,7 @@
     )[None]
     masked = jnp.where(allowed, scores, -1e30)
     peak = jnp.max(masked, axis=-1)
-    probs = jnp.where(allowed, jnp.exp(masked - peak[..., None]), 0.0)
+    probs = jnp.exp(masked - peak[..., None])
     total = jnp.sum(probs, axis=-1)
     accum = jnp.einsum("hqk,kd->hqd", probs, value_rows)
     attended = (

time: 243 us -> 242 us (level)
  transfers between devices with their start and end apart: 15 -> 15, of which waited for: 3 -> 3; matrix products, arithmetic and copies ran while one was open for 21% -> 20% of each run, Pallas kernels for 0% -> 0%
where the time goes in v13:
time: 242 us; the launch traced here: 241 us
  starting transfers between devices  66.5 us (27%)
  blocking collectives  56.1 us (23%)
  waiting for transfers between devices  31.9 us (13%)
  matrix products  31.2 us (13%)
  other arithmetic  24 us (10%)
  local copies, waits for them, and re-layouts  16.6 us (7%)
  between operations  15.1 us (6%)
    all_to_all x1, blocking collectives, local(): arrived = lax.all_to_all(buffer, ('seq', 'mp'), 0, 0, tiled=True)  34.1 us
    ppermute x8, starting transfers between devices, local(): fetched.append(lax.ppermute(kv_own, ('seq', 'mp'), pairs))  34 us
    all_to_all x1, waiting for transfers between devices, local(): returned = lax.all_to_all(outgoing, ('seq', 'mp'), 0, 0, tiled=True)  22.9 us
    all_to_all x2, starting transfers between devices, gather_seq(): return lax.all_to_all(spread, 'seq', 0, 0, tiled=True)  22.5 us
    all_gather x1, blocking collectives, local(): whole = lax.all_gather(hidden_in, 'mp', axis=1, tiled=True)  22 us
    reduce_sum x1, other arithmetic, local(): total = jnp.sum(probs, axis=-1)  8.52 us
    all_to_all x1, waiting for transfers between devices, local(): lax.all_to_all(partial_out.astype(jnp.bfloat16), 'mp', 1, 0, tiled=True)  8.38 us
    dot_general x1, matrix products, local(): jnp.dot(active, w_down, preferred_element_type=jnp.float32)  7.18 us
  transfers between devices with their start and end apart: 15, of which 3 were waited for; matrix products, arithmetic and copies ran while one was open for 20% of the time, Pallas kernels for 0%

profile of v13, /device:TPU:1, one launch (start us, length us, event | category | flops | bytes accessed | tf_op | source)
XLA Modules:
  0.0 241.3 jit_solution(10361400104252657166)
XLA Ops:
  9.5 11.3 %all-to-all-start = ((bf16[32,48,512]{2,1,0:T(8,128)(2,1)}), bf16[32,48,512]{2,1,0:T(8,128)(2,1)S(1)}, u32[]{:S(2)}, u32[]{:S(2)}) async-start(bf16[32,48,512]{2,1,0:T(8,128)(2,1)} %broadcast_in_dim.37), calls=%async_computation | async-start | bytes 3145728 | tf_op jit(solution)/shard_map/all_to_all | solution.py:47
  20.9 2.5 %pad_maximum_fusion = bf16[3,192,1536]{2,1,0:T(8,128)(2,1)} fusion(bf16[1,192,1536]{2,1,0:T(8,128)(2,1)S(1)} %copy-done.2, bf16[1,192,1536]{2,1,0:T(8,128)(2,1)S(1)} %copy-done.3, bf16[1,192,1536]{2,1,0:T(8,128)(2,1)} %param.17), kind=kLoop, calls=%fused_computation.36 | loop fusion | flops 1769472 | bytes 3538944 | tf_op jit(solution)/shard_map/concatenate | solution.py:63
  26.0 22.0 %all_gather.6 = bf16[256,1536]{1,0:T(8,128)(2,1)S(1)} all-gather(bf16[256,384]{1,0:T(8,128)(2,1)S(1)} %copy-done.1), channel_id=1, replica_groups=mesh['seq'=32,'mp'=4] {'mp'}, dimensions={1}, use_global_device_ids=true | all-gather | bytes 983040 | tf_op jit(solution)/shard_map/all_gather | solution.py:71
  51.0 5.1 %collective-permute-start.1 = (bf16[256,256]{1,0:T(8,128)(2,1)S(1)}, bf16[256,256]{1,0:T(8,128)(2,1)S(1)}, u32[]{:S(2)}, u32[]{:S(2)}) collective-permute-start(bf16[256,256]{1,0:T(8,128)(2,1)S(1)} %pad_maximum_fusion.1), channel_id=1, source_target_pairs={{0,4},{1,9},{2,6},{3,11},{4,8},{5,13},{6,10},{7,15},{8,12},{9,17},... | collective-permute-start | bytes 393224 | tf_op jit(solution)/shard_map/ppermute | solution.py:105
  56.7 5.0 %collective-permute-start.2 = (bf16[256,256]{1,0:T(8,128)(2,1)S(1)}, bf16[256,256]{1,0:T(8,128)(2,1)S(1)}, u32[]{:S(2)}, u32[]{:S(2)}) collective-permute-start(bf16[256,256]{1,0:T(8,128)(2,1)S(1)} %pad_maximum_fusion.1), channel_id=1, source_target_pairs={{0,12},{1,17},{2,14},{3,19},{4,16},{5,21},{6,18},{7,23},{8,20},{9,... | collective-permute-start | bytes 393224 | tf_op jit(solution)/shard_map/ppermute | solution.py:105
  61.7 8.5 %collective-permute-start.3 = (bf16[256,256]{1,0:T(8,128)(2,1)S(1)}, bf16[256,256]{1,0:T(8,128)(2,1)S(1)}, u32[]{:S(2)}, u32[]{:S(2)}) collective-permute-start(bf16[256,256]{1,0:T(8,128)(2,1)S(1)} %pad_maximum_fusion.1), channel_id=1, source_target_pairs={{0,20},{1,25},{2,22},{3,27},{4,24},{5,29},{6,26},{7,31},{8,28},{9,... | collective-permute-start | bytes 393224 | tf_op jit(solution)/shard_map/ppermute | solution.py:105
  70.3 2.1 collective-permute-start.4
  72.4 2.1 collective-permute-start.5
  74.5 4.3 %collective-permute-start.6 = (bf16[256,256]{1,0:T(8,128)(2,1)S(1)}, bf16[256,256]{1,0:T(8,128)(2,1)S(1)}, u32[]{:S(2)}, u32[]{:S(2)}) collective-permute-start(bf16[256,256]{1,0:T(8,128)(2,1)S(1)} %pad_maximum_fusion.1), channel_id=1, source_target_pairs={{0,44},{1,49},{2,46},{3,51},{4,48},{5,53},{6,50},{7,55},{8,52},{9,... | collective-permute-start | bytes 393224 | tf_op jit(solution)/shard_map/ppermute | solution.py:105
  79.5 1.9 collective-permute-start.7
  82.1 4.9 %collective-permute-start.8 = (bf16[256,256]{1,0:T(8,128)(2,1)S(1)}, bf16[256,256]{1,0:T(8,128)(2,1)S(1)}, u32[]{:S(2)}, u32[]{:S(2)}) collective-permute-start(bf16[256,256]{1,0:T(8,128)(2,1)S(1)} %pad_maximum_fusion.1), channel_id=1, source_target_pairs={{0,60},{1,65},{2,62},{3,67},{4,64},{5,69},{6,66},{7,71},{8,68},{9,... | collective-permute-start | bytes 393224 | tf_op jit(solution)/shard_map/ppermute | solution.py:105
  95.9 11.1 %all-to-all-start.1 = ((bf16[32,48,384]{2,1,0:T(8,128)(2,1)}), bf16[32,48,384]{2,1,0:T(8,128)(2,1)S(1)}, u32[]{:S(2)}, u32[]{:S(2)}) async-start(bf16[32,48,384]{2,1,0:T(8,128)(2,1)} %broadcast_in_dim.44), calls=%async_computation.1 | async-start | bytes 2359296 | tf_op jit(solution)/shard_map/all_to_all | solution.py:47
  110.0 6.4 %fusion = (f32[3,256]{1,0:T(4,128)S(1)}, f32[3,256,4352]{2,1,0:T(8,128)}) fusion(pred[256,4352]{1,0:T(8,128)(4,1)S(1)} %fusion.10, bf16[4352,256]{1,0:T(8,128)(2,1)S(1)} %maximum_maximum_fusion, bf16[256,3,64]{2,0,1:T(8,128)(2,1)S(1)} %get-tuple-element.14, bf16[256,3,64]{2,0,1:T(8,128)(2,1)S(1)} %get-tuple-element.13), kind=kOutput, calls=%fused_computation.2 | convolution fusion | flops 866057472 | bytes 15993856 | tf_op jit(solution)/shard_map/hqd,kd->hqk/dot_general | solution.py:131
  116.4 8.5 %fusion.1 = f32[3,256]{1,0:T(4,128)S(1)} fusion(f32[3,256,4352]{2,1,0:T(8,128)} %get-tuple-element.26, f32[3,256]{1,0:T(4,128)S(1)} %get-tuple-element.25, pred[256,4352]{1,0:T(8,128)(4,1)S(1)} %fusion.10), kind=kLoop, calls=%fused_computation.3 | loop fusion | flops 13368576 | bytes 14489600 | tf_op jit(solution)/shard_map/reduce_sum | solution.py:146
  124.9 7.0 %fusion.27 = bf16[256,3,128]{0,2,1:T(8,128)(2,1)S(1)} fusion(bf16[4352,256]{1,0:T(8,128)(2,1)S(1)} %maximum_maximum_fusion, f32[3,256,4352]{2,1,0:T(8,128)} %get-tuple-element.26, f32[3,256]{1,0:T(4,128)S(1)} %get-tuple-element.25, pred[256,4352]{1,0:T(8,128)(4,1)S(1)} %fusion.10, f32[256,3]{0,1:T(4,128)S(1)} %bitcast.108), kind=kOutput, calls=%fused_computation.54 | convolution fusion | flops 865861632 | bytes 15802368 | tf_op jit(solution)/shard_map/hqk,kd->hqd/dot_general | solution.py:147
  133.6 3.7 %all-to-all-start.2 = ((bf16[256,4,384]{2,0,1:T(8,128)(2,1)}), bf16[256,4,384]{2,0,1:T(8,128)(2,1)S(1)}, u32[]{:S(2)}, u32[]{:S(2)}) async-start(bf16[256,4,384]{2,0,1:T(8,128)(2,1)} %bitcast.94), calls=%async_computation.2 | async-start | bytes 1572864 | tf_op jit(solution)/shard_map/all_to_all | solution.py:157
  139.7 8.4 %all-to-all-done.2 = bf16[256,4,384]{2,0,1:T(8,128)(2,1)S(1)} async-done(((bf16[256,4,384]{2,0,1:T(8,128)(2,1)}), bf16[256,4,384]{2,0,1:T(8,128)(2,1)S(1)}, u32[]{:S(2)}, u32[]{:S(2)}) %all-to-all-start.2) | async-done | bytes 786464 | tf_op jit(solution)/shard_map/all_to_all | solution.py:157
  148.9 34.1 %all_to_all.52 = bf16[128,16,384]{2,1,0:T(8,128)(2,1)S(1)} all-to-all(bf16[128,16,384]{2,1,0:T(8,128)(2,1)S(1)} %bitcast.96), channel_id=1, replica_groups=mesh['seq'=32,'mp'=4] {'seq','mp'}, dimensions={0} | all-to-all | bytes 3145728 | tf_op jit(solution)/shard_map/all_to_all | solution.py:183
  184.8 4.2 %fusion.15 = f32[512,768]{1,0:T(8,128)} fusion(bf16[512,1536]{1,0:T(8,128)(2,1)S(1)} %bitcast.103, bf16[3,768,1536]{2,1,0:T(8,128)(2,1)} %all-gather.2.cloned.1.call-done), kind=kOutput, calls=%fused_computation.30 | convolution fusion | flops 1207959552 | bytes 5505024 | tf_op jit(solution)/shard_map/dot_general | solution.py:201
  189.0 7.2 %convolution_convert_fusion = bf16[512,1536]{1,0:T(8,128)(2,1)} fusion(bf16[3,768,1536]{2,1,0:T(8,128)(2,1)} %all-gather.2.cloned.1.call-done, f32[512,768]{1,0:T(8,128)} %fusion.15, bf16[512,1536]{1,0:T(8,128)(2,1)S(1)} %bitcast.104), kind=kOutput, calls=%fused_computation.25 | convolution fusion | flops 2417885184 | bytes 9437184 | tf_op jit(solution)/shard_map/dot_general | solution.py:205
  196.2 3.0 %reshape.382 = bf16[32,16,4,384]{3,2,1,0:T(4,128)(2,1)S(1)} reshape(bf16[512,1536]{1,0:T(8,128)(2,1)} %convolution_convert_fusion) | data formatting | bytes 3145728 | tf_op jit(solution)/shard_map/reshape | solution.py:207
  200.6 5.6 %all-to-all-start.4 = ((bf16[128,16,384]{2,1,0:T(8,128)(2,1)}), bf16[128,16,384]{2,1,0:T(8,128)(2,1)}, u32[]{:S(2)}, u32[]{:S(2)}) async-start(bf16[128,16,384]{2,1,0:T(8,128)(2,1)} %bitcast.32), calls=%async_computation.4 | async-start | bytes 3145728 | tf_op jit(solution)/shard_map/all_to_all | solution.py:211
  207.7 22.9 %all-to-all-done.4 = bf16[128,16,384]{2,1,0:T(8,128)(2,1)} async-done(((bf16[128,16,384]{2,1,0:T(8,128)(2,1)}), bf16[128,16,384]{2,1,0:T(8,128)(2,1)}, u32[]{:S(2)}, u32[]{:S(2)}) %all-to-all-start.4) | async-done | bytes 1572896 | tf_op jit(solution)/shard_map/all_to_all | solution.py:211
  230.6 3.9 %fusion.21 = bf16[256,384]{1,0:T(8,128)(2,1)} fusion(f32[256,2048]{1,0:T(8,128)S(1)} %select_reduce_fusion, bf16[2048,384]{1,0:T(8,128)(2,1)} %bitcast.33, f32[256,384]{1,0:T(8,128)S(1)} %convert_reduce_fusion, bf16[256,384]{1,0:T(8,128)(2,1)S(1)} %copy-done.1), kind=kOutput, calls=%fused_computation.44 | convolution fusion | flops 2416508928 | bytes 4456448 | tf_op jit(solution)/shard_map/dot_general | solution.py:220
  (95 shorter events, 30.3 us)
Async XLA Ops:
  6.5 0.8 copy-start
  8.1 12.8 %copy-start.2 = (bf16[1,192,1536]{2,1,0:T(8,128)(2,1)S(1)}, bf16[1,192,1536]{2,1,0:T(8,128)(2,1)}, u32[]{:S(2)}) copy-start(bf16[1,192,1536]{2,1,0:T(8,128)(2,1)} %param.19) | copy-start | bytes 1769476
  8.1 12.8 %copy-start.3 = (bf16[1,192,1536]{2,1,0:T(8,128)(2,1)S(1)}, bf16[1,192,1536]{2,1,0:T(8,128)(2,1)}, u32[]{:S(2)}) copy-start(bf16[1,192,1536]{2,1,0:T(8,128)(2,1)} %param.18) | copy-start | bytes 1769476
  9.5 38.8 %all-to-all-start = ((bf16[32,48,512]{2,1,0:T(8,128)(2,1)}), bf16[32,48,512]{2,1,0:T(8,128)(2,1)S(1)}, u32[]{:S(2)}, u32[]{:S(2)}) async-start(bf16[32,48,512]{2,1,0:T(8,128)(2,1)} %broadcast_in_dim.37), calls=%async_computation | async-start | bytes 3145728 | tf_op jit(solution)/shard_map/all_to_all | solution.py:47
  20.8 2.8 %copy-start.7 = (s32[3]{0:T(128)S(1)}, s32[3]{0:T(128)}, u32[]{:S(2)}) copy-start(s32[3]{0:T(128)} %param.14) | copy-start | bytes 40
  20.8 5.2 %copy-start.1 = (bf16[256,384]{1,0:T(8,128)(2,1)S(1)}, bf16[256,384]{1,0:T(8,128)(2,1)}, u32[]{:S(2)}) copy-start(bf16[256,384]{1,0:T(8,128)(2,1)} %param.10) | copy-start | bytes 589828
  20.8 163.9 %all-gather.2.cloned.1.call-start = ((), (), s32[]{:S(2)}) async-start(), calls=%async_computation.5 | async-start | bytes 8847360 | tf_op jit(solution)/shard_map/all_gather | solution.py:62
  49.6 1.3 collective-permute-start
  51.0 23.5 %collective-permute-start.1 = (bf16[256,256]{1,0:T(8,128)(2,1)S(1)}, bf16[256,256]{1,0:T(8,128)(2,1)S(1)}, u32[]{:S(2)}, u32[]{:S(2)}) collective-permute-start(bf16[256,256]{1,0:T(8,128)(2,1)S(1)} %pad_maximum_fusion.1), channel_id=1, source_target_pairs={{0,4},{1,9},{2,6},{3,11},{4,8},{5,13},{6,10},{7,15},{8,12},{9,17},... | collective-permute-start | bytes 393224 | tf_op jit(solution)/shard_map/ppermute | solution.py:105
  56.7 22.8 %collective-permute-start.2 = (bf16[256,256]{1,0:T(8,128)(2,1)S(1)}, bf16[256,256]{1,0:T(8,128)(2,1)S(1)}, u32[]{:S(2)}, u32[]{:S(2)}) collective-permute-start(bf16[256,256]{1,0:T(8,128)(2,1)S(1)} %pad_maximum_fusion.1), channel_id=1, source_target_pairs={{0,12},{1,17},{2,14},{3,19},{4,16},{5,21},{6,18},{7,23},{8,20},{9,... | collective-permute-start | bytes 393224 | tf_op jit(solution)/shard_map/ppermute | solution.py:105
  61.7 20.4 %collective-permute-start.3 = (bf16[256,256]{1,0:T(8,128)(2,1)S(1)}, bf16[256,256]{1,0:T(8,128)(2,1)S(1)}, u32[]{:S(2)}, u32[]{:S(2)}) collective-permute-start(bf16[256,256]{1,0:T(8,128)(2,1)S(1)} %pad_maximum_fusion.1), channel_id=1, source_target_pairs={{0,20},{1,25},{2,22},{3,27},{4,24},{5,29},{6,26},{7,31},{8,28},{9,... | collective-permute-start | bytes 393224 | tf_op jit(solution)/shard_map/ppermute | solution.py:105
  70.3 17.4 %collective-permute-start.4 = (bf16[256,256]{1,0:T(8,128)(2,1)S(1)}, bf16[256,256]{1,0:T(8,128)(2,1)S(1)}, u32[]{:S(2)}, u32[]{:S(2)}) collective-permute-start(bf16[256,256]{1,0:T(8,128)(2,1)S(1)} %pad_maximum_fusion.1), channel_id=1, source_target_pairs={{0,28},{1,33},{2,30},{3,35},{4,32},{5,37},{6,34},{7,39},{8,36},{9,... | collective-permute-start | bytes 393224 | tf_op jit(solution)/shard_map/ppermute | solution.py:105
  72.4 15.9 %collective-permute-start.5 = (bf16[256,256]{1,0:T(8,128)(2,1)S(1)}, bf16[256,256]{1,0:T(8,128)(2,1)S(1)}, u32[]{:S(2)}, u32[]{:S(2)}) collective-permute-start(bf16[256,256]{1,0:T(8,128)(2,1)S(1)} %pad_maximum_fusion.1), channel_id=1, source_target_pairs={{0,36},{1,41},{2,38},{3,43},{4,40},{5,45},{6,42},{7,47},{8,44},{9,... | collective-permute-start | bytes 393224 | tf_op jit(solution)/shard_map/ppermute | solution.py:105
  74.5 14.5 %collective-permute-start.6 = (bf16[256,256]{1,0:T(8,128)(2,1)S(1)}, bf16[256,256]{1,0:T(8,128)(2,1)S(1)}, u32[]{:S(2)}, u32[]{:S(2)}) collective-permute-start(bf16[256,256]{1,0:T(8,128)(2,1)S(1)} %pad_maximum_fusion.1), channel_id=1, source_target_pairs={{0,44},{1,49},{2,46},{3,51},{4,48},{5,53},{6,50},{7,55},{8,52},{9,... | collective-permute-start | bytes 393224 | tf_op jit(solution)/shard_map/ppermute | solution.py:105
  79.5 10.1 %collective-permute-start.7 = (bf16[256,256]{1,0:T(8,128)(2,1)S(1)}, bf16[256,256]{1,0:T(8,128)(2,1)S(1)}, u32[]{:S(2)}, u32[]{:S(2)}) collective-permute-start(bf16[256,256]{1,0:T(8,128)(2,1)S(1)} %pad_maximum_fusion.1), channel_id=1, source_target_pairs={{0,52},{1,57},{2,54},{3,59},{4,56},{5,61},{6,58},{7,63},{8,60},{9,... | collective-permute-start | bytes 393224 | tf_op jit(solution)/shard_map/ppermute | solution.py:105
  82.1 8.2 %collective-permute-start.8 = (bf16[256,256]{1,0:T(8,128)(2,1)S(1)}, bf16[256,256]{1,0:T(8,128)(2,1)S(1)}, u32[]{:S(2)}, u32[]{:S(2)}) collective-permute-start(bf16[256,256]{1,0:T(8,128)(2,1)S(1)} %pad_maximum_fusion.1), channel_id=1, source_target_pairs={{0,60},{1,65},{2,62},{3,67},{4,64},{5,69},{6,66},{7,71},{8,68},{9,... | collective-permute-start | bytes 393224 | tf_op jit(solution)/shard_map/ppermute | solution.py:105
  91.0 17.2 %collective-permute-start.9 = (bf16[8,256,256]{2,1,0:T(8,128)(2,1)}, bf16[8,256,256]{2,1,0:T(8,128)(2,1)}, u32[]{:S(2)}, u32[]{:S(2)}) collective-permute-start(bf16[8,256,256]{2,1,0:T(8,128)(2,1)} %bitcast_dynamic-update-slice_fusion), channel_id=1, source_target_pairs={{0,1},{1,0},{2,3},{3,2},{4,5},{5,4},{6,7},{7,6},{8,9},{9,8},{10,11... | collective-permute-start | bytes 3145736 | tf_op jit(solution)/shard_map/ppermute | solution.py:107
  91.4 3.4 %copy-start.4 = (bf16[384,48]{0,1:T(8,128)(2,1)S(1)}, bf16[384,48]{0,1:T(8,128)(2,1)}, u32[]{:S(2)}) copy-start(bf16[384,48]{0,1:T(8,128)(2,1)} %param.13) | copy-start | bytes 110596
  95.9 36.0 %all-to-all-start.1 = ((bf16[32,48,384]{2,1,0:T(8,128)(2,1)}), bf16[32,48,384]{2,1,0:T(8,128)(2,1)S(1)}, u32[]{:S(2)}, u32[]{:S(2)}) async-start(bf16[32,48,384]{2,1,0:T(8,128)(2,1)} %broadcast_in_dim.44), calls=%async_computation.1 | async-start | bytes 2359296 | tf_op jit(solution)/shard_map/all_to_all | solution.py:47
  132.0 5.3 %copy-start.6 = (s32[256,4]{0,1:T(4,128)S(1)}, s32[256,4]{0,1:T(4,128)}, u32[]{:S(2)}) copy-start(s32[256,4]{0,1:T(4,128)} %param.15) | copy-start | bytes 12292
  133.6 14.5 %all-to-all-start.2 = ((bf16[256,4,384]{2,0,1:T(8,128)(2,1)}), bf16[256,4,384]{2,0,1:T(8,128)(2,1)S(1)}, u32[]{:S(2)}, u32[]{:S(2)}) async-start(bf16[256,4,384]{2,0,1:T(8,128)(2,1)} %bitcast.94), calls=%async_computation.2 | async-start | bytes 1572864 | tf_op jit(solution)/shard_map/all_to_all | solution.py:157
  200.6 5.6 %copy-start.5 = (f32[256,4]{0,1:T(4,128)S(1)}, f32[256,4]{0,1:T(4,128)}, u32[]{:S(2)}) copy-start(f32[256,4]{0,1:T(4,128)} %param.16) | copy-start | bytes 12292
  200.6 30.0 %all-to-all-start.4 = ((bf16[128,16,384]{2,1,0:T(8,128)(2,1)}), bf16[128,16,384]{2,1,0:T(8,128)(2,1)}, u32[]{:S(2)}, u32[]{:S(2)}) async-start(bf16[128,16,384]{2,1,0:T(8,128)(2,1)} %bitcast.32), calls=%async_computation.4 | async-start | bytes 3145728 | tf_op jit(solution)/shard_map/all_to_all | solution.py:211
Sparse Core Ops, SparseCore 0:
  23.6 85.0 all-gather.1

commit v14 on v11

--- a/solution.py
+++ b/solution.py
@@ -59,8 +59,6 @@
     q_cols = heads_here * HD
     kv_group = mp_index * heads_here // (HQ // KVH)
 
-    expert_own = jnp.concatenate([expert_gate, expert_up, expert_down], axis=0)
-    across = lax.ppermute(expert_own, "mp", [(m, m ^ 2) for m in range(mp_count)])
 
     core = mp_index % 2
     kv_col = jnp.where(core == 0, kv_group * HD, KVH * HD + kv_group * HD)
@@ -73,12 +71,13 @@
         whole_f * lax.rsqrt(jnp.sum(whole_f * whole_f, axis=-1, keepdims=True) / D + EPSILON)
     ).astype(jnp.bfloat16)
     lin = jnp.dot(normed, w_qkv, preferred_element_type=jnp.float32)
-    across, lin = lax.optimization_barrier((across, lin))
-    beside = lax.ppermute(
-        jnp.stack([expert_own, across]), "mp", [(m, m ^ 1) for m in range(mp_count)]
-    )
-    expert_pieces = [expert_own, across, beside[0], beside[1]]
-    wo_rows = lax.all_gather(wo.T, "seq", axis=0, tiled=True)
+    expert_own = jnp.concatenate([expert_gate, expert_up, expert_down], axis=0)
+    wo_piece, expert_own, lin = lax.optimization_barrier((wo.T, expert_own, lin))
+    expert_quarters = lax.all_to_all(
+        jnp.broadcast_to(expert_own[None], (mp_count,) + expert_own.shape),
+        "mp", 0, 0, tiled=True,
+    )
+    wo_rows = gather_seq(wo_piece, seq_count)
     own_index = seq_index * tok_rows + jnp.arange(tok_rows, dtype=jnp.int32)
     _, own_pos = prompt_ids(own_index, lengths)
     queries = (
@@ -122,6 +121,7 @@
     kv_win = jnp.concatenate(
         [odd.reshape(-1, 2 * HD), even.reshape(-1, 2 * HD), kv_own], axis=0
     )
+    expert_quarters, kv_win = lax.optimization_barrier((expert_quarters, kv_win))
     key_rows = kv_win[:, :HD]
     value_rows = kv_win[:, HD:].astype(jnp.float32)
     key_index = (
@@ -145,7 +145,7 @@
     )[None]
     masked = jnp.where(allowed, scores, -1e30)
     peak = jnp.max(masked, axis=-1)
-    probs = jnp.where(allowed, jnp.exp(masked - peak[..., None]), 0.0)
+    probs = jnp.exp(masked - peak[..., None])
     total = jnp.sum(probs, axis=-1)
     accum = jnp.einsum("hqk,kd->hqd", probs, value_rows)
     attended = (
@@ -196,7 +196,8 @@
         * lax.rsqrt(jnp.sum(arrived_rows * arrived_rows, axis=-1, keepdims=True) / D + EPSILON)
     ).astype(jnp.bfloat16)
     result_f = None
-    for piece in expert_pieces:
+    for quarter in range(mp_count):
+        piece = expert_quarters[quarter]
         gate_act = lax.dot_general(
             moe_in, piece[0], (((1,), (1,)), ((), ())), preferred_element_type=jnp.float32
         )

time: 291 us -> 314 us (1.079)
  starting transfers between devices: 63.5 us -> 136 us
  waiting for transfers between devices: 51.7 us -> 33.1 us
  between operations: 15.2 us -> 1.82 us
  local copies, waits for them, and re-layouts: 21.4 us -> 14 us
  blocking collectives: 60.8 us -> 55.5 us
    ppermute x8, starting transfers between devices: 29 us -> 100 us  [local(): fetched.append(lax.ppermute(kv_own, ('seq', 'mp'), pairs))]
    all_gather x1, blocking collectives: 60.8 us -> 21.1 us  [local(): whole = lax.all_gather(hidden_in, 'mp', axis=1, tiled=True)]
    all_to_all x0 -> x1, blocking collectives: none -> 34.4 us  [local(): arrived = lax.all_to_all(buffer, ('seq', 'mp'), 0, 0, tiled=True)]
    all_to_all x1, waiting for transfers between devices: 19.9 us -> 0.01 us  [local(): lax.all_to_all(jnp.broadcast_to(expert_own[None], (mp_count,) + expert_ow...]
    unnamed x37 -> x41, local copies, waits for them, and re-layouts: 11.3 us -> 2.58 us
    all_to_all x1 -> x2, starting transfers between devices: 11.6 us -> 20 us  [gather_seq(): return lax.all_to_all(spread, 'seq', 0, 0, tiled=True)]
    dot_general x2 -> x4, matrix products: 2.85 us -> 7.68 us  [local(): lax.dot_general(moe_in, piece[0], (((1,), (1,)), ((), ())), preferred_ele...]
    dot_general x2 -> x0, matrix products: 4.2 us -> none  [local(): lax.dot_general(moe_in, piece[1], (((1,), (1,)), ((), ())), preferred_ele...]
  transfers between devices with their start and end apart: 17 -> 15, of which waited for: 5 -> 3; matrix products, arithmetic and copies ran while one was open for 24% -> 14% of each run, Pallas kernels for 0% -> 0%
where the time goes in v14:
time: 314 us; the launch traced here: 313 us
  starting transfers between devices  136 us (43%)
  blocking collectives  55.5 us (18%)
  matrix products  48.2 us (15%)
  waiting for transfers between devices  33.1 us (11%)
  other arithmetic  24.8 us (8%)
  local copies, waits for them, and re-layouts  14 us (4%)
    ppermute x8, starting transfers between devices, local(): fetched.append(lax.ppermute(kv_own, ('seq', 'mp'), pairs))  100 us
    all_to_all x1, blocking collectives, local(): arrived = lax.all_to_all(buffer, ('seq', 'mp'), 0, 0, tiled=True)  34.4 us
    all_to_all x1, waiting for transfers between devices, local(): returned = lax.all_to_all(outgoing, ('seq', 'mp'), 0, 0, tiled=True)  22.9 us
    all_gather x1, blocking collectives, local(): whole = lax.all_gather(hidden_in, 'mp', axis=1, tiled=True)  21.1 us
    all_to_all x2, starting transfers between devices, gather_seq(): return lax.all_to_all(spread, 'seq', 0, 0, tiled=True)  20 us
    dot_general x4, matrix products, local(): part = jnp.dot(active, piece[2], preferred_element_type=jnp.float32)  18.2 us
    reduce_sum x1, other arithmetic, local(): total = jnp.sum(probs, axis=-1)  8.67 us
    all_to_all x1, waiting for transfers between devices, local(): lax.all_to_all(partial_out.astype(jnp.bfloat16), 'mp', 1, 0, tiled=True)  8.38 us
  transfers between devices with their start and end apart: 15, of which 3 were waited for; matrix products, arithmetic and copies ran while one was open for 14% of the time, Pallas kernels for 0%

profile of v14, /device:TPU:1, one launch (start us, length us, event | category | flops | bytes accessed | tf_op | source)
XLA Modules:
  0.0 313.0 jit_solution(11654775971105246766)
XLA Ops:
  2.9 11.6 %all-to-all-start = ((bf16[32,48,512]{2,1,0:T(8,128)(2,1)}), bf16[32,48,512]{2,1,0:T(8,128)(2,1)}, u32[]{:S(2)}, u32[]{:S(2)}) async-start(bf16[32,48,512]{2,1,0:T(8,128)(2,1)} %broadcast_in_dim.39), calls=%async_computation | async-start | bytes 3145728 | tf_op jit(solution)/shard_map/all_to_all | solution.py:47
  17.1 21.1 %all_gather.3 = bf16[256,1536]{1,0:T(8,128)(2,1)S(1)} all-gather(bf16[256,384]{1,0:T(8,128)(2,1)S(1)} %copy-done.5), channel_id=1, replica_groups=mesh['seq'=32,'mp'=4] {'mp'}, dimensions={1}, use_global_device_ids=true | all-gather | bytes 983040 | tf_op jit(solution)/shard_map/all_gather | solution.py:68
  43.5 3.5 %broadcast_in_dim.41 = bf16[4,3,192,1536]{3,2,1,0:T(8,128)(2,1)} broadcast(bf16[3,192,1536]{2,1,0:T(8,128)(2,1)S(1)} %pad_maximum_fusion), dimensions={1,2,3} | broadcast | bytes 8847360 | tf_op jit(solution)/shard_map/broadcast_in_dim | solution.py:77
  47.0 5.7 %all-to-all-start.1 = ((bf16[4,3,192,1536]{3,2,1,0:T(8,128)(2,1)}), bf16[4,3,192,1536]{3,2,1,0:T(8,128)(2,1)}, u32[]{:S(2)}, u32[]{:S(2)}) async-start(bf16[4,3,192,1536]{3,2,1,0:T(8,128)(2,1)} %broadcast_in_dim.41), calls=%async_computation.1 | async-start | bytes 14155776 | tf_op jit(solution)/shard_map/all_to_all | solution.py:76
  52.7 4.9 %collective-permute-start.1 = (bf16[256,256]{1,0:T(8,128)(2,1)S(1)}, bf16[256,256]{1,0:T(8,128)(2,1)S(1)}, u32[]{:S(2)}, u32[]{:S(2)}) collective-permute-start(bf16[256,256]{1,0:T(8,128)(2,1)S(1)} %pad_maximum_fusion.1), channel_id=1, source_target_pairs={{0,4},{1,9},{2,6},{3,11},{4,8},{5,13},{6,10},{7,15},{8,12},{9,17},... | collective-permute-start | bytes 393224 | tf_op jit(solution)/shard_map/ppermute | solution.py:107
  58.2 5.7 %collective-permute-start.2 = (bf16[256,256]{1,0:T(8,128)(2,1)S(1)}, bf16[256,256]{1,0:T(8,128)(2,1)S(1)}, u32[]{:S(2)}, u32[]{:S(2)}) collective-permute-start(bf16[256,256]{1,0:T(8,128)(2,1)S(1)} %pad_maximum_fusion.1), channel_id=1, source_target_pairs={{0,12},{1,17},{2,14},{3,19},{4,16},{5,21},{6,18},{7,23},{8,20},{9,... | collective-permute-start | bytes 393224 | tf_op jit(solution)/shard_map/ppermute | solution.py:107
  63.9 5.9 %collective-permute-start.3 = (bf16[256,256]{1,0:T(8,128)(2,1)S(1)}, bf16[256,256]{1,0:T(8,128)(2,1)S(1)}, u32[]{:S(2)}, u32[]{:S(2)}) collective-permute-start(bf16[256,256]{1,0:T(8,128)(2,1)S(1)} %pad_maximum_fusion.1), channel_id=1, source_target_pairs={{0,20},{1,25},{2,22},{3,27},{4,24},{5,29},{6,26},{7,31},{8,28},{9,... | collective-permute-start | bytes 393224 | tf_op jit(solution)/shard_map/ppermute | solution.py:107
  75.0 71.2 %collective-permute-start.6 = (bf16[256,256]{1,0:T(8,128)(2,1)S(1)}, bf16[256,256]{1,0:T(8,128)(2,1)S(1)}, u32[]{:S(2)}, u32[]{:S(2)}) collective-permute-start(bf16[256,256]{1,0:T(8,128)(2,1)S(1)} %pad_maximum_fusion.1), channel_id=1, source_target_pairs={{0,44},{1,49},{2,46},{3,51},{4,48},{5,53},{6,50},{7,55},{8,52},{9,... | collective-permute-start | bytes 393224 | tf_op jit(solution)/shard_map/ppermute | solution.py:107
  146.2 3.1 collective-permute-start.7
  149.3 4.3 %collective-permute-start.8 = (bf16[256,256]{1,0:T(8,128)(2,1)S(1)}, bf16[256,256]{1,0:T(8,128)(2,1)S(1)}, u32[]{:S(2)}, u32[]{:S(2)}) collective-permute-start(bf16[256,256]{1,0:T(8,128)(2,1)S(1)} %pad_maximum_fusion.1), channel_id=1, source_target_pairs={{0,60},{1,65},{2,62},{3,67},{4,64},{5,69},{6,66},{7,71},{8,68},{9,... | collective-permute-start | bytes 393224 | tf_op jit(solution)/shard_map/ppermute | solution.py:107
  166.5 8.4 %all-to-all-start.2 = ((bf16[32,48,384]{2,1,0:T(8,128)(2,1)}), bf16[32,48,384]{2,1,0:T(8,128)(2,1)S(1)}, u32[]{:S(2)}, u32[]{:S(2)}) async-start(bf16[32,48,384]{2,1,0:T(8,128)(2,1)} %broadcast_in_dim.47), calls=%async_computation.2 | async-start | bytes 2359296 | tf_op jit(solution)/shard_map/all_to_all | solution.py:47
  174.9 7.6 %fusion = (f32[3,256]{1,0:T(4,128)S(1)}, f32[3,256,4352]{2,1,0:T(8,128)}) fusion(pred[256,4352]{1,0:T(8,128)(4,1)S(1)} %fusion.10, bf16[4352,256]{1,0:T(8,128)(2,1)} %maximum_maximum_fusion, bf16[256,3,64]{2,0,1:T(8,128)(2,1)S(1)} %copy-done.10, bf16[256,3,64]{2,0,1:T(8,128)(2,1)S(1)} %copy-done.9), kind=kOutput, calls=%fused_computation.2 | convolution fusion | flops 866057472 | bytes 15797248 | tf_op jit(solution)/shard_map/hqd,kd->hqk/dot_general | solution.py:134
  182.5 8.7 %fusion.1 = f32[3,256]{1,0:T(4,128)S(1)} fusion(f32[3,256,4352]{2,1,0:T(8,128)} %get-tuple-element.32, f32[3,256]{1,0:T(4,128)S(1)} %get-tuple-element.31, pred[256,4352]{1,0:T(8,128)(4,1)S(1)} %fusion.10), kind=kLoop, calls=%fused_computation.3 | loop fusion | flops 13368576 | bytes 14489600 | tf_op jit(solution)/shard_map/reduce_sum | solution.py:149
  191.2 7.0 %fusion.37 = bf16[256,3,128]{0,2,1:T(8,128)(2,1)S(1)} fusion(bf16[4352,256]{1,0:T(8,128)(2,1)S(1)} %copy-done.4, f32[3,256,4352]{2,1,0:T(8,128)} %get-tuple-element.32, f32[3,256]{1,0:T(4,128)S(1)} %get-tuple-element.31, pred[256,4352]{1,0:T(8,128)(4,1)S(1)} %fusion.10, f32[256,3]{0,1:T(4,128)S(1)} %bitcast.146), kind=kOutput, calls=%fused_computation.66 | convolution fusion | flops 865861632 | bytes 15802368 | tf_op jit(solution)/shard_map/hqk,kd->hqd/dot_general | solution.py:150
  199.8 3.8 %all-to-all-start.3 = ((bf16[256,4,384]{2,0,1:T(8,128)(2,1)}), bf16[256,4,384]{2,0,1:T(8,128)(2,1)S(1)}, u32[]{:S(2)}, u32[]{:S(2)}) async-start(bf16[256,4,384]{2,0,1:T(8,128)(2,1)} %bitcast.127), calls=%async_computation.3 | async-start | bytes 1572864 | tf_op jit(solution)/shard_map/all_to_all | solution.py:160
  206.0 8.4 %all-to-all-done.3 = bf16[256,4,384]{2,0,1:T(8,128)(2,1)S(1)} async-done(((bf16[256,4,384]{2,0,1:T(8,128)(2,1)}), bf16[256,4,384]{2,0,1:T(8,128)(2,1)S(1)}, u32[]{:S(2)}, u32[]{:S(2)}) %all-to-all-start.3) | async-done | bytes 786464 | tf_op jit(solution)/shard_map/all_to_all | solution.py:160
  215.2 34.4 %all_to_all.57 = bf16[128,16,384]{2,1,0:T(8,128)(2,1)S(1)} all-to-all(bf16[128,16,384]{2,1,0:T(8,128)(2,1)S(1)} %bitcast.137), channel_id=1, replica_groups=mesh['seq'=32,'mp'=4] {'seq','mp'}, dimensions={0} | all-to-all | bytes 3145728 | tf_op jit(solution)/shard_map/all_to_all | solution.py:186
  259.1 4.2 %fusion.25 = f32[512,1536]{1,0:T(8,128)} fusion(f32[512,192]{0,1:T(8,128)S(1)} %convolution_maximum_fusion.3, bf16[512,1536]{1,0:T(8,128)(2,1)S(1)} %bitcast.132, bf16[4,3,192,1536]{3,2,1,0:T(8,128)(2,1)} %all-to-all-done.1), kind=kOutput, calls=%fused_computation.54 | convolution fusion | flops 604176384 | bytes 6291456 | tf_op jit(solution)/shard_map/dot_general | solution.py:208
  263.3 5.2 %convolution_add_fusion.2 = f32[512,1536]{1,0:T(8,128)} fusion(f32[512,1536]{1,0:T(8,128)} %fusion.25, f32[512,192]{0,1:T(8,128)S(1)} %convolution_maximum_fusion.2, bf16[512,1536]{1,0:T(8,128)(2,1)S(1)} %bitcast.133, bf16[4,3,192,1536]{3,2,1,0:T(8,128)(2,1)} %all-to-all-done.1), kind=kOutput, calls=%fused_computation.25 | convolution fusion | flops 604962816 | bytes 9437184 | tf_op jit(solution)/shard_map/dot_general | solution.py:208
  268.5 5.2 %convolution_add_fusion.1 = f32[512,1536]{1,0:T(8,128)} fusion(f32[512,1536]{1,0:T(8,128)} %convolution_add_fusion.2, f32[512,192]{0,1:T(8,128)S(1)} %convolution_maximum_fusion.1, bf16[512,1536]{1,0:T(8,128)(2,1)S(1)} %bitcast.134, bf16[4,3,192,1536]{3,2,1,0:T(8,128)(2,1)} %all-to-all-done.1), kind=kOutput, calls=%fused_computation.24 | convolution fusion | flops 604962816 | bytes 9437184 | tf_op jit(solution)/shard_map/dot_general | solution.py:208
  273.6 3.6 %fusion.15 = bf16[512,1536]{1,0:T(8,128)(2,1)S(1)} fusion(f32[512,1536]{1,0:T(8,128)} %convolution_add_fusion.1, f32[512,192]{0,1:T(8,128)} %convolution_maximum_fusion, bf16[512,1536]{1,0:T(8,128)(2,1)S(1)} %bitcast.135, bf16[4,3,192,1536]{3,2,1,0:T(8,128)(2,1)} %all-to-all-done.1), kind=kOutput, calls=%fused_computation.28 | convolution fusion | flops 605749248 | bytes 7864320 | tf_op jit(solution)/shard_map/dot_general | solution.py:208
  279.1 5.6 %all-to-all-start.5 = ((bf16[128,16,384]{2,1,0:T(8,128)(2,1)}), bf16[128,16,384]{2,1,0:T(8,128)(2,1)}, u32[]{:S(2)}, u32[]{:S(2)}) async-start(bf16[128,16,384]{2,1,0:T(8,128)(2,1)} %bitcast.41), calls=%async_computation.5 | async-start | bytes 3145728 | tf_op jit(solution)/shard_map/all_to_all | solution.py:216
  286.2 22.9 %all-to-all-done.5 = bf16[128,16,384]{2,1,0:T(8,128)(2,1)} async-done(((bf16[128,16,384]{2,1,0:T(8,128)(2,1)}), bf16[128,16,384]{2,1,0:T(8,128)(2,1)}, u32[]{:S(2)}, u32[]{:S(2)}) %all-to-all-start.5) | async-done | bytes 1572896 | tf_op jit(solution)/shard_map/all_to_all | solution.py:216
  309.1 3.9 %fusion.20 = bf16[256,384]{1,0:T(8,128)(2,1)} fusion(f32[256,2048]{1,0:T(8,128)S(1)} %select_reduce_fusion, bf16[2048,384]{1,0:T(8,128)(2,1)} %bitcast.42, f32[256,384]{1,0:T(8,128)S(1)} %copy-done.3, bf16[256,384]{1,0:T(8,128)(2,1)S(1)} %copy-done.5), kind=kOutput, calls=%fused_computation.49 | convolution fusion | flops 2416508928 | bytes 4456448 | tf_op jit(solution)/shard_map/dot_general | solution.py:225
  (115 shorter events, 45.5 us)
Async XLA Ops:
  1.6 13.1 %copy-start.14 = (s32[3]{0:T(128)S(1)}, s32[3]{0:T(128)}, u32[]{:S(2)}) copy-start(s32[3]{0:T(128)} %param.14) | copy-start | bytes 40
  1.6 15.5 %copy-start.5 = (bf16[256,384]{1,0:T(8,128)(2,1)S(1)}, bf16[256,384]{1,0:T(8,128)(2,1)}, u32[]{:S(2)}) copy-start(bf16[256,384]{1,0:T(8,128)(2,1)} %param.10) | copy-start | bytes 589828
  2.9 35.6 %copy-start.8 = (bf16[1,192,1536]{2,1,0:T(8,128)(2,1)S(1)}, bf16[1,192,1536]{2,1,0:T(8,128)(2,1)}, u32[]{:S(2)}) copy-start(bf16[1,192,1536]{2,1,0:T(8,128)(2,1)} %param.19) | copy-start | bytes 1769476
  2.9 37.0 %all-to-all-start = ((bf16[32,48,512]{2,1,0:T(8,128)(2,1)}), bf16[32,48,512]{2,1,0:T(8,128)(2,1)}, u32[]{:S(2)}, u32[]{:S(2)}) async-start(bf16[32,48,512]{2,1,0:T(8,128)(2,1)} %broadcast_in_dim.39), calls=%async_computation | async-start | bytes 3145728 | tf_op jit(solution)/shard_map/all_to_all | solution.py:47
  42.7 10.0 %collective-permute-start = (bf16[256,128]{1,0:T(8,128)(2,1)S(1)}, bf16[256,128]{1,0:T(8,128)(2,1)S(1)}, u32[]{:S(2)}, u32[]{:S(2)}) collective-permute-start(bf16[256,128]{1,0:T(8,128)(2,1)S(1)} %fusion.84), channel_id=1, source_target_pairs={{0,1},{1,0},{2,3},{3,2},{4,5},{5,4},{6,7},{7,6},{8,9},{9,8},{10,11... | collective-permute-start | bytes 196616 | tf_op jit(solution)/shard_map/ppermute | solution.py:92
  47.0 118.3 %all-to-all-start.1 = ((bf16[4,3,192,1536]{3,2,1,0:T(8,128)(2,1)}), bf16[4,3,192,1536]{3,2,1,0:T(8,128)(2,1)}, u32[]{:S(2)}, u32[]{:S(2)}) async-start(bf16[4,3,192,1536]{3,2,1,0:T(8,128)(2,1)} %broadcast_in_dim.41), calls=%async_computation.1 | async-start | bytes 14155776 | tf_op jit(solution)/shard_map/all_to_all | solution.py:76
  52.7 105.8 %copy-start.7 = (f32[256,512]{1,0:T(8,128)S(1)}, f32[256,512]{1,0:T(8,128)}, u32[]{:S(2)}) copy-start(f32[256,512]{1,0:T(8,128)} %copy-done.6) | copy-start | bytes 1572868
  52.7 22.2 %collective-permute-start.1 = (bf16[256,256]{1,0:T(8,128)(2,1)S(1)}, bf16[256,256]{1,0:T(8,128)(2,1)S(1)}, u32[]{:S(2)}, u32[]{:S(2)}) collective-permute-start(bf16[256,256]{1,0:T(8,128)(2,1)S(1)} %pad_maximum_fusion.1), channel_id=1, source_target_pairs={{0,4},{1,9},{2,6},{3,11},{4,8},{5,13},{6,10},{7,15},{8,12},{9,17},... | collective-permute-start | bytes 393224 | tf_op jit(solution)/shard_map/ppermute | solution.py:107
  58.2 88.0 %collective-permute-start.2 = (bf16[256,256]{1,0:T(8,128)(2,1)S(1)}, bf16[256,256]{1,0:T(8,128)(2,1)S(1)}, u32[]{:S(2)}, u32[]{:S(2)}) collective-permute-start(bf16[256,256]{1,0:T(8,128)(2,1)S(1)} %pad_maximum_fusion.1), channel_id=1, source_target_pairs={{0,12},{1,17},{2,14},{3,19},{4,16},{5,21},{6,18},{7,23},{8,20},{9,... | collective-permute-start | bytes 393224 | tf_op jit(solution)/shard_map/ppermute | solution.py:107
  63.9 85.5 %collective-permute-start.3 = (bf16[256,256]{1,0:T(8,128)(2,1)S(1)}, bf16[256,256]{1,0:T(8,128)(2,1)S(1)}, u32[]{:S(2)}, u32[]{:S(2)}) collective-permute-start(bf16[256,256]{1,0:T(8,128)(2,1)S(1)} %pad_maximum_fusion.1), channel_id=1, source_target_pairs={{0,20},{1,25},{2,22},{3,27},{4,24},{5,29},{6,26},{7,31},{8,28},{9,... | collective-permute-start | bytes 393224 | tf_op jit(solution)/shard_map/ppermute | solution.py:107
  69.8 83.9 %collective-permute-start.4 = (bf16[256,256]{1,0:T(8,128)(2,1)S(1)}, bf16[256,256]{1,0:T(8,128)(2,1)S(1)}, u32[]{:S(2)}, u32[]{:S(2)}) collective-permute-start(bf16[256,256]{1,0:T(8,128)(2,1)S(1)} %pad_maximum_fusion.1), channel_id=1, source_target_pairs={{0,28},{1,33},{2,30},{3,35},{4,32},{5,37},{6,34},{7,39},{8,36},{9,... | collective-permute-start | bytes 393224 | tf_op jit(solution)/shard_map/ppermute | solution.py:107
  72.2 81.5 %collective-permute-start.5 = (bf16[256,256]{1,0:T(8,128)(2,1)S(1)}, bf16[256,256]{1,0:T(8,128)(2,1)S(1)}, u32[]{:S(2)}, u32[]{:S(2)}) collective-permute-start(bf16[256,256]{1,0:T(8,128)(2,1)S(1)} %pad_maximum_fusion.1), channel_id=1, source_target_pairs={{0,36},{1,41},{2,38},{3,43},{4,40},{5,45},{6,42},{7,47},{8,44},{9,... | collective-permute-start | bytes 393224 | tf_op jit(solution)/shard_map/ppermute | solution.py:107
  75.0 78.8 %collective-permute-start.6 = (bf16[256,256]{1,0:T(8,128)(2,1)S(1)}, bf16[256,256]{1,0:T(8,128)(2,1)S(1)}, u32[]{:S(2)}, u32[]{:S(2)}) collective-permute-start(bf16[256,256]{1,0:T(8,128)(2,1)S(1)} %pad_maximum_fusion.1), channel_id=1, source_target_pairs={{0,44},{1,49},{2,46},{3,51},{4,48},{5,53},{6,50},{7,55},{8,52},{9,... | collective-permute-start | bytes 393224 | tf_op jit(solution)/shard_map/ppermute | solution.py:107
  146.2 7.5 %collective-permute-start.7 = (bf16[256,256]{1,0:T(8,128)(2,1)S(1)}, bf16[256,256]{1,0:T(8,128)(2,1)S(1)}, u32[]{:S(2)}, u32[]{:S(2)}) collective-permute-start(bf16[256,256]{1,0:T(8,128)(2,1)S(1)} %pad_maximum_fusion.1), channel_id=1, source_target_pairs={{0,52},{1,57},{2,54},{3,59},{4,56},{5,61},{6,58},{7,63},{8,60},{9,... | collective-permute-start | bytes 393224 | tf_op jit(solution)/shard_map/ppermute | solution.py:107
  149.3 6.2 %collective-permute-start.8 = (bf16[256,256]{1,0:T(8,128)(2,1)S(1)}, bf16[256,256]{1,0:T(8,128)(2,1)S(1)}, u32[]{:S(2)}, u32[]{:S(2)}) collective-permute-start(bf16[256,256]{1,0:T(8,128)(2,1)S(1)} %pad_maximum_fusion.1), channel_id=1, source_target_pairs={{0,60},{1,65},{2,62},{3,67},{4,64},{5,69},{6,66},{7,71},{8,68},{9,... | collective-permute-start | bytes 393224 | tf_op jit(solution)/shard_map/ppermute | solution.py:107
  155.6 6.8 %collective-permute-start.9 = (bf16[8,256,256]{2,1,0:T(8,128)(2,1)S(1)}, bf16[8,256,256]{2,1,0:T(8,128)(2,1)}, u32[]{:S(2)}, u32[]{:S(2)}) collective-permute-start(bf16[8,256,256]{2,1,0:T(8,128)(2,1)S(1)} %bitcast_dynamic-update-slice_fusion), channel_id=1, source_target_pairs={{0,1},{1,0},{2,3},{3,2},{4,5},{5,4},{6,7},{7,6},{8,9},{9,8},{10,11... | collective-permute-start | bytes 3145736 | tf_op jit(solution)/shard_map/ppermute | solution.py:109
  165.3 9.6 %copy-start.9 = (bf16[256,3,64]{2,0,1:T(8,128)(2,1)S(1)}, bf16[256,3,64]{2,0,1:T(8,128)(2,1)}, u32[]{:S(2)}) copy-start(bf16[256,3,64]{2,0,1:T(8,128)(2,1)} %get-tuple-element.19) | copy-start | bytes 294916
  165.3 9.6 %copy-start.10 = (bf16[256,3,64]{2,0,1:T(8,128)(2,1)S(1)}, bf16[256,3,64]{2,0,1:T(8,128)(2,1)}, u32[]{:S(2)}) copy-start(bf16[256,3,64]{2,0,1:T(8,128)(2,1)} %get-tuple-element.20) | copy-start | bytes 294916
  166.5 31.7 %all-to-all-start.2 = ((bf16[32,48,384]{2,1,0:T(8,128)(2,1)}), bf16[32,48,384]{2,1,0:T(8,128)(2,1)S(1)}, u32[]{:S(2)}, u32[]{:S(2)}) async-start(bf16[32,48,384]{2,1,0:T(8,128)(2,1)} %broadcast_in_dim.47), calls=%async_computation.2 | async-start | bytes 2359296 | tf_op jit(solution)/shard_map/all_to_all | solution.py:47
  182.5 8.7 %copy-start.4 = (bf16[4352,256]{1,0:T(8,128)(2,1)S(1)}, bf16[4352,256]{1,0:T(8,128)(2,1)}, u32[]{:S(2)}) copy-start(bf16[4352,256]{1,0:T(8,128)(2,1)} %maximum_maximum_fusion) | copy-start | bytes 6684676
  199.8 14.5 %all-to-all-start.3 = ((bf16[256,4,384]{2,0,1:T(8,128)(2,1)}), bf16[256,4,384]{2,0,1:T(8,128)(2,1)S(1)}, u32[]{:S(2)}, u32[]{:S(2)}) async-start(bf16[256,4,384]{2,0,1:T(8,128)(2,1)} %bitcast.127), calls=%async_computation.3 | async-start | bytes 1572864 | tf_op jit(solution)/shard_map/all_to_all | solution.py:160
  214.5 35.1 %copy-start.2 = (f32[256,384]{1,0:T(8,128)}, f32[256,384]{1,0:T(8,128)S(1)}, u32[]{:S(2)}) copy-start(f32[256,384]{1,0:T(8,128)S(1)} %convert_reduce_fusion) | copy-start | bytes 1179652
  279.1 30.0 %copy-start.3 = (f32[256,384]{1,0:T(8,128)S(1)}, f32[256,384]{1,0:T(8,128)}, u32[]{:S(2)}) copy-start(f32[256,384]{1,0:T(8,128)} %copy-done.2) | copy-start | bytes 1179652
  279.1 30.0 %all-to-all-start.5 = ((bf16[128,16,384]{2,1,0:T(8,128)(2,1)}), bf16[128,16,384]{2,1,0:T(8,128)(2,1)}, u32[]{:S(2)}, u32[]{:S(2)}) async-start(bf16[128,16,384]{2,1,0:T(8,128)(2,1)} %bitcast.41), calls=%async_computation.5 | async-start | bytes 3145728 | tf_op jit(solution)/shard_map/all_to_all | solution.py:216
  (6 other events, 22.3 us)

commit v15 on v13

--- a/solution.py
+++ b/solution.py
@@ -217,11 +217,10 @@
         ).reshape(tok_rows, top_count, experts * capacity),
         axis=1,
     )
-    moe_total = jnp.dot(
-        combine,
-        returned.astype(jnp.float32),
-        precision=lax.Precision.HIGHEST,
-        preferred_element_type=jnp.float32,
+    combine_hi = combine.astype(jnp.bfloat16)
+    combine_lo = (combine - combine_hi.astype(jnp.float32)).astype(jnp.bfloat16)
+    moe_total = jnp.dot(combine_hi, returned, preferred_element_type=jnp.float32) + jnp.dot(
+        combine_lo, returned, preferred_element_type=jnp.float32
     )
     return (residual_f + moe_total).astype(jnp.bfloat16)
 

time: 242 us -> 243 us (level)
    dot_general x1 -> x2, matrix products: 3.89 us -> 4.94 us  [the longest x1 2.82 us: local(): jnp.dot(combine_lo, returned, preferred_element_type=jnp.float32)]
where the time goes in v15:
time: 243 us; the launch traced here: 242 us
  starting transfers between devices  66.5 us (27%)
  blocking collectives  56.1 us (23%)
  matrix products  32.2 us (13%)
  waiting for transfers between devices  31.9 us (13%)
  other arithmetic  24 us (10%)
  local copies, waits for them, and re-layouts  16.7 us (7%)
  between operations  15.1 us (6%)
    all_to_all x1, blocking collectives, local(): arrived = lax.all_to_all(buffer, ('seq', 'mp'), 0, 0, tiled=True)  34.1 us
    ppermute x8, starting transfers between devices, local(): fetched.append(lax.ppermute(kv_own, ('seq', 'mp'), pairs))  34 us
    all_to_all x1, waiting for transfers between devices, local(): returned = lax.all_to_all(outgoing, ('seq', 'mp'), 0, 0, tiled=True)  22.9 us
    all_to_all x2, starting transfers between devices, gather_seq(): return lax.all_to_all(spread, 'seq', 0, 0, tiled=True)  22.5 us
    all_gather x1, blocking collectives, local(): whole = lax.all_gather(hidden_in, 'mp', axis=1, tiled=True)  22 us
    reduce_sum x1, other arithmetic, local(): total = jnp.sum(probs, axis=-1)  8.52 us
    all_to_all x1, waiting for transfers between devices, local(): lax.all_to_all(partial_out.astype(jnp.bfloat16), 'mp', 1, 0, tiled=True)  8.39 us
    dot_general x1, matrix products, local(): jnp.dot(active, w_down, preferred_element_type=jnp.float32)  7.18 us
  transfers between devices with their start and end apart: 15, of which 3 were waited for; matrix products, arithmetic and copies ran while one was open for 20% of the time, Pallas kernels for 0%

profile of v15, /device:TPU:1, one launch (start us, length us, event | category | flops | bytes accessed | tf_op | source)
XLA Modules:
  0.0 242.4 jit_solution(2169323665571691847)
XLA Ops:
  9.5 11.3 %all-to-all-start = ((bf16[32,48,512]{2,1,0:T(8,128)(2,1)}), bf16[32,48,512]{2,1,0:T(8,128)(2,1)S(1)}, u32[]{:S(2)}, u32[]{:S(2)}) async-start(bf16[32,48,512]{2,1,0:T(8,128)(2,1)} %broadcast_in_dim.37), calls=%async_computation | async-start | bytes 3145728 | tf_op jit(solution)/shard_map/all_to_all | solution.py:47
  20.9 2.5 %pad_maximum_fusion = bf16[3,192,1536]{2,1,0:T(8,128)(2,1)} fusion(bf16[1,192,1536]{2,1,0:T(8,128)(2,1)S(1)} %copy-done.2, bf16[1,192,1536]{2,1,0:T(8,128)(2,1)S(1)} %copy-done.3, bf16[1,192,1536]{2,1,0:T(8,128)(2,1)} %param.17), kind=kLoop, calls=%fused_computation.37 | loop fusion | flops 1769472 | bytes 3538944 | tf_op jit(solution)/shard_map/concatenate | solution.py:63
  26.0 22.0 %all_gather.6 = bf16[256,1536]{1,0:T(8,128)(2,1)S(1)} all-gather(bf16[256,384]{1,0:T(8,128)(2,1)S(1)} %copy-done.1), channel_id=1, replica_groups=mesh['seq'=32,'mp'=4] {'mp'}, dimensions={1}, use_global_device_ids=true | all-gather | bytes 983040 | tf_op jit(solution)/shard_map/all_gather | solution.py:71
  51.0 5.1 %collective-permute-start.1 = (bf16[256,256]{1,0:T(8,128)(2,1)S(1)}, bf16[256,256]{1,0:T(8,128)(2,1)S(1)}, u32[]{:S(2)}, u32[]{:S(2)}) collective-permute-start(bf16[256,256]{1,0:T(8,128)(2,1)S(1)} %pad_maximum_fusion.1), channel_id=1, source_target_pairs={{0,4},{1,9},{2,6},{3,11},{4,8},{5,13},{6,10},{7,15},{8,12},{9,17},... | collective-permute-start | bytes 393224 | tf_op jit(solution)/shard_map/ppermute | solution.py:105
  56.7 5.0 %collective-permute-start.2 = (bf16[256,256]{1,0:T(8,128)(2,1)S(1)}, bf16[256,256]{1,0:T(8,128)(2,1)S(1)}, u32[]{:S(2)}, u32[]{:S(2)}) collective-permute-start(bf16[256,256]{1,0:T(8,128)(2,1)S(1)} %pad_maximum_fusion.1), channel_id=1, source_target_pairs={{0,12},{1,17},{2,14},{3,19},{4,16},{5,21},{6,18},{7,23},{8,20},{9,... | collective-permute-start | bytes 393224 | tf_op jit(solution)/shard_map/ppermute | solution.py:105
  61.7 8.5 %collective-permute-start.3 = (bf16[256,256]{1,0:T(8,128)(2,1)S(1)}, bf16[256,256]{1,0:T(8,128)(2,1)S(1)}, u32[]{:S(2)}, u32[]{:S(2)}) collective-permute-start(bf16[256,256]{1,0:T(8,128)(2,1)S(1)} %pad_maximum_fusion.1), channel_id=1, source_target_pairs={{0,20},{1,25},{2,22},{3,27},{4,24},{5,29},{6,26},{7,31},{8,28},{9,... | collective-permute-start | bytes 393224 | tf_op jit(solution)/shard_map/ppermute | solution.py:105
  70.3 2.1 collective-permute-start.4
  72.4 2.1 collective-permute-start.5
  74.5 4.3 %collective-permute-start.6 = (bf16[256,256]{1,0:T(8,128)(2,1)S(1)}, bf16[256,256]{1,0:T(8,128)(2,1)S(1)}, u32[]{:S(2)}, u32[]{:S(2)}) collective-permute-start(bf16[256,256]{1,0:T(8,128)(2,1)S(1)} %pad_maximum_fusion.1), channel_id=1, source_target_pairs={{0,44},{1,49},{2,46},{3,51},{4,48},{5,53},{6,50},{7,55},{8,52},{9,... | collective-permute-start | bytes 393224 | tf_op jit(solution)/shard_map/ppermute | solution.py:105
  82.1 4.9 %collective-permute-start.8 = (bf16[256,256]{1,0:T(8,128)(2,1)S(1)}, bf16[256,256]{1,0:T(8,128)(2,1)S(1)}, u32[]{:S(2)}, u32[]{:S(2)}) collective-permute-start(bf16[256,256]{1,0:T(8,128)(2,1)S(1)} %pad_maximum_fusion.1), channel_id=1, source_target_pairs={{0,60},{1,65},{2,62},{3,67},{4,64},{5,69},{6,66},{7,71},{8,68},{9,... | collective-permute-start | bytes 393224 | tf_op jit(solution)/shard_map/ppermute | solution.py:105
  95.9 11.1 %all-to-all-start.1 = ((bf16[32,48,384]{2,1,0:T(8,128)(2,1)}), bf16[32,48,384]{2,1,0:T(8,128)(2,1)S(1)}, u32[]{:S(2)}, u32[]{:S(2)}) async-start(bf16[32,48,384]{2,1,0:T(8,128)(2,1)} %broadcast_in_dim.44), calls=%async_computation.1 | async-start | bytes 2359296 | tf_op jit(solution)/shard_map/all_to_all | solution.py:47
  110.0 6.4 %fusion = (f32[3,256]{1,0:T(4,128)S(1)}, f32[3,256,4352]{2,1,0:T(8,128)}) fusion(pred[256,4352]{1,0:T(8,128)(4,1)S(1)} %fusion.10, bf16[4352,256]{1,0:T(8,128)(2,1)S(1)} %maximum_maximum_fusion, bf16[256,3,64]{2,0,1:T(8,128)(2,1)S(1)} %get-tuple-element.14, bf16[256,3,64]{2,0,1:T(8,128)(2,1)S(1)} %get-tuple-element.13), kind=kOutput, calls=%fused_computation.2 | convolution fusion | flops 866057472 | bytes 15993856 | tf_op jit(solution)/shard_map/hqd,kd->hqk/dot_general | solution.py:131
  116.4 8.5 %fusion.1 = f32[3,256]{1,0:T(4,128)S(1)} fusion(f32[3,256,4352]{2,1,0:T(8,128)} %get-tuple-element.26, f32[3,256]{1,0:T(4,128)S(1)} %get-tuple-element.25, pred[256,4352]{1,0:T(8,128)(4,1)S(1)} %fusion.10), kind=kLoop, calls=%fused_computation.3 | loop fusion | flops 13368576 | bytes 14489600 | tf_op jit(solution)/shard_map/reduce_sum | solution.py:146
  124.9 7.0 %fusion.28 = bf16[256,3,128]{0,2,1:T(8,128)(2,1)S(1)} fusion(bf16[4352,256]{1,0:T(8,128)(2,1)S(1)} %maximum_maximum_fusion, f32[3,256,4352]{2,1,0:T(8,128)} %get-tuple-element.26, f32[3,256]{1,0:T(4,128)S(1)} %get-tuple-element.25, pred[256,4352]{1,0:T(8,128)(4,1)S(1)} %fusion.10, f32[256,3]{0,1:T(4,128)S(1)} %bitcast.108), kind=kOutput, calls=%fused_computation.56 | convolution fusion | flops 865861632 | bytes 15802368 | tf_op jit(solution)/shard_map/hqk,kd->hqd/dot_general | solution.py:147
  133.6 3.8 %all-to-all-start.2 = ((bf16[256,4,384]{2,0,1:T(8,128)(2,1)}), bf16[256,4,384]{2,0,1:T(8,128)(2,1)S(1)}, u32[]{:S(2)}, u32[]{:S(2)}) async-start(bf16[256,4,384]{2,0,1:T(8,128)(2,1)} %bitcast.94), calls=%async_computation.2 | async-start | bytes 1572864 | tf_op jit(solution)/shard_map/all_to_all | solution.py:157
  139.7 8.4 %all-to-all-done.2 = bf16[256,4,384]{2,0,1:T(8,128)(2,1)S(1)} async-done(((bf16[256,4,384]{2,0,1:T(8,128)(2,1)}), bf16[256,4,384]{2,0,1:T(8,128)(2,1)S(1)}, u32[]{:S(2)}, u32[]{:S(2)}) %all-to-all-start.2) | async-done | bytes 786464 | tf_op jit(solution)/shard_map/all_to_all | solution.py:157
  148.9 34.1 %all_to_all.52 = bf16[128,16,384]{2,1,0:T(8,128)(2,1)S(1)} all-to-all(bf16[128,16,384]{2,1,0:T(8,128)(2,1)S(1)} %bitcast.96), channel_id=1, replica_groups=mesh['seq'=32,'mp'=4] {'seq','mp'}, dimensions={0} | all-to-all | bytes 3145728 | tf_op jit(solution)/shard_map/all_to_all | solution.py:183
  184.8 4.2 %fusion.15 = f32[512,768]{1,0:T(8,128)} fusion(bf16[512,1536]{1,0:T(8,128)(2,1)S(1)} %bitcast.103, bf16[3,768,1536]{2,1,0:T(8,128)(2,1)} %all-gather.2.cloned.1.call-done), kind=kOutput, calls=%fused_computation.30 | convolution fusion | flops 1207959552 | bytes 5505024 | tf_op jit(solution)/shard_map/dot_general | solution.py:201
  189.0 7.2 %convolution_convert_fusion = bf16[512,1536]{1,0:T(8,128)(2,1)} fusion(bf16[3,768,1536]{2,1,0:T(8,128)(2,1)} %all-gather.2.cloned.1.call-done, f32[512,768]{1,0:T(8,128)} %fusion.15, bf16[512,1536]{1,0:T(8,128)(2,1)S(1)} %bitcast.104), kind=kOutput, calls=%fused_computation.25 | convolution fusion | flops 2417885184 | bytes 9437184 | tf_op jit(solution)/shard_map/dot_general | solution.py:205
  196.2 3.0 %reshape.382 = bf16[32,16,4,384]{3,2,1,0:T(4,128)(2,1)S(1)} reshape(bf16[512,1536]{1,0:T(8,128)(2,1)} %convolution_convert_fusion) | data formatting | bytes 3145728 | tf_op jit(solution)/shard_map/reshape | solution.py:207
  200.6 5.6 %all-to-all-start.4 = ((bf16[128,16,384]{2,1,0:T(8,128)(2,1)}), bf16[128,16,384]{2,1,0:T(8,128)(2,1)}, u32[]{:S(2)}, u32[]{:S(2)}) async-start(bf16[128,16,384]{2,1,0:T(8,128)(2,1)} %bitcast.32), calls=%async_computation.4 | async-start | bytes 3145728 | tf_op jit(solution)/shard_map/all_to_all | solution.py:211
  207.7 22.9 %all-to-all-done.4 = bf16[128,16,384]{2,1,0:T(8,128)(2,1)} async-done(((bf16[128,16,384]{2,1,0:T(8,128)(2,1)}), bf16[128,16,384]{2,1,0:T(8,128)(2,1)}, u32[]{:S(2)}, u32[]{:S(2)}) %all-to-all-start.4) | async-done | bytes 1572896 | tf_op jit(solution)/shard_map/all_to_all | solution.py:211
  230.6 2.1 fusion.34
  232.7 2.8 %fusion.22 = bf16[256,384]{1,0:T(8,128)(2,1)} fusion(f32[256,384]{1,0:T(8,128)S(1)} %fusion.34, bf16[2048,384]{1,0:T(8,128)(2,1)} %bitcast.33, f32[256,2048]{1,0:T(8,128)S(1)} %select_reduce_fusion, f32[256,384]{1,0:T(8,128)S(1)} %convert_reduce_fusion, bf16[256,384]{1,0:T(8,128)(2,1)S(1)} %copy-done.1), kind=kOutput, calls=%fused_computation.46 | convolution fusion | flops 405438464 | bytes 4849664 | tf_op jit(solution)/shard_map/dot_general | solution.py:222
  (96 shorter events, 32.2 us)
Async XLA Ops:
  6.5 0.8 copy-start
  8.1 12.8 %copy-start.2 = (bf16[1,192,1536]{2,1,0:T(8,128)(2,1)S(1)}, bf16[1,192,1536]{2,1,0:T(8,128)(2,1)}, u32[]{:S(2)}) copy-start(bf16[1,192,1536]{2,1,0:T(8,128)(2,1)} %param.19) | copy-start | bytes 1769476
  8.1 12.8 %copy-start.3 = (bf16[1,192,1536]{2,1,0:T(8,128)(2,1)S(1)}, bf16[1,192,1536]{2,1,0:T(8,128)(2,1)}, u32[]{:S(2)}) copy-start(bf16[1,192,1536]{2,1,0:T(8,128)(2,1)} %param.18) | copy-start | bytes 1769476
  9.5 38.8 %all-to-all-start = ((bf16[32,48,512]{2,1,0:T(8,128)(2,1)}), bf16[32,48,512]{2,1,0:T(8,128)(2,1)S(1)}, u32[]{:S(2)}, u32[]{:S(2)}) async-start(bf16[32,48,512]{2,1,0:T(8,128)(2,1)} %broadcast_in_dim.37), calls=%async_computation | async-start | bytes 3145728 | tf_op jit(solution)/shard_map/all_to_all | solution.py:47
  20.8 2.8 %copy-start.7 = (s32[3]{0:T(128)S(1)}, s32[3]{0:T(128)}, u32[]{:S(2)}) copy-start(s32[3]{0:T(128)} %param.14) | copy-start | bytes 40
  20.8 5.2 %copy-start.1 = (bf16[256,384]{1,0:T(8,128)(2,1)S(1)}, bf16[256,384]{1,0:T(8,128)(2,1)}, u32[]{:S(2)}) copy-start(bf16[256,384]{1,0:T(8,128)(2,1)} %param.10) | copy-start | bytes 589828
  20.8 164.0 %all-gather.2.cloned.1.call-start = ((), (), s32[]{:S(2)}) async-start(), calls=%async_computation.5 | async-start | bytes 8847360 | tf_op jit(solution)/shard_map/all_gather | solution.py:62
  49.6 1.3 collective-permute-start
  51.0 23.5 %collective-permute-start.1 = (bf16[256,256]{1,0:T(8,128)(2,1)S(1)}, bf16[256,256]{1,0:T(8,128)(2,1)S(1)}, u32[]{:S(2)}, u32[]{:S(2)}) collective-permute-start(bf16[256,256]{1,0:T(8,128)(2,1)S(1)} %pad_maximum_fusion.1), channel_id=1, source_target_pairs={{0,4},{1,9},{2,6},{3,11},{4,8},{5,13},{6,10},{7,15},{8,12},{9,17},... | collective-permute-start | bytes 393224 | tf_op jit(solution)/shard_map/ppermute | solution.py:105
  56.7 22.8 %collective-permute-start.2 = (bf16[256,256]{1,0:T(8,128)(2,1)S(1)}, bf16[256,256]{1,0:T(8,128)(2,1)S(1)}, u32[]{:S(2)}, u32[]{:S(2)}) collective-permute-start(bf16[256,256]{1,0:T(8,128)(2,1)S(1)} %pad_maximum_fusion.1), channel_id=1, source_target_pairs={{0,12},{1,17},{2,14},{3,19},{4,16},{5,21},{6,18},{7,23},{8,20},{9,... | collective-permute-start | bytes 393224 | tf_op jit(solution)/shard_map/ppermute | solution.py:105
  61.7 20.4 %collective-permute-start.3 = (bf16[256,256]{1,0:T(8,128)(2,1)S(1)}, bf16[256,256]{1,0:T(8,128)(2,1)S(1)}, u32[]{:S(2)}, u32[]{:S(2)}) collective-permute-start(bf16[256,256]{1,0:T(8,128)(2,1)S(1)} %pad_maximum_fusion.1), channel_id=1, source_target_pairs={{0,20},{1,25},{2,22},{3,27},{4,24},{5,29},{6,26},{7,31},{8,28},{9,... | collective-permute-start | bytes 393224 | tf_op jit(solution)/shard_map/ppermute | solution.py:105
  70.3 17.4 %collective-permute-start.4 = (bf16[256,256]{1,0:T(8,128)(2,1)S(1)}, bf16[256,256]{1,0:T(8,128)(2,1)S(1)}, u32[]{:S(2)}, u32[]{:S(2)}) collective-permute-start(bf16[256,256]{1,0:T(8,128)(2,1)S(1)} %pad_maximum_fusion.1), channel_id=1, source_target_pairs={{0,28},{1,33},{2,30},{3,35},{4,32},{5,37},{6,34},{7,39},{8,36},{9,... | collective-permute-start | bytes 393224 | tf_op jit(solution)/shard_map/ppermute | solution.py:105
  72.4 15.9 %collective-permute-start.5 = (bf16[256,256]{1,0:T(8,128)(2,1)S(1)}, bf16[256,256]{1,0:T(8,128)(2,1)S(1)}, u32[]{:S(2)}, u32[]{:S(2)}) collective-permute-start(bf16[256,256]{1,0:T(8,128)(2,1)S(1)} %pad_maximum_fusion.1), channel_id=1, source_target_pairs={{0,36},{1,41},{2,38},{3,43},{4,40},{5,45},{6,42},{7,47},{8,44},{9,... | collective-permute-start | bytes 393224 | tf_op jit(solution)/shard_map/ppermute | solution.py:105
  74.5 14.5 %collective-permute-start.6 = (bf16[256,256]{1,0:T(8,128)(2,1)S(1)}, bf16[256,256]{1,0:T(8,128)(2,1)S(1)}, u32[]{:S(2)}, u32[]{:S(2)}) collective-permute-start(bf16[256,256]{1,0:T(8,128)(2,1)S(1)} %pad_maximum_fusion.1), channel_id=1, source_target_pairs={{0,44},{1,49},{2,46},{3,51},{4,48},{5,53},{6,50},{7,55},{8,52},{9,... | collective-permute-start | bytes 393224 | tf_op jit(solution)/shard_map/ppermute | solution.py:105
  79.5 10.1 %collective-permute-start.7 = (bf16[256,256]{1,0:T(8,128)(2,1)S(1)}, bf16[256,256]{1,0:T(8,128)(2,1)S(1)}, u32[]{:S(2)}, u32[]{:S(2)}) collective-permute-start(bf16[256,256]{1,0:T(8,128)(2,1)S(1)} %pad_maximum_fusion.1), channel_id=1, source_target_pairs={{0,52},{1,57},{2,54},{3,59},{4,56},{5,61},{6,58},{7,63},{8,60},{9,... | collective-permute-start | bytes 393224 | tf_op jit(solution)/shard_map/ppermute | solution.py:105
  82.1 8.2 %collective-permute-start.8 = (bf16[256,256]{1,0:T(8,128)(2,1)S(1)}, bf16[256,256]{1,0:T(8,128)(2,1)S(1)}, u32[]{:S(2)}, u32[]{:S(2)}) collective-permute-start(bf16[256,256]{1,0:T(8,128)(2,1)S(1)} %pad_maximum_fusion.1), channel_id=1, source_target_pairs={{0,60},{1,65},{2,62},{3,67},{4,64},{5,69},{6,66},{7,71},{8,68},{9,... | collective-permute-start | bytes 393224 | tf_op jit(solution)/shard_map/ppermute | solution.py:105
  91.0 17.2 %collective-permute-start.9 = (bf16[8,256,256]{2,1,0:T(8,128)(2,1)}, bf16[8,256,256]{2,1,0:T(8,128)(2,1)}, u32[]{:S(2)}, u32[]{:S(2)}) collective-permute-start(bf16[8,256,256]{2,1,0:T(8,128)(2,1)} %bitcast_dynamic-update-slice_fusion), channel_id=1, source_target_pairs={{0,1},{1,0},{2,3},{3,2},{4,5},{5,4},{6,7},{7,6},{8,9},{9,8},{10,11... | collective-permute-start | bytes 3145736 | tf_op jit(solution)/shard_map/ppermute | solution.py:107
  93.0 1.8 copy-start.4
  95.9 36.0 %all-to-all-start.1 = ((bf16[32,48,384]{2,1,0:T(8,128)(2,1)}), bf16[32,48,384]{2,1,0:T(8,128)(2,1)S(1)}, u32[]{:S(2)}, u32[]{:S(2)}) async-start(bf16[32,48,384]{2,1,0:T(8,128)(2,1)} %broadcast_in_dim.44), calls=%async_computation.1 | async-start | bytes 2359296 | tf_op jit(solution)/shard_map/all_to_all | solution.py:47
  132.6 4.7 %copy-start.6 = (s32[256,4]{0,1:T(4,128)S(1)}, s32[256,4]{0,1:T(4,128)}, u32[]{:S(2)}) copy-start(s32[256,4]{0,1:T(4,128)} %param.15) | copy-start | bytes 12292
  133.6 14.6 %all-to-all-start.2 = ((bf16[256,4,384]{2,0,1:T(8,128)(2,1)}), bf16[256,4,384]{2,0,1:T(8,128)(2,1)S(1)}, u32[]{:S(2)}, u32[]{:S(2)}) async-start(bf16[256,4,384]{2,0,1:T(8,128)(2,1)} %bitcast.94), calls=%async_computation.2 | async-start | bytes 1572864 | tf_op jit(solution)/shard_map/all_to_all | solution.py:157
  200.6 5.6 %copy-start.5 = (f32[256,4]{0,1:T(4,128)S(1)}, f32[256,4]{0,1:T(4,128)}, u32[]{:S(2)}) copy-start(f32[256,4]{0,1:T(4,128)} %param.16) | copy-start | bytes 12292
  200.6 30.0 %all-to-all-start.4 = ((bf16[128,16,384]{2,1,0:T(8,128)(2,1)}), bf16[128,16,384]{2,1,0:T(8,128)(2,1)}, u32[]{:S(2)}, u32[]{:S(2)}) async-start(bf16[128,16,384]{2,1,0:T(8,128)(2,1)} %bitcast.32), calls=%async_computation.4 | async-start | bytes 3145728 | tf_op jit(solution)/shard_map/all_to_all | solution.py:211
Sparse Core Ops, SparseCore 0:
  23.6 85.0 all-gather.1

commit v16 on v5

--- a/solution.py
+++ b/solution.py
@@ -59,9 +59,6 @@
     q_cols = heads_here * HD
     kv_group = mp_index * heads_here // (HQ // KVH)
 
-    expert_all = lax.all_gather(
-        jnp.concatenate([expert_gate, expert_up, expert_down], axis=0), "mp", axis=1, tiled=True
-    )
 
     core = mp_index % 2
     kv_col = jnp.where(core == 0, kv_group * HD, KVH * HD + kv_group * HD)
@@ -69,6 +66,10 @@
     w_qkv = gather_seq(jnp.concatenate([wq, kv_cols], axis=1), seq_count)
 
     whole = lax.all_gather(hidden_in, "mp", axis=1, tiled=True)
+    expert_own, whole = lax.optimization_barrier(
+        (jnp.concatenate([expert_gate, expert_up, expert_down], axis=0), whole)
+    )
+    expert_all = lax.all_gather(expert_own, "mp", axis=1, tiled=True)
     whole_f = whole.astype(jnp.float32)
     normed = (
         whole_f * lax.rsqrt(jnp.sum(whole_f * whole_f, axis=-1, keepdims=True) / D + EPSILON)

time: 243 us -> 244 us (level)
  starting transfers between devices: 66.5 us -> 60.7 us
  blocking collectives: 56.1 us -> 61.6 us
    ppermute x8, starting transfers between devices: 34 us -> 28.5 us  [local(): fetched.append(lax.ppermute(kv_own, ('seq', 'mp'), pairs))]
    all_to_all x1, blocking collectives: 34.1 us -> 37.8 us  [local(): arrived = lax.all_to_all(buffer, ('seq', 'mp'), 0, 0, tiled=True)]
    unnamed x27 -> x25, local copies, waits for them, and re-layouts: 6.19 us -> 6.18 us
  transfers between devices with their start and end apart: 15 -> 15, of which waited for: 3 -> 4; matrix products, arithmetic and copies ran while one was open for 21% -> 21% of each run, Pallas kernels for 0% -> 0%
where the time goes in v16:
time: 244 us; the launch traced here: 243 us
  blocking collectives  61.6 us (25%)
  starting transfers between devices  60.7 us (25%)
  waiting for transfers between devices  33 us (14%)
  matrix products  31.2 us (13%)
  other arithmetic  25 us (10%)
  local copies, waits for them, and re-layouts  16.6 us (7%)
  between operations  15.1 us (6%)
    all_to_all x1, blocking collectives, local(): arrived = lax.all_to_all(buffer, ('seq', 'mp'), 0, 0, tiled=True)  37.8 us
    ppermute x8, starting transfers between devices, local(): fetched.append(lax.ppermute(kv_own, ('seq', 'mp'), pairs))  28.5 us
    all_gather x1, blocking collectives, local(): whole = lax.all_gather(hidden_in, 'mp', axis=1, tiled=True)  23.8 us
    all_to_all x1, waiting for transfers between devices, local(): returned = lax.all_to_all(outgoing, ('seq', 'mp'), 0, 0, tiled=True)  22.9 us
    all_to_all x2, starting transfers between devices, gather_seq(): return lax.all_to_all(spread, 'seq', 0, 0, tiled=True)  20.6 us
    all_to_all x1, waiting for transfers between devices, local(): lax.all_to_all(partial_out.astype(jnp.bfloat16), 'mp', 1, 0, tiled=True)  9.18 us
    reduce_sum x1, other arithmetic, local(): total = jnp.sum(probs, axis=-1)  9.02 us
    dot_general x1, matrix products, local(): jnp.dot(active, w_down, preferred_element_type=jnp.float32)  7.18 us
  transfers between devices with their start and end apart: 15, of which 4 were waited for; matrix products, arithmetic and copies ran while one was open for 21% of the time, Pallas kernels for 0%

profile of v16, /device:TPU:1, one launch (start us, length us, event | category | flops | bytes accessed | tf_op | source)
XLA Modules:
  0.0 243.3 jit_solution(5810584629084836297)
XLA Ops:
  9.4 11.5 %all-to-all-start = ((bf16[32,48,512]{2,1,0:T(8,128)(2,1)}), bf16[32,48,512]{2,1,0:T(8,128)(2,1)S(1)}, u32[]{:S(2)}, u32[]{:S(2)}) async-start(bf16[32,48,512]{2,1,0:T(8,128)(2,1)} %broadcast_in_dim.47), calls=%async_computation | async-start | bytes 3145728 | tf_op jit(solution)/shard_map/all_to_all | solution.py:47
  21.0 23.8 %all_gather.6 = bf16[256,1536]{1,0:T(8,128)(2,1)S(1)} all-gather(bf16[256,384]{1,0:T(8,128)(2,1)S(1)} %copy-done.1), channel_id=1, replica_groups=mesh['seq'=32,'mp'=4] {'mp'}, dimensions={1}, use_global_device_ids=true | all-gather | bytes 983040 | tf_op jit(solution)/shard_map/all_gather | solution.py:68
  44.7 2.7 %pad_maximum_fusion = bf16[3,192,1536]{2,1,0:T(8,128)(2,1)} fusion(bf16[1,192,1536]{2,1,0:T(8,128)(2,1)S(1)} %copy-done.2, bf16[1,192,1536]{2,1,0:T(8,128)(2,1)} %param.18, bf16[1,192,1536]{2,1,0:T(8,128)(2,1)} %param.17), kind=kLoop, calls=%fused_computation.37 | loop fusion | flops 1769472 | bytes 3538944 | tf_op jit(solution)/shard_map/concatenate | solution.py:70
  53.2 4.8 %collective-permute-start.1 = (bf16[256,256]{1,0:T(8,128)(2,1)S(1)}, bf16[256,256]{1,0:T(8,128)(2,1)S(1)}, u32[]{:S(2)}, u32[]{:S(2)}) collective-permute-start(bf16[256,256]{1,0:T(8,128)(2,1)S(1)} %pad_maximum_fusion.1), channel_id=1, source_target_pairs={{0,4},{1,9},{2,6},{3,11},{4,8},{5,13},{6,10},{7,15},{8,12},{9,17},... | collective-permute-start | bytes 393224 | tf_op jit(solution)/shard_map/ppermute | solution.py:106
  58.7 5.4 %collective-permute-start.2 = (bf16[256,256]{1,0:T(8,128)(2,1)S(1)}, bf16[256,256]{1,0:T(8,128)(2,1)S(1)}, u32[]{:S(2)}, u32[]{:S(2)}) collective-permute-start(bf16[256,256]{1,0:T(8,128)(2,1)S(1)} %pad_maximum_fusion.1), channel_id=1, source_target_pairs={{0,12},{1,17},{2,14},{3,19},{4,16},{5,21},{6,18},{7,23},{8,20},{9,... | collective-permute-start | bytes 393224 | tf_op jit(solution)/shard_map/ppermute | solution.py:106
  64.1 6.1 %collective-permute-start.3 = (bf16[256,256]{1,0:T(8,128)(2,1)S(1)}, bf16[256,256]{1,0:T(8,128)(2,1)S(1)}, u32[]{:S(2)}, u32[]{:S(2)}) collective-permute-start(bf16[256,256]{1,0:T(8,128)(2,1)S(1)} %pad_maximum_fusion.1), channel_id=1, source_target_pairs={{0,20},{1,25},{2,22},{3,27},{4,24},{5,29},{6,26},{7,31},{8,28},{9,... | collective-permute-start | bytes 393224 | tf_op jit(solution)/shard_map/ppermute | solution.py:106
  70.2 2.5 %collective-permute-start.4 = (bf16[256,256]{1,0:T(8,128)(2,1)S(1)}, bf16[256,256]{1,0:T(8,128)(2,1)S(1)}, u32[]{:S(2)}, u32[]{:S(2)}) collective-permute-start(bf16[256,256]{1,0:T(8,128)(2,1)S(1)} %pad_maximum_fusion.1), channel_id=1, source_target_pairs={{0,28},{1,33},{2,30},{3,35},{4,32},{5,37},{6,34},{7,39},{8,36},{9,... | collective-permute-start | bytes 393224 | tf_op jit(solution)/shard_map/ppermute | solution.py:106
  72.7 2.7 %collective-permute-start.5 = (bf16[256,256]{1,0:T(8,128)(2,1)S(1)}, bf16[256,256]{1,0:T(8,128)(2,1)S(1)}, u32[]{:S(2)}, u32[]{:S(2)}) collective-permute-start(bf16[256,256]{1,0:T(8,128)(2,1)S(1)} %pad_maximum_fusion.1), channel_id=1, source_target_pairs={{0,36},{1,41},{2,38},{3,43},{4,40},{5,45},{6,42},{7,47},{8,44},{9,... | collective-permute-start | bytes 393224 | tf_op jit(solution)/shard_map/ppermute | solution.py:106
  75.4 2.6 %collective-permute-start.6 = (bf16[256,256]{1,0:T(8,128)(2,1)S(1)}, bf16[256,256]{1,0:T(8,128)(2,1)S(1)}, u32[]{:S(2)}, u32[]{:S(2)}) collective-permute-start(bf16[256,256]{1,0:T(8,128)(2,1)S(1)} %pad_maximum_fusion.1), channel_id=1, source_target_pairs={{0,44},{1,49},{2,46},{3,51},{4,48},{5,53},{6,50},{7,55},{8,52},{9,... | collective-permute-start | bytes 393224 | tf_op jit(solution)/shard_map/ppermute | solution.py:106
  78.7 2.7 %collective-permute-start.7 = (bf16[256,256]{1,0:T(8,128)(2,1)S(1)}, bf16[256,256]{1,0:T(8,128)(2,1)S(1)}, u32[]{:S(2)}, u32[]{:S(2)}) collective-permute-start(bf16[256,256]{1,0:T(8,128)(2,1)S(1)} %pad_maximum_fusion.1), channel_id=1, source_target_pairs={{0,52},{1,57},{2,54},{3,59},{4,56},{5,61},{6,58},{7,63},{8,60},{9,... | collective-permute-start | bytes 393224 | tf_op jit(solution)/shard_map/ppermute | solution.py:106
  88.2 2.1 collective-permute-start.9
  94.8 9.1 %all-to-all-start.1 = ((bf16[32,48,384]{2,1,0:T(8,128)(2,1)}), bf16[32,48,384]{2,1,0:T(8,128)(2,1)S(1)}, u32[]{:S(2)}, u32[]{:S(2)}) async-start(bf16[32,48,384]{2,1,0:T(8,128)(2,1)} %broadcast_in_dim.51), calls=%async_computation.1 | async-start | bytes 2359296 | tf_op jit(solution)/shard_map/all_to_all | solution.py:47
  106.9 6.4 %fusion = (f32[3,256]{1,0:T(4,128)S(1)}, f32[3,256,4352]{2,1,0:T(8,128)}) fusion(pred[256,4352]{1,0:T(8,128)(4,1)S(1)} %fusion.11, bf16[4352,256]{1,0:T(8,128)(2,1)S(1)} %maximum_maximum_fusion, bf16[256,3,64]{2,0,1:T(8,128)(2,1)S(1)} %get-tuple-element.18, bf16[256,3,64]{2,0,1:T(8,128)(2,1)S(1)} %get-tuple-element.17), kind=kOutput, calls=%fused_computation.2 | convolution fusion | flops 866057472 | bytes 15993856 | tf_op jit(solution)/shard_map/hqd,kd->hqk/dot_general | solution.py:132
  113.3 9.0 %fusion.1 = f32[3,256]{1,0:T(4,128)S(1)} fusion(f32[3,256,4352]{2,1,0:T(8,128)} %get-tuple-element.30, f32[3,256]{1,0:T(4,128)S(1)} %get-tuple-element.29, pred[256,4352]{1,0:T(8,128)(4,1)S(1)} %fusion.11), kind=kLoop, calls=%fused_computation.3 | loop fusion | flops 16710912 | bytes 14489600 | tf_op jit(solution)/shard_map/reduce_sum | solution.py:147
  122.3 7.0 %fusion.28 = bf16[256,3,128]{0,2,1:T(8,128)(2,1)S(1)} fusion(bf16[4352,256]{1,0:T(8,128)(2,1)S(1)} %maximum_maximum_fusion, f32[3,256,4352]{2,1,0:T(8,128)} %get-tuple-element.30, f32[3,256]{1,0:T(4,128)S(1)} %get-tuple-element.29, pred[256,4352]{1,0:T(8,128)(4,1)S(1)} %fusion.11, f32[256,3]{0,1:T(4,128)S(1)} %bitcast.108), kind=kOutput, calls=%fused_computation.55 | convolution fusion | flops 869203968 | bytes 15802368 | tf_op jit(solution)/shard_map/hqk,kd->hqd/dot_general | solution.py:148
  130.9 3.8 %all-to-all-start.2 = ((bf16[256,4,384]{2,0,1:T(8,128)(2,1)}), bf16[256,4,384]{2,0,1:T(8,128)(2,1)S(1)}, u32[]{:S(2)}, u32[]{:S(2)}) async-start(bf16[256,4,384]{2,0,1:T(8,128)(2,1)} %bitcast.94), calls=%async_computation.2 | async-start | bytes 1572864 | tf_op jit(solution)/shard_map/all_to_all | solution.py:158
  137.1 9.2 %all-to-all-done.2 = bf16[256,4,384]{2,0,1:T(8,128)(2,1)S(1)} async-done(((bf16[256,4,384]{2,0,1:T(8,128)(2,1)}), bf16[256,4,384]{2,0,1:T(8,128)(2,1)S(1)}, u32[]{:S(2)}, u32[]{:S(2)}) %all-to-all-start.2) | async-done | bytes 786464 | tf_op jit(solution)/shard_map/all_to_all | solution.py:158
  147.1 37.8 %all_to_all.52 = bf16[128,16,384]{2,1,0:T(8,128)(2,1)S(1)} all-to-all(bf16[128,16,384]{2,1,0:T(8,128)(2,1)S(1)} %bitcast.96), channel_id=1, replica_groups=mesh['seq'=32,'mp'=4] {'seq','mp'}, dimensions={0} | all-to-all | bytes 3145728 | tf_op jit(solution)/shard_map/all_to_all | solution.py:184
  186.7 4.2 %fusion.16 = f32[512,768]{1,0:T(8,128)} fusion(bf16[512,1536]{1,0:T(8,128)(2,1)S(1)} %bitcast.103, bf16[3,768,1536]{2,1,0:T(8,128)(2,1)} %all-gather.2.cloned.1.call-done), kind=kOutput, calls=%fused_computation.31 | convolution fusion | flops 1207959552 | bytes 5505024 | tf_op jit(solution)/shard_map/dot_general | solution.py:202
  191.0 7.2 %convolution_convert_fusion = bf16[512,1536]{1,0:T(8,128)(2,1)} fusion(bf16[3,768,1536]{2,1,0:T(8,128)(2,1)} %all-gather.2.cloned.1.call-done, f32[512,768]{1,0:T(8,128)} %fusion.16, bf16[512,1536]{1,0:T(8,128)(2,1)S(1)} %bitcast.104), kind=kOutput, calls=%fused_computation.26 | convolution fusion | flops 2417885184 | bytes 9437184 | tf_op jit(solution)/shard_map/dot_general | solution.py:206
  198.1 3.0 %reshape.382 = bf16[32,16,4,384]{3,2,1,0:T(4,128)(2,1)S(1)} reshape(bf16[512,1536]{1,0:T(8,128)(2,1)} %convolution_convert_fusion) | data formatting | bytes 3145728 | tf_op jit(solution)/shard_map/reshape | solution.py:208
  202.6 5.5 %all-to-all-start.4 = ((bf16[128,16,384]{2,1,0:T(8,128)(2,1)}), bf16[128,16,384]{2,1,0:T(8,128)(2,1)}, u32[]{:S(2)}, u32[]{:S(2)}) async-start(bf16[128,16,384]{2,1,0:T(8,128)(2,1)} %bitcast.32), calls=%async_computation.4 | async-start | bytes 3145728 | tf_op jit(solution)/shard_map/all_to_all | solution.py:212
  209.6 22.9 %all-to-all-done.4 = bf16[128,16,384]{2,1,0:T(8,128)(2,1)} async-done(((bf16[128,16,384]{2,1,0:T(8,128)(2,1)}), bf16[128,16,384]{2,1,0:T(8,128)(2,1)}, u32[]{:S(2)}, u32[]{:S(2)}) %all-to-all-start.4) | async-done | bytes 1572896 | tf_op jit(solution)/shard_map/all_to_all | solution.py:212
  232.5 3.9 %fusion.22 = bf16[256,384]{1,0:T(8,128)(2,1)} fusion(f32[256,2048]{1,0:T(8,128)S(1)} %select_reduce_fusion, bf16[2048,384]{1,0:T(8,128)(2,1)} %bitcast.33, f32[256,384]{1,0:T(8,128)S(1)} %convert_reduce_fusion, bf16[256,384]{1,0:T(8,128)(2,1)S(1)} %copy-done.1), kind=kOutput, calls=%fused_computation.45 | convolution fusion | flops 2416508928 | bytes 4456448 | tf_op jit(solution)/shard_map/dot_general | solution.py:221
  (93 shorter events, 32.3 us)
Async XLA Ops:
  6.5 0.8 copy-start
  8.1 12.9 %copy-start.1 = (bf16[256,384]{1,0:T(8,128)(2,1)S(1)}, bf16[256,384]{1,0:T(8,128)(2,1)}, u32[]{:S(2)}) copy-start(bf16[256,384]{1,0:T(8,128)(2,1)} %param.10) | copy-start | bytes 589828
  9.4 35.3 %copy-start.2 = (bf16[1,192,1536]{2,1,0:T(8,128)(2,1)S(1)}, bf16[1,192,1536]{2,1,0:T(8,128)(2,1)}, u32[]{:S(2)}) copy-start(bf16[1,192,1536]{2,1,0:T(8,128)(2,1)} %param.19) | copy-start | bytes 1769476
  9.4 41.0 %all-to-all-start = ((bf16[32,48,512]{2,1,0:T(8,128)(2,1)}), bf16[32,48,512]{2,1,0:T(8,128)(2,1)S(1)}, u32[]{:S(2)}, u32[]{:S(2)}) async-start(bf16[32,48,512]{2,1,0:T(8,128)(2,1)} %broadcast_in_dim.47), calls=%async_computation | async-start | bytes 3145728 | tf_op jit(solution)/shard_map/all_to_all | solution.py:47
  20.9 165.8 %all-gather.2.cloned.1.call-start = ((), (), s32[]{:S(2)}) async-start(), calls=%async_computation.5 | async-start | bytes 8847360 | tf_op jit(solution)/shard_map/all_gather | solution.py:72
  44.7 2.9 %copy-start.6 = (s32[3]{0:T(128)S(1)}, s32[3]{0:T(128)}, u32[]{:S(2)}) copy-start(s32[3]{0:T(128)} %param.14) | copy-start | bytes 40
  51.8 1.3 collective-permute-start
  53.2 22.2 %collective-permute-start.1 = (bf16[256,256]{1,0:T(8,128)(2,1)S(1)}, bf16[256,256]{1,0:T(8,128)(2,1)S(1)}, u32[]{:S(2)}, u32[]{:S(2)}) collective-permute-start(bf16[256,256]{1,0:T(8,128)(2,1)S(1)} %pad_maximum_fusion.1), channel_id=1, source_target_pairs={{0,4},{1,9},{2,6},{3,11},{4,8},{5,13},{6,10},{7,15},{8,12},{9,17},... | collective-permute-start | bytes 393224 | tf_op jit(solution)/shard_map/ppermute | solution.py:106
  58.7 20.0 %collective-permute-start.2 = (bf16[256,256]{1,0:T(8,128)(2,1)S(1)}, bf16[256,256]{1,0:T(8,128)(2,1)S(1)}, u32[]{:S(2)}, u32[]{:S(2)}) collective-permute-start(bf16[256,256]{1,0:T(8,128)(2,1)S(1)} %pad_maximum_fusion.1), channel_id=1, source_target_pairs={{0,12},{1,17},{2,14},{3,19},{4,16},{5,21},{6,18},{7,23},{8,20},{9,... | collective-permute-start | bytes 393224 | tf_op jit(solution)/shard_map/ppermute | solution.py:106
  64.1 18.0 %collective-permute-start.3 = (bf16[256,256]{1,0:T(8,128)(2,1)S(1)}, bf16[256,256]{1,0:T(8,128)(2,1)S(1)}, u32[]{:S(2)}, u32[]{:S(2)}) collective-permute-start(bf16[256,256]{1,0:T(8,128)(2,1)S(1)} %pad_maximum_fusion.1), channel_id=1, source_target_pairs={{0,20},{1,25},{2,22},{3,27},{4,24},{5,29},{6,26},{7,31},{8,28},{9,... | collective-permute-start | bytes 393224 | tf_op jit(solution)/shard_map/ppermute | solution.py:106
  70.2 14.3 %collective-permute-start.4 = (bf16[256,256]{1,0:T(8,128)(2,1)S(1)}, bf16[256,256]{1,0:T(8,128)(2,1)S(1)}, u32[]{:S(2)}, u32[]{:S(2)}) collective-permute-start(bf16[256,256]{1,0:T(8,128)(2,1)S(1)} %pad_maximum_fusion.1), channel_id=1, source_target_pairs={{0,28},{1,33},{2,30},{3,35},{4,32},{5,37},{6,34},{7,39},{8,36},{9,... | collective-permute-start | bytes 393224 | tf_op jit(solution)/shard_map/ppermute | solution.py:106
  72.7 12.4 %collective-permute-start.5 = (bf16[256,256]{1,0:T(8,128)(2,1)S(1)}, bf16[256,256]{1,0:T(8,128)(2,1)S(1)}, u32[]{:S(2)}, u32[]{:S(2)}) collective-permute-start(bf16[256,256]{1,0:T(8,128)(2,1)S(1)} %pad_maximum_fusion.1), channel_id=1, source_target_pairs={{0,36},{1,41},{2,38},{3,43},{4,40},{5,45},{6,42},{7,47},{8,44},{9,... | collective-permute-start | bytes 393224 | tf_op jit(solution)/shard_map/ppermute | solution.py:106
  75.4 10.4 %collective-permute-start.6 = (bf16[256,256]{1,0:T(8,128)(2,1)S(1)}, bf16[256,256]{1,0:T(8,128)(2,1)S(1)}, u32[]{:S(2)}, u32[]{:S(2)}) collective-permute-start(bf16[256,256]{1,0:T(8,128)(2,1)S(1)} %pad_maximum_fusion.1), channel_id=1, source_target_pairs={{0,44},{1,49},{2,46},{3,51},{4,48},{5,53},{6,50},{7,55},{8,52},{9,... | collective-permute-start | bytes 393224 | tf_op jit(solution)/shard_map/ppermute | solution.py:106
  78.7 7.8 %collective-permute-start.7 = (bf16[256,256]{1,0:T(8,128)(2,1)S(1)}, bf16[256,256]{1,0:T(8,128)(2,1)S(1)}, u32[]{:S(2)}, u32[]{:S(2)}) collective-permute-start(bf16[256,256]{1,0:T(8,128)(2,1)S(1)} %pad_maximum_fusion.1), channel_id=1, source_target_pairs={{0,52},{1,57},{2,54},{3,59},{4,56},{5,61},{6,58},{7,63},{8,60},{9,... | collective-permute-start | bytes 393224 | tf_op jit(solution)/shard_map/ppermute | solution.py:106
  82.1 5.4 %collective-permute-start.8 = (bf16[256,256]{1,0:T(8,128)(2,1)S(1)}, bf16[256,256]{1,0:T(8,128)(2,1)S(1)}, u32[]{:S(2)}, u32[]{:S(2)}) collective-permute-start(bf16[256,256]{1,0:T(8,128)(2,1)S(1)} %pad_maximum_fusion.1), channel_id=1, source_target_pairs={{0,60},{1,65},{2,62},{3,67},{4,64},{5,69},{6,66},{7,71},{8,68},{9,... | collective-permute-start | bytes 393224 | tf_op jit(solution)/shard_map/ppermute | solution.py:106
  88.2 16.8 %collective-permute-start.9 = (bf16[8,256,256]{2,1,0:T(8,128)(2,1)}, bf16[8,256,256]{2,1,0:T(8,128)(2,1)}, u32[]{:S(2)}, u32[]{:S(2)}) collective-permute-start(bf16[8,256,256]{2,1,0:T(8,128)(2,1)} %bitcast_dynamic-update-slice_fusion), channel_id=1, source_target_pairs={{0,1},{1,0},{2,3},{3,2},{4,5},{5,4},{6,7},{7,6},{8,9},{9,8},{10,11... | collective-permute-start | bytes 3145736 | tf_op jit(solution)/shard_map/ppermute | solution.py:108
  90.3 3.4 %copy-start.3 = (bf16[384,48]{0,1:T(8,128)(2,1)S(1)}, bf16[384,48]{0,1:T(8,128)(2,1)}, u32[]{:S(2)}) copy-start(bf16[384,48]{0,1:T(8,128)(2,1)} %param.13) | copy-start | bytes 110596
  94.8 34.5 %all-to-all-start.1 = ((bf16[32,48,384]{2,1,0:T(8,128)(2,1)}), bf16[32,48,384]{2,1,0:T(8,128)(2,1)S(1)}, u32[]{:S(2)}, u32[]{:S(2)}) async-start(bf16[32,48,384]{2,1,0:T(8,128)(2,1)} %broadcast_in_dim.51), calls=%async_computation.1 | async-start | bytes 2359296 | tf_op jit(solution)/shard_map/all_to_all | solution.py:47
  129.3 5.4 %copy-start.5 = (s32[256,4]{0,1:T(4,128)S(1)}, s32[256,4]{0,1:T(4,128)}, u32[]{:S(2)}) copy-start(s32[256,4]{0,1:T(4,128)} %param.15) | copy-start | bytes 12292
  130.9 15.3 %all-to-all-start.2 = ((bf16[256,4,384]{2,0,1:T(8,128)(2,1)}), bf16[256,4,384]{2,0,1:T(8,128)(2,1)S(1)}, u32[]{:S(2)}, u32[]{:S(2)}) async-start(bf16[256,4,384]{2,0,1:T(8,128)(2,1)} %bitcast.94), calls=%async_computation.2 | async-start | bytes 1572864 | tf_op jit(solution)/shard_map/all_to_all | solution.py:158
  202.6 5.6 %copy-start.4 = (f32[256,4]{0,1:T(4,128)S(1)}, f32[256,4]{0,1:T(4,128)}, u32[]{:S(2)}) copy-start(f32[256,4]{0,1:T(4,128)} %param.16) | copy-start | bytes 12292
  202.6 30.0 %all-to-all-start.4 = ((bf16[128,16,384]{2,1,0:T(8,128)(2,1)}), bf16[128,16,384]{2,1,0:T(8,128)(2,1)}, u32[]{:S(2)}, u32[]{:S(2)}) async-start(bf16[128,16,384]{2,1,0:T(8,128)(2,1)} %bitcast.32), calls=%async_computation.4 | async-start | bytes 3145728 | tf_op jit(solution)/shard_map/all_to_all | solution.py:212
Sparse Core Ops, SparseCore 0:
  47.6 91.6 all-gather.1

commit v17 on v5

--- a/solution.py
+++ b/solution.py
@@ -175,40 +175,46 @@
     ).astype(jnp.bfloat16)
     earlier_all = jnp.dot(before, one_hot.astype(jnp.bfloat16), preferred_element_type=jnp.float32)
     earlier_count = jnp.sum(earlier_all.astype(jnp.int32) * one_hot, axis=1)
-    slot_index = flat_ids * capacity + earlier_count
+    slot_index = (
+        (earlier_count // part_cap) * (experts * part_cap)
+        + flat_ids * part_cap
+        + earlier_count % part_cap
+    )
     slots = jnp.arange(experts * capacity, dtype=jnp.int32)
     pick = (slot_index[None, :] == slots[:, None]).reshape(experts * capacity, tok_rows, top_count)
     select = jnp.sum(pick.astype(jnp.bfloat16), axis=2)
     buffer = jnp.dot(select, residual, preferred_element_type=jnp.float32).astype(jnp.bfloat16)
-    arrived = lax.all_to_all(buffer, ("seq", "mp"), 0, 0, tiled=True)
+    arrived = lax.all_to_all(buffer, ("mp", "seq"), 0, 0, tiled=True)
     feat = D // mp_count
-    arrived_rows = (
-        arrived.reshape(seq_count, mp_count, part_cap, feat)
-        .transpose(0, 2, 1, 3)
-        .reshape(seq_count * part_cap, D)
-        .astype(jnp.float32)
-    )
-    moe_in = (
-        arrived_rows
-        * lax.rsqrt(jnp.sum(arrived_rows * arrived_rows, axis=-1, keepdims=True) / D + EPSILON)
-    ).astype(jnp.bfloat16)
+    arrived_q = arrived.reshape(mp_count, seq_count * part_cap, feat).astype(jnp.float32)
+    square_sum = jnp.sum(jnp.sum(arrived_q * arrived_q, axis=2), axis=0)
+    moe_in = (arrived_q * lax.rsqrt(square_sum / D + EPSILON)[None, :, None]).astype(jnp.bfloat16)
     w_gate = expert_all[0]
     w_up = expert_all[1]
     w_down = expert_all[2]
-    gate_act = lax.dot_general(
-        moe_in, w_gate, (((1,), (1,)), ((), ())), preferred_element_type=jnp.float32
-    )
-    up_act = lax.dot_general(
-        moe_in, w_up, (((1,), (1,)), ((), ())), preferred_element_type=jnp.float32
-    )
+    gate_act = None
+    up_act = None
+    for q in range(mp_count):
+        g = lax.dot_general(
+            moe_in[q], w_gate[:, q * feat : (q + 1) * feat], (((1,), (1,)), ((), ())),
+            preferred_element_type=jnp.float32,
+        )
+        u = lax.dot_general(
+            moe_in[q], w_up[:, q * feat : (q + 1) * feat], (((1,), (1,)), ((), ())),
+            preferred_element_type=jnp.float32,
+        )
+        gate_act = g if gate_act is None else gate_act + g
+        up_act = u if up_act is None else up_act + u
     active = (jnp.maximum(gate_act, 0.0) * up_act).astype(jnp.bfloat16)
-    result = jnp.dot(active, w_down, preferred_element_type=jnp.float32).astype(jnp.bfloat16)
-    outgoing = (
-        result.reshape(seq_count, part_cap, mp_count, feat)
-        .transpose(0, 2, 1, 3)
-        .reshape(seq_count * mp_count * part_cap, feat)
-    )
-    returned = lax.all_to_all(outgoing, ("seq", "mp"), 0, 0, tiled=True)
+    outgoing = jnp.stack(
+        [
+            jnp.dot(
+                active, w_down[:, q * feat : (q + 1) * feat], preferred_element_type=jnp.float32
+            ).astype(jnp.bfloat16)
+            for q in range(mp_count)
+        ]
+    ).reshape(mp_count * seq_count * part_cap, feat)
+    returned = lax.all_to_all(outgoing, ("mp", "seq"), 0, 0, tiled=True)
 
     gate_weights = jax.nn.softmax(gate_logits, axis=-1)
     combine = jnp.sum(

time: 243 us -> 239 us (0.984)
  matrix products: 31.2 us -> 27.1 us
    reshape x2 -> x0, local copies, waits for them, and re-layouts: 4.42 us -> none  [local(): result.reshape(seq_count, part_cap, mp_count, feat).transpose(0, 2, 1, 3)]
    dot_general x2 -> x12, matrix products: 11.4 us -> 7.26 us  [the longest x4 2.6 us: local(): lax.dot_general(moe_in[q], w_up[:, q * feat:(q + 1) * feat], (((1,), (1,)...]
    squeeze x0 -> x1, local copies, waits for them, and re-layouts: none -> 3.55 us  [local(): w_down = expert_all[2]]
    unnamed x27 -> x36, local copies, waits for them, and re-layouts: 6.19 us -> 5.93 us
where the time goes in v17:
time: 239 us; the launch traced here: 238 us
  starting transfers between devices  66.9 us (28%)
  blocking collectives  55.5 us (23%)
  waiting for transfers between devices  31.6 us (13%)
  matrix products  27.1 us (11%)
  other arithmetic  26.4 us (11%)
  between operations  15.3 us (6%)
  local copies, waits for them, and re-layouts  14.9 us (6%)
    all_to_all x1, blocking collectives, local(): arrived = lax.all_to_all(buffer, ('mp', 'seq'), 0, 0, tiled=True)  33.9 us
    ppermute x8, starting transfers between devices, local(): fetched.append(lax.ppermute(kv_own, ('seq', 'mp'), pairs))  33.7 us
    all_to_all x1, waiting for transfers between devices, local(): returned = lax.all_to_all(outgoing, ('mp', 'seq'), 0, 0, tiled=True)  22.8 us
    all_to_all x2, starting transfers between devices, gather_seq(): return lax.all_to_all(spread, 'seq', 0, 0, tiled=True)  22.8 us
    all_gather x1, blocking collectives, local(): whole = lax.all_gather(hidden_in, 'mp', axis=1, tiled=True)  21.6 us
    reduce_sum x1, other arithmetic, local(): total = jnp.sum(probs, axis=-1)  9.02 us
    all_to_all x1, waiting for transfers between devices, local(): lax.all_to_all(partial_out.astype(jnp.bfloat16), 'mp', 1, 0, tiled=True)  8.37 us
    dot_general x1, matrix products, local(): accum = jnp.einsum('hqk,kd->hqd', probs, value_rows)  7.01 us
  transfers between devices with their start and end apart: 15, of which 3 were waited for; matrix products, arithmetic and copies ran while one was open for 21% of the time, Pallas kernels for 0%

profile of v17, /device:TPU:1, one launch (start us, length us, event | category | flops | bytes accessed | tf_op | source)
XLA Modules:
  0.0 237.7 jit_solution(5725906846995998218)
XLA Ops:
  9.5 11.3 %all-to-all-start = ((bf16[32,48,512]{2,1,0:T(8,128)(2,1)}), bf16[32,48,512]{2,1,0:T(8,128)(2,1)S(1)}, u32[]{:S(2)}, u32[]{:S(2)}) async-start(bf16[32,48,512]{2,1,0:T(8,128)(2,1)} %broadcast_in_dim.47), calls=%async_computation | async-start | bytes 3145728 | tf_op jit(solution)/shard_map/all_to_all | solution.py:47
  20.9 2.5 %pad_maximum_fusion = bf16[3,192,1536]{2,1,0:T(8,128)(2,1)} fusion(bf16[1,192,1536]{2,1,0:T(8,128)(2,1)S(1)} %copy-done.7, bf16[1,192,1536]{2,1,0:T(8,128)(2,1)S(1)} %copy-done.8, bf16[1,192,1536]{2,1,0:T(8,128)(2,1)} %param.17), kind=kLoop, calls=%fused_computation.33 | loop fusion | flops 1769472 | bytes 3538944 | tf_op jit(solution)/shard_map/concatenate | solution.py:63
  26.3 21.6 %all_gather.6 = bf16[256,1536]{1,0:T(8,128)(2,1)S(1)} all-gather(bf16[256,384]{1,0:T(8,128)(2,1)S(1)} %copy-done.2), channel_id=1, replica_groups=mesh['seq'=32,'mp'=4] {'mp'}, dimensions={1}, use_global_device_ids=true | all-gather | bytes 983040 | tf_op jit(solution)/shard_map/all_gather | solution.py:71
  50.9 5.2 %collective-permute-start.1 = (bf16[256,256]{1,0:T(8,128)(2,1)S(1)}, bf16[256,256]{1,0:T(8,128)(2,1)S(1)}, u32[]{:S(2)}, u32[]{:S(2)}) collective-permute-start(bf16[256,256]{1,0:T(8,128)(2,1)S(1)} %pad_maximum_fusion.2), channel_id=1, source_target_pairs={{0,4},{1,9},{2,6},{3,11},{4,8},{5,13},{6,10},{7,15},{8,12},{9,17},... | collective-permute-start | bytes 393224 | tf_op jit(solution)/shard_map/ppermute | solution.py:105
  56.8 5.1 %collective-permute-start.2 = (bf16[256,256]{1,0:T(8,128)(2,1)S(1)}, bf16[256,256]{1,0:T(8,128)(2,1)S(1)}, u32[]{:S(2)}, u32[]{:S(2)}) collective-permute-start(bf16[256,256]{1,0:T(8,128)(2,1)S(1)} %pad_maximum_fusion.2), channel_id=1, source_target_pairs={{0,12},{1,17},{2,14},{3,19},{4,16},{5,21},{6,18},{7,23},{8,20},{9,... | collective-permute-start | bytes 393224 | tf_op jit(solution)/shard_map/ppermute | solution.py:105
  61.9 8.5 %collective-permute-start.3 = (bf16[256,256]{1,0:T(8,128)(2,1)S(1)}, bf16[256,256]{1,0:T(8,128)(2,1)S(1)}, u32[]{:S(2)}, u32[]{:S(2)}) collective-permute-start(bf16[256,256]{1,0:T(8,128)(2,1)S(1)} %pad_maximum_fusion.2), channel_id=1, source_target_pairs={{0,20},{1,25},{2,22},{3,27},{4,24},{5,29},{6,26},{7,31},{8,28},{9,... | collective-permute-start | bytes 393224 | tf_op jit(solution)/shard_map/ppermute | solution.py:105
  70.4 2.1 collective-permute-start.4
  72.6 2.1 collective-permute-start.5
  74.7 4.3 %collective-permute-start.6 = (bf16[256,256]{1,0:T(8,128)(2,1)S(1)}, bf16[256,256]{1,0:T(8,128)(2,1)S(1)}, u32[]{:S(2)}, u32[]{:S(2)}) collective-permute-start(bf16[256,256]{1,0:T(8,128)(2,1)S(1)} %pad_maximum_fusion.2), channel_id=1, source_target_pairs={{0,44},{1,49},{2,46},{3,51},{4,48},{5,53},{6,50},{7,55},{8,52},{9,... | collective-permute-start | bytes 393224 | tf_op jit(solution)/shard_map/ppermute | solution.py:105
  79.6 1.9 collective-permute-start.7
  82.2 4.5 %collective-permute-start.8 = (bf16[256,256]{1,0:T(8,128)(2,1)S(1)}, bf16[256,256]{1,0:T(8,128)(2,1)S(1)}, u32[]{:S(2)}, u32[]{:S(2)}) collective-permute-start(bf16[256,256]{1,0:T(8,128)(2,1)S(1)} %pad_maximum_fusion.2), channel_id=1, source_target_pairs={{0,60},{1,65},{2,62},{3,67},{4,64},{5,69},{6,66},{7,71},{8,68},{9,... | collective-permute-start | bytes 393224 | tf_op jit(solution)/shard_map/ppermute | solution.py:105
  91.2 1.6 fusion.11
  95.7 11.4 %all-to-all-start.1 = ((bf16[32,48,384]{2,1,0:T(8,128)(2,1)}), bf16[32,48,384]{2,1,0:T(8,128)(2,1)S(1)}, u32[]{:S(2)}, u32[]{:S(2)}) async-start(bf16[32,48,384]{2,1,0:T(8,128)(2,1)} %broadcast_in_dim.51), calls=%async_computation.1 | async-start | bytes 2359296 | tf_op jit(solution)/shard_map/all_to_all | solution.py:47
  108.2 1.7 broadcast_select_fusion.1
  110.1 6.5 %fusion = (f32[3,256]{1,0:T(4,128)S(1)}, f32[3,256,4352]{2,1,0:T(8,128)}) fusion(pred[256,4352]{1,0:T(8,128)(4,1)S(1)} %fusion.11, bf16[4352,256]{1,0:T(8,128)(2,1)S(1)} %maximum_maximum_fusion, bf16[256,3,64]{2,0,1:T(8,128)(2,1)S(1)} %get-tuple-element.17, bf16[256,3,64]{2,0,1:T(8,128)(2,1)S(1)} %get-tuple-element.16), kind=kOutput, calls=%fused_computation.2 | convolution fusion | flops 866057472 | bytes 15993856 | tf_op jit(solution)/shard_map/hqd,kd->hqk/dot_general | solution.py:131
  116.6 9.0 %fusion.1 = f32[3,256]{1,0:T(4,128)S(1)} fusion(f32[3,256,4352]{2,1,0:T(8,128)} %get-tuple-element.29, f32[3,256]{1,0:T(4,128)S(1)} %get-tuple-element.28, pred[256,4352]{1,0:T(8,128)(4,1)S(1)} %fusion.11), kind=kLoop, calls=%fused_computation.3 | loop fusion | flops 16710912 | bytes 14489600 | tf_op jit(solution)/shard_map/reduce_sum | solution.py:146
  125.6 7.0 %fusion.28 = bf16[256,3,128]{0,2,1:T(8,128)(2,1)S(1)} fusion(bf16[4352,256]{1,0:T(8,128)(2,1)S(1)} %maximum_maximum_fusion, f32[3,256,4352]{2,1,0:T(8,128)} %get-tuple-element.29, f32[3,256]{1,0:T(4,128)S(1)} %get-tuple-element.28, pred[256,4352]{1,0:T(8,128)(4,1)S(1)} %fusion.11, f32[256,3]{0,1:T(4,128)S(1)} %bitcast.119), kind=kOutput, calls=%fused_computation.59 | convolution fusion | flops 869203968 | bytes 15802368 | tf_op jit(solution)/shard_map/hqk,kd->hqd/dot_general | solution.py:147
  134.2 3.7 %all-to-all-start.2 = ((bf16[256,4,384]{2,0,1:T(8,128)(2,1)}), bf16[256,4,384]{2,0,1:T(8,128)(2,1)S(1)}, u32[]{:S(2)}, u32[]{:S(2)}) async-start(bf16[256,4,384]{2,0,1:T(8,128)(2,1)} %bitcast.107), calls=%async_computation.2 | async-start | bytes 1572864 | tf_op jit(solution)/shard_map/all_to_all | solution.py:157
  140.4 8.4 %all-to-all-done.2 = bf16[256,4,384]{2,0,1:T(8,128)(2,1)S(1)} async-done(((bf16[256,4,384]{2,0,1:T(8,128)(2,1)}), bf16[256,4,384]{2,0,1:T(8,128)(2,1)S(1)}, u32[]{:S(2)}, u32[]{:S(2)}) %all-to-all-start.2) | async-done | bytes 786464 | tf_op jit(solution)/shard_map/all_to_all | solution.py:157
  149.6 33.9 %all_to_all.52 = bf16[128,16,384]{2,1,0:T(8,128)(2,1)S(1)} all-to-all(bf16[128,16,384]{2,1,0:T(8,128)(2,1)S(1)} %bitcast.110), channel_id=1, replica_groups=mesh['seq'=32,'mp'=4] {'mp','seq'}, dimensions={0} | all-to-all | bytes 3145728 | tf_op jit(solution)/shard_map/all_to_all | solution.py:187
  184.6 3.6 %slice_bitcast_fusion = (bf16[768,1536]{1,0:T(8,128)(2,1)S(1)}, bf16[768,1536]{1,0:T(8,128)(2,1)S(1)}, bf16[768,1536]{1,0:T(8,128)(2,1)S(1)}) fusion(bf16[3,768,1536]{2,1,0:T(8,128)(2,1)} %all-gather.2.cloned.1.call-done), kind=kLoop, calls=%fused_computation.27 | loop fusion | bytes 14155776 | tf_op jit(solution)/shard_map/squeeze | solution.py:194
  196.8 5.9 %all-to-all-start.4 = ((bf16[128,16,384]{2,1,0:T(8,128)(2,1)}), bf16[128,16,384]{2,1,0:T(8,128)(2,1)}, u32[]{:S(2)}, u32[]{:S(2)}) async-start(bf16[128,16,384]{2,1,0:T(8,128)(2,1)} %bitcast.37), calls=%async_computation.4 | async-start | bytes 3145728 | tf_op jit(solution)/shard_map/all_to_all | solution.py:217
  204.2 22.8 %all-to-all-done.4 = bf16[128,16,384]{2,1,0:T(8,128)(2,1)} async-done(((bf16[128,16,384]{2,1,0:T(8,128)(2,1)}), bf16[128,16,384]{2,1,0:T(8,128)(2,1)}, u32[]{:S(2)}, u32[]{:S(2)}) %all-to-all-start.4) | async-done | bytes 1572896 | tf_op jit(solution)/shard_map/all_to_all | solution.py:217
  227.0 3.9 %fusion.22 = bf16[256,384]{1,0:T(8,128)(2,1)} fusion(f32[256,2048]{1,0:T(8,128)S(1)} %select_reduce_fusion, bf16[2048,384]{1,0:T(8,128)(2,1)} %bitcast.38, f32[256,384]{1,0:T(8,128)S(1)} %convert_reduce_fusion, bf16[256,384]{1,0:T(8,128)(2,1)S(1)} %copy-done.2), kind=kOutput, calls=%fused_computation.49 | convolution fusion | flops 2416508928 | bytes 4456448 | tf_op jit(solution)/shard_map/dot_general | solution.py:226
  (116 shorter events, 33.8 us)
Async XLA Ops:
  8.1 12.8 %copy-start.7 = (bf16[1,192,1536]{2,1,0:T(8,128)(2,1)S(1)}, bf16[1,192,1536]{2,1,0:T(8,128)(2,1)}, u32[]{:S(2)}) copy-start(bf16[1,192,1536]{2,1,0:T(8,128)(2,1)} %param.19) | copy-start | bytes 1769476
  8.1 12.8 %copy-start.8 = (bf16[1,192,1536]{2,1,0:T(8,128)(2,1)S(1)}, bf16[1,192,1536]{2,1,0:T(8,128)(2,1)}, u32[]{:S(2)}) copy-start(bf16[1,192,1536]{2,1,0:T(8,128)(2,1)} %param.18) | copy-start | bytes 1769476
  9.5 38.7 %all-to-all-start = ((bf16[32,48,512]{2,1,0:T(8,128)(2,1)}), bf16[32,48,512]{2,1,0:T(8,128)(2,1)S(1)}, u32[]{:S(2)}, u32[]{:S(2)}) async-start(bf16[32,48,512]{2,1,0:T(8,128)(2,1)} %broadcast_in_dim.47), calls=%async_computation | async-start | bytes 3145728 | tf_op jit(solution)/shard_map/all_to_all | solution.py:47
  20.8 2.9 %copy-start.12 = (s32[3]{0:T(128)S(1)}, s32[3]{0:T(128)}, u32[]{:S(2)}) copy-start(s32[3]{0:T(128)} %param.14) | copy-start | bytes 40
  20.8 5.5 %copy-start.2 = (bf16[256,384]{1,0:T(8,128)(2,1)S(1)}, bf16[256,384]{1,0:T(8,128)(2,1)}, u32[]{:S(2)}) copy-start(bf16[256,384]{1,0:T(8,128)(2,1)} %param.10) | copy-start | bytes 589828
  20.8 163.7 %all-gather.2.cloned.1.call-start = ((), (), s32[]{:S(2)}) async-start(), calls=%async_computation.5 | async-start | bytes 8847360 | tf_op jit(solution)/shard_map/all_gather | solution.py:62
  49.5 1.3 collective-permute-start
  50.9 40.3 %copy-start.3 = (bf16[256,128]{1,0:T(8,128)(2,1)}, bf16[256,128]{1,0:T(8,128)(2,1)S(1)}, u32[]{:S(2)}) copy-start(bf16[256,128]{1,0:T(8,128)(2,1)S(1)} %get-tuple-element.22) | copy-start | bytes 196612
  50.9 40.3 %copy-start.5 = (bf16[256,128]{1,0:T(8,128)(2,1)}, bf16[256,128]{1,0:T(8,128)(2,1)S(1)}, u32[]{:S(2)}) copy-start(bf16[256,128]{1,0:T(8,128)(2,1)S(1)} %get-tuple-element.23) | copy-start | bytes 196612
  50.9 23.7 %collective-permute-start.1 = (bf16[256,256]{1,0:T(8,128)(2,1)S(1)}, bf16[256,256]{1,0:T(8,128)(2,1)S(1)}, u32[]{:S(2)}, u32[]{:S(2)}) collective-permute-start(bf16[256,256]{1,0:T(8,128)(2,1)S(1)} %pad_maximum_fusion.2), channel_id=1, source_target_pairs={{0,4},{1,9},{2,6},{3,11},{4,8},{5,13},{6,10},{7,15},{8,12},{9,17},... | collective-permute-start | bytes 393224 | tf_op jit(solution)/shard_map/ppermute | solution.py:105
  56.8 22.8 %collective-permute-start.2 = (bf16[256,256]{1,0:T(8,128)(2,1)S(1)}, bf16[256,256]{1,0:T(8,128)(2,1)S(1)}, u32[]{:S(2)}, u32[]{:S(2)}) collective-permute-start(bf16[256,256]{1,0:T(8,128)(2,1)S(1)} %pad_maximum_fusion.2), channel_id=1, source_target_pairs={{0,12},{1,17},{2,14},{3,19},{4,16},{5,21},{6,18},{7,23},{8,20},{9,... | collective-permute-start | bytes 393224 | tf_op jit(solution)/shard_map/ppermute | solution.py:105
  61.9 20.3 %collective-permute-start.3 = (bf16[256,256]{1,0:T(8,128)(2,1)S(1)}, bf16[256,256]{1,0:T(8,128)(2,1)S(1)}, u32[]{:S(2)}, u32[]{:S(2)}) collective-permute-start(bf16[256,256]{1,0:T(8,128)(2,1)S(1)} %pad_maximum_fusion.2), channel_id=1, source_target_pairs={{0,20},{1,25},{2,22},{3,27},{4,24},{5,29},{6,26},{7,31},{8,28},{9,... | collective-permute-start | bytes 393224 | tf_op jit(solution)/shard_map/ppermute | solution.py:105
  70.4 17.0 %collective-permute-start.4 = (bf16[256,256]{1,0:T(8,128)(2,1)S(1)}, bf16[256,256]{1,0:T(8,128)(2,1)S(1)}, u32[]{:S(2)}, u32[]{:S(2)}) collective-permute-start(bf16[256,256]{1,0:T(8,128)(2,1)S(1)} %pad_maximum_fusion.2), channel_id=1, source_target_pairs={{0,28},{1,33},{2,30},{3,35},{4,32},{5,37},{6,34},{7,39},{8,36},{9,... | collective-permute-start | bytes 393224 | tf_op jit(solution)/shard_map/ppermute | solution.py:105
  72.6 15.5 %collective-permute-start.5 = (bf16[256,256]{1,0:T(8,128)(2,1)S(1)}, bf16[256,256]{1,0:T(8,128)(2,1)S(1)}, u32[]{:S(2)}, u32[]{:S(2)}) collective-permute-start(bf16[256,256]{1,0:T(8,128)(2,1)S(1)} %pad_maximum_fusion.2), channel_id=1, source_target_pairs={{0,36},{1,41},{2,38},{3,43},{4,40},{5,45},{6,42},{7,47},{8,44},{9,... | collective-permute-start | bytes 393224 | tf_op jit(solution)/shard_map/ppermute | solution.py:105
  74.7 14.1 %collective-permute-start.6 = (bf16[256,256]{1,0:T(8,128)(2,1)S(1)}, bf16[256,256]{1,0:T(8,128)(2,1)S(1)}, u32[]{:S(2)}, u32[]{:S(2)}) collective-permute-start(bf16[256,256]{1,0:T(8,128)(2,1)S(1)} %pad_maximum_fusion.2), channel_id=1, source_target_pairs={{0,44},{1,49},{2,46},{3,51},{4,48},{5,53},{6,50},{7,55},{8,52},{9,... | collective-permute-start | bytes 393224 | tf_op jit(solution)/shard_map/ppermute | solution.py:105
  79.6 9.7 %collective-permute-start.7 = (bf16[256,256]{1,0:T(8,128)(2,1)S(1)}, bf16[256,256]{1,0:T(8,128)(2,1)S(1)}, u32[]{:S(2)}, u32[]{:S(2)}) collective-permute-start(bf16[256,256]{1,0:T(8,128)(2,1)S(1)} %pad_maximum_fusion.2), channel_id=1, source_target_pairs={{0,52},{1,57},{2,54},{3,59},{4,56},{5,61},{6,58},{7,63},{8,60},{9,... | collective-permute-start | bytes 393224 | tf_op jit(solution)/shard_map/ppermute | solution.py:105
  82.2 7.8 %collective-permute-start.8 = (bf16[256,256]{1,0:T(8,128)(2,1)S(1)}, bf16[256,256]{1,0:T(8,128)(2,1)S(1)}, u32[]{:S(2)}, u32[]{:S(2)}) collective-permute-start(bf16[256,256]{1,0:T(8,128)(2,1)S(1)} %pad_maximum_fusion.2), channel_id=1, source_target_pairs={{0,60},{1,65},{2,62},{3,67},{4,64},{5,69},{6,66},{7,71},{8,68},{9,... | collective-permute-start | bytes 393224 | tf_op jit(solution)/shard_map/ppermute | solution.py:105
  90.7 17.5 %collective-permute-start.9 = (bf16[8,256,256]{2,1,0:T(8,128)(2,1)}, bf16[8,256,256]{2,1,0:T(8,128)(2,1)}, u32[]{:S(2)}, u32[]{:S(2)}) collective-permute-start(bf16[8,256,256]{2,1,0:T(8,128)(2,1)} %bitcast_dynamic-update-slice_fusion), channel_id=1, source_target_pairs={{0,1},{1,0},{2,3},{3,2},{4,5},{5,4},{6,7},{7,6},{8,9},{9,8},{10,11... | collective-permute-start | bytes 3145736 | tf_op jit(solution)/shard_map/ppermute | solution.py:107
  95.7 36.9 %all-to-all-start.1 = ((bf16[32,48,384]{2,1,0:T(8,128)(2,1)}), bf16[32,48,384]{2,1,0:T(8,128)(2,1)S(1)}, u32[]{:S(2)}, u32[]{:S(2)}) async-start(bf16[32,48,384]{2,1,0:T(8,128)(2,1)} %broadcast_in_dim.51), calls=%async_computation.1 | async-start | bytes 2359296 | tf_op jit(solution)/shard_map/all_to_all | solution.py:47
  133.2 4.7 %copy-start.11 = (s32[256,4]{0,1:T(4,128)S(1)}, s32[256,4]{0,1:T(4,128)}, u32[]{:S(2)}) copy-start(s32[256,4]{0,1:T(4,128)} %param.15) | copy-start | bytes 12292
  134.2 14.5 %all-to-all-start.2 = ((bf16[256,4,384]{2,0,1:T(8,128)(2,1)}), bf16[256,4,384]{2,0,1:T(8,128)(2,1)S(1)}, u32[]{:S(2)}, u32[]{:S(2)}) async-start(bf16[256,4,384]{2,0,1:T(8,128)(2,1)} %bitcast.107), calls=%async_computation.2 | async-start | bytes 1572864 | tf_op jit(solution)/shard_map/all_to_all | solution.py:157
  196.8 5.9 %copy-start.10 = (f32[256,4]{0,1:T(4,128)S(1)}, f32[256,4]{0,1:T(4,128)}, u32[]{:S(2)}) copy-start(f32[256,4]{0,1:T(4,128)} %param.16) | copy-start | bytes 12292
  196.8 30.1 %all-to-all-start.4 = ((bf16[128,16,384]{2,1,0:T(8,128)(2,1)}), bf16[128,16,384]{2,1,0:T(8,128)(2,1)}, u32[]{:S(2)}, u32[]{:S(2)}) async-start(bf16[128,16,384]{2,1,0:T(8,128)(2,1)} %bitcast.37), calls=%async_computation.4 | async-start | bytes 3145728 | tf_op jit(solution)/shard_map/all_to_all | solution.py:217
  227.0 3.9 %copy-start.1 = (bf16[48,512]{1,0:T(8,128)(2,1)S(1)}, bf16[48,512]{1,0:T(8,128)(2,1)}, u32[]{:S(2)}) copy-start(bf16[48,512]{1,0:T(8,128)(2,1)} %param.12) | copy-start | bytes 147460
  (4 other events, 6.1 us)
Sparse Core Ops, SparseCore 0:
  23.6 84.9 all-gather.1

commit v18 on v17

--- a/solution.py
+++ b/solution.py
@@ -142,7 +142,7 @@
     )[None]
     masked = jnp.where(allowed, scores, -1e30)
     peak = jnp.max(masked, axis=-1)
-    probs = jnp.where(allowed, jnp.exp(masked - peak[..., None]), 0.0)
+    probs = jnp.exp(masked - peak[..., None])
     total = jnp.sum(probs, axis=-1)
     accum = jnp.einsum("hqk,kd->hqd", probs, value_rows)
     attended = (
@@ -223,11 +223,10 @@
         ).reshape(tok_rows, top_count, experts * capacity),
         axis=1,
     )
-    moe_total = jnp.dot(
-        combine,
-        returned.astype(jnp.float32),
-        precision=lax.Precision.HIGHEST,
-        preferred_element_type=jnp.float32,
+    combine_hi = combine.astype(jnp.bfloat16)
+    combine_lo = (combine - combine_hi.astype(jnp.float32)).astype(jnp.bfloat16)
+    moe_total = jnp.dot(combine_hi, returned, preferred_element_type=jnp.float32) + jnp.dot(
+        combine_lo, returned, preferred_element_type=jnp.float32
     )
     return (residual_f + moe_total).astype(jnp.bfloat16)
 

time: 239 us -> 239 us (level)
    dot_general x1 -> x2, matrix products: 3.89 us -> 4.94 us  [the longest x1 2.81 us: local(): jnp.dot(combine_lo, returned, preferred_element_type=jnp.float32)]
  transfers between devices with their start and end apart: 15 -> 15, of which waited for: 3 -> 3; matrix products, arithmetic and copies ran while one was open for 21% -> 20% of each run, Pallas kernels for 0% -> 0%
where the time goes in v18:
time: 239 us; the launch traced here: 238 us
  starting transfers between devices  66.9 us (28%)
  blocking collectives  55.5 us (23%)
  waiting for transfers between devices  31.6 us (13%)
  matrix products  28.1 us (12%)
  other arithmetic  25.9 us (11%)
  between operations  15.3 us (6%)
  local copies, waits for them, and re-layouts  14.9 us (6%)
    all_to_all x1, blocking collectives, local(): arrived = lax.all_to_all(buffer, ('mp', 'seq'), 0, 0, tiled=True)  33.9 us
    ppermute x8, starting transfers between devices, local(): fetched.append(lax.ppermute(kv_own, ('seq', 'mp'), pairs))  33.7 us
    all_to_all x1, waiting for transfers between devices, local(): returned = lax.all_to_all(outgoing, ('mp', 'seq'), 0, 0, tiled=True)  22.8 us
    all_to_all x2, starting transfers between devices, gather_seq(): return lax.all_to_all(spread, 'seq', 0, 0, tiled=True)  22.8 us
    all_gather x1, blocking collectives, local(): whole = lax.all_gather(hidden_in, 'mp', axis=1, tiled=True)  21.6 us
    reduce_sum x1, other arithmetic, local(): total = jnp.sum(probs, axis=-1)  8.52 us
    all_to_all x1, waiting for transfers between devices, local(): lax.all_to_all(partial_out.astype(jnp.bfloat16), 'mp', 1, 0, tiled=True)  8.37 us
    dot_general x1, matrix products, local(): accum = jnp.einsum('hqk,kd->hqd', probs, value_rows)  7.01 us
  transfers between devices with their start and end apart: 15, of which 3 were waited for; matrix products, arithmetic and copies ran while one was open for 20% of the time, Pallas kernels for 0%

profile of v18, /device:TPU:1, one launch (start us, length us, event | category | flops | bytes accessed | tf_op | source)
XLA Modules:
  0.0 238.3 jit_solution(1071478074592923487)
XLA Ops:
  9.5 11.3 %all-to-all-start = ((bf16[32,48,512]{2,1,0:T(8,128)(2,1)}), bf16[32,48,512]{2,1,0:T(8,128)(2,1)S(1)}, u32[]{:S(2)}, u32[]{:S(2)}) async-start(bf16[32,48,512]{2,1,0:T(8,128)(2,1)} %broadcast_in_dim.37), calls=%async_computation | async-start | bytes 3145728 | tf_op jit(solution)/shard_map/all_to_all | solution.py:47
  20.9 2.5 %pad_maximum_fusion = bf16[3,192,1536]{2,1,0:T(8,128)(2,1)} fusion(bf16[1,192,1536]{2,1,0:T(8,128)(2,1)S(1)} %copy-done.7, bf16[1,192,1536]{2,1,0:T(8,128)(2,1)S(1)} %copy-done.8, bf16[1,192,1536]{2,1,0:T(8,128)(2,1)} %param.17), kind=kLoop, calls=%fused_computation.33 | loop fusion | flops 1769472 | bytes 3538944 | tf_op jit(solution)/shard_map/concatenate | solution.py:63
  26.3 21.6 %all_gather.6 = bf16[256,1536]{1,0:T(8,128)(2,1)S(1)} all-gather(bf16[256,384]{1,0:T(8,128)(2,1)S(1)} %copy-done.2), channel_id=1, replica_groups=mesh['seq'=32,'mp'=4] {'mp'}, dimensions={1}, use_global_device_ids=true | all-gather | bytes 983040 | tf_op jit(solution)/shard_map/all_gather | solution.py:71
  50.9 5.2 %collective-permute-start.1 = (bf16[256,256]{1,0:T(8,128)(2,1)S(1)}, bf16[256,256]{1,0:T(8,128)(2,1)S(1)}, u32[]{:S(2)}, u32[]{:S(2)}) collective-permute-start(bf16[256,256]{1,0:T(8,128)(2,1)S(1)} %pad_maximum_fusion.2), channel_id=1, source_target_pairs={{0,4},{1,9},{2,6},{3,11},{4,8},{5,13},{6,10},{7,15},{8,12},{9,17},... | collective-permute-start | bytes 393224 | tf_op jit(solution)/shard_map/ppermute | solution.py:105
  56.8 5.1 %collective-permute-start.2 = (bf16[256,256]{1,0:T(8,128)(2,1)S(1)}, bf16[256,256]{1,0:T(8,128)(2,1)S(1)}, u32[]{:S(2)}, u32[]{:S(2)}) collective-permute-start(bf16[256,256]{1,0:T(8,128)(2,1)S(1)} %pad_maximum_fusion.2), channel_id=1, source_target_pairs={{0,12},{1,17},{2,14},{3,19},{4,16},{5,21},{6,18},{7,23},{8,20},{9,... | collective-permute-start | bytes 393224 | tf_op jit(solution)/shard_map/ppermute | solution.py:105
  61.9 8.5 %collective-permute-start.3 = (bf16[256,256]{1,0:T(8,128)(2,1)S(1)}, bf16[256,256]{1,0:T(8,128)(2,1)S(1)}, u32[]{:S(2)}, u32[]{:S(2)}) collective-permute-start(bf16[256,256]{1,0:T(8,128)(2,1)S(1)} %pad_maximum_fusion.2), channel_id=1, source_target_pairs={{0,20},{1,25},{2,22},{3,27},{4,24},{5,29},{6,26},{7,31},{8,28},{9,... | collective-permute-start | bytes 393224 | tf_op jit(solution)/shard_map/ppermute | solution.py:105
  70.4 2.1 collective-permute-start.4
  72.6 2.1 collective-permute-start.5
  74.7 4.3 %collective-permute-start.6 = (bf16[256,256]{1,0:T(8,128)(2,1)S(1)}, bf16[256,256]{1,0:T(8,128)(2,1)S(1)}, u32[]{:S(2)}, u32[]{:S(2)}) collective-permute-start(bf16[256,256]{1,0:T(8,128)(2,1)S(1)} %pad_maximum_fusion.2), channel_id=1, source_target_pairs={{0,44},{1,49},{2,46},{3,51},{4,48},{5,53},{6,50},{7,55},{8,52},{9,... | collective-permute-start | bytes 393224 | tf_op jit(solution)/shard_map/ppermute | solution.py:105
  79.6 1.9 collective-permute-start.7
  82.2 4.5 %collective-permute-start.8 = (bf16[256,256]{1,0:T(8,128)(2,1)S(1)}, bf16[256,256]{1,0:T(8,128)(2,1)S(1)}, u32[]{:S(2)}, u32[]{:S(2)}) collective-permute-start(bf16[256,256]{1,0:T(8,128)(2,1)S(1)} %pad_maximum_fusion.2), channel_id=1, source_target_pairs={{0,60},{1,65},{2,62},{3,67},{4,64},{5,69},{6,66},{7,71},{8,68},{9,... | collective-permute-start | bytes 393224 | tf_op jit(solution)/shard_map/ppermute | solution.py:105
  95.7 11.4 %all-to-all-start.1 = ((bf16[32,48,384]{2,1,0:T(8,128)(2,1)}), bf16[32,48,384]{2,1,0:T(8,128)(2,1)S(1)}, u32[]{:S(2)}, u32[]{:S(2)}) async-start(bf16[32,48,384]{2,1,0:T(8,128)(2,1)} %broadcast_in_dim.44), calls=%async_computation.1 | async-start | bytes 2359296 | tf_op jit(solution)/shard_map/all_to_all | solution.py:47
  108.2 1.7 broadcast_select_fusion.1
  110.1 6.5 %fusion = (f32[3,256]{1,0:T(4,128)S(1)}, f32[3,256,4352]{2,1,0:T(8,128)}) fusion(pred[256,4352]{1,0:T(8,128)(4,1)S(1)} %fusion.10, bf16[4352,256]{1,0:T(8,128)(2,1)S(1)} %maximum_maximum_fusion, bf16[256,3,64]{2,0,1:T(8,128)(2,1)S(1)} %get-tuple-element.17, bf16[256,3,64]{2,0,1:T(8,128)(2,1)S(1)} %get-tuple-element.16), kind=kOutput, calls=%fused_computation.2 | convolution fusion | flops 866057472 | bytes 15993856 | tf_op jit(solution)/shard_map/hqd,kd->hqk/dot_general | solution.py:131
  116.6 8.5 %fusion.1 = f32[3,256]{1,0:T(4,128)S(1)} fusion(f32[3,256,4352]{2,1,0:T(8,128)} %get-tuple-element.29, f32[3,256]{1,0:T(4,128)S(1)} %get-tuple-element.28, pred[256,4352]{1,0:T(8,128)(4,1)S(1)} %fusion.10), kind=kLoop, calls=%fused_computation.3 | loop fusion | flops 13368576 | bytes 14489600 | tf_op jit(solution)/shard_map/reduce_sum | solution.py:146
  125.1 7.0 %fusion.28 = bf16[256,3,128]{0,2,1:T(8,128)(2,1)S(1)} fusion(bf16[4352,256]{1,0:T(8,128)(2,1)S(1)} %maximum_maximum_fusion, f32[3,256,4352]{2,1,0:T(8,128)} %get-tuple-element.29, f32[3,256]{1,0:T(4,128)S(1)} %get-tuple-element.28, pred[256,4352]{1,0:T(8,128)(4,1)S(1)} %fusion.10, f32[256,3]{0,1:T(4,128)S(1)} %bitcast.119), kind=kOutput, calls=%fused_computation.60 | convolution fusion | flops 865861632 | bytes 15802368 | tf_op jit(solution)/shard_map/hqk,kd->hqd/dot_general | solution.py:147
  133.7 3.7 %all-to-all-start.2 = ((bf16[256,4,384]{2,0,1:T(8,128)(2,1)}), bf16[256,4,384]{2,0,1:T(8,128)(2,1)S(1)}, u32[]{:S(2)}, u32[]{:S(2)}) async-start(bf16[256,4,384]{2,0,1:T(8,128)(2,1)} %bitcast.107), calls=%async_computation.2 | async-start | bytes 1572864 | tf_op jit(solution)/shard_map/all_to_all | solution.py:157
  139.9 8.4 %all-to-all-done.2 = bf16[256,4,384]{2,0,1:T(8,128)(2,1)S(1)} async-done(((bf16[256,4,384]{2,0,1:T(8,128)(2,1)}), bf16[256,4,384]{2,0,1:T(8,128)(2,1)S(1)}, u32[]{:S(2)}, u32[]{:S(2)}) %all-to-all-start.2) | async-done | bytes 786464 | tf_op jit(solution)/shard_map/all_to_all | solution.py:157
  149.1 33.9 %all_to_all.52 = bf16[128,16,384]{2,1,0:T(8,128)(2,1)S(1)} all-to-all(bf16[128,16,384]{2,1,0:T(8,128)(2,1)S(1)} %bitcast.110), channel_id=1, replica_groups=mesh['seq'=32,'mp'=4] {'mp','seq'}, dimensions={0} | all-to-all | bytes 3145728 | tf_op jit(solution)/shard_map/all_to_all | solution.py:187
  184.1 3.6 %slice_bitcast_fusion = (bf16[768,1536]{1,0:T(8,128)(2,1)S(1)}, bf16[768,1536]{1,0:T(8,128)(2,1)S(1)}, bf16[768,1536]{1,0:T(8,128)(2,1)S(1)}) fusion(bf16[3,768,1536]{2,1,0:T(8,128)(2,1)} %all-gather.2.cloned.1.call-done), kind=kLoop, calls=%fused_computation.26 | loop fusion | bytes 14155776 | tf_op jit(solution)/shard_map/squeeze | solution.py:194
  196.3 5.9 %all-to-all-start.4 = ((bf16[128,16,384]{2,1,0:T(8,128)(2,1)}), bf16[128,16,384]{2,1,0:T(8,128)(2,1)}, u32[]{:S(2)}, u32[]{:S(2)}) async-start(bf16[128,16,384]{2,1,0:T(8,128)(2,1)} %bitcast.37), calls=%async_computation.4 | async-start | bytes 3145728 | tf_op jit(solution)/shard_map/all_to_all | solution.py:217
  203.7 22.8 %all-to-all-done.4 = bf16[128,16,384]{2,1,0:T(8,128)(2,1)} async-done(((bf16[128,16,384]{2,1,0:T(8,128)(2,1)}), bf16[128,16,384]{2,1,0:T(8,128)(2,1)}, u32[]{:S(2)}, u32[]{:S(2)}) %all-to-all-start.4) | async-done | bytes 1572896 | tf_op jit(solution)/shard_map/all_to_all | solution.py:217
  226.5 2.1 fusion.52
  228.6 2.8 %fusion.22 = bf16[256,384]{1,0:T(8,128)(2,1)} fusion(f32[256,384]{1,0:T(8,128)S(1)} %fusion.52, bf16[2048,384]{1,0:T(8,128)(2,1)} %bitcast.38, f32[256,2048]{1,0:T(8,128)S(1)} %select_reduce_fusion, f32[256,384]{1,0:T(8,128)S(1)} %convert_reduce_fusion, bf16[256,384]{1,0:T(8,128)(2,1)S(1)} %copy-done.2), kind=kOutput, calls=%fused_computation.50 | convolution fusion | flops 405438464 | bytes 4849664 | tf_op jit(solution)/shard_map/dot_general | solution.py:228
  (117 shorter events, 35.4 us)
Async XLA Ops:
  8.1 12.8 %copy-start.7 = (bf16[1,192,1536]{2,1,0:T(8,128)(2,1)S(1)}, bf16[1,192,1536]{2,1,0:T(8,128)(2,1)}, u32[]{:S(2)}) copy-start(bf16[1,192,1536]{2,1,0:T(8,128)(2,1)} %param.19) | copy-start | bytes 1769476
  8.1 12.8 %copy-start.8 = (bf16[1,192,1536]{2,1,0:T(8,128)(2,1)S(1)}, bf16[1,192,1536]{2,1,0:T(8,128)(2,1)}, u32[]{:S(2)}) copy-start(bf16[1,192,1536]{2,1,0:T(8,128)(2,1)} %param.18) | copy-start | bytes 1769476
  9.5 38.7 %all-to-all-start = ((bf16[32,48,512]{2,1,0:T(8,128)(2,1)}), bf16[32,48,512]{2,1,0:T(8,128)(2,1)S(1)}, u32[]{:S(2)}, u32[]{:S(2)}) async-start(bf16[32,48,512]{2,1,0:T(8,128)(2,1)} %broadcast_in_dim.37), calls=%async_computation | async-start | bytes 3145728 | tf_op jit(solution)/shard_map/all_to_all | solution.py:47
  20.8 2.9 %copy-start.12 = (s32[3]{0:T(128)S(1)}, s32[3]{0:T(128)}, u32[]{:S(2)}) copy-start(s32[3]{0:T(128)} %param.14) | copy-start | bytes 40
  20.8 5.5 %copy-start.2 = (bf16[256,384]{1,0:T(8,128)(2,1)S(1)}, bf16[256,384]{1,0:T(8,128)(2,1)}, u32[]{:S(2)}) copy-start(bf16[256,384]{1,0:T(8,128)(2,1)} %param.10) | copy-start | bytes 589828
  20.8 163.2 %all-gather.2.cloned.1.call-start = ((), (), s32[]{:S(2)}) async-start(), calls=%async_computation.5 | async-start | bytes 8847360 | tf_op jit(solution)/shard_map/all_gather | solution.py:62
  49.5 1.3 collective-permute-start
  50.9 40.3 %copy-start.3 = (bf16[256,128]{1,0:T(8,128)(2,1)}, bf16[256,128]{1,0:T(8,128)(2,1)S(1)}, u32[]{:S(2)}) copy-start(bf16[256,128]{1,0:T(8,128)(2,1)S(1)} %get-tuple-element.22) | copy-start | bytes 196612
  50.9 40.3 %copy-start.5 = (bf16[256,128]{1,0:T(8,128)(2,1)}, bf16[256,128]{1,0:T(8,128)(2,1)S(1)}, u32[]{:S(2)}) copy-start(bf16[256,128]{1,0:T(8,128)(2,1)S(1)} %get-tuple-element.23) | copy-start | bytes 196612
  50.9 23.7 %collective-permute-start.1 = (bf16[256,256]{1,0:T(8,128)(2,1)S(1)}, bf16[256,256]{1,0:T(8,128)(2,1)S(1)}, u32[]{:S(2)}, u32[]{:S(2)}) collective-permute-start(bf16[256,256]{1,0:T(8,128)(2,1)S(1)} %pad_maximum_fusion.2), channel_id=1, source_target_pairs={{0,4},{1,9},{2,6},{3,11},{4,8},{5,13},{6,10},{7,15},{8,12},{9,17},... | collective-permute-start | bytes 393224 | tf_op jit(solution)/shard_map/ppermute | solution.py:105
  56.8 22.8 %collective-permute-start.2 = (bf16[256,256]{1,0:T(8,128)(2,1)S(1)}, bf16[256,256]{1,0:T(8,128)(2,1)S(1)}, u32[]{:S(2)}, u32[]{:S(2)}) collective-permute-start(bf16[256,256]{1,0:T(8,128)(2,1)S(1)} %pad_maximum_fusion.2), channel_id=1, source_target_pairs={{0,12},{1,17},{2,14},{3,19},{4,16},{5,21},{6,18},{7,23},{8,20},{9,... | collective-permute-start | bytes 393224 | tf_op jit(solution)/shard_map/ppermute | solution.py:105
  61.9 20.3 %collective-permute-start.3 = (bf16[256,256]{1,0:T(8,128)(2,1)S(1)}, bf16[256,256]{1,0:T(8,128)(2,1)S(1)}, u32[]{:S(2)}, u32[]{:S(2)}) collective-permute-start(bf16[256,256]{1,0:T(8,128)(2,1)S(1)} %pad_maximum_fusion.2), channel_id=1, source_target_pairs={{0,20},{1,25},{2,22},{3,27},{4,24},{5,29},{6,26},{7,31},{8,28},{9,... | collective-permute-start | bytes 393224 | tf_op jit(solution)/shard_map/ppermute | solution.py:105
  70.4 17.0 %collective-permute-start.4 = (bf16[256,256]{1,0:T(8,128)(2,1)S(1)}, bf16[256,256]{1,0:T(8,128)(2,1)S(1)}, u32[]{:S(2)}, u32[]{:S(2)}) collective-permute-start(bf16[256,256]{1,0:T(8,128)(2,1)S(1)} %pad_maximum_fusion.2), channel_id=1, source_target_pairs={{0,28},{1,33},{2,30},{3,35},{4,32},{5,37},{6,34},{7,39},{8,36},{9,... | collective-permute-start | bytes 393224 | tf_op jit(solution)/shard_map/ppermute | solution.py:105
  72.6 15.5 %collective-permute-start.5 = (bf16[256,256]{1,0:T(8,128)(2,1)S(1)}, bf16[256,256]{1,0:T(8,128)(2,1)S(1)}, u32[]{:S(2)}, u32[]{:S(2)}) collective-permute-start(bf16[256,256]{1,0:T(8,128)(2,1)S(1)} %pad_maximum_fusion.2), channel_id=1, source_target_pairs={{0,36},{1,41},{2,38},{3,43},{4,40},{5,45},{6,42},{7,47},{8,44},{9,... | collective-permute-start | bytes 393224 | tf_op jit(solution)/shard_map/ppermute | solution.py:105
  74.7 14.1 %collective-permute-start.6 = (bf16[256,256]{1,0:T(8,128)(2,1)S(1)}, bf16[256,256]{1,0:T(8,128)(2,1)S(1)}, u32[]{:S(2)}, u32[]{:S(2)}) collective-permute-start(bf16[256,256]{1,0:T(8,128)(2,1)S(1)} %pad_maximum_fusion.2), channel_id=1, source_target_pairs={{0,44},{1,49},{2,46},{3,51},{4,48},{5,53},{6,50},{7,55},{8,52},{9,... | collective-permute-start | bytes 393224 | tf_op jit(solution)/shard_map/ppermute | solution.py:105
  79.6 9.7 %collective-permute-start.7 = (bf16[256,256]{1,0:T(8,128)(2,1)S(1)}, bf16[256,256]{1,0:T(8,128)(2,1)S(1)}, u32[]{:S(2)}, u32[]{:S(2)}) collective-permute-start(bf16[256,256]{1,0:T(8,128)(2,1)S(1)} %pad_maximum_fusion.2), channel_id=1, source_target_pairs={{0,52},{1,57},{2,54},{3,59},{4,56},{5,61},{6,58},{7,63},{8,60},{9,... | collective-permute-start | bytes 393224 | tf_op jit(solution)/shard_map/ppermute | solution.py:105
  82.2 7.8 %collective-permute-start.8 = (bf16[256,256]{1,0:T(8,128)(2,1)S(1)}, bf16[256,256]{1,0:T(8,128)(2,1)S(1)}, u32[]{:S(2)}, u32[]{:S(2)}) collective-permute-start(bf16[256,256]{1,0:T(8,128)(2,1)S(1)} %pad_maximum_fusion.2), channel_id=1, source_target_pairs={{0,60},{1,65},{2,62},{3,67},{4,64},{5,69},{6,66},{7,71},{8,68},{9,... | collective-permute-start | bytes 393224 | tf_op jit(solution)/shard_map/ppermute | solution.py:105
  90.7 17.5 %collective-permute-start.9 = (bf16[8,256,256]{2,1,0:T(8,128)(2,1)}, bf16[8,256,256]{2,1,0:T(8,128)(2,1)}, u32[]{:S(2)}, u32[]{:S(2)}) collective-permute-start(bf16[8,256,256]{2,1,0:T(8,128)(2,1)} %bitcast_dynamic-update-slice_fusion), channel_id=1, source_target_pairs={{0,1},{1,0},{2,3},{3,2},{4,5},{5,4},{6,7},{7,6},{8,9},{9,8},{10,11... | collective-permute-start | bytes 3145736 | tf_op jit(solution)/shard_map/ppermute | solution.py:107
  95.7 36.4 %all-to-all-start.1 = ((bf16[32,48,384]{2,1,0:T(8,128)(2,1)}), bf16[32,48,384]{2,1,0:T(8,128)(2,1)S(1)}, u32[]{:S(2)}, u32[]{:S(2)}) async-start(bf16[32,48,384]{2,1,0:T(8,128)(2,1)} %broadcast_in_dim.44), calls=%async_computation.1 | async-start | bytes 2359296 | tf_op jit(solution)/shard_map/all_to_all | solution.py:47
  132.7 4.7 %copy-start.11 = (s32[256,4]{0,1:T(4,128)S(1)}, s32[256,4]{0,1:T(4,128)}, u32[]{:S(2)}) copy-start(s32[256,4]{0,1:T(4,128)} %param.15) | copy-start | bytes 12292
  133.7 14.5 %all-to-all-start.2 = ((bf16[256,4,384]{2,0,1:T(8,128)(2,1)}), bf16[256,4,384]{2,0,1:T(8,128)(2,1)S(1)}, u32[]{:S(2)}, u32[]{:S(2)}) async-start(bf16[256,4,384]{2,0,1:T(8,128)(2,1)} %bitcast.107), calls=%async_computation.2 | async-start | bytes 1572864 | tf_op jit(solution)/shard_map/all_to_all | solution.py:157
  196.3 5.9 %copy-start.10 = (f32[256,4]{0,1:T(4,128)S(1)}, f32[256,4]{0,1:T(4,128)}, u32[]{:S(2)}) copy-start(f32[256,4]{0,1:T(4,128)} %param.16) | copy-start | bytes 12292
  196.3 30.1 %all-to-all-start.4 = ((bf16[128,16,384]{2,1,0:T(8,128)(2,1)}), bf16[128,16,384]{2,1,0:T(8,128)(2,1)}, u32[]{:S(2)}, u32[]{:S(2)}) async-start(bf16[128,16,384]{2,1,0:T(8,128)(2,1)} %bitcast.37), calls=%async_computation.4 | async-start | bytes 3145728 | tf_op jit(solution)/shard_map/all_to_all | solution.py:217
  226.5 4.9 %copy-start.1 = (bf16[48,512]{1,0:T(8,128)(2,1)S(1)}, bf16[48,512]{1,0:T(8,128)(2,1)}, u32[]{:S(2)}) copy-start(bf16[48,512]{1,0:T(8,128)(2,1)} %param.12) | copy-start | bytes 147460
  (4 other events, 6.1 us)
Sparse Core Ops, SparseCore 0:
  23.6 84.9 all-gather.1

commit v19 on v17

--- a/solution.py
+++ b/solution.py
@@ -192,19 +192,17 @@
     w_gate = expert_all[0]
     w_up = expert_all[1]
     w_down = expert_all[2]
-    gate_act = None
-    up_act = None
+    hidden_units = w_gate.shape[0]
+    w_gate_up = expert_all[:2].reshape(2 * hidden_units, D)
+    both = None
     for q in range(mp_count):
-        g = lax.dot_general(
-            moe_in[q], w_gate[:, q * feat : (q + 1) * feat], (((1,), (1,)), ((), ())),
+        part = lax.dot_general(
+            moe_in[q], w_gate_up[:, q * feat : (q + 1) * feat], (((1,), (1,)), ((), ())),
             preferred_element_type=jnp.float32,
         )
-        u = lax.dot_general(
-            moe_in[q], w_up[:, q * feat : (q + 1) * feat], (((1,), (1,)), ((), ())),
-            preferred_element_type=jnp.float32,
-        )
-        gate_act = g if gate_act is None else gate_act + g
-        up_act = u if up_act is None else up_act + u
+        both = part if both is None else both + part
+    gate_act = both[:, :hidden_units]
+    up_act = both[:, hidden_units:]
     active = (jnp.maximum(gate_act, 0.0) * up_act).astype(jnp.bfloat16)
     outgoing = jnp.stack(
         [

time: 239 us -> 239 us (level)
    slice x0 -> x1, local copies, waits for them, and re-layouts: none -> 2.64 us  [local(): w_gate_up = expert_all[:2].reshape(2 * hidden_units, D)]
    dot_general x8 -> x4, matrix products: 4.98 us -> 4.18 us  [local(): lax.dot_general(moe_in[q], w_gate_up[:, q * feat:(q + 1) * feat], (((1,),...]
where the time goes in v19:
time: 239 us; the launch traced here: 238 us
  starting transfers between devices  66.8 us (28%)
  blocking collectives  55.8 us (23%)
  waiting for transfers between devices  31.7 us (13%)
  other arithmetic  26.4 us (11%)
  matrix products  26.3 us (11%)
  local copies, waits for them, and re-layouts  15.8 us (7%)
  between operations  15.2 us (6%)
    all_to_all x1, blocking collectives, local(): arrived = lax.all_to_all(buffer, ('mp', 'seq'), 0, 0, tiled=True)  33.9 us
    ppermute x8, starting transfers between devices, local(): fetched.append(lax.ppermute(kv_own, ('seq', 'mp'), pairs))  33.9 us
    all_to_all x1, waiting for transfers between devices, local(): returned = lax.all_to_all(outgoing, ('mp', 'seq'), 0, 0, tiled=True)  22.8 us
    all_to_all x2, starting transfers between devices, gather_seq(): return lax.all_to_all(spread, 'seq', 0, 0, tiled=True)  22.7 us
    all_gather x1, blocking collectives, local(): whole = lax.all_gather(hidden_in, 'mp', axis=1, tiled=True)  21.9 us
    reduce_sum x1, other arithmetic, local(): total = jnp.sum(probs, axis=-1)  9.02 us
    all_to_all x1, waiting for transfers between devices, local(): lax.all_to_all(partial_out.astype(jnp.bfloat16), 'mp', 1, 0, tiled=True)  8.37 us
    dot_general x1, matrix products, local(): accum = jnp.einsum('hqk,kd->hqd', probs, value_rows)  7 us
  transfers between devices with their start and end apart: 15, of which 3 were waited for; matrix products, arithmetic and copies ran while one was open for 21% of the time, Pallas kernels for 0%

profile of v19, /device:TPU:1, one launch (start us, length us, event | category | flops | bytes accessed | tf_op | source)
XLA Modules:
  0.0 237.9 jit_solution(533282031465702591)
XLA Ops:
  9.5 11.3 %all-to-all-start = ((bf16[32,48,512]{2,1,0:T(8,128)(2,1)}), bf16[32,48,512]{2,1,0:T(8,128)(2,1)S(1)}, u32[]{:S(2)}, u32[]{:S(2)}) async-start(bf16[32,48,512]{2,1,0:T(8,128)(2,1)} %broadcast_in_dim.47), calls=%async_computation | async-start | bytes 3145728 | tf_op jit(solution)/shard_map/all_to_all | solution.py:47
  20.9 2.6 %pad_maximum_fusion = bf16[3,192,1536]{2,1,0:T(8,128)(2,1)} fusion(bf16[1,192,1536]{2,1,0:T(8,128)(2,1)S(1)} %copy-done.7, bf16[1,192,1536]{2,1,0:T(8,128)(2,1)S(1)} %copy-done.8, bf16[1,192,1536]{2,1,0:T(8,128)(2,1)} %param.17), kind=kLoop, calls=%fused_computation.34 | loop fusion | flops 1769472 | bytes 3538944 | tf_op jit(solution)/shard_map/concatenate | solution.py:63
  26.2 21.9 %all_gather.6 = bf16[256,1536]{1,0:T(8,128)(2,1)S(1)} all-gather(bf16[256,384]{1,0:T(8,128)(2,1)S(1)} %copy-done.2), channel_id=1, replica_groups=mesh['seq'=32,'mp'=4] {'mp'}, dimensions={1}, use_global_device_ids=true | all-gather | bytes 983040 | tf_op jit(solution)/shard_map/all_gather | solution.py:71
  51.0 5.1 %collective-permute-start.1 = (bf16[256,256]{1,0:T(8,128)(2,1)S(1)}, bf16[256,256]{1,0:T(8,128)(2,1)S(1)}, u32[]{:S(2)}, u32[]{:S(2)}) collective-permute-start(bf16[256,256]{1,0:T(8,128)(2,1)S(1)} %pad_maximum_fusion.2), channel_id=1, source_target_pairs={{0,4},{1,9},{2,6},{3,11},{4,8},{5,13},{6,10},{7,15},{8,12},{9,17},... | collective-permute-start | bytes 393224 | tf_op jit(solution)/shard_map/ppermute | solution.py:105
  56.8 5.0 %collective-permute-start.2 = (bf16[256,256]{1,0:T(8,128)(2,1)S(1)}, bf16[256,256]{1,0:T(8,128)(2,1)S(1)}, u32[]{:S(2)}, u32[]{:S(2)}) collective-permute-start(bf16[256,256]{1,0:T(8,128)(2,1)S(1)} %pad_maximum_fusion.2), channel_id=1, source_target_pairs={{0,12},{1,17},{2,14},{3,19},{4,16},{5,21},{6,18},{7,23},{8,20},{9,... | collective-permute-start | bytes 393224 | tf_op jit(solution)/shard_map/ppermute | solution.py:105
  61.8 8.6 %collective-permute-start.3 = (bf16[256,256]{1,0:T(8,128)(2,1)S(1)}, bf16[256,256]{1,0:T(8,128)(2,1)S(1)}, u32[]{:S(2)}, u32[]{:S(2)}) collective-permute-start(bf16[256,256]{1,0:T(8,128)(2,1)S(1)} %pad_maximum_fusion.2), channel_id=1, source_target_pairs={{0,20},{1,25},{2,22},{3,27},{4,24},{5,29},{6,26},{7,31},{8,28},{9,... | collective-permute-start | bytes 393224 | tf_op jit(solution)/shard_map/ppermute | solution.py:105
  70.3 2.1 collective-permute-start.4
  72.5 2.1 collective-permute-start.5
  74.6 4.3 %collective-permute-start.6 = (bf16[256,256]{1,0:T(8,128)(2,1)S(1)}, bf16[256,256]{1,0:T(8,128)(2,1)S(1)}, u32[]{:S(2)}, u32[]{:S(2)}) collective-permute-start(bf16[256,256]{1,0:T(8,128)(2,1)S(1)} %pad_maximum_fusion.2), channel_id=1, source_target_pairs={{0,44},{1,49},{2,46},{3,51},{4,48},{5,53},{6,50},{7,55},{8,52},{9,... | collective-permute-start | bytes 393224 | tf_op jit(solution)/shard_map/ppermute | solution.py:105
  79.6 1.9 collective-permute-start.7
  82.2 4.7 %collective-permute-start.8 = (bf16[256,256]{1,0:T(8,128)(2,1)S(1)}, bf16[256,256]{1,0:T(8,128)(2,1)S(1)}, u32[]{:S(2)}, u32[]{:S(2)}) collective-permute-start(bf16[256,256]{1,0:T(8,128)(2,1)S(1)} %pad_maximum_fusion.2), channel_id=1, source_target_pairs={{0,60},{1,65},{2,62},{3,67},{4,64},{5,69},{6,66},{7,71},{8,68},{9,... | collective-permute-start | bytes 393224 | tf_op jit(solution)/shard_map/ppermute | solution.py:105
  95.8 11.3 %all-to-all-start.1 = ((bf16[32,48,384]{2,1,0:T(8,128)(2,1)}), bf16[32,48,384]{2,1,0:T(8,128)(2,1)S(1)}, u32[]{:S(2)}, u32[]{:S(2)}) async-start(bf16[32,48,384]{2,1,0:T(8,128)(2,1)} %broadcast_in_dim.51), calls=%async_computation.1 | async-start | bytes 2359296 | tf_op jit(solution)/shard_map/all_to_all | solution.py:47
  108.1 1.7 broadcast_select_fusion.1
  110.0 6.4 %fusion = (f32[3,256]{1,0:T(4,128)S(1)}, f32[3,256,4352]{2,1,0:T(8,128)}) fusion(pred[256,4352]{1,0:T(8,128)(4,1)S(1)} %fusion.11, bf16[4352,256]{1,0:T(8,128)(2,1)S(1)} %maximum_maximum_fusion, bf16[256,3,64]{2,0,1:T(8,128)(2,1)S(1)} %get-tuple-element.14, bf16[256,3,64]{2,0,1:T(8,128)(2,1)S(1)} %get-tuple-element.13), kind=kOutput, calls=%fused_computation.2 | convolution fusion | flops 866057472 | bytes 15993856 | tf_op jit(solution)/shard_map/hqd,kd->hqk/dot_general | solution.py:131
  116.5 9.0 %fusion.1 = f32[3,256]{1,0:T(4,128)S(1)} fusion(f32[3,256,4352]{2,1,0:T(8,128)} %get-tuple-element.26, f32[3,256]{1,0:T(4,128)S(1)} %get-tuple-element.25, pred[256,4352]{1,0:T(8,128)(4,1)S(1)} %fusion.11), kind=kLoop, calls=%fused_computation.3 | loop fusion | flops 16710912 | bytes 14489600 | tf_op jit(solution)/shard_map/reduce_sum | solution.py:146
  125.5 7.0 %fusion.34 = bf16[256,3,128]{0,2,1:T(8,128)(2,1)S(1)} fusion(bf16[4352,256]{1,0:T(8,128)(2,1)S(1)} %maximum_maximum_fusion, f32[3,256,4352]{2,1,0:T(8,128)} %get-tuple-element.26, f32[3,256]{1,0:T(4,128)S(1)} %get-tuple-element.25, pred[256,4352]{1,0:T(8,128)(4,1)S(1)} %fusion.11, f32[256,3]{0,1:T(4,128)S(1)} %bitcast.116), kind=kOutput, calls=%fused_computation.67 | convolution fusion | flops 869203968 | bytes 15802368 | tf_op jit(solution)/shard_map/hqk,kd->hqd/dot_general | solution.py:147
  134.1 3.8 %all-to-all-start.2 = ((bf16[256,4,384]{2,0,1:T(8,128)(2,1)}), bf16[256,4,384]{2,0,1:T(8,128)(2,1)S(1)}, u32[]{:S(2)}, u32[]{:S(2)}) async-start(bf16[256,4,384]{2,0,1:T(8,128)(2,1)} %bitcast.100), calls=%async_computation.2 | async-start | bytes 1572864 | tf_op jit(solution)/shard_map/all_to_all | solution.py:157
  140.3 8.4 %all-to-all-done.2 = bf16[256,4,384]{2,0,1:T(8,128)(2,1)S(1)} async-done(((bf16[256,4,384]{2,0,1:T(8,128)(2,1)}), bf16[256,4,384]{2,0,1:T(8,128)(2,1)S(1)}, u32[]{:S(2)}, u32[]{:S(2)}) %all-to-all-start.2) | async-done | bytes 786464 | tf_op jit(solution)/shard_map/all_to_all | solution.py:157
  149.5 33.9 %all_to_all.52 = bf16[128,16,384]{2,1,0:T(8,128)(2,1)S(1)} all-to-all(bf16[128,16,384]{2,1,0:T(8,128)(2,1)S(1)} %bitcast.107), channel_id=1, replica_groups=mesh['seq'=32,'mp'=4] {'mp','seq'}, dimensions={0} | all-to-all | bytes 3145728 | tf_op jit(solution)/shard_map/all_to_all | solution.py:187
  184.5 2.6 %slice.118 = bf16[2,768,1536]{2,1,0:T(8,128)(2,1)S(1)} slice(bf16[3,768,1536]{2,1,0:T(8,128)(2,1)} %all-gather.2.cloned.1.call-done), slice={[0:2], [0:768], [0:1536]} | slice | bytes 9437184 | tf_op jit(solution)/shard_map/slice | solution.py:196
  191.5 1.8 slice_bitcast_fusion
  197.1 5.9 %all-to-all-start.4 = ((bf16[128,16,384]{2,1,0:T(8,128)(2,1)}), bf16[128,16,384]{2,1,0:T(8,128)(2,1)}, u32[]{:S(2)}, u32[]{:S(2)}) async-start(bf16[128,16,384]{2,1,0:T(8,128)(2,1)} %bitcast.36), calls=%async_computation.4 | async-start | bytes 3145728 | tf_op jit(solution)/shard_map/all_to_all | solution.py:215
  204.4 22.8 %all-to-all-done.4 = bf16[128,16,384]{2,1,0:T(8,128)(2,1)} async-done(((bf16[128,16,384]{2,1,0:T(8,128)(2,1)}), bf16[128,16,384]{2,1,0:T(8,128)(2,1)}, u32[]{:S(2)}, u32[]{:S(2)}) %all-to-all-start.4) | async-done | bytes 1572896 | tf_op jit(solution)/shard_map/all_to_all | solution.py:215
  227.2 3.9 %fusion.28 = bf16[256,384]{1,0:T(8,128)(2,1)} fusion(f32[256,2048]{1,0:T(8,128)S(1)} %select_reduce_fusion, bf16[2048,384]{1,0:T(8,128)(2,1)} %bitcast.37, f32[256,384]{1,0:T(8,128)S(1)} %convert_reduce_fusion, bf16[256,384]{1,0:T(8,128)(2,1)S(1)} %copy-done.2), kind=kOutput, calls=%fused_computation.57 | convolution fusion | flops 2416508928 | bytes 4456448 | tf_op jit(solution)/shard_map/dot_general | solution.py:224
  (114 shorter events, 34.6 us)
Async XLA Ops:
  8.1 12.8 %copy-start.7 = (bf16[1,192,1536]{2,1,0:T(8,128)(2,1)S(1)}, bf16[1,192,1536]{2,1,0:T(8,128)(2,1)}, u32[]{:S(2)}) copy-start(bf16[1,192,1536]{2,1,0:T(8,128)(2,1)} %param.19) | copy-start | bytes 1769476
  8.1 12.8 %copy-start.8 = (bf16[1,192,1536]{2,1,0:T(8,128)(2,1)S(1)}, bf16[1,192,1536]{2,1,0:T(8,128)(2,1)}, u32[]{:S(2)}) copy-start(bf16[1,192,1536]{2,1,0:T(8,128)(2,1)} %param.18) | copy-start | bytes 1769476
  9.5 38.8 %all-to-all-start = ((bf16[32,48,512]{2,1,0:T(8,128)(2,1)}), bf16[32,48,512]{2,1,0:T(8,128)(2,1)S(1)}, u32[]{:S(2)}, u32[]{:S(2)}) async-start(bf16[32,48,512]{2,1,0:T(8,128)(2,1)} %broadcast_in_dim.47), calls=%async_computation | async-start | bytes 3145728 | tf_op jit(solution)/shard_map/all_to_all | solution.py:47
  20.8 5.3 %copy-start.2 = (bf16[256,384]{1,0:T(8,128)(2,1)S(1)}, bf16[256,384]{1,0:T(8,128)(2,1)}, u32[]{:S(2)}) copy-start(bf16[256,384]{1,0:T(8,128)(2,1)} %param.10) | copy-start | bytes 589828
  20.8 163.6 %all-gather.2.cloned.1.call-start = ((), (), s32[]{:S(2)}) async-start(), calls=%async_computation.5 | async-start | bytes 8847360 | tf_op jit(solution)/shard_map/all_gather | solution.py:62
  49.6 1.3 collective-permute-start
  51.0 40.3 %copy-start.3 = (bf16[256,128]{1,0:T(8,128)(2,1)}, bf16[256,128]{1,0:T(8,128)(2,1)S(1)}, u32[]{:S(2)}) copy-start(bf16[256,128]{1,0:T(8,128)(2,1)S(1)} %get-tuple-element.19) | copy-start | bytes 196612
  51.0 40.3 %copy-start.5 = (bf16[256,128]{1,0:T(8,128)(2,1)}, bf16[256,128]{1,0:T(8,128)(2,1)S(1)}, u32[]{:S(2)}) copy-start(bf16[256,128]{1,0:T(8,128)(2,1)S(1)} %get-tuple-element.20) | copy-start | bytes 196612
  51.0 23.6 %collective-permute-start.1 = (bf16[256,256]{1,0:T(8,128)(2,1)S(1)}, bf16[256,256]{1,0:T(8,128)(2,1)S(1)}, u32[]{:S(2)}, u32[]{:S(2)}) collective-permute-start(bf16[256,256]{1,0:T(8,128)(2,1)S(1)} %pad_maximum_fusion.2), channel_id=1, source_target_pairs={{0,4},{1,9},{2,6},{3,11},{4,8},{5,13},{6,10},{7,15},{8,12},{9,17},... | collective-permute-start | bytes 393224 | tf_op jit(solution)/shard_map/ppermute | solution.py:105
  56.8 22.8 %collective-permute-start.2 = (bf16[256,256]{1,0:T(8,128)(2,1)S(1)}, bf16[256,256]{1,0:T(8,128)(2,1)S(1)}, u32[]{:S(2)}, u32[]{:S(2)}) collective-permute-start(bf16[256,256]{1,0:T(8,128)(2,1)S(1)} %pad_maximum_fusion.2), channel_id=1, source_target_pairs={{0,12},{1,17},{2,14},{3,19},{4,16},{5,21},{6,18},{7,23},{8,20},{9,... | collective-permute-start | bytes 393224 | tf_op jit(solution)/shard_map/ppermute | solution.py:105
  61.8 20.4 %collective-permute-start.3 = (bf16[256,256]{1,0:T(8,128)(2,1)S(1)}, bf16[256,256]{1,0:T(8,128)(2,1)S(1)}, u32[]{:S(2)}, u32[]{:S(2)}) collective-permute-start(bf16[256,256]{1,0:T(8,128)(2,1)S(1)} %pad_maximum_fusion.2), channel_id=1, source_target_pairs={{0,20},{1,25},{2,22},{3,27},{4,24},{5,29},{6,26},{7,31},{8,28},{9,... | collective-permute-start | bytes 393224 | tf_op jit(solution)/shard_map/ppermute | solution.py:105
  70.3 17.2 %collective-permute-start.4 = (bf16[256,256]{1,0:T(8,128)(2,1)S(1)}, bf16[256,256]{1,0:T(8,128)(2,1)S(1)}, u32[]{:S(2)}, u32[]{:S(2)}) collective-permute-start(bf16[256,256]{1,0:T(8,128)(2,1)S(1)} %pad_maximum_fusion.2), channel_id=1, source_target_pairs={{0,28},{1,33},{2,30},{3,35},{4,32},{5,37},{6,34},{7,39},{8,36},{9,... | collective-permute-start | bytes 393224 | tf_op jit(solution)/shard_map/ppermute | solution.py:105
  72.5 15.7 %collective-permute-start.5 = (bf16[256,256]{1,0:T(8,128)(2,1)S(1)}, bf16[256,256]{1,0:T(8,128)(2,1)S(1)}, u32[]{:S(2)}, u32[]{:S(2)}) collective-permute-start(bf16[256,256]{1,0:T(8,128)(2,1)S(1)} %pad_maximum_fusion.2), channel_id=1, source_target_pairs={{0,36},{1,41},{2,38},{3,43},{4,40},{5,45},{6,42},{7,47},{8,44},{9,... | collective-permute-start | bytes 393224 | tf_op jit(solution)/shard_map/ppermute | solution.py:105
  74.6 14.3 %collective-permute-start.6 = (bf16[256,256]{1,0:T(8,128)(2,1)S(1)}, bf16[256,256]{1,0:T(8,128)(2,1)S(1)}, u32[]{:S(2)}, u32[]{:S(2)}) collective-permute-start(bf16[256,256]{1,0:T(8,128)(2,1)S(1)} %pad_maximum_fusion.2), channel_id=1, source_target_pairs={{0,44},{1,49},{2,46},{3,51},{4,48},{5,53},{6,50},{7,55},{8,52},{9,... | collective-permute-start | bytes 393224 | tf_op jit(solution)/shard_map/ppermute | solution.py:105
  79.6 10.0 %collective-permute-start.7 = (bf16[256,256]{1,0:T(8,128)(2,1)S(1)}, bf16[256,256]{1,0:T(8,128)(2,1)S(1)}, u32[]{:S(2)}, u32[]{:S(2)}) collective-permute-start(bf16[256,256]{1,0:T(8,128)(2,1)S(1)} %pad_maximum_fusion.2), channel_id=1, source_target_pairs={{0,52},{1,57},{2,54},{3,59},{4,56},{5,61},{6,58},{7,63},{8,60},{9,... | collective-permute-start | bytes 393224 | tf_op jit(solution)/shard_map/ppermute | solution.py:105
  82.2 8.1 %collective-permute-start.8 = (bf16[256,256]{1,0:T(8,128)(2,1)S(1)}, bf16[256,256]{1,0:T(8,128)(2,1)S(1)}, u32[]{:S(2)}, u32[]{:S(2)}) collective-permute-start(bf16[256,256]{1,0:T(8,128)(2,1)S(1)} %pad_maximum_fusion.2), channel_id=1, source_target_pairs={{0,60},{1,65},{2,62},{3,67},{4,64},{5,69},{6,66},{7,71},{8,68},{9,... | collective-permute-start | bytes 393224 | tf_op jit(solution)/shard_map/ppermute | solution.py:105
  90.9 17.2 %collective-permute-start.9 = (bf16[8,256,256]{2,1,0:T(8,128)(2,1)}, bf16[8,256,256]{2,1,0:T(8,128)(2,1)}, u32[]{:S(2)}, u32[]{:S(2)}) collective-permute-start(bf16[8,256,256]{2,1,0:T(8,128)(2,1)} %bitcast_dynamic-update-slice_fusion), channel_id=1, source_target_pairs={{0,1},{1,0},{2,3},{3,2},{4,5},{5,4},{6,7},{7,6},{8,9},{9,8},{10,11... | collective-permute-start | bytes 3145736 | tf_op jit(solution)/shard_map/ppermute | solution.py:107
  91.3 3.4 %copy-start.9 = (bf16[384,48]{0,1:T(8,128)(2,1)S(1)}, bf16[384,48]{0,1:T(8,128)(2,1)}, u32[]{:S(2)}) copy-start(bf16[384,48]{0,1:T(8,128)(2,1)} %param.13) | copy-start | bytes 110596
  95.8 36.8 %all-to-all-start.1 = ((bf16[32,48,384]{2,1,0:T(8,128)(2,1)}), bf16[32,48,384]{2,1,0:T(8,128)(2,1)S(1)}, u32[]{:S(2)}, u32[]{:S(2)}) async-start(bf16[32,48,384]{2,1,0:T(8,128)(2,1)} %broadcast_in_dim.51), calls=%async_computation.1 | async-start | bytes 2359296 | tf_op jit(solution)/shard_map/all_to_all | solution.py:47
  132.5 5.4 %copy-start.11 = (s32[256,4]{0,1:T(4,128)S(1)}, s32[256,4]{0,1:T(4,128)}, u32[]{:S(2)}) copy-start(s32[256,4]{0,1:T(4,128)} %param.15) | copy-start | bytes 12292
  134.1 14.6 %all-to-all-start.2 = ((bf16[256,4,384]{2,0,1:T(8,128)(2,1)}), bf16[256,4,384]{2,0,1:T(8,128)(2,1)S(1)}, u32[]{:S(2)}, u32[]{:S(2)}) async-start(bf16[256,4,384]{2,0,1:T(8,128)(2,1)} %bitcast.100), calls=%async_computation.2 | async-start | bytes 1572864 | tf_op jit(solution)/shard_map/all_to_all | solution.py:157
  197.1 5.9 %copy-start.10 = (f32[256,4]{0,1:T(4,128)S(1)}, f32[256,4]{0,1:T(4,128)}, u32[]{:S(2)}) copy-start(f32[256,4]{0,1:T(4,128)} %param.16) | copy-start | bytes 12292
  197.1 30.1 %all-to-all-start.4 = ((bf16[128,16,384]{2,1,0:T(8,128)(2,1)}), bf16[128,16,384]{2,1,0:T(8,128)(2,1)}, u32[]{:S(2)}, u32[]{:S(2)}) async-start(bf16[128,16,384]{2,1,0:T(8,128)(2,1)} %bitcast.36), calls=%async_computation.4 | async-start | bytes 3145728 | tf_op jit(solution)/shard_map/all_to_all | solution.py:215
  203.0 28.1 %copy-start.1 = (bf16[48,512]{1,0:T(8,128)(2,1)S(1)}, bf16[48,512]{1,0:T(8,128)(2,1)}, u32[]{:S(2)}) copy-start(bf16[48,512]{1,0:T(8,128)(2,1)} %param.12) | copy-start | bytes 147460
  (4 other events, 7.2 us)
Sparse Core Ops, SparseCore 0:
  23.6 85.0 all-gather.1

commit v20 on v17

--- a/solution.py
+++ b/solution.py
@@ -68,7 +68,9 @@
     kv_cols = lax.dynamic_slice_in_dim(wkv, kv_col, HD, 1)
     w_qkv = gather_seq(jnp.concatenate([wq, kv_cols], axis=1), seq_count)
 
-    whole = lax.all_gather(hidden_in, "mp", axis=1, tiled=True)
+    whole = lax.all_to_all(
+        jnp.broadcast_to(hidden_in[None], (mp_count,) + hidden_in.shape), "mp", 0, 2, tiled=True
+    ).reshape(tok_rows, D)
     whole_f = whole.astype(jnp.float32)
     normed = (
         whole_f * lax.rsqrt(jnp.sum(whole_f * whole_f, axis=-1, keepdims=True) / D + EPSILON)

time: 239 us -> 244 us (1.021)
  waiting for transfers between devices: 31.6 us -> 64.8 us
  blocking collectives: 55.5 us -> 33.9 us
  starting transfers between devices: 66.9 us -> 62.7 us
  other arithmetic: 26.4 us -> 23.1 us
    all_to_all x2, waiting for transfers between devices: 0.01 us -> 23.4 us  [gather_seq(): return lax.all_to_all(spread, 'seq', 0, 0, tiled=True)]
    all_gather x1 -> x0, blocking collectives: 21.6 us -> none  [local(): whole = lax.all_gather(hidden_in, 'mp', axis=1, tiled=True)]
    ppermute x8, starting transfers between devices: 33.7 us -> 24.2 us  [local(): fetched.append(lax.ppermute(kv_own, ('seq', 'mp'), pairs))]
    all_to_all x0 -> x1, waiting for transfers between devices: none -> 9.16 us  [local(): lax.all_to_all(jnp.broadcast_to(hidden_in[None], (mp_count,) + hidden_in....]
    all_to_all x0 -> x1, starting transfers between devices: none -> 4.88 us  [local(): lax.all_to_all(jnp.broadcast_to(hidden_in[None], (mp_count,) + hidden_in....]
    unnamed x36 -> x33, local copies, waits for them, and re-layouts: 5.93 us -> 6.31 us
  transfers between devices with their start and end apart: 15 -> 16, of which waited for: 3 -> 6; matrix products, arithmetic and copies ran while one was open for 21% -> 20% of each run, Pallas kernels for 0% -> 0%
where the time goes in v20:
time: 244 us; the launch traced here: 243 us
  waiting for transfers between devices  64.8 us (27%)
  starting transfers between devices  62.7 us (26%)
  blocking collectives  33.9 us (14%)
  matrix products  27.1 us (11%)
  other arithmetic  23.1 us (9%)
  local copies, waits for them, and re-layouts  16.2 us (7%)
  between operations  15.3 us (6%)
    all_to_all x1, blocking collectives, local(): arrived = lax.all_to_all(buffer, ('mp', 'seq'), 0, 0, tiled=True)  33.9 us
    ppermute x8, starting transfers between devices, local(): fetched.append(lax.ppermute(kv_own, ('seq', 'mp'), pairs))  24.2 us
    all_to_all x2, waiting for transfers between devices, gather_seq(): return lax.all_to_all(spread, 'seq', 0, 0, tiled=True)  23.4 us
    all_to_all x1, waiting for transfers between devices, local(): returned = lax.all_to_all(outgoing, ('mp', 'seq'), 0, 0, tiled=True)  22.8 us
    all_to_all x2, starting transfers between devices, gather_seq(): return lax.all_to_all(spread, 'seq', 0, 0, tiled=True)  20.4 us
    all_to_all x1, waiting for transfers between devices, local(): lax.all_to_all(jnp.broadcast_to(hidden_in[None], (mp_count,) + hidden_in....  9.16 us
    reduce_sum x1, other arithmetic, local(): total = jnp.sum(probs, axis=-1)  9.02 us
    all_to_all x1, waiting for transfers between devices, local(): lax.all_to_all(partial_out.astype(jnp.bfloat16), 'mp', 1, 0, tiled=True)  8.37 us
  transfers between devices with their start and end apart: 16, of which 6 were waited for; matrix products, arithmetic and copies ran while one was open for 20% of the time, Pallas kernels for 0%

profile of v20, /device:TPU:1, one launch (start us, length us, event | category | flops | bytes accessed | tf_op | source)
XLA Modules:
  0.0 243.2 jit_solution(6893393957985808252)
XLA Ops:
  8.7 4.9 %all-to-all-start = ((bf16[4,256,384]{1,2,0:T(8,128)(2,1)}), bf16[4,256,384]{1,2,0:T(8,128)(2,1)S(1)}, u32[]{:S(2)}, u32[]{:S(2)}) async-start(bf16[4,256,384]{1,2,0:T(8,128)(2,1)} %broadcast_in_dim.49), calls=%async_computation | async-start | bytes 1572864 | tf_op jit(solution)/shard_map/all_to_all | solution.py:71
  13.6 1.5 pad_maximum_fusion
  15.2 9.2 %all-to-all-done = bf16[4,256,384]{1,2,0:T(8,128)(2,1)S(1)} async-done(((bf16[4,256,384]{1,2,0:T(8,128)(2,1)}), bf16[4,256,384]{1,2,0:T(8,128)(2,1)S(1)}, u32[]{:S(2)}, u32[]{:S(2)}) %all-to-all-start) | async-done | bytes 786464 | tf_op jit(solution)/shard_map/all_to_all | solution.py:71
  25.7 10.6 %all-to-all-start.1 = ((bf16[32,48,512]{2,1,0:T(8,128)(2,1)}), bf16[32,48,512]{2,1,0:T(8,128)(2,1)S(1)}, u32[]{:S(2)}, u32[]{:S(2)}) async-start(bf16[32,48,512]{2,1,0:T(8,128)(2,1)} %broadcast_in_dim.50), calls=%async_computation.1 | async-start | bytes 3145728 | tf_op jit(solution)/shard_map/all_to_all | solution.py:47
  39.5 23.4 %all-to-all-done.1 = bf16[32,48,512]{2,1,0:T(8,128)(2,1)S(1)} async-done(((bf16[32,48,512]{2,1,0:T(8,128)(2,1)}), bf16[32,48,512]{2,1,0:T(8,128)(2,1)S(1)}, u32[]{:S(2)}, u32[]{:S(2)}) %all-to-all-start.1) | async-done | bytes 1572896 | tf_op jit(solution)/shard_map/all_to_all | solution.py:47
  64.3 2.4 collective-permute-start
  69.6 3.7 %collective-permute-start.2 = (bf16[256,256]{1,0:T(8,128)(2,1)S(1)}, bf16[256,256]{1,0:T(8,128)(2,1)S(1)}, u32[]{:S(2)}, u32[]{:S(2)}) collective-permute-start(bf16[256,256]{1,0:T(8,128)(2,1)S(1)} %pad_maximum_fusion.2), channel_id=1, source_target_pairs={{0,12},{1,17},{2,14},{3,19},{4,16},{5,21},{6,18},{7,23},{8,20},{9,... | collective-permute-start | bytes 393224 | tf_op jit(solution)/shard_map/ppermute | solution.py:107
  73.3 7.0 %collective-permute-start.3 = (bf16[256,256]{1,0:T(8,128)(2,1)S(1)}, bf16[256,256]{1,0:T(8,128)(2,1)S(1)}, u32[]{:S(2)}, u32[]{:S(2)}) collective-permute-start(bf16[256,256]{1,0:T(8,128)(2,1)S(1)} %pad_maximum_fusion.2), channel_id=1, source_target_pairs={{0,20},{1,25},{2,22},{3,27},{4,24},{5,29},{6,26},{7,31},{8,28},{9,... | collective-permute-start | bytes 393224 | tf_op jit(solution)/shard_map/ppermute | solution.py:107
  80.3 2.8 %collective-permute-start.4 = (bf16[256,256]{1,0:T(8,128)(2,1)S(1)}, bf16[256,256]{1,0:T(8,128)(2,1)S(1)}, u32[]{:S(2)}, u32[]{:S(2)}) collective-permute-start(bf16[256,256]{1,0:T(8,128)(2,1)S(1)} %pad_maximum_fusion.2), channel_id=1, source_target_pairs={{0,28},{1,33},{2,30},{3,35},{4,32},{5,37},{6,34},{7,39},{8,36},{9,... | collective-permute-start | bytes 393224 | tf_op jit(solution)/shard_map/ppermute | solution.py:107
  83.1 2.5 %collective-permute-start.5 = (bf16[256,256]{1,0:T(8,128)(2,1)S(1)}, bf16[256,256]{1,0:T(8,128)(2,1)S(1)}, u32[]{:S(2)}, u32[]{:S(2)}) collective-permute-start(bf16[256,256]{1,0:T(8,128)(2,1)S(1)} %pad_maximum_fusion.2), channel_id=1, source_target_pairs={{0,36},{1,41},{2,38},{3,43},{4,40},{5,45},{6,42},{7,47},{8,44},{9,... | collective-permute-start | bytes 393224 | tf_op jit(solution)/shard_map/ppermute | solution.py:107
  85.6 4.3 %collective-permute-start.6 = (bf16[256,256]{1,0:T(8,128)(2,1)S(1)}, bf16[256,256]{1,0:T(8,128)(2,1)S(1)}, u32[]{:S(2)}, u32[]{:S(2)}) collective-permute-start(bf16[256,256]{1,0:T(8,128)(2,1)S(1)} %pad_maximum_fusion.2), channel_id=1, source_target_pairs={{0,44},{1,49},{2,46},{3,51},{4,48},{5,53},{6,50},{7,55},{8,52},{9,... | collective-permute-start | bytes 393224 | tf_op jit(solution)/shard_map/ppermute | solution.py:107
  100.0 1.6 fusion.11
  103.9 9.8 %all-to-all-start.2 = ((bf16[32,48,384]{2,1,0:T(8,128)(2,1)}), bf16[32,48,384]{2,1,0:T(8,128)(2,1)S(1)}, u32[]{:S(2)}, u32[]{:S(2)}) async-start(bf16[32,48,384]{2,1,0:T(8,128)(2,1)} %broadcast_in_dim.54), calls=%async_computation.2 | async-start | bytes 2359296 | tf_op jit(solution)/shard_map/all_to_all | solution.py:47
  113.8 1.7 broadcast_select_fusion.1
  115.6 6.5 %fusion = (f32[3,256]{1,0:T(4,128)S(1)}, f32[3,256,4352]{2,1,0:T(8,128)}) fusion(pred[256,4352]{1,0:T(8,128)(4,1)S(1)} %fusion.11, bf16[4352,256]{1,0:T(8,128)(2,1)S(1)} %maximum_maximum_fusion, bf16[256,3,64]{2,0,1:T(8,128)(2,1)S(1)} %get-tuple-element.17, bf16[256,3,64]{2,0,1:T(8,128)(2,1)S(1)} %get-tuple-element.16), kind=kOutput, calls=%fused_computation.2 | convolution fusion | flops 866057472 | bytes 15993856 | tf_op jit(solution)/shard_map/hqd,kd->hqk/dot_general | solution.py:133
  122.1 9.0 %fusion.1 = f32[3,256]{1,0:T(4,128)S(1)} fusion(f32[3,256,4352]{2,1,0:T(8,128)} %get-tuple-element.29, f32[3,256]{1,0:T(4,128)S(1)} %get-tuple-element.28, pred[256,4352]{1,0:T(8,128)(4,1)S(1)} %fusion.11), kind=kLoop, calls=%fused_computation.3 | loop fusion | flops 16710912 | bytes 14489600 | tf_op jit(solution)/shard_map/reduce_sum | solution.py:148
  131.1 7.0 %fusion.28 = bf16[256,3,128]{0,2,1:T(8,128)(2,1)S(1)} fusion(bf16[4352,256]{1,0:T(8,128)(2,1)S(1)} %maximum_maximum_fusion, f32[3,256,4352]{2,1,0:T(8,128)} %get-tuple-element.29, f32[3,256]{1,0:T(4,128)S(1)} %get-tuple-element.28, pred[256,4352]{1,0:T(8,128)(4,1)S(1)} %fusion.11, f32[256,3]{0,1:T(4,128)S(1)} %bitcast.128), kind=kOutput, calls=%fused_computation.59 | convolution fusion | flops 869203968 | bytes 15802368 | tf_op jit(solution)/shard_map/hqk,kd->hqd/dot_general | solution.py:149
  139.7 3.7 %all-to-all-start.3 = ((bf16[256,4,384]{2,0,1:T(8,128)(2,1)}), bf16[256,4,384]{2,0,1:T(8,128)(2,1)S(1)}, u32[]{:S(2)}, u32[]{:S(2)}) async-start(bf16[256,4,384]{2,0,1:T(8,128)(2,1)} %bitcast.115), calls=%async_computation.3 | async-start | bytes 1572864 | tf_op jit(solution)/shard_map/all_to_all | solution.py:159
  145.9 8.4 %all-to-all-done.3 = bf16[256,4,384]{2,0,1:T(8,128)(2,1)S(1)} async-done(((bf16[256,4,384]{2,0,1:T(8,128)(2,1)}), bf16[256,4,384]{2,0,1:T(8,128)(2,1)S(1)}, u32[]{:S(2)}, u32[]{:S(2)}) %all-to-all-start.3) | async-done | bytes 786464 | tf_op jit(solution)/shard_map/all_to_all | solution.py:159
  155.1 33.9 %all_to_all.61 = bf16[128,16,384]{2,1,0:T(8,128)(2,1)S(1)} all-to-all(bf16[128,16,384]{2,1,0:T(8,128)(2,1)S(1)} %bitcast.118), channel_id=1, replica_groups=mesh['seq'=32,'mp'=4] {'mp','seq'}, dimensions={0} | all-to-all | bytes 3145728 | tf_op jit(solution)/shard_map/all_to_all | solution.py:189
  190.1 3.6 %slice_bitcast_fusion = (bf16[768,1536]{1,0:T(8,128)(2,1)S(1)}, bf16[768,1536]{1,0:T(8,128)(2,1)S(1)}, bf16[768,1536]{1,0:T(8,128)(2,1)S(1)}) fusion(bf16[3,768,1536]{2,1,0:T(8,128)(2,1)} %all-gather.2.cloned.1.call-done), kind=kLoop, calls=%fused_computation.27 | loop fusion | bytes 14155776 | tf_op jit(solution)/shard_map/squeeze | solution.py:196
  202.3 5.9 %all-to-all-start.5 = ((bf16[128,16,384]{2,1,0:T(8,128)(2,1)}), bf16[128,16,384]{2,1,0:T(8,128)(2,1)}, u32[]{:S(2)}, u32[]{:S(2)}) async-start(bf16[128,16,384]{2,1,0:T(8,128)(2,1)} %bitcast.41), calls=%async_computation.5 | async-start | bytes 3145728 | tf_op jit(solution)/shard_map/all_to_all | solution.py:219
  209.7 22.8 %all-to-all-done.5 = bf16[128,16,384]{2,1,0:T(8,128)(2,1)} async-done(((bf16[128,16,384]{2,1,0:T(8,128)(2,1)}), bf16[128,16,384]{2,1,0:T(8,128)(2,1)}, u32[]{:S(2)}, u32[]{:S(2)}) %all-to-all-start.5) | async-done | bytes 1572896 | tf_op jit(solution)/shard_map/all_to_all | solution.py:219
  232.5 3.9 %fusion.22 = bf16[256,384]{1,0:T(8,128)(2,1)} fusion(f32[256,2048]{1,0:T(8,128)S(1)} %select_reduce_fusion, bf16[2048,384]{1,0:T(8,128)(2,1)} %bitcast.42, f32[256,384]{1,0:T(8,128)S(1)} %convert_reduce_fusion, bf16[256,384]{1,0:T(8,128)(2,1)S(1)} %copy-done.2), kind=kOutput, calls=%fused_computation.49 | convolution fusion | flops 2416508928 | bytes 4456448 | tf_op jit(solution)/shard_map/dot_general | solution.py:228
  (116 shorter events, 38.0 us)
Async XLA Ops:
  6.5 8.6 %copy-start = (bf16[48,512]{1,0:T(8,128)(2,1)S(1)}, bf16[48,512]{1,0:T(8,128)(2,1)}, u32[]{:S(2)}) copy-start(bf16[48,512]{1,0:T(8,128)(2,1)} %param.12) | copy-start | bytes 147460
  6.5 7.0 %copy-start.5 = (bf16[1,192,1536]{2,1,0:T(8,128)(2,1)S(1)}, bf16[1,192,1536]{2,1,0:T(8,128)(2,1)}, u32[]{:S(2)}) copy-start(bf16[1,192,1536]{2,1,0:T(8,128)(2,1)} %param.17) | copy-start | bytes 1769476
  6.5 7.0 %copy-start.4 = (bf16[1,192,1536]{2,1,0:T(8,128)(2,1)S(1)}, bf16[1,192,1536]{2,1,0:T(8,128)(2,1)}, u32[]{:S(2)}) copy-start(bf16[1,192,1536]{2,1,0:T(8,128)(2,1)} %param.18) | copy-start | bytes 1769476
  6.5 7.1 %copy-start.3 = (bf16[1,192,1536]{2,1,0:T(8,128)(2,1)S(1)}, bf16[1,192,1536]{2,1,0:T(8,128)(2,1)}, u32[]{:S(2)}) copy-start(bf16[1,192,1536]{2,1,0:T(8,128)(2,1)} %param.19) | copy-start | bytes 1769476
  8.7 15.7 %all-to-all-start = ((bf16[4,256,384]{1,2,0:T(8,128)(2,1)}), bf16[4,256,384]{1,2,0:T(8,128)(2,1)S(1)}, u32[]{:S(2)}, u32[]{:S(2)}) async-start(bf16[4,256,384]{1,2,0:T(8,128)(2,1)} %broadcast_in_dim.49), calls=%async_computation | async-start | bytes 1572864 | tf_op jit(solution)/shard_map/all_to_all | solution.py:71
  13.6 176.5 %all-gather.2.cloned.1.call-start = ((), (), s32[]{:S(2)}) async-start(), calls=%async_computation.6 | async-start | bytes 8847360 | tf_op jit(solution)/shard_map/all_gather | solution.py:62
  15.2 21.3 %copy-start.10 = (s32[3]{0:T(128)S(1)}, s32[3]{0:T(128)}, u32[]{:S(2)}) copy-start(s32[3]{0:T(128)} %param.14) | copy-start | bytes 40
  25.7 37.3 %all-to-all-start.1 = ((bf16[32,48,512]{2,1,0:T(8,128)(2,1)}), bf16[32,48,512]{2,1,0:T(8,128)(2,1)S(1)}, u32[]{:S(2)}, u32[]{:S(2)}) async-start(bf16[32,48,512]{2,1,0:T(8,128)(2,1)} %broadcast_in_dim.50), calls=%async_computation.1 | async-start | bytes 3145728 | tf_op jit(solution)/shard_map/all_to_all | solution.py:47
  64.3 3.3 %collective-permute-start = (bf16[256,128]{1,0:T(8,128)(2,1)S(1)}, bf16[256,128]{1,0:T(8,128)(2,1)S(1)}, u32[]{:S(2)}, u32[]{:S(2)}) collective-permute-start(bf16[256,128]{1,0:T(8,128)(2,1)S(1)} %fusion.57), channel_id=1, source_target_pairs={{0,1},{1,0},{2,3},{3,2},{4,5},{5,4},{6,7},{7,6},{8,9},{9,8},{10,11... | collective-permute-start | bytes 196616 | tf_op jit(solution)/shard_map/ppermute | solution.py:92
  67.6 18.0 %collective-permute-start.1 = (bf16[256,256]{1,0:T(8,128)(2,1)S(1)}, bf16[256,256]{1,0:T(8,128)(2,1)S(1)}, u32[]{:S(2)}, u32[]{:S(2)}) collective-permute-start(bf16[256,256]{1,0:T(8,128)(2,1)S(1)} %pad_maximum_fusion.2), channel_id=1, source_target_pairs={{0,4},{1,9},{2,6},{3,11},{4,8},{5,13},{6,10},{7,15},{8,12},{9,17},... | collective-permute-start | bytes 393224 | tf_op jit(solution)/shard_map/ppermute | solution.py:107
  69.6 21.0 %collective-permute-start.2 = (bf16[256,256]{1,0:T(8,128)(2,1)S(1)}, bf16[256,256]{1,0:T(8,128)(2,1)S(1)}, u32[]{:S(2)}, u32[]{:S(2)}) collective-permute-start(bf16[256,256]{1,0:T(8,128)(2,1)S(1)} %pad_maximum_fusion.2), channel_id=1, source_target_pairs={{0,12},{1,17},{2,14},{3,19},{4,16},{5,21},{6,18},{7,23},{8,20},{9,... | collective-permute-start | bytes 393224 | tf_op jit(solution)/shard_map/ppermute | solution.py:107
  73.3 19.3 %collective-permute-start.3 = (bf16[256,256]{1,0:T(8,128)(2,1)S(1)}, bf16[256,256]{1,0:T(8,128)(2,1)S(1)}, u32[]{:S(2)}, u32[]{:S(2)}) collective-permute-start(bf16[256,256]{1,0:T(8,128)(2,1)S(1)} %pad_maximum_fusion.2), channel_id=1, source_target_pairs={{0,20},{1,25},{2,22},{3,27},{4,24},{5,29},{6,26},{7,31},{8,28},{9,... | collective-permute-start | bytes 393224 | tf_op jit(solution)/shard_map/ppermute | solution.py:107
  80.3 14.2 %collective-permute-start.4 = (bf16[256,256]{1,0:T(8,128)(2,1)S(1)}, bf16[256,256]{1,0:T(8,128)(2,1)S(1)}, u32[]{:S(2)}, u32[]{:S(2)}) collective-permute-start(bf16[256,256]{1,0:T(8,128)(2,1)S(1)} %pad_maximum_fusion.2), channel_id=1, source_target_pairs={{0,28},{1,33},{2,30},{3,35},{4,32},{5,37},{6,34},{7,39},{8,36},{9,... | collective-permute-start | bytes 393224 | tf_op jit(solution)/shard_map/ppermute | solution.py:107
  83.1 12.1 %collective-permute-start.5 = (bf16[256,256]{1,0:T(8,128)(2,1)S(1)}, bf16[256,256]{1,0:T(8,128)(2,1)S(1)}, u32[]{:S(2)}, u32[]{:S(2)}) collective-permute-start(bf16[256,256]{1,0:T(8,128)(2,1)S(1)} %pad_maximum_fusion.2), channel_id=1, source_target_pairs={{0,36},{1,41},{2,38},{3,43},{4,40},{5,45},{6,42},{7,47},{8,44},{9,... | collective-permute-start | bytes 393224 | tf_op jit(solution)/shard_map/ppermute | solution.py:107
  85.6 10.2 %collective-permute-start.6 = (bf16[256,256]{1,0:T(8,128)(2,1)S(1)}, bf16[256,256]{1,0:T(8,128)(2,1)S(1)}, u32[]{:S(2)}, u32[]{:S(2)}) collective-permute-start(bf16[256,256]{1,0:T(8,128)(2,1)S(1)} %pad_maximum_fusion.2), channel_id=1, source_target_pairs={{0,44},{1,49},{2,46},{3,51},{4,48},{5,53},{6,50},{7,55},{8,52},{9,... | collective-permute-start | bytes 393224 | tf_op jit(solution)/shard_map/ppermute | solution.py:107
  90.6 5.9 %collective-permute-start.7 = (bf16[256,256]{1,0:T(8,128)(2,1)S(1)}, bf16[256,256]{1,0:T(8,128)(2,1)S(1)}, u32[]{:S(2)}, u32[]{:S(2)}) collective-permute-start(bf16[256,256]{1,0:T(8,128)(2,1)S(1)} %pad_maximum_fusion.2), channel_id=1, source_target_pairs={{0,52},{1,57},{2,54},{3,59},{4,56},{5,61},{6,58},{7,63},{8,60},{9,... | collective-permute-start | bytes 393224 | tf_op jit(solution)/shard_map/ppermute | solution.py:107
  92.6 5.4 %collective-permute-start.8 = (bf16[256,256]{1,0:T(8,128)(2,1)S(1)}, bf16[256,256]{1,0:T(8,128)(2,1)S(1)}, u32[]{:S(2)}, u32[]{:S(2)}) collective-permute-start(bf16[256,256]{1,0:T(8,128)(2,1)S(1)} %pad_maximum_fusion.2), channel_id=1, source_target_pairs={{0,60},{1,65},{2,62},{3,67},{4,64},{5,69},{6,66},{7,71},{8,68},{9,... | collective-permute-start | bytes 393224 | tf_op jit(solution)/shard_map/ppermute | solution.py:107
  98.7 15.1 %collective-permute-start.9 = (bf16[8,256,256]{2,1,0:T(8,128)(2,1)}, bf16[8,256,256]{2,1,0:T(8,128)(2,1)}, u32[]{:S(2)}, u32[]{:S(2)}) collective-permute-start(bf16[8,256,256]{2,1,0:T(8,128)(2,1)} %bitcast_dynamic-update-slice_fusion), channel_id=1, source_target_pairs={{0,1},{1,0},{2,3},{3,2},{4,5},{5,4},{6,7},{7,6},{8,9},{9,8},{10,11... | collective-permute-start | bytes 3145736 | tf_op jit(solution)/shard_map/ppermute | solution.py:109
  103.9 34.2 %all-to-all-start.2 = ((bf16[32,48,384]{2,1,0:T(8,128)(2,1)}), bf16[32,48,384]{2,1,0:T(8,128)(2,1)S(1)}, u32[]{:S(2)}, u32[]{:S(2)}) async-start(bf16[32,48,384]{2,1,0:T(8,128)(2,1)} %broadcast_in_dim.54), calls=%async_computation.2 | async-start | bytes 2359296 | tf_op jit(solution)/shard_map/all_to_all | solution.py:47
  138.7 4.7 %copy-start.9 = (s32[256,4]{0,1:T(4,128)S(1)}, s32[256,4]{0,1:T(4,128)}, u32[]{:S(2)}) copy-start(s32[256,4]{0,1:T(4,128)} %param.15) | copy-start | bytes 12292
  139.7 14.5 %all-to-all-start.3 = ((bf16[256,4,384]{2,0,1:T(8,128)(2,1)}), bf16[256,4,384]{2,0,1:T(8,128)(2,1)S(1)}, u32[]{:S(2)}, u32[]{:S(2)}) async-start(bf16[256,4,384]{2,0,1:T(8,128)(2,1)} %bitcast.115), calls=%async_computation.3 | async-start | bytes 1572864 | tf_op jit(solution)/shard_map/all_to_all | solution.py:159
  143.5 10.9 %copy-start.2 = (bf16[256,384]{1,0:T(8,128)(2,1)S(1)}, bf16[256,384]{1,0:T(8,128)(2,1)}, u32[]{:S(2)}) copy-start(bf16[256,384]{1,0:T(8,128)(2,1)} %param.10) | copy-start | bytes 589828
  202.3 5.9 %copy-start.8 = (f32[256,4]{0,1:T(4,128)S(1)}, f32[256,4]{0,1:T(4,128)}, u32[]{:S(2)}) copy-start(f32[256,4]{0,1:T(4,128)} %param.16) | copy-start | bytes 12292
  202.3 30.1 %all-to-all-start.5 = ((bf16[128,16,384]{2,1,0:T(8,128)(2,1)}), bf16[128,16,384]{2,1,0:T(8,128)(2,1)}, u32[]{:S(2)}, u32[]{:S(2)}) async-start(bf16[128,16,384]{2,1,0:T(8,128)(2,1)} %bitcast.41), calls=%async_computation.5 | async-start | bytes 3145728 | tf_op jit(solution)/shard_map/all_to_all | solution.py:219
  (3 other events, 6.6 us)
Sparse Core Ops, SparseCore 0:
  16.1 95.7 all-gather.1
